TPU v7x, 32 devices: a whole 2x2x4 slice. The times are simulated.
32 devices in a mesh: brick: 4 (over z), batch: 8 (over y, x, core).
Axes of the slice: x: 2, y: 2, z: 4, core: 2. Of those that a mesh axis runs over, the one named last changes fastest.
Arguments:
- coarse: bfloat16 [8, 4, 4, 8, 1024], P('batch', 'brick'), may hold values from -6 to 6
- coarse_mask: int32 [8, 4, 256], P('batch', 'brick'), may hold values 0 or 1
- skip: bfloat16 [8, 4, 8, 16, 1024], P('batch', 'brick'), may hold values from -6 to 6
- fine_mask: int32 [8, 4, 2048], P('batch', 'brick'), may hold values 0 or 1
- up_weight: bfloat16 [27, 64, 128], replicated, may hold values from -0.25 to 0.25
- fine_grad: bfloat16 [8, 4, 8, 16, 1024], P('batch', 'brick'), may hold values from -6 to 6
Outputs:
- fine_out: bfloat16 [8, 4, 8, 16, 1024], P('batch', 'brick')
- coarse_grad: bfloat16 [8, 4, 4, 8, 1024], P('batch', 'brick')
- weight_grad: float32 [27, 64, 128], replicated
All inputs are finite; a program needn't handle non-finite values. No bound on the sum of `coarse_mask` or of `fine_mask` on one device may be relied on, other than what follows from the above.
Results may differ from a plain program's by a relative error of at most 0.0035.
Values may be sent and summed in bfloat16 or wider, within the bound.
No kernel may reach another device: no remote copies, remote signals or barrier semaphores. Data moves between devices by JAX's collectives and lax.ppermute only.
A program may use at most 64 MiB of HBM per device.

v0:
```python
import math

import jax
import jax.numpy as jnp
from jax import lax
from jax.sharding import PartitionSpec as P

EVEN_TAPS = ((1, 0),)
ODD_TAPS = ((2, 0), (0, 1))
DIRECTIONS = ((1, 0, 0), (0, 1, 0), (0, 0, 1), (1, 1, 0), (1, 0, 1), (0, 1, 1), (1, 1, 1))
STRIDES = (4, 2, 1)


def from_behind(shard, axis, by):
    size = lax.axis_size(axis)
    pairs = [(i, i + by) for i in range(size) if 0 <= i + by < size]
    return lax.ppermute(shard, axis, pairs)


def tap_pairs(parity):
    if parity == 0:
        return EVEN_TAPS
    return ODD_TAPS


def spread(padded, weight):
    counts = (padded.shape[0] - 1, padded.shape[1] - 1, padded.shape[2] - 1)
    outputs = weight.shape[1]
    parts = []
    for parity_x in range(2):
        for parity_y in range(2):
            for parity_z in range(2):
                total = jnp.zeros(counts + (outputs,), jnp.float32)
                for tap_x, start_x in tap_pairs(parity_x):
                    for tap_y, start_y in tap_pairs(parity_y):
                        for tap_z, start_z in tap_pairs(parity_z):
                            window = padded[
                                start_x : start_x + counts[0],
                                start_y : start_y + counts[1],
                                start_z : start_z + counts[2],
                            ]
                            total = total + jnp.einsum(
                                "abci,oi->abco",
                                window,
                                weight[9 * tap_x + 3 * tap_y + tap_z],
                                preferred_element_type=jnp.float32,
                            )
                parts.append(total)
    stacked = jnp.stack(parts).reshape((2, 2, 2) + counts + (outputs,))
    return stacked.transpose(3, 0, 4, 1, 5, 2, 6).reshape(
        2 * counts[0], 2 * counts[1], 2 * counts[2], outputs
    )


def pick(field, tap, count, axis):
    return lax.slice_in_dim(field, tap, tap + 2 * count - 1, 2, axis)


def adjoint(widened, masked, weight):
    counts = masked.shape[:3]
    back = jnp.zeros(masked.shape, jnp.float32)
    grads = []
    for tap_x in range(3):
        along_x = pick(widened, tap_x, counts[0], 0)
        for tap_y in range(3):
            along_y = pick(along_x, tap_y, counts[1], 1)
            for tap_z in range(3):
                chosen = pick(along_y, tap_z, counts[2], 2)
                index = 9 * tap_x + 3 * tap_y + tap_z
                back = back + jnp.einsum(
                    "abco,oi->abci", chosen, weight[index], preferred_element_type=jnp.float32
                )
                grads.append(
                    jnp.einsum("abco,abci->oi", chosen, masked, preferred_element_type=jnp.float32)
                )
    return (back, jnp.stack(grads))


def offset(direction):
    return 4 * direction[0] + 2 * direction[1] + direction[2]


def allowed(direction, grid_y, grid_z, side):
    result = grid_y >= 0
    if direction[1]:
        result = result & (grid_y == side)
    if direction[2]:
        result = result & (grid_z == side)
    return result


def flatten(piece):
    return piece.reshape(piece.shape[0], -1)


def segment_index(other, axis, edge):
    if other < axis:
        return slice(1, None)
    if other > axis:
        return slice(None)
    return edge


def unit_of(axis):
    return tuple((1 if other == axis else 0 for other in range(3)))


def body(coarse, coarse_mask, skip, fine_mask, up_weight, fine_grad):
    rank = lax.axis_index("brick")
    grid_y = rank // 2 % 2
    grid_z = rank % 2
    size_x, size_y, merged = coarse.shape[2:]
    channels_out = up_weight.shape[1]
    channels_in = up_weight.shape[2]
    size_z = merged // channels_in
    fine_x, fine_y, fine_merged = skip.shape[2:]
    fine_z = fine_merged // channels_out
    coarse_keep = coarse_mask.reshape(size_x, size_y, size_z, 1).astype(jnp.bfloat16)
    masked = coarse.reshape(size_x, size_y, size_z, channels_in) * coarse_keep
    extended = spread(jnp.pad(masked, ((1, 1), (1, 1), (1, 1), (0, 0))), up_weight)[1:, 1:, 1:]
    for axis in range(3):
        source = tuple((segment_index(other, axis, slice(0, 1)) for other in range(3)))
        piece = extended[source]
        got = from_behind(flatten(piece).astype(jnp.bfloat16), "brick", -STRIDES[axis]).astype(
            jnp.float32
        )
        got = jnp.where(allowed(unit_of(axis), grid_y, grid_z, 0), got, 0.0).reshape(piece.shape)
        target = tuple((segment_index(other, axis, slice(-1, None)) for other in range(3)))
        extended = extended.at[target].add(got)
    up = extended[1:, 1:, 1:]
    fine_keep = fine_mask.reshape(fine_x, fine_y, fine_z, 1)
    fine = fine_keep.astype(jnp.float32) * (
        skip.reshape(fine_x, fine_y, fine_z, channels_out).astype(jnp.float32) + up
    )
    fine_out = fine.astype(jnp.bfloat16).reshape(skip.shape)
    cotangent = fine_grad.reshape(fine_x, fine_y, fine_z, channels_out) * fine_keep.astype(
        jnp.bfloat16
    )
    widened = jnp.pad(cotangent, ((1, 0), (1, 0), (1, 0), (0, 0)))
    for direction in DIRECTIONS:
        source = tuple((slice(-1, None) if flag else slice(None) for flag in direction))
        piece = cotangent[source]
        got = from_behind(flatten(piece), "brick", offset(direction))
        got = jnp.where(allowed(direction, grid_y, grid_z, 1), got, 0.0).reshape(piece.shape)
        target = tuple((slice(0, 1) if flag else slice(1, None) for flag in direction))
        widened = widened.at[target].set(got)
    back, grads = adjoint(widened, masked, up_weight)
    coarse_grad = (
        (back * coarse_keep.astype(jnp.float32)).astype(jnp.bfloat16).reshape(coarse.shape)
    )
    summed = lax.psum(grads, ("brick", "batch"))
    scale = 1.0 / math.sqrt(
        lax.axis_size("brick") * lax.axis_size("batch") * size_x * size_y * size_z
    )
    return (fine_out, coarse_grad, summed * scale)


def solution(mesh):
    in_specs = (
        P("batch", "brick", None, None, None),
        P("batch", "brick", None),
        P("batch", "brick", None, None, None),
        P("batch", "brick", None),
        P(),
        P("batch", "brick", None, None, None),
    )
    out_specs = (P("batch", "brick", None, None, None), P("batch", "brick", None, None, None), P())
    return jax.shard_map(body, mesh=mesh, in_specs=in_specs, out_specs=out_specs, check_vma=False)
```

profile of v0, /device:TPU:0, one launch (start us, length us, event | category | flops | bytes accessed | tf_op | source)
XLA Modules:
  0.0 260.1 jit_solution(2375744965565836065)
XLA Ops:
  7.2 1.4 reshape.523
  11.3 5.9 %collective-permute-start.4 = (bf16[8,1024]{1,0:T(8,128)(2,1)S(1)}, bf16[8,1024]{1,0:T(8,128)(2,1)S(1)}, u32[]{:S(2)}, u32[]{:S(2)}) collective-permute-start(bf16[8,1024]{1,0:T(8,128)(2,1)S(1)} %reshape.526), channel_id=1, source_target_pairs={{0,16},{8,24},{1,17},{9,25},{2,18},{10,26},{3,19},{11,27},{4,20},{... | collective-permute-start | bytes 49160 | tf_op jit(solution)/shard_map/ppermute | solution.py:17
  17.6 3.5 %collective-permute-start.5 = (bf16[8,1024]{1,0:T(8,128)(2,1)S(1)}, bf16[8,1024]{1,0:T(8,128)(2,1)S(1)}, u32[]{:S(2)}, u32[]{:S(2)}) collective-permute-start(bf16[8,1024]{1,0:T(8,128)(2,1)S(1)} %reshape.528), channel_id=1, source_target_pairs={{0,8},{8,16},{16,24},{1,9},{9,17},{17,25},{2,10},{10,18},{18,26},{... | collective-permute-start | bytes 49160 | tf_op jit(solution)/shard_map/ppermute | solution.py:17
  31.6 2.0 copy.82
  33.7 2.4 reshape.518
  36.1 1.5 slice.770
  37.6 1.3 pad.47
  39.8 2.2 reshape.539
  42.7 1.3 collective-permute-start.8
  44.0 1.3 collective-permute-done.8
  46.0 1.3 collective-permute-start
  48.5 1.4 scatter.26
  50.5 1.1 fusion.189
  51.6 1.3 slice.733
  53.0 1.3 slice.734
  54.2 1.3 slice.735
  55.5 1.3 slice.737
  56.8 1.3 slice.738
  58.1 1.3 slice.739
  59.4 1.3 slice.741
  60.6 1.3 slice.742
  61.9 1.3 slice.743
  63.2 2.4 fusion.190
  65.6 2.8 %slice.746 = bf16[4,8,8,64]{3,2,1,0:T(8,128)(2,1)} slice(bf16[4,8,17,64]{3,2,1,0:T(8,128)(2,1)} %get-tuple-element.135), slice={[0:4:1], [0:8:1], [0:15:2], [0:64:1]} | slice | bytes 65536 | tf_op jit(solution)/shard_map/slice | solution.py:56
  68.4 2.8 %slice.747 = bf16[4,8,8,64]{3,2,1,0:T(8,128)(2,1)} slice(bf16[4,8,17,64]{3,2,1,0:T(8,128)(2,1)} %get-tuple-element.135), slice={[0:4:1], [0:8:1], [1:16:2], [0:64:1]} | slice | bytes 65536 | tf_op jit(solution)/shard_map/slice | solution.py:56
  71.1 2.8 %slice.748 = bf16[4,8,8,64]{3,2,1,0:T(8,128)(2,1)} slice(bf16[4,8,17,64]{3,2,1,0:T(8,128)(2,1)} %get-tuple-element.135), slice={[0:4:1], [0:8:1], [2:17:2], [0:64:1]} | slice | bytes 65536 | tf_op jit(solution)/shard_map/slice | solution.py:56
  74.0 2.8 %slice.750 = bf16[4,8,8,64]{3,2,1,0:T(8,128)(2,1)} slice(bf16[4,8,17,64]{3,2,1,0:T(8,128)(2,1)} %get-tuple-element.136), slice={[0:4:1], [0:8:1], [0:15:2], [0:64:1]} | slice | bytes 65536 | tf_op jit(solution)/shard_map/slice | solution.py:56
  76.7 2.7 %slice.751 = bf16[4,8,8,64]{3,2,1,0:T(8,128)(2,1)} slice(bf16[4,8,17,64]{3,2,1,0:T(8,128)(2,1)} %get-tuple-element.136), slice={[0:4:1], [0:8:1], [1:16:2], [0:64:1]} | slice | bytes 65536 | tf_op jit(solution)/shard_map/slice | solution.py:56
  79.5 2.8 %slice.752 = bf16[4,8,8,64]{3,2,1,0:T(8,128)(2,1)} slice(bf16[4,8,17,64]{3,2,1,0:T(8,128)(2,1)} %get-tuple-element.136), slice={[0:4:1], [0:8:1], [2:17:2], [0:64:1]} | slice | bytes 65536 | tf_op jit(solution)/shard_map/slice | solution.py:56
  82.3 1.3 slice.754
  83.6 1.3 slice.755
  84.9 1.3 slice.756
  86.1 1.3 slice.759
  87.4 1.3 slice.760
  88.7 1.3 slice.761
  91.1 1.7 fusion.43
  92.9 1.0 fusion.110
  93.9 1.7 fusion.42
  95.6 1.7 fusion.41
  97.3 1.7 fusion.40
  98.9 1.7 fusion.39
  104.7 1.7 fusion.33
  106.4 1.7 fusion.32
  120.4 1.0 convolution_add_fusion.44
  121.4 1.0 convolution_add_fusion.43
  122.5 1.0 convolution_add_fusion.42
  123.5 1.0 convolution_add_fusion.41
  126.9 1.0 convolution_add_fusion.35
  127.9 1.0 convolution_add_fusion.34
  136.7 1.5 convolution_add_fusion.21
  138.3 1.7 fusion.48
  142.7 1.3 collective-permute-start.1
  144.0 1.1 convolution_add_fusion.20
  145.1 4.1 %collective-permute-done.1 = bf16[8,1088]{1,0:T(8,128)(2,1)S(1)} collective-permute-done((bf16[8,1088]{1,0:T(8,128)(2,1)S(1)}, bf16[8,1088]{1,0:T(8,128)(2,1)S(1)}, u32[]{:S(2)}, u32[]{:S(2)}) %collective-permute-start.1) | collective-permute-done | bytes 17440 | tf_op jit(solution)/shard_map/ppermute | solution.py:17
  149.3 1.6 fusion.47
  150.9 1.2 fusion.50
  152.2 1.3 collective-permute-start.2
  155.1 2.8 %collective-permute-done.2 = bf16[8,1024]{1,0:T(8,128)(2,1)S(1)} collective-permute-done((bf16[8,1024]{1,0:T(8,128)(2,1)S(1)}, bf16[8,1024]{1,0:T(8,128)(2,1)S(1)}, u32[]{:S(2)}, u32[]{:S(2)}) %collective-permute-start.2) | collective-permute-done | bytes 16416 | tf_op jit(solution)/shard_map/ppermute | solution.py:17
  158.0 1.1 slice_add_fusion.3
  159.1 3.0 %scatter-add.14 = f32[9,17,17,64]{3,2,1,0:T(8,128)} dynamic-update-slice(f32[9,17,17,64]{3,2,1,0:T(8,128)} %fusion.47, f32[8,16,1,64]{3,2,1,0:T(1,128)S(1)} %slice_add_fusion.3, s32[]{:T(128)} %constant.355.clone.1, s32[]{:T(128)} %constant.355.clone.1, s32[]{:T(128)} %constant.361.clone.1, s32[]{:T(128)} %constant.356.clone.1) | dynamic-update-slice | bytes 65540 | tf_op jit(solution)/shard_map/scatter-add | solution.py:129
  162.1 1.7 fusion.45
  163.8 1.1 reshape.522
  164.9 86.2 %all-reduce.4.cloned.1.call-done = f32[27,64,128]{2,1,0:T(8,128)} async-done(((f32[27,64,128]{2,1,0:T(8,128)}), f32[27,64,128]{2,1,0:T(8,128)}) %all-reduce.4.cloned.1.call-update) | async-done | bytes 884752 | tf_op jit(solution)/shard_map/psum | solution.py:151
  251.1 2.2 broadcast_multiply_fusion
  (208 shorter events, 49.5 us)
Async XLA Ops:
  7.2 18.2 %copy-start.2 = (bf16[27,64,128]{2,1,0:T(8,128)(2,1)S(1)}, bf16[27,64,128]{2,1,0:T(8,128)(2,1)}, u32[]{:S(2)}) copy-start(bf16[27,64,128]{2,1,0:T(8,128)(2,1)} %param.30) | copy-start | bytes 1327108
  7.2 243.9 %all-reduce.4.cloned.1.call-start = ((), (), s32[]{:S(2)}) async-start(), calls=%async_computation | async-start | bytes 1769472 | tf_op jit(solution)/shard_map/psum | solution.py:151
  9.8 17.7 %copy-start.1 = (bf16[8,16,16,64]{3,2,1,0:T(8,128)(2,1)}, bf16[8,16,16,64]{3,2,1,0:T(8,128)(2,1)S(1)}, u32[]{:S(2)}) copy-start(bf16[8,16,16,64]{3,2,1,0:T(8,128)(2,1)S(1)} %broadcast_multiply_fusion.1) | copy-start | bytes 786436
  10.6 37.2 %collective-permute-start.3 = (bf16[1,16384]{1,0:T(2,128)(2,1)}, bf16[1,16384]{1,0:T(2,128)(2,1)S(1)}, u32[]{:S(2)}, u32[]{:S(2)}) collective-permute-start(bf16[1,16384]{1,0:T(2,128)(2,1)} %reshape.524), channel_id=1, source_target_pairs={} | collective-permute-start | bytes 98312 | tf_op jit(solution)/shard_map/ppermute | solution.py:17
  11.3 36.1 %collective-permute-start.4 = (bf16[8,1024]{1,0:T(8,128)(2,1)S(1)}, bf16[8,1024]{1,0:T(8,128)(2,1)S(1)}, u32[]{:S(2)}, u32[]{:S(2)}) collective-permute-start(bf16[8,1024]{1,0:T(8,128)(2,1)S(1)} %reshape.526), channel_id=1, source_target_pairs={{0,16},{8,24},{1,17},{9,25},{2,18},{10,26},{3,19},{11,27},{4,20},{... | collective-permute-start | bytes 49160 | tf_op jit(solution)/shard_map/ppermute | solution.py:17
  17.6 29.9 %collective-permute-start.5 = (bf16[8,1024]{1,0:T(8,128)(2,1)S(1)}, bf16[8,1024]{1,0:T(8,128)(2,1)S(1)}, u32[]{:S(2)}, u32[]{:S(2)}) collective-permute-start(bf16[8,1024]{1,0:T(8,128)(2,1)S(1)} %reshape.528), channel_id=1, source_target_pairs={{0,8},{8,16},{16,24},{1,9},{9,17},{17,25},{2,10},{10,18},{18,26},{... | collective-permute-start | bytes 49160 | tf_op jit(solution)/shard_map/ppermute | solution.py:17
  21.2 24.8 %collective-permute-start.6 = (bf16[1,1024]{1,0:T(2,128)(2,1)S(1)}, bf16[1,1024]{1,0:T(2,128)(2,1)S(1)}, u32[]{:S(2)}, u32[]{:S(2)}) collective-permute-start(bf16[1,1024]{1,0:T(2,128)(2,1)S(1)} %reshape.530), channel_id=1, source_target_pairs={} | collective-permute-start | bytes 6152 | tf_op jit(solution)/shard_map/ppermute | solution.py:17
  21.9 20.8 %collective-permute-start.9 = (bf16[1,64]{1,0:T(2,128)(2,1)S(1)}, bf16[1,64]{1,0:T(2,128)(2,1)S(1)}, u32[]{:S(2)}, u32[]{:S(2)}) collective-permute-start(bf16[1,64]{1,0:T(2,128)(2,1)S(1)} %slice_bitcast_fusion), channel_id=1, source_target_pairs={} | collective-permute-start | bytes 392 | tf_op jit(solution)/shard_map/ppermute | solution.py:17
  36.1 1.5 copy-start.34
  42.7 2.6 collective-permute-start.8
  45.3 2.0 collective-permute-start.7
  46.0 92.3 %collective-permute-start = (bf16[1,18496]{1,0:T(2,128)(2,1)}, bf16[1,18496]{1,0:T(2,128)(2,1)}, u32[]{:S(2)}, u32[]{:S(2)}) collective-permute-start(bf16[1,18496]{1,0:T(2,128)(2,1)} %convert_element_type.107), channel_id=1, source_target_pairs={} | collective-permute-start | bytes 110984 | tf_op jit(solution)/shard_map/ppermute | solution.py:17
  56.8 36.1 %copy-start.3 = (bf16[27,64,128]{2,1,0:T(8,128)(2,1)S(1)}, bf16[27,64,128]{2,1,0:T(8,128)(2,1)}, u32[]{:S(2)}) copy-start(bf16[27,64,128]{2,1,0:T(8,128)(2,1)} %param.30) | copy-start | bytes 1327108
  90.0 10.6 %copy-start.29 = (bf16[4,8,8,64]{3,2,1,0:T(8,128)(2,1)S(1)}, bf16[4,8,8,64]{3,2,1,0:T(8,128)(2,1)}, u32[]{:S(2)}) copy-start(bf16[4,8,8,64]{3,2,1,0:T(8,128)(2,1)} %slice.739) | copy-start | bytes 98308
  90.2 25.3 %copy-start.7 = (bf16[4,8,8,64]{3,2,1,0:T(8,128)(2,1)}, bf16[4,8,8,64]{3,2,1,0:T(8,128)(2,1)S(1)}, u32[]{:S(2)}) copy-start(bf16[4,8,8,64]{3,2,1,0:T(8,128)(2,1)S(1)} %slice.763) | copy-start | bytes 98308
  90.5 10.9 %copy-start.31 = (bf16[4,8,8,64]{3,2,1,0:T(8,128)(2,1)S(1)}, bf16[4,8,8,64]{3,2,1,0:T(8,128)(2,1)}, u32[]{:S(2)}) copy-start(bf16[4,8,8,64]{3,2,1,0:T(8,128)(2,1)} %slice.741) | copy-start | bytes 98308
  90.9 27.8 %copy-start.6 = (bf16[4,8,8,64]{3,2,1,0:T(8,128)(2,1)}, bf16[4,8,8,64]{3,2,1,0:T(8,128)(2,1)S(1)}, u32[]{:S(2)}) copy-start(bf16[4,8,8,64]{3,2,1,0:T(8,128)(2,1)S(1)} %slice.768) | copy-start | bytes 98308
  91.1 28.4 %copy-start.4 = (bf16[4,8,8,64]{3,2,1,0:T(8,128)(2,1)}, bf16[4,8,8,64]{3,2,1,0:T(8,128)(2,1)S(1)}, u32[]{:S(2)}) copy-start(bf16[4,8,8,64]{3,2,1,0:T(8,128)(2,1)S(1)} %slice.769) | copy-start | bytes 98308
  91.1 11.2 %copy-start.25 = (bf16[4,8,8,64]{3,2,1,0:T(8,128)(2,1)S(1)}, bf16[4,8,8,64]{3,2,1,0:T(8,128)(2,1)}, u32[]{:S(2)}) copy-start(bf16[4,8,8,64]{3,2,1,0:T(8,128)(2,1)} %slice.742) | copy-start | bytes 98308
  91.1 12.0 %copy-start.21 = (bf16[4,8,8,64]{3,2,1,0:T(8,128)(2,1)S(1)}, bf16[4,8,8,64]{3,2,1,0:T(8,128)(2,1)}, u32[]{:S(2)}) copy-start(bf16[4,8,8,64]{3,2,1,0:T(8,128)(2,1)} %slice.743) | copy-start | bytes 98308
  91.1 12.8 %copy-start.33 = (bf16[4,8,8,64]{3,2,1,0:T(8,128)(2,1)S(1)}, bf16[4,8,8,64]{3,2,1,0:T(8,128)(2,1)}, u32[]{:S(2)}) copy-start(bf16[4,8,8,64]{3,2,1,0:T(8,128)(2,1)} %slice.746) | copy-start | bytes 98308
  91.1 16.9 %copy-start.32 = (bf16[4,8,8,64]{3,2,1,0:T(8,128)(2,1)S(1)}, bf16[4,8,8,64]{3,2,1,0:T(8,128)(2,1)}, u32[]{:S(2)}) copy-start(bf16[4,8,8,64]{3,2,1,0:T(8,128)(2,1)} %slice.750) | copy-start | bytes 98308
  92.9 16.0 %copy-start.27 = (bf16[4,8,8,64]{3,2,1,0:T(8,128)(2,1)S(1)}, bf16[4,8,8,64]{3,2,1,0:T(8,128)(2,1)}, u32[]{:S(2)}) copy-start(bf16[4,8,8,64]{3,2,1,0:T(8,128)(2,1)} %slice.751) | copy-start | bytes 98308
  95.6 14.1 %copy-start.23 = (bf16[4,8,8,64]{3,2,1,0:T(8,128)(2,1)S(1)}, bf16[4,8,8,64]{3,2,1,0:T(8,128)(2,1)}, u32[]{:S(2)}) copy-start(bf16[4,8,8,64]{3,2,1,0:T(8,128)(2,1)} %slice.752) | copy-start | bytes 98308
  97.3 13.3 %copy-start.19 = (bf16[4,8,8,64]{3,2,1,0:T(8,128)(2,1)S(1)}, bf16[4,8,8,64]{3,2,1,0:T(8,128)(2,1)}, u32[]{:S(2)}) copy-start(bf16[4,8,8,64]{3,2,1,0:T(8,128)(2,1)} %slice.754) | copy-start | bytes 98308
  98.9 12.4 %copy-start.17 = (bf16[4,8,8,64]{3,2,1,0:T(8,128)(2,1)S(1)}, bf16[4,8,8,64]{3,2,1,0:T(8,128)(2,1)}, u32[]{:S(2)}) copy-start(bf16[4,8,8,64]{3,2,1,0:T(8,128)(2,1)} %slice.755) | copy-start | bytes 98308
  100.6 11.5 %copy-start.15 = (bf16[4,8,8,64]{3,2,1,0:T(8,128)(2,1)S(1)}, bf16[4,8,8,64]{3,2,1,0:T(8,128)(2,1)}, u32[]{:S(2)}) copy-start(bf16[4,8,8,64]{3,2,1,0:T(8,128)(2,1)} %slice.756) | copy-start | bytes 98308
  101.5 11.5 %copy-start.13 = (bf16[4,8,8,64]{3,2,1,0:T(8,128)(2,1)S(1)}, bf16[4,8,8,64]{3,2,1,0:T(8,128)(2,1)}, u32[]{:S(2)}) copy-start(bf16[4,8,8,64]{3,2,1,0:T(8,128)(2,1)} %slice.759) | copy-start | bytes 98308
  102.3 11.5 %copy-start.11 = (bf16[4,8,8,64]{3,2,1,0:T(8,128)(2,1)S(1)}, bf16[4,8,8,64]{3,2,1,0:T(8,128)(2,1)}, u32[]{:S(2)}) copy-start(bf16[4,8,8,64]{3,2,1,0:T(8,128)(2,1)} %slice.760) | copy-start | bytes 98308
  103.1 11.5 %copy-start.9 = (bf16[4,8,8,64]{3,2,1,0:T(8,128)(2,1)S(1)}, bf16[4,8,8,64]{3,2,1,0:T(8,128)(2,1)}, u32[]{:S(2)}) copy-start(bf16[4,8,8,64]{3,2,1,0:T(8,128)(2,1)} %slice.761) | copy-start | bytes 98308
  113.8 10.7 %copy-start.30 = (bf16[4,8,8,64]{3,2,1,0:T(8,128)(2,1)S(1)}, bf16[4,8,8,64]{3,2,1,0:T(8,128)(2,1)}, u32[]{:S(2)}) copy-start(bf16[4,8,8,64]{3,2,1,0:T(8,128)(2,1)} %slice.739) | copy-start | bytes 98308
  115.4 10.2 %copy-start.26 = (bf16[4,8,8,64]{3,2,1,0:T(8,128)(2,1)S(1)}, bf16[4,8,8,64]{3,2,1,0:T(8,128)(2,1)}, u32[]{:S(2)}) copy-start(bf16[4,8,8,64]{3,2,1,0:T(8,128)(2,1)} %slice.742) | copy-start | bytes 98308
  116.2 9.6 %copy-start.22 = (bf16[4,8,8,64]{3,2,1,0:T(8,128)(2,1)S(1)}, bf16[4,8,8,64]{3,2,1,0:T(8,128)(2,1)}, u32[]{:S(2)}) copy-start(bf16[4,8,8,64]{3,2,1,0:T(8,128)(2,1)} %slice.743) | copy-start | bytes 98308
  118.7 11.2 %copy-start.28 = (bf16[4,8,8,64]{3,2,1,0:T(8,128)(2,1)S(1)}, bf16[4,8,8,64]{3,2,1,0:T(8,128)(2,1)}, u32[]{:S(2)}) copy-start(bf16[4,8,8,64]{3,2,1,0:T(8,128)(2,1)} %slice.751) | copy-start | bytes 98308
  119.5 10.6 %copy-start.24 = (bf16[4,8,8,64]{3,2,1,0:T(8,128)(2,1)S(1)}, bf16[4,8,8,64]{3,2,1,0:T(8,128)(2,1)}, u32[]{:S(2)}) copy-start(bf16[4,8,8,64]{3,2,1,0:T(8,128)(2,1)} %slice.752) | copy-start | bytes 98308
  120.3 9.9 %copy-start.20 = (bf16[4,8,8,64]{3,2,1,0:T(8,128)(2,1)S(1)}, bf16[4,8,8,64]{3,2,1,0:T(8,128)(2,1)}, u32[]{:S(2)}) copy-start(bf16[4,8,8,64]{3,2,1,0:T(8,128)(2,1)} %slice.754) | copy-start | bytes 98308
  120.3 10.1 %copy-start.18 = (bf16[4,8,8,64]{3,2,1,0:T(8,128)(2,1)S(1)}, bf16[4,8,8,64]{3,2,1,0:T(8,128)(2,1)}, u32[]{:S(2)}) copy-start(bf16[4,8,8,64]{3,2,1,0:T(8,128)(2,1)} %slice.755) | copy-start | bytes 98308
  120.4 10.2 %copy-start.16 = (bf16[4,8,8,64]{3,2,1,0:T(8,128)(2,1)S(1)}, bf16[4,8,8,64]{3,2,1,0:T(8,128)(2,1)}, u32[]{:S(2)}) copy-start(bf16[4,8,8,64]{3,2,1,0:T(8,128)(2,1)} %slice.756) | copy-start | bytes 98308
  120.4 11.2 %copy-start.14 = (bf16[4,8,8,64]{3,2,1,0:T(8,128)(2,1)S(1)}, bf16[4,8,8,64]{3,2,1,0:T(8,128)(2,1)}, u32[]{:S(2)}) copy-start(bf16[4,8,8,64]{3,2,1,0:T(8,128)(2,1)} %slice.759) | copy-start | bytes 98308
  121.4 11.0 %copy-start.12 = (bf16[4,8,8,64]{3,2,1,0:T(8,128)(2,1)S(1)}, bf16[4,8,8,64]{3,2,1,0:T(8,128)(2,1)}, u32[]{:S(2)}) copy-start(bf16[4,8,8,64]{3,2,1,0:T(8,128)(2,1)} %slice.760) | copy-start | bytes 98308
  122.5 10.8 %copy-start.10 = (bf16[4,8,8,64]{3,2,1,0:T(8,128)(2,1)S(1)}, bf16[4,8,8,64]{3,2,1,0:T(8,128)(2,1)}, u32[]{:S(2)}) copy-start(bf16[4,8,8,64]{3,2,1,0:T(8,128)(2,1)} %slice.761) | copy-start | bytes 98308
  123.5 10.7 %copy-start.8 = (bf16[4,8,8,64]{3,2,1,0:T(8,128)(2,1)S(1)}, bf16[4,8,8,64]{3,2,1,0:T(8,128)(2,1)}, u32[]{:S(2)}) copy-start(bf16[4,8,8,64]{3,2,1,0:T(8,128)(2,1)} %copy-done.7) | copy-start | bytes 98308
  130.1 23.4 %copy-start.5 = (bf16[4,8,8,64]{3,2,1,0:T(8,128)(2,1)S(1)}, bf16[4,8,8,64]{3,2,1,0:T(8,128)(2,1)}, u32[]{:S(2)}) copy-start(bf16[4,8,8,64]{3,2,1,0:T(8,128)(2,1)} %copy-done.4) | copy-start | bytes 98308
  130.6 31.5 %copy-start = (f32[8,16,16,64]{3,2,1,0:T(8,128)S(1)}, f32[8,16,16,64]{3,2,1,0:T(8,128)}, u32[]{:S(2)}) copy-start(f32[8,16,16,64]{3,2,1,0:T(8,128)} %reshape.539) | copy-start | bytes 1572868
  142.7 6.5 %collective-permute-start.1 = (bf16[8,1088]{1,0:T(8,128)(2,1)S(1)}, bf16[8,1088]{1,0:T(8,128)(2,1)S(1)}, u32[]{:S(2)}, u32[]{:S(2)}) collective-permute-start(bf16[8,1088]{1,0:T(8,128)(2,1)S(1)} %convert_element_type.109), channel_id=1, source_target_pairs={{16,0},{24,8},{17,1},{25,9},{18,2},{26,10},{19,3},{27,11},{20,4},{... | collective-permute-start | bytes 52232 | tf_op jit(solution)/shard_map/ppermute | solution.py:17
  152.2 5.6 %collective-permute-start.2 = (bf16[8,1024]{1,0:T(8,128)(2,1)S(1)}, bf16[8,1024]{1,0:T(8,128)(2,1)S(1)}, u32[]{:S(2)}, u32[]{:S(2)}) collective-permute-start(bf16[8,1024]{1,0:T(8,128)(2,1)S(1)} %convert_element_type.111), channel_id=1, source_target_pairs={{8,0},{16,8},{24,16},{9,1},{17,9},{25,17},{10,2},{18,10},{26,18},{... | collective-permute-start | bytes 49160 | tf_op jit(solution)/shard_map/ppermute | solution.py:17
Sparse Core Ops, SparseCore 0:
  120.5 130.5 all-reduce.3
where the time goes:
time: 263 us; the launch traced here: 260 us
  waiting for transfers between devices  94.5 us (36%)
  local copies, waits for them, and re-layouts  65.6 us (25%)
  matrix products  55.9 us (21%)
  starting transfers between devices  17.2 us (7%)
  between operations  14.9 us (6%)
  other arithmetic  12.1 us (5%)
    psum x1, waiting for transfers between devices, body(): summed = lax.psum(grads, ('brick', 'batch'))  86.2 us
    slice x30, local copies, waits for them, and re-layouts, pick(): return lax.slice_in_dim(field, tap, tap + 2 * count - 1, 2, axis)  40.5 us
    dot_general x27, matrix products, adjoint(): jnp.einsum('abco,abci->oi', chosen, masked, preferred_element_type=jnp.fl...  28.1 us
    dot_general x27, matrix products, adjoint(): jnp.einsum('abco,oi->abci', chosen, weight[index], preferred_element_type...  20.8 us
    ppermute x10, starting transfers between devices, from_behind(): return lax.ppermute(shard, axis, pairs)  17.2 us
    ppermute x10, waiting for transfers between devices, from_behind(): return lax.ppermute(shard, axis, pairs)  8.22 us
    dot_general x27, matrix products, spread(): jnp.einsum('abci,oi->abco', window, weight[9 * tap_x + 3 * tap_y + tap_z]...  7.06 us
  transfers between devices with their start and end apart: 11, of which 4 were waited for; matrix products, arithmetic and copies ran while one was open for 49% of the time, Pallas kernels for 0%

commit v1 on v0

v1 whole, which is shorter than its diff:
```python
import math

import jax
import jax.numpy as jnp
from jax import lax
from jax.sharding import PartitionSpec as P

OFFSETS = tuple((dx, dy, dz) for dx in range(2) for dy in range(2) for dz in range(2))
DIRECTIONS = OFFSETS[1:]
AXES = ("brick", "batch")


def region_of(rank):
    return (rank // 4, rank // 2 % 2, rank % 2)


def neighbour_pairs(regions, direction, sign):
    grid = (regions // 4, 2, 2)
    pairs = []
    for dst in range(regions):
        spot = region_of(dst)
        src = tuple(spot[a] + sign * direction[a] for a in range(3))
        if all(0 <= src[a] < grid[a] for a in range(3)):
            pairs.append((4 * src[0] + 2 * src[1] + src[2], dst))
    return pairs


def exchange(piece, regions, direction, sign):
    pairs = neighbour_pairs(regions, direction, sign)
    if not pairs:
        return jnp.zeros_like(piece)
    return lax.ppermute(piece, "brick", pairs)


def forward_tap(d, p):
    k = p + 1 - 2 * d
    return k if 0 <= k <= 2 else None


def forward_weight(up_weight):
    zero = jnp.zeros(up_weight.shape[1:], up_weight.dtype)
    rows = []
    for d in OFFSETS:
        row = []
        for p in OFFSETS:
            taps = [forward_tap(d[a], p[a]) for a in range(3)]
            if any(t is None for t in taps):
                row.append(zero)
            else:
                row.append(up_weight[9 * taps[0] + 3 * taps[1] + taps[2]])
        rows.append(jnp.stack(row))
    return jnp.stack(rows)


def all_reduce(grads):
    devices = lax.axis_size("brick") * lax.axis_size("batch")
    flat = grads.reshape(-1)
    size = flat.shape[0]
    chunk = -(-size // devices)
    flat = jnp.pad(flat, (0, chunk * devices - size))
    parts = lax.all_to_all(flat.reshape(devices, chunk), AXES, 0, 0, tiled=True)
    return parts.sum(axis=0), (devices, chunk, size)


def all_spread(reduced, plan):
    devices, chunk, size = plan
    spread = jnp.broadcast_to(reduced[None], (devices, chunk))
    whole = lax.all_to_all(spread, AXES, 0, 0, tiled=True)
    return whole.reshape(-1)[:size]


def body(coarse, coarse_mask, skip, fine_mask, up_weight, fine_grad):
    regions = lax.axis_size("brick")
    size_x, size_y, merged = coarse.shape[2:]
    channels_out = up_weight.shape[1]
    channels_in = up_weight.shape[2]
    size_z = merged // channels_in
    fine_x, fine_y, fine_merged = skip.shape[2:]
    fine_z = fine_merged // channels_out
    counts = (size_x, size_y, size_z)

    coarse_keep = coarse_mask.reshape(size_x, size_y, size_z, 1).astype(jnp.bfloat16)
    masked = coarse.reshape(size_x, size_y, size_z, channels_in) * coarse_keep
    fine_keep = fine_mask.reshape(fine_x, fine_y, fine_z, 1)
    cotangent = fine_grad.reshape(fine_x, fine_y, fine_z, channels_out) * fine_keep.astype(
        jnp.bfloat16
    )

    widened = jnp.pad(cotangent, ((1, 1), (1, 1), (1, 1), (0, 0)))
    for direction in DIRECTIONS:
        source = tuple(slice(-1, None) if flag else slice(None) for flag in direction)
        got = exchange(cotangent[source], regions, direction, -1)
        target = tuple(
            slice(0, 1) if flag else slice(1, 1 + cotangent.shape[a])
            for a, flag in enumerate(direction)
        )
        widened = widened.at[target].set(got)
    extended = jnp.pad(masked, ((0, 1), (0, 1), (0, 1), (0, 0)))
    for direction in DIRECTIONS:
        source = tuple(slice(0, 1) if flag else slice(None) for flag in direction)
        got = exchange(masked[source], regions, direction, 1)
        target = tuple(
            slice(counts[a], counts[a] + 1) if flag else slice(0, counts[a])
            for a, flag in enumerate(direction)
        )
        extended = extended.at[target].set(got)

    paired = widened.reshape(size_x + 1, 2, size_y + 1, 2, size_z + 1, 2, channels_out)
    windows = []
    for kx in range(3):
        for ky in range(3):
            for kz in range(3):
                index = []
                for k, count in zip((kx, ky, kz), counts):
                    start = 1 if k == 2 else 0
                    index += [slice(start, start + count), 0 if k != 1 else 1]
                windows.append(paired[tuple(index)])
    gathered = jnp.stack(windows)
    grads = jnp.einsum(
        "kabco,abci->koi", gathered, masked, preferred_element_type=jnp.float32
    )
    reduced, plan = all_reduce(grads)

    back = jnp.einsum(
        "kabco,koi->abci", gathered, up_weight, preferred_element_type=jnp.float32
    )
    coarse_grad = (
        (back * coarse_keep.astype(jnp.float32)).astype(jnp.bfloat16).reshape(coarse.shape)
    )

    shifted = jnp.stack(
        [
            extended[dx : dx + size_x, dy : dy + size_y, dz : dz + size_z]
            for dx, dy, dz in OFFSETS
        ]
    )
    parities = jnp.einsum(
        "dabci,dpoi->abcpo",
        shifted,
        forward_weight(up_weight),
        preferred_element_type=jnp.float32,
    )
    up = (
        parities.reshape(size_x, size_y, size_z, 2, 2, 2, channels_out)
        .transpose(0, 3, 1, 4, 2, 5, 6)
        .reshape(fine_x, fine_y, fine_z, channels_out)
    )
    fine = fine_keep.astype(jnp.float32) * (
        skip.reshape(fine_x, fine_y, fine_z, channels_out).astype(jnp.float32) + up
    )
    fine_out = fine.astype(jnp.bfloat16).reshape(skip.shape)

    scale = 1.0 / math.sqrt(regions * lax.axis_size("batch") * size_x * size_y * size_z)
    weight_grad = all_spread(reduced * scale, plan).reshape(grads.shape)
    return (fine_out, coarse_grad, weight_grad)


def solution(mesh):
    in_specs = (
        P("batch", "brick", None, None, None),
        P("batch", "brick", None),
        P("batch", "brick", None, None, None),
        P("batch", "brick", None),
        P(),
        P("batch", "brick", None, None, None),
    )
    out_specs = (P("batch", "brick", None, None, None), P("batch", "brick", None, None, None), P())
    return jax.shard_map(body, mesh=mesh, in_specs=in_specs, out_specs=out_specs, check_vma=False)
```

time: 263 us -> 93.7 us (0.36)
  waiting for transfers between devices: 94.5 us -> 36.2 us
  matrix products: 55.9 us -> 5.63 us
  local copies, waits for them, and re-layouts: 65.6 us -> 16.8 us
  between operations: 14.9 us -> 1.4 us
  starting transfers between devices: 17.2 us -> 26.1 us
  other arithmetic: 12.1 us -> 6.93 us
    psum x1 -> x0, waiting for transfers between devices: 86.2 us -> none  [body(): summed = lax.psum(grads, ('brick', 'batch'))]
    dot_general x81 -> x3, matrix products: 55.9 us -> 5.63 us  [the longest x1 2.07 us: body(): jnp.einsum('kabco,koi->abci', gathered, up_weight, preferred_element_type...]
    slice x40 -> x10, local copies, waits for them, and re-layouts: 44.4 us -> 3.96 us  [the longest x2 3.81 us: body(): windows.append(paired[tuple(index)])]
    all_to_all x0 -> x2, waiting for transfers between devices: none -> 36.2 us  [the longest x1 21.6 us: all_reduce(): parts = lax.all_to_all(flat.reshape(devices, chunk), AXES, 0, 0, tiled=True)]
    all_to_all x0 -> x2, starting transfers between devices: none -> 11.5 us  [the longest x1 7.86 us: all_reduce(): parts = lax.all_to_all(flat.reshape(devices, chunk), AXES, 0, 0, tiled=True)]
    ppermute x10 -> x6, waiting for transfers between devices: 8.22 us -> 0.02 us  [exchange(): return lax.ppermute(piece, 'brick', pairs)]
    reshape x9 -> x2, local copies, waits for them, and re-layouts: 6.61 us -> 1.32 us  [the longest x1 0.94 us: body(): up = parities.reshape(size_x, size_y, size_z, 2, 2, 2, channels_out).tran...]
    unnamed x71 -> x60, local copies, waits for them, and re-layouts: 0.15 us -> 3.9 us
  transfers between devices with their start and end apart: 11 -> 8, of which waited for: 4 -> 2; matrix products, arithmetic and copies ran while one was open for 49% -> 26% of each run, Pallas kernels for 0% -> 0%
where the time goes in v1:
time: 93.7 us; the launch traced here: 93.1 us
  waiting for transfers between devices  36.2 us (39%)
  starting transfers between devices  26.1 us (28%)
  local copies, waits for them, and re-layouts  16.8 us (18%)
  other arithmetic  6.93 us (7%)
  matrix products  5.63 us (6%)
  between operations  1.4 us (1%)
    all_to_all x1, waiting for transfers between devices, all_reduce(): parts = lax.all_to_all(flat.reshape(devices, chunk), AXES, 0, 0, tiled=True)  21.6 us
    all_to_all x1, waiting for transfers between devices, all_spread(): whole = lax.all_to_all(spread, AXES, 0, 0, tiled=True)  14.6 us
    ppermute x6, starting transfers between devices, exchange(): return lax.ppermute(piece, 'brick', pairs)  14.6 us
    all_to_all x1, starting transfers between devices, all_reduce(): parts = lax.all_to_all(flat.reshape(devices, chunk), AXES, 0, 0, tiled=True)  7.86 us
    unnamed x60, local copies, waits for them, and re-layouts  3.9 us
    slice x2, local copies, waits for them, and re-layouts, body(): windows.append(paired[tuple(index)])  3.81 us
    all_to_all x1, starting transfers between devices, all_spread(): whole = lax.all_to_all(spread, AXES, 0, 0, tiled=True)  3.62 us
    unnamed x4, other arithmetic  2.76 us
  transfers between devices with their start and end apart: 8, of which 2 were waited for; matrix products, arithmetic and copies ran while one was open for 26% of the time, Pallas kernels for 0%

profile of v1, /device:TPU:0, one launch (start us, length us, event | category | flops | bytes accessed | tf_op | source)
XLA Modules:
  0.0 93.1 jit_solution(4946918157015679034)
XLA Ops:
  0.6 0.0 copy-start.4
  0.6 0.0 copy-start.2
  0.7 0.0 copy-start.1
  0.7 1.4 %reshape.613 = bf16[8,16,16,64]{3,2,1,0:T(8,128)(2,1)S(1)} reshape(bf16[1,1,8,16,1024]{4,3,2,1,0:T(8,128)(2,1)} %param.39) | data formatting | bytes 524288 | tf_op jit(solution)/shard_map/reshape | solution.py:85
  2.1 0.7 convert_reduce_fusion
  2.8 0.1 convert_element_type.66
  2.9 0.3 broadcast_multiply_fusion
  3.2 0.1 slice.805
  3.3 4.9 %collective-permute-start.3 = (bf16[8,16,1,64]{3,2,1,0:T(2,128)(2,1)S(1)}, bf16[8,16,1,64]{3,2,1,0:T(2,128)(2,1)S(1)}, u32[]{:S(2)}, u32[]{:S(2)}) collective-permute-start(bf16[8,16,1,64]{3,2,1,0:T(2,128)(2,1)S(1)} %slice.805), channel_id=1, source_target_pairs={{0,8},{16,24},{1,9},{17,25},{2,10},{18,26},{3,11},{19,27},{4,12},{... | collective-permute-start | bytes 49160 | tf_op jit(solution)/shard_map/ppermute | solution.py:32
  8.3 4.5 %collective-permute-start.4 = (bf16[8,1,16,64]{3,2,1,0:T(8,128)(2,1)S(1)}, bf16[8,1,16,64]{3,2,1,0:T(8,128)(2,1)S(1)}, u32[]{:S(2)}, u32[]{:S(2)}) collective-permute-start(bf16[8,1,16,64]{3,2,1,0:T(8,128)(2,1)S(1)} %slice.806), channel_id=1, source_target_pairs={{0,16},{8,24},{1,17},{9,25},{2,18},{10,26},{3,19},{11,27},{4,20},{... | collective-permute-start | bytes 49160 | tf_op jit(solution)/shard_map/ppermute | solution.py:32
  12.8 1.3 %collective-permute-start.5 = (bf16[8,1,1,64]{3,2,1,0:T(2,128)(2,1)S(1)}, bf16[8,1,1,64]{3,2,1,0:T(2,128)(2,1)S(1)}, u32[]{:S(2)}, u32[]{:S(2)}) collective-permute-start(bf16[8,1,1,64]{3,2,1,0:T(2,128)(2,1)S(1)} %slice.807), channel_id=1, source_target_pairs={{0,24},{1,25},{2,26},{3,27},{4,28},{5,29},{6,30},{7,31}} | collective-permute-start | bytes 3080 | tf_op jit(solution)/shard_map/ppermute | solution.py:32
  14.1 0.0 copy-done.4
  14.1 0.1 convert_element_type.63
  14.2 0.0 copy-done.2
  14.2 0.1 bitcast_multiply_fusion
  14.3 1.3 %collective-permute-start = (bf16[4,8,1,128]{3,2,1,0:T(2,128)(2,1)S(1)}, bf16[4,8,1,128]{3,2,1,0:T(2,128)(2,1)S(1)}, u32[]{:S(2)}, u32[]{:S(2)}) collective-permute-start(bf16[4,8,1,128]{3,2,1,0:T(2,128)(2,1)S(1)} %slice.794), channel_id=1, source_target_pairs={{8,0},{24,16},{9,1},{25,17},{10,2},{26,18},{11,3},{27,19},{12,4},{... | collective-permute-start | bytes 24584 | tf_op jit(solution)/shard_map/ppermute | solution.py:32
  15.6 1.3 %collective-permute-start.1 = (bf16[4,1,8,128]{3,2,1,0:T(8,128)(2,1)S(1)}, bf16[4,1,8,128]{3,2,1,0:T(8,128)(2,1)S(1)}, u32[]{:S(2)}, u32[]{:S(2)}) collective-permute-start(bf16[4,1,8,128]{3,2,1,0:T(8,128)(2,1)S(1)} %slice.795), channel_id=1, source_target_pairs={{16,0},{24,8},{17,1},{25,9},{18,2},{26,10},{19,3},{27,11},{20,4},{... | collective-permute-start | bytes 24584 | tf_op jit(solution)/shard_map/ppermute | solution.py:32
  17.0 0.0 copy-done.1
  17.2 0.7 fusion.13
  17.9 0.7 bitcast_dynamic-update-slice_fusion.2
  18.6 0.7 fusion.9
  19.3 0.7 bitcast_dynamic-update-slice_fusion.1
  20.0 0.7 fusion.14
  20.7 0.7 bitcast_dynamic-update-slice_fusion
  21.4 0.7 fusion.12
  22.0 0.7 fusion.15
  22.7 0.3 pad.65
  23.0 0.0 collective-permute-done.3
  23.0 1.3 %collective-permute-start.2 = (bf16[4,1,1,128]{3,2,1,0:T(2,128)(2,1)S(1)}, bf16[4,1,1,128]{3,2,1,0:T(2,128)(2,1)S(1)}, u32[]{:S(2)}, u32[]{:S(2)}) collective-permute-start(bf16[4,1,1,128]{3,2,1,0:T(2,128)(2,1)S(1)} %slice.796), channel_id=1, source_target_pairs={{24,0},{25,1},{26,2},{27,3},{28,4},{29,5},{30,6},{31,7}} | collective-permute-start | bytes 3080 | tf_op jit(solution)/shard_map/ppermute | solution.py:32
  24.3 1.4 %scatter.59 = bf16[10,18,18,64]{3,2,1,0:T(8,128)(2,1)S(1)} dynamic-update-slice(bf16[10,18,18,64]{3,2,1,0:T(8,128)(2,1)S(1)} %pad.65, bf16[8,16,1,64]{3,2,1,0:T(2,128)(2,1)S(1)} %collective-permute-done.3, s32[]{:T(128)} %constant.478.clone.1, s32[]{:T(128)} %constant.478.clone.1, s32[]{:T(128)} %constant.475.clone.1, s32[]{:T(128)} %constant.475.clone.1) | dynamic-update-slice | bytes 32772 | tf_op jit(solution)/shard_map/scatter | solution.py:97
  25.7 0.0 collective-permute-done.4
  25.8 0.2 scatter.60
  26.0 0.0 collective-permute-done.5
  26.1 0.3 scatter.64
  26.4 0.1 scatter.65
  26.4 0.2 scatter.66
  26.7 0.4 reshape.614
  27.1 1.0 %fusion.19 = (bf16[4,1,8,1,8,1,64]{6,5,4,3,2,1,0:T(2,128)(2,1)S(1)}, bf16[4,1,8,1,8,1,64]{6,5,4,3,2,1,0:T(2,128)(2,1)S(1)}, bf16[4,1,8,1,8,1,64]{6,5,4,3,2,1,0:T...) fusion(bf16[5,2,9,2,9,2,64]{6,5,4,3,2,1,0:T(2,128)(2,1)S(1)} %r, ...), kind=kLoop, calls=%fused_computation.131 | loop fusion | bytes 524288 | tf_op jit(solution)/shard_map/slice | solution.py:117
  28.0 2.8 %fusion.18 = (bf16[4,1,8,1,8,1,64]{6,5,4,3,2,1,0:T(2,128)(2,1)S(1)}, bf16[4,1,8,1,8,1,64]{6,5,4,3,2,1,0:T(2,128)(2,1)S(1)}, bf16[4,1,8,1,8,1,64]{6,5,4,3,2,1,0:T...) fusion(bf16[5,2,9,2,9,2,64]{6,5,4,3,2,1,0:T(2,128)(2,1)S(1)} %r, ...), kind=kLoop, calls=%fused_computation.130 | loop fusion | bytes 1245184 | tf_op jit(solution)/shard_map/slice | solution.py:117
  31.7 0.0 copy-start
  31.7 1.6 %fusion.16 = f32[27,64,128,1,1]{2,1,0,4,3:T(8,128)} fusion(bf16[27,4,8,8,64]{4,3,0,2,1:T(8,128)(2,1)S(1)} %constant_dynamic-update-slice_fusion.27, bf16[4,8,8,128]{3,2,1,0:T(8,128)(2,1)S(1)} %bitcast_multiply_fusion), kind=kOutput, calls=%fused_computation.117 | convolution fusion | flops 113246208 | bytes 1835008 | tf_op jit(solution)/shard_map/kabco,abci->koi/dot_general | solution.py:119
  33.3 0.0 copy-done
  33.3 0.0 copy-start.3
  33.3 7.9 %all-to-all-start = ((f32[32,1,6912]{2,1,0:T(1,128)}), f32[32,1,6912]{2,1,0:T(1,128)S(1)}, u32[]{:S(2)}, u32[]{:S(2)}) async-start(f32[32,1,6912]{2,1,0:T(1,128)} %bitcast.72), calls=%async_computation | async-start | bytes 1769472 | tf_op jit(solution)/shard_map/all_to_all | solution.py:61
  41.2 0.0 copy-done.3
  41.3 0.1 convert_element_type.60
  41.4 0.3 mul.45
  41.7 0.3 mul.46
  42.0 0.0 collective-permute-done
  42.1 0.0 collective-permute-done.1
  42.1 0.0 collective-permute-done.2
  42.3 21.6 %all-to-all-done = f32[32,1,6912]{2,1,0:T(1,128)S(1)} async-done(((f32[32,1,6912]{2,1,0:T(1,128)}), f32[32,1,6912]{2,1,0:T(1,128)S(1)}, u32[]{:S(2)}, u32[]{:S(2)}) %all-to-all-start) | async-done | bytes 884768 | tf_op jit(solution)/shard_map/all_to_all | solution.py:61
  63.9 0.5 reduce_sum.9
  64.4 1.4 %broadcast_in_dim.2 = f32[32,1,6912]{2,1,0:T(1,128)} broadcast(f32[6912]{0:T(1024)S(1)} %broadcast_multiply_fusion.1), dimensions={2} | broadcast | bytes 912384 | tf_op jit(solution)/shard_map/broadcast_in_dim | solution.py:67
  65.8 3.6 %all-to-all-start.1 = ((f32[32,1,6912]{2,1,0:T(1,128)}), f32[32,1,6912]{2,1,0:T(1,128)S(1)}, u32[]{:S(2)}, u32[]{:S(2)}) async-start(f32[32,1,6912]{2,1,0:T(1,128)} %broadcast_in_dim.2), calls=%async_computation.1 | async-start | bytes 1769472 | tf_op jit(solution)/shard_map/all_to_all | solution.py:68
  69.6 2.0 %fusion.2 = f32[4,8,8,8,64,1]{4,2,5,3,1,0:T(8,128)S(1)} fusion(bf16[8,8,64,128]{3,2,0,1:T(8,128)(2,1)} %fusion.15, bf16[8,4,8,8,128]{4,3,0,2,1:T(8,128)(2,1)S(1)} %constant_dynamic-update-slice_fusion), kind=kOutput, calls=%fused_computation.3 | convolution fusion | flops 268435456 | bytes 2097152 | tf_op jit(solution)/shard_map/dabci,dpoi->abcpo/dot_general | solution.py:137
  71.5 0.6 copy.105
  72.1 0.9 %reshape.612 = f32[1,1,8,16,1024]{4,3,2,1,0:T(8,128)S(1)} reshape(f32[4,2,8,2,8,2,64]{6,5,4,3,2,1,0:T(2,128)S(1)} %copy.105) | data formatting | bytes 1048576 | tf_op jit(solution)/shard_map/reshape | solution.py:146
  73.1 1.8 %multiply_convert_fusion = bf16[1,1,8,16,1024]{4,3,2,1,0:T(8,128)(2,1)} fusion(f32[1,1,8,16,1024]{4,3,2,1,0:T(8,128)S(1)} %mul.46, f32[1,1,8,16,1024]{4,3,2,1,0:T(8,128)S(1)} %reshape.612, bf16[1,1,8,16,1024]{4,3,2,1,0:T(8,128)(2,1)} %param.36), kind=kLoop, calls=%fused_computation.6 | loop fusion | flops 524288 | bytes 1572864 | tf_op jit(solution)/shard_map/convert_element_type | solution.py:151
  74.8 2.1 %fusion.1 = bf16[4,8,8,128]{3,2,1,0:T(8,128)(2,1)S(1)} fusion(bf16[27,4,8,8,64]{4,3,0,2,1:T(8,128)(2,1)} %copy-done, bf16[27,64,128]{2,1,0:T(8,128)(2,1)} %param.38, f32[4,8,8]{2,1,0:T(8,128)S(1)} %convert_element_type.67), kind=kOutput, calls=%fused_computation.2 | convolution fusion | flops 113311744 | bytes 1393664 | tf_op jit(solution)/shard_map/kabco,koi->abci/dot_general | solution.py:124
  76.9 0.7 reshape.615
  77.6 14.6 %all-to-all-done.1 = f32[32,1,6912]{2,1,0:T(1,128)S(1)} async-done(((f32[32,1,6912]{2,1,0:T(1,128)}), f32[32,1,6912]{2,1,0:T(1,128)S(1)}, u32[]{:S(2)}, u32[]{:S(2)}) %all-to-all-start.1) | async-done | bytes 884768 | tf_op jit(solution)/shard_map/all_to_all | solution.py:68
  92.2 0.9 copy.322
  (76 shorter events, 1.4 us)
Async XLA Ops:
  0.6 13.4 %copy-start.4 = (s32[1,1,256]{2,1,0:T(1,128)S(1)}, s32[1,1,256]{2,1,0:T(1,128)}, u32[]{:S(2)}) copy-start(s32[1,1,256]{2,1,0:T(1,128)} %param.35) | copy-start | bytes 3076
  0.6 13.6 %copy-start.2 = (bf16[1,1,4,8,1024]{4,3,2,1,0:T(8,128)(2,1)S(1)}, bf16[1,1,4,8,1024]{4,3,2,1,0:T(8,128)(2,1)}, u32[]{:S(2)}) copy-start(bf16[1,1,4,8,1024]{4,3,2,1,0:T(8,128)(2,1)} %param.34) | copy-start | bytes 196612
  0.7 16.3 %copy-start.1 = (bf16[27,64,128]{2,1,0:T(8,128)(2,1)S(1)}, bf16[27,64,128]{2,1,0:T(8,128)(2,1)}, u32[]{:S(2)}) copy-start(bf16[27,64,128]{2,1,0:T(8,128)(2,1)} %param.38) | copy-start | bytes 1327108
  3.3 19.7 %collective-permute-start.3 = (bf16[8,16,1,64]{3,2,1,0:T(2,128)(2,1)S(1)}, bf16[8,16,1,64]{3,2,1,0:T(2,128)(2,1)S(1)}, u32[]{:S(2)}, u32[]{:S(2)}) collective-permute-start(bf16[8,16,1,64]{3,2,1,0:T(2,128)(2,1)S(1)} %slice.805), channel_id=1, source_target_pairs={{0,8},{16,24},{1,9},{17,25},{2,10},{18,26},{3,11},{19,27},{4,12},{... | collective-permute-start | bytes 49160 | tf_op jit(solution)/shard_map/ppermute | solution.py:32
  8.3 17.5 %collective-permute-start.4 = (bf16[8,1,16,64]{3,2,1,0:T(8,128)(2,1)S(1)}, bf16[8,1,16,64]{3,2,1,0:T(8,128)(2,1)S(1)}, u32[]{:S(2)}, u32[]{:S(2)}) collective-permute-start(bf16[8,1,16,64]{3,2,1,0:T(8,128)(2,1)S(1)} %slice.806), channel_id=1, source_target_pairs={{0,16},{8,24},{1,17},{9,25},{2,18},{10,26},{3,19},{11,27},{4,20},{... | collective-permute-start | bytes 49160 | tf_op jit(solution)/shard_map/ppermute | solution.py:32
  12.8 13.2 %collective-permute-start.5 = (bf16[8,1,1,64]{3,2,1,0:T(2,128)(2,1)S(1)}, bf16[8,1,1,64]{3,2,1,0:T(2,128)(2,1)S(1)}, u32[]{:S(2)}, u32[]{:S(2)}) collective-permute-start(bf16[8,1,1,64]{3,2,1,0:T(2,128)(2,1)S(1)} %slice.807), channel_id=1, source_target_pairs={{0,24},{1,25},{2,26},{3,27},{4,28},{5,29},{6,30},{7,31}} | collective-permute-start | bytes 3080 | tf_op jit(solution)/shard_map/ppermute | solution.py:32
  14.3 27.7 %collective-permute-start = (bf16[4,8,1,128]{3,2,1,0:T(2,128)(2,1)S(1)}, bf16[4,8,1,128]{3,2,1,0:T(2,128)(2,1)S(1)}, u32[]{:S(2)}, u32[]{:S(2)}) collective-permute-start(bf16[4,8,1,128]{3,2,1,0:T(2,128)(2,1)S(1)} %slice.794), channel_id=1, source_target_pairs={{8,0},{24,16},{9,1},{25,17},{10,2},{26,18},{11,3},{27,19},{12,4},{... | collective-permute-start | bytes 24584 | tf_op jit(solution)/shard_map/ppermute | solution.py:32
  15.6 26.4 %collective-permute-start.1 = (bf16[4,1,8,128]{3,2,1,0:T(8,128)(2,1)S(1)}, bf16[4,1,8,128]{3,2,1,0:T(8,128)(2,1)S(1)}, u32[]{:S(2)}, u32[]{:S(2)}) collective-permute-start(bf16[4,1,8,128]{3,2,1,0:T(8,128)(2,1)S(1)} %slice.795), channel_id=1, source_target_pairs={{16,0},{24,8},{17,1},{25,9},{18,2},{26,10},{19,3},{27,11},{20,4},{... | collective-permute-start | bytes 24584 | tf_op jit(solution)/shard_map/ppermute | solution.py:32
  23.0 19.1 %collective-permute-start.2 = (bf16[4,1,1,128]{3,2,1,0:T(2,128)(2,1)S(1)}, bf16[4,1,1,128]{3,2,1,0:T(2,128)(2,1)S(1)}, u32[]{:S(2)}, u32[]{:S(2)}) collective-permute-start(bf16[4,1,1,128]{3,2,1,0:T(2,128)(2,1)S(1)} %slice.796), channel_id=1, source_target_pairs={{24,0},{25,1},{26,2},{27,3},{28,4},{29,5},{30,6},{31,7}} | collective-permute-start | bytes 3080 | tf_op jit(solution)/shard_map/ppermute | solution.py:32
  31.7 1.6 %copy-start = (bf16[27,4,8,8,64]{4,3,0,2,1:T(8,128)(2,1)}, bf16[27,4,8,8,64]{4,3,0,2,1:T(8,128)(2,1)S(1)}, u32[]{:S(2)}) copy-start(bf16[27,4,8,8,64]{4,3,0,2,1:T(8,128)(2,1)S(1)} %constant_dynamic-update-slice_fusion.27) | copy-start | bytes 2654212
  33.3 7.9 %copy-start.3 = (s32[1,1,2048]{2,1,0:T(1,128)S(1)}, s32[1,1,2048]{2,1,0:T(1,128)}, u32[]{:S(2)}) copy-start(s32[1,1,2048]{2,1,0:T(1,128)} %param.37) | copy-start | bytes 24580
  33.3 30.6 %all-to-all-start = ((f32[32,1,6912]{2,1,0:T(1,128)}), f32[32,1,6912]{2,1,0:T(1,128)S(1)}, u32[]{:S(2)}, u32[]{:S(2)}) async-start(f32[32,1,6912]{2,1,0:T(1,128)} %bitcast.72), calls=%async_computation | async-start | bytes 1769472 | tf_op jit(solution)/shard_map/all_to_all | solution.py:61
  65.8 26.4 %all-to-all-start.1 = ((f32[32,1,6912]{2,1,0:T(1,128)}), f32[32,1,6912]{2,1,0:T(1,128)S(1)}, u32[]{:S(2)}, u32[]{:S(2)}) async-start(f32[32,1,6912]{2,1,0:T(1,128)} %broadcast_in_dim.2), calls=%async_computation.1 | async-start | bytes 1769472 | tf_op jit(solution)/shard_map/all_to_all | solution.py:68

commit v2 on v1

--- a/solution.py
+++ b/solution.py
@@ -32,24 +32,12 @@
     return lax.ppermute(piece, "brick", pairs)
 
 
-def forward_tap(d, p):
-    k = p + 1 - 2 * d
-    return k if 0 <= k <= 2 else None
-
-
 def forward_weight(up_weight):
-    zero = jnp.zeros(up_weight.shape[1:], up_weight.dtype)
-    rows = []
-    for d in OFFSETS:
-        row = []
-        for p in OFFSETS:
-            taps = [forward_tap(d[a], p[a]) for a in range(3)]
-            if any(t is None for t in taps):
-                row.append(zero)
-            else:
-                row.append(up_weight[9 * taps[0] + 3 * taps[1] + taps[2]])
-        rows.append(jnp.stack(row))
-    return jnp.stack(rows)
+    channels = up_weight.shape[1:]
+    taps = jnp.pad(up_weight.reshape((3, 3, 3) + channels), ((0, 1), (0, 1), (0, 1), (0, 0), (0, 0)))
+    for axis in range(3):
+        taps = jnp.roll(taps, -1, axis=axis)
+    return taps.reshape((2, 2, 2, 2, 2, 2) + channels)
 
 
 def all_reduce(grads):
@@ -95,16 +83,6 @@
             for a, flag in enumerate(direction)
         )
         widened = widened.at[target].set(got)
-    extended = jnp.pad(masked, ((0, 1), (0, 1), (0, 1), (0, 0)))
-    for direction in DIRECTIONS:
-        source = tuple(slice(0, 1) if flag else slice(None) for flag in direction)
-        got = exchange(masked[source], regions, direction, 1)
-        target = tuple(
-            slice(counts[a], counts[a] + 1) if flag else slice(0, counts[a])
-            for a, flag in enumerate(direction)
-        )
-        extended = extended.at[target].set(got)
-
     paired = widened.reshape(size_x + 1, 2, size_y + 1, 2, size_z + 1, 2, channels_out)
     windows = []
     for kx in range(3):
@@ -120,6 +98,7 @@
         "kabco,abci->koi", gathered, masked, preferred_element_type=jnp.float32
     )
     reduced, plan = all_reduce(grads)
+    reduced, masked_late, weight_late = lax.optimization_barrier((reduced, masked, up_weight))
 
     back = jnp.einsum(
         "kabco,koi->abci", gathered, up_weight, preferred_element_type=jnp.float32
@@ -128,23 +107,29 @@
         (back * coarse_keep.astype(jnp.float32)).astype(jnp.bfloat16).reshape(coarse.shape)
     )
 
+    extended = jnp.pad(masked_late, ((0, 1), (0, 1), (0, 1), (0, 0)))
+    for direction in DIRECTIONS:
+        source = tuple(slice(0, 1) if flag else slice(None) for flag in direction)
+        got = exchange(masked_late[source], regions, direction, 1)
+        target = tuple(
+            slice(counts[a], counts[a] + 1) if flag else slice(0, counts[a])
+            for a, flag in enumerate(direction)
+        )
+        extended = extended.at[target].set(got)
+
     shifted = jnp.stack(
         [
             extended[dx : dx + size_x, dy : dy + size_y, dz : dz + size_z]
             for dx, dy, dz in OFFSETS
         ]
-    )
+    ).reshape((2, 2, 2, size_x, size_y, size_z, channels_in))
     parities = jnp.einsum(
-        "dabci,dpoi->abcpo",
+        "xyzabci,xpyqzroi->apbqcro",
         shifted,
-        forward_weight(up_weight),
+        forward_weight(weight_late),
         preferred_element_type=jnp.float32,
     )
-    up = (
-        parities.reshape(size_x, size_y, size_z, 2, 2, 2, channels_out)
-        .transpose(0, 3, 1, 4, 2, 5, 6)
-        .reshape(fine_x, fine_y, fine_z, channels_out)
-    )
+    up = parities.reshape(fine_x, fine_y, fine_z, channels_out)
     fine = fine_keep.astype(jnp.float32) * (
         skip.reshape(fine_x, fine_y, fine_z, channels_out).astype(jnp.float32) + up
     )

time: 93.7 us -> 90.8 us (0.969)
  other arithmetic: 6.93 us -> 2.79 us
  starting transfers between devices: 26.1 us -> 28 us
  waiting for transfers between devices: 36.2 us -> 37.8 us
  matrix products: 5.63 us -> 4.36 us
    all_to_all x1, starting transfers between devices: 3.62 us -> 7.98 us  [all_spread(): whole = lax.all_to_all(spread, AXES, 0, 0, tiled=True)]
    all_to_all x1, waiting for transfers between devices: 14.6 us -> 18.8 us  [all_spread(): whole = lax.all_to_all(spread, AXES, 0, 0, tiled=True)]
    unnamed x4 -> x0, other arithmetic: 2.76 us -> none
    all_to_all x1, waiting for transfers between devices: 21.6 us -> 19 us  [all_reduce(): parts = lax.all_to_all(flat.reshape(devices, chunk), AXES, 0, 0, tiled=True)]
    all_to_all x1, starting transfers between devices: 7.86 us -> 5.39 us  [all_reduce(): parts = lax.all_to_all(flat.reshape(devices, chunk), AXES, 0, 0, tiled=True)]
    dot_general x1, matrix products: 1.96 us -> 0.73 us  [body(): jnp.einsum('xyzabci,xpyqzroi->apbqcro', shifted, forward_weight(weight_la...]
    convert_element_type x1, other arithmetic: 1.76 us -> 0.81 us  [body(): fine_out = fine.astype(jnp.bfloat16).reshape(skip.shape)]
    unnamed x60 -> x51, local copies, waits for them, and re-layouts: 3.9 us -> 3.29 us
  transfers between devices with their start and end apart: 8 -> 8, of which waited for: 2 -> 2; matrix products, arithmetic and copies ran while one was open for 26% -> 12% of each run, Pallas kernels for 0% -> 0%
where the time goes in v2:
time: 90.8 us; the launch traced here: 90.2 us
  waiting for transfers between devices  37.8 us (42%)
  starting transfers between devices  28 us (31%)
  local copies, waits for them, and re-layouts  16 us (18%)
  matrix products  4.36 us (5%)
  other arithmetic  2.79 us (3%)
  between operations  1.27 us (1%)
    all_to_all x1, waiting for transfers between devices, all_reduce(): parts = lax.all_to_all(flat.reshape(devices, chunk), AXES, 0, 0, tiled=True)  19 us
    all_to_all x1, waiting for transfers between devices, all_spread(): whole = lax.all_to_all(spread, AXES, 0, 0, tiled=True)  18.8 us
    ppermute x6, starting transfers between devices, exchange(): return lax.ppermute(piece, 'brick', pairs)  14.6 us
    all_to_all x1, starting transfers between devices, all_spread(): whole = lax.all_to_all(spread, AXES, 0, 0, tiled=True)  7.98 us
    all_to_all x1, starting transfers between devices, all_reduce(): parts = lax.all_to_all(flat.reshape(devices, chunk), AXES, 0, 0, tiled=True)  5.39 us
    slice x2, local copies, waits for them, and re-layouts, body(): windows.append(paired[tuple(index)])  3.81 us
    unnamed x51, local copies, waits for them, and re-layouts  3.29 us
    scatter x7, local copies, waits for them, and re-layouts, body(): widened = widened.at[target].set(got)  2.25 us
  transfers between devices with their start and end apart: 8, of which 2 were waited for; matrix products, arithmetic and copies ran while one was open for 12% of the time, Pallas kernels for 0%

profile of v2, /device:TPU:0, one launch (start us, length us, event | category | flops | bytes accessed | tf_op | source)
XLA Modules:
  0.0 90.2 jit_solution(7941847479949342867)
XLA Ops:
  0.6 0.0 copy-start.7
  0.6 0.0 copy-start.4
  0.7 1.4 %reshape.613 = bf16[8,16,16,64]{3,2,1,0:T(8,128)(2,1)S(1)} reshape(bf16[1,1,8,16,1024]{4,3,2,1,0:T(8,128)(2,1)} %param.39) | data formatting | bytes 524288 | tf_op jit(solution)/shard_map/reshape | solution.py:73
  2.0 0.7 convert_reduce_fusion
  2.7 0.1 convert_element_type.65
  2.8 0.3 broadcast_multiply_fusion
  3.2 0.1 slice.734
  3.3 4.9 %collective-permute-start = (bf16[8,16,1,64]{3,2,1,0:T(2,128)(2,1)S(1)}, bf16[8,16,1,64]{3,2,1,0:T(2,128)(2,1)S(1)}, u32[]{:S(2)}, u32[]{:S(2)}) collective-permute-start(bf16[8,16,1,64]{3,2,1,0:T(2,128)(2,1)S(1)} %slice.734), channel_id=1, source_target_pairs={{0,8},{16,24},{1,9},{17,25},{2,10},{18,26},{3,11},{19,27},{4,12},{... | collective-permute-start | bytes 49160 | tf_op jit(solution)/shard_map/ppermute | solution.py:32
  8.2 4.5 %collective-permute-start.1 = (bf16[8,1,16,64]{3,2,1,0:T(8,128)(2,1)S(1)}, bf16[8,1,16,64]{3,2,1,0:T(8,128)(2,1)S(1)}, u32[]{:S(2)}, u32[]{:S(2)}) collective-permute-start(bf16[8,1,16,64]{3,2,1,0:T(8,128)(2,1)S(1)} %slice.735), channel_id=1, source_target_pairs={{0,16},{8,24},{1,17},{9,25},{2,18},{10,26},{3,19},{11,27},{4,20},{... | collective-permute-start | bytes 49160 | tf_op jit(solution)/shard_map/ppermute | solution.py:32
  12.7 1.3 %collective-permute-start.2 = (bf16[8,1,1,64]{3,2,1,0:T(2,128)(2,1)S(1)}, bf16[8,1,1,64]{3,2,1,0:T(2,128)(2,1)S(1)}, u32[]{:S(2)}, u32[]{:S(2)}) collective-permute-start(bf16[8,1,1,64]{3,2,1,0:T(2,128)(2,1)S(1)} %slice.736), channel_id=1, source_target_pairs={{0,24},{1,25},{2,26},{3,27},{4,28},{5,29},{6,30},{7,31}} | collective-permute-start | bytes 3080 | tf_op jit(solution)/shard_map/ppermute | solution.py:32
  14.0 0.0 copy-done.7
  14.1 0.1 convert_element_type.67
  14.2 0.0 copy-done.4
  14.2 0.1 bitcast_multiply_fusion
  14.3 0.0 copy-start.1
  14.3 0.3 pad.68
  14.6 0.0 collective-permute-done
  14.6 1.4 %scatter.46 = bf16[10,18,18,64]{3,2,1,0:T(8,128)(2,1)S(1)} dynamic-update-slice(bf16[10,18,18,64]{3,2,1,0:T(8,128)(2,1)S(1)} %pad.68, bf16[8,16,1,64]{3,2,1,0:T(2,128)(2,1)S(1)} %collective-permute-done, s32[]{:T(128)} %constant.472.clone.1, s32[]{:T(128)} %constant.472.clone.1, s32[]{:T(128)} %constant.473.clone.1, s32[]{:T(128)} %constant.473.clone.1) | dynamic-update-slice | bytes 32772 | tf_op jit(solution)/shard_map/scatter | solution.py:85
  16.0 0.0 collective-permute-done.1
  16.0 0.2 scatter.49
  16.3 0.0 collective-permute-done.2
  16.3 0.3 scatter.51
  16.6 0.1 scatter.54
  16.7 0.2 scatter.55
  17.0 0.4 reshape.614
  17.3 1.0 %fusion.20 = (bf16[4,1,8,1,8,1,64]{6,5,4,3,2,1,0:T(2,128)(2,1)S(1)}, bf16[4,1,8,1,8,1,64]{6,5,4,3,2,1,0:T(2,128)(2,1)S(1)}, bf16[4,1,8,1,8,1,64]{6,5,4,3,2,1,0:T...) fusion(bf16[5,2,9,2,9,2,64]{6,5,4,3,2,1,0:T(2,128)(2,1)S(1)} %r, ...), kind=kLoop, calls=%fused_computation.106 | loop fusion | bytes 524288 | tf_op jit(solution)/shard_map/slice | solution.py:95
  18.3 2.8 %fusion.19 = (bf16[4,1,8,1,8,1,64]{6,5,4,3,2,1,0:T(2,128)(2,1)S(1)}, bf16[4,1,8,1,8,1,64]{6,5,4,3,2,1,0:T(2,128)(2,1)S(1)}, bf16[4,1,8,1,8,1,64]{6,5,4,3,2,1,0:T...) fusion(bf16[5,2,9,2,9,2,64]{6,5,4,3,2,1,0:T(2,128)(2,1)S(1)} %r, ...), kind=kLoop, calls=%fused_computation.105 | loop fusion | bytes 1245184 | tf_op jit(solution)/shard_map/slice | solution.py:95
  21.8 0.0 copy-start.6
  21.8 1.6 %fusion.17 = f32[27,64,128,1,1]{2,1,4,0,3:T(8,128)} fusion(bf16[27,4,8,8,64]{4,3,2,0,1:T(8,128)(2,1)S(1)} %constant_dynamic-update-slice_fusion, bf16[4,8,8,128]{3,2,1,0:T(8,128)(2,1)S(1)} %bitcast_multiply_fusion), kind=kOutput, calls=%fused_computation.92 | convolution fusion | flops 113246208 | bytes 1835008 | tf_op jit(solution)/shard_map/kabco,abci->koi/dot_general | solution.py:97
  23.5 0.0 copy-done.6
  23.5 5.4 %all-to-all-start = ((f32[32,1,6912]{2,1,0:T(1,128)}), f32[32,1,6912]{2,1,0:T(1,128)S(1)}, u32[]{:S(2)}, u32[]{:S(2)}) async-start(f32[32,1,6912]{2,1,0:T(1,128)} %bitcast.31), calls=%async_computation | async-start | bytes 1769472 | tf_op jit(solution)/shard_map/all_to_all | solution.py:49
  28.9 0.0 copy-start
  28.9 0.0 copy-done.5
  28.9 0.1 convert_element_type.62
  29.0 0.3 mul.41
  29.4 0.3 mul.42
  29.7 0.2 copy-done
  29.9 2.0 %fusion.8 = bf16[4,8,8,128]{3,2,0,1:T(8,128)(2,1)S(1)} fusion(bf16[27,4,8,8,64]{4,3,2,0,1:T(8,128)(2,1)} %copy-done.6, bf16[27,64,128]{2,1,0:T(8,128)(2,1)S(1)} %copy-done, f32[4,8,8]{2,0,1:T(4,128)S(1)} %copy.144), kind=kOutput, calls=%fused_computation.7 | convolution fusion | flops 113311744 | bytes 1393664 | tf_op jit(solution)/shard_map/kabco,koi->abci/dot_general | solution.py:103
  31.9 0.7 copy.145
  32.6 19.0 %all-to-all-done = f32[32,1,6912]{2,1,0:T(1,128)S(1)} async-done(((f32[32,1,6912]{2,1,0:T(1,128)}), f32[32,1,6912]{2,1,0:T(1,128)S(1)}, u32[]{:S(2)}, u32[]{:S(2)}) %all-to-all-start) | async-done | bytes 884768 | tf_op jit(solution)/shard_map/all_to_all | solution.py:49
  51.6 0.5 reduce_sum.9
  52.1 0.0 copy-done.1
  52.2 0.1 pad_slice_fusion.1
  52.3 1.3 %collective-permute-start.3 = (bf16[4,8,1,128]{3,2,1,0:T(2,128)(2,1)S(1)}, bf16[4,8,1,128]{3,2,1,0:T(2,128)(2,1)S(1)}, u32[]{:S(2)}, u32[]{:S(2)}) collective-permute-start(bf16[4,8,1,128]{3,2,1,0:T(2,128)(2,1)S(1)} %slice.723), channel_id=1, source_target_pairs={{8,0},{24,16},{9,1},{25,17},{10,2},{26,18},{11,3},{27,19},{12,4},{... | collective-permute-start | bytes 24584 | tf_op jit(solution)/shard_map/ppermute | solution.py:32
  53.6 1.3 %collective-permute-start.4 = (bf16[4,1,8,128]{3,2,1,0:T(8,128)(2,1)S(1)}, bf16[4,1,8,128]{3,2,1,0:T(8,128)(2,1)S(1)}, u32[]{:S(2)}, u32[]{:S(2)}) collective-permute-start(bf16[4,1,8,128]{3,2,1,0:T(8,128)(2,1)S(1)} %slice.724), channel_id=1, source_target_pairs={{16,0},{24,8},{17,1},{25,9},{18,2},{26,10},{19,3},{27,11},{20,4},{... | collective-permute-start | bytes 24584 | tf_op jit(solution)/shard_map/ppermute | solution.py:32
  54.9 1.3 %collective-permute-start.5 = (bf16[4,1,1,128]{3,2,1,0:T(2,128)(2,1)S(1)}, bf16[4,1,1,128]{3,2,1,0:T(2,128)(2,1)S(1)}, u32[]{:S(2)}, u32[]{:S(2)}) collective-permute-start(bf16[4,1,1,128]{3,2,1,0:T(2,128)(2,1)S(1)} %slice.725), channel_id=1, source_target_pairs={{24,0},{25,1},{26,2},{27,3},{28,4},{29,5},{30,6},{31,7}} | collective-permute-start | bytes 3080 | tf_op jit(solution)/shard_map/ppermute | solution.py:32
  56.2 0.1 fusion.14
  56.3 0.1 fusion.12
  56.4 0.1 slice.766
  56.5 0.0 copy-start.2
  56.5 0.1 fusion.11
  56.6 0.7 copy-done.2
  57.4 1.4 %broadcast_in_dim.2 = f32[32,1,6912]{2,1,0:T(1,128)} broadcast(f32[6912]{0:T(1024)S(1)} %broadcast_multiply_fusion.1), dimensions={2} | broadcast | bytes 912384 | tf_op jit(solution)/shard_map/broadcast_in_dim | solution.py:55
  58.7 8.0 %all-to-all-start.1 = ((f32[32,1,6912]{2,1,0:T(1,128)}), f32[32,1,6912]{2,1,0:T(1,128)S(1)}, u32[]{:S(2)}, u32[]{:S(2)}) async-start(f32[32,1,6912]{2,1,0:T(1,128)} %broadcast_in_dim.2), calls=%async_computation.1 | async-start | bytes 1769472 | tf_op jit(solution)/shard_map/all_to_all | solution.py:56
  66.7 0.0 collective-permute-done.3
  66.8 0.0 collective-permute-done.4
  66.8 0.0 collective-permute-done.5
  67.1 0.7 convolution_bitcast_fusion
  67.9 0.0 copy-start.3
  67.9 0.8 copy.142
  68.7 0.9 %reshape.619 = f32[1,1,8,16,1024]{4,3,2,1,0:T(8,128)S(1)} reshape(f32[4,2,8,2,8,2,64]{6,5,4,3,2,1,0:T(2,128)S(1)} %copy.142) | data formatting | bytes 1048576 | tf_op jit(solution)/shard_map/reshape | solution.py:132
  69.6 0.8 multiply_convert_fusion
  70.5 18.8 %all-to-all-done.1 = f32[32,1,6912]{2,1,0:T(1,128)S(1)} async-done(((f32[32,1,6912]{2,1,0:T(1,128)}), f32[32,1,6912]{2,1,0:T(1,128)S(1)}, u32[]{:S(2)}, u32[]{:S(2)}) %all-to-all-start.1) | async-done | bytes 884768 | tf_op jit(solution)/shard_map/all_to_all | solution.py:56
  89.3 0.9 %copy.327 = f32[27,64,128]{2,1,0:T(8,128)} copy(f32[27,64,128]{2,1,0:T(8,128)S(1)} %bitcast.187) | data formatting | bytes 1769472
  (62 shorter events, 1.2 us)
Async XLA Ops:
  0.6 13.4 %copy-start.7 = (s32[1,1,256]{2,1,0:T(1,128)S(1)}, s32[1,1,256]{2,1,0:T(1,128)}, u32[]{:S(2)}) copy-start(s32[1,1,256]{2,1,0:T(1,128)} %param.35) | copy-start | bytes 3076
  0.6 13.5 %copy-start.4 = (bf16[1,1,4,8,1024]{4,3,2,1,0:T(8,128)(2,1)S(1)}, bf16[1,1,4,8,1024]{4,3,2,1,0:T(8,128)(2,1)}, u32[]{:S(2)}) copy-start(bf16[1,1,4,8,1024]{4,3,2,1,0:T(8,128)(2,1)} %param.34) | copy-start | bytes 196612
  3.3 11.3 %collective-permute-start = (bf16[8,16,1,64]{3,2,1,0:T(2,128)(2,1)S(1)}, bf16[8,16,1,64]{3,2,1,0:T(2,128)(2,1)S(1)}, u32[]{:S(2)}, u32[]{:S(2)}) collective-permute-start(bf16[8,16,1,64]{3,2,1,0:T(2,128)(2,1)S(1)} %slice.734), channel_id=1, source_target_pairs={{0,8},{16,24},{1,9},{17,25},{2,10},{18,26},{3,11},{19,27},{4,12},{... | collective-permute-start | bytes 49160 | tf_op jit(solution)/shard_map/ppermute | solution.py:32
  8.2 7.8 %collective-permute-start.1 = (bf16[8,1,16,64]{3,2,1,0:T(8,128)(2,1)S(1)}, bf16[8,1,16,64]{3,2,1,0:T(8,128)(2,1)S(1)}, u32[]{:S(2)}, u32[]{:S(2)}) collective-permute-start(bf16[8,1,16,64]{3,2,1,0:T(8,128)(2,1)S(1)} %slice.735), channel_id=1, source_target_pairs={{0,16},{8,24},{1,17},{9,25},{2,18},{10,26},{3,19},{11,27},{4,20},{... | collective-permute-start | bytes 49160 | tf_op jit(solution)/shard_map/ppermute | solution.py:32
  12.7 3.5 %collective-permute-start.2 = (bf16[8,1,1,64]{3,2,1,0:T(2,128)(2,1)S(1)}, bf16[8,1,1,64]{3,2,1,0:T(2,128)(2,1)S(1)}, u32[]{:S(2)}, u32[]{:S(2)}) collective-permute-start(bf16[8,1,1,64]{3,2,1,0:T(2,128)(2,1)S(1)} %slice.736), channel_id=1, source_target_pairs={{0,24},{1,25},{2,26},{3,27},{4,28},{5,29},{6,30},{7,31}} | collective-permute-start | bytes 3080 | tf_op jit(solution)/shard_map/ppermute | solution.py:32
  14.3 37.9 %copy-start.1 = (bf16[4,8,8,128]{3,2,1,0:T(8,128)(2,1)}, bf16[4,8,8,128]{3,2,1,0:T(8,128)(2,1)S(1)}, u32[]{:S(2)}) copy-start(bf16[4,8,8,128]{3,2,1,0:T(8,128)(2,1)S(1)} %bitcast_multiply_fusion) | copy-start | bytes 196612
  21.8 1.6 %copy-start.6 = (bf16[27,4,8,8,64]{4,3,2,0,1:T(8,128)(2,1)}, bf16[27,4,8,8,64]{4,3,2,0,1:T(8,128)(2,1)S(1)}, u32[]{:S(2)}) copy-start(bf16[27,4,8,8,64]{4,3,2,0,1:T(8,128)(2,1)S(1)} %constant_dynamic-update-slice_fusion) | copy-start | bytes 2654212
  23.5 5.4 %copy-start.5 = (s32[1,1,2048]{2,1,0:T(1,128)S(1)}, s32[1,1,2048]{2,1,0:T(1,128)}, u32[]{:S(2)}) copy-start(s32[1,1,2048]{2,1,0:T(1,128)} %param.37) | copy-start | bytes 24580
  23.5 28.1 %all-to-all-start = ((f32[32,1,6912]{2,1,0:T(1,128)}), f32[32,1,6912]{2,1,0:T(1,128)S(1)}, u32[]{:S(2)}, u32[]{:S(2)}) async-start(f32[32,1,6912]{2,1,0:T(1,128)} %bitcast.31), calls=%async_computation | async-start | bytes 1769472 | tf_op jit(solution)/shard_map/all_to_all | solution.py:49
  28.9 1.0 %copy-start = (bf16[27,64,128]{2,1,0:T(8,128)(2,1)S(1)}, bf16[27,64,128]{2,1,0:T(8,128)(2,1)}, u32[]{:S(2)}) copy-start(bf16[27,64,128]{2,1,0:T(8,128)(2,1)} %param.38) | copy-start | bytes 1327108
  52.3 14.4 %collective-permute-start.3 = (bf16[4,8,1,128]{3,2,1,0:T(2,128)(2,1)S(1)}, bf16[4,8,1,128]{3,2,1,0:T(2,128)(2,1)S(1)}, u32[]{:S(2)}, u32[]{:S(2)}) collective-permute-start(bf16[4,8,1,128]{3,2,1,0:T(2,128)(2,1)S(1)} %slice.723), channel_id=1, source_target_pairs={{8,0},{24,16},{9,1},{25,17},{10,2},{26,18},{11,3},{27,19},{12,4},{... | collective-permute-start | bytes 24584 | tf_op jit(solution)/shard_map/ppermute | solution.py:32
  53.6 13.1 %collective-permute-start.4 = (bf16[4,1,8,128]{3,2,1,0:T(8,128)(2,1)S(1)}, bf16[4,1,8,128]{3,2,1,0:T(8,128)(2,1)S(1)}, u32[]{:S(2)}, u32[]{:S(2)}) collective-permute-start(bf16[4,1,8,128]{3,2,1,0:T(8,128)(2,1)S(1)} %slice.724), channel_id=1, source_target_pairs={{16,0},{24,8},{17,1},{25,9},{18,2},{26,10},{19,3},{27,11},{20,4},{... | collective-permute-start | bytes 24584 | tf_op jit(solution)/shard_map/ppermute | solution.py:32
  54.9 11.9 %collective-permute-start.5 = (bf16[4,1,1,128]{3,2,1,0:T(2,128)(2,1)S(1)}, bf16[4,1,1,128]{3,2,1,0:T(2,128)(2,1)S(1)}, u32[]{:S(2)}, u32[]{:S(2)}) collective-permute-start(bf16[4,1,1,128]{3,2,1,0:T(2,128)(2,1)S(1)} %slice.725), channel_id=1, source_target_pairs={{24,0},{25,1},{26,2},{27,3},{28,4},{29,5},{30,6},{31,7}} | collective-permute-start | bytes 3080 | tf_op jit(solution)/shard_map/ppermute | solution.py:32
  56.5 0.8 copy-start.2
  58.7 30.5 %all-to-all-start.1 = ((f32[32,1,6912]{2,1,0:T(1,128)}), f32[32,1,6912]{2,1,0:T(1,128)S(1)}, u32[]{:S(2)}, u32[]{:S(2)}) async-start(f32[32,1,6912]{2,1,0:T(1,128)} %broadcast_in_dim.2), calls=%async_computation.1 | async-start | bytes 1769472 | tf_op jit(solution)/shard_map/all_to_all | solution.py:56
  67.9 1.8 %copy-start.3 = (bf16[1,1,8,16,1024]{4,3,2,1,0:T(8,128)(2,1)S(1)}, bf16[1,1,8,16,1024]{4,3,2,1,0:T(8,128)(2,1)}, u32[]{:S(2)}) copy-start(bf16[1,1,8,16,1024]{4,3,2,1,0:T(8,128)(2,1)} %param.36) | copy-start | bytes 786436

commit v3 on v2

--- a/solution.py
+++ b/solution.py
@@ -97,8 +97,8 @@
     grads = jnp.einsum(
         "kabco,abci->koi", gathered, masked, preferred_element_type=jnp.float32
     )
+    grads, masked_late, weight_late = lax.optimization_barrier((grads, masked, up_weight))
     reduced, plan = all_reduce(grads)
-    reduced, masked_late, weight_late = lax.optimization_barrier((reduced, masked, up_weight))
 
     back = jnp.einsum(
         "kabco,koi->abci", gathered, up_weight, preferred_element_type=jnp.float32

time: 90.8 us -> 90.8 us (level)
  local copies, waits for them, and re-layouts: 16 us -> 19.5 us
  waiting for transfers between devices: 37.8 us -> 35 us
    all_to_all x1, starting transfers between devices: 7.98 us -> 3.8 us  [all_spread(): whole = lax.all_to_all(spread, AXES, 0, 0, tiled=True)]
    all_to_all x1, starting transfers between devices: 5.39 us -> 9.02 us  [all_reduce(): parts = lax.all_to_all(flat.reshape(devices, chunk), AXES, 0, 0, tiled=True)]
    all_to_all x1, waiting for transfers between devices: 19 us -> 16 us  [all_reduce(): parts = lax.all_to_all(flat.reshape(devices, chunk), AXES, 0, 0, tiled=True)]
    unnamed x51 -> x53, local copies, waits for them, and re-layouts: 3.29 us -> 4.76 us
    scatter x7, local copies, waits for them, and re-layouts: 0.09 us -> 1.5 us  [body(): extended = extended.at[target].set(got)]
  transfers between devices with their start and end apart: 8 -> 8, of which waited for: 2 -> 2; matrix products, arithmetic and copies ran while one was open for 12% -> 13% of each run, Pallas kernels for 0% -> 0%
where the time goes in v3:
time: 90.8 us; the launch traced here: 90.1 us
  waiting for transfers between devices  35 us (39%)
  starting transfers between devices  27.4 us (30%)
  local copies, waits for them, and re-layouts  19.5 us (21%)
  matrix products  3.53 us (4%)
  other arithmetic  3.42 us (4%)
  between operations  1.21 us (1%)
    all_to_all x1, waiting for transfers between devices, all_spread(): whole = lax.all_to_all(spread, AXES, 0, 0, tiled=True)  19 us
    all_to_all x1, waiting for transfers between devices, all_reduce(): parts = lax.all_to_all(flat.reshape(devices, chunk), AXES, 0, 0, tiled=True)  16 us
    ppermute x6, starting transfers between devices, exchange(): return lax.ppermute(piece, 'brick', pairs)  14.6 us
    all_to_all x1, starting transfers between devices, all_reduce(): parts = lax.all_to_all(flat.reshape(devices, chunk), AXES, 0, 0, tiled=True)  9.02 us
    unnamed x53, local copies, waits for them, and re-layouts  4.76 us
    all_to_all x1, starting transfers between devices, all_spread(): whole = lax.all_to_all(spread, AXES, 0, 0, tiled=True)  3.8 us
    slice x2, local copies, waits for them, and re-layouts, body(): windows.append(paired[tuple(index)])  3.59 us
    scatter x7, local copies, waits for them, and re-layouts, body(): widened = widened.at[target].set(got)  2.25 us
  transfers between devices with their start and end apart: 8, of which 2 were waited for; matrix products, arithmetic and copies ran while one was open for 13% of the time, Pallas kernels for 0%

profile of v3, /device:TPU:0, one launch (start us, length us, event | category | flops | bytes accessed | tf_op | source)
XLA Modules:
  0.0 90.1 jit_solution(16483294098965372998)
XLA Ops:
  0.6 0.0 copy-start.5
  0.6 0.0 copy-start.8
  0.7 0.0 copy-start.4
  0.7 1.4 %reshape.616 = bf16[8,16,16,64]{3,2,1,0:T(8,128)(2,1)S(1)} reshape(bf16[1,1,8,16,1024]{4,3,2,1,0:T(8,128)(2,1)} %param.39) | data formatting | bytes 524288 | tf_op jit(solution)/shard_map/reshape | solution.py:73
  2.0 0.7 convert_reduce_fusion
  2.8 0.1 convert_element_type.65
  2.9 0.3 broadcast_multiply_fusion
  3.2 0.1 slice.734
  3.3 4.9 %collective-permute-start = (bf16[8,16,1,64]{3,2,1,0:T(2,128)(2,1)S(1)}, bf16[8,16,1,64]{3,2,1,0:T(2,128)(2,1)S(1)}, u32[]{:S(2)}, u32[]{:S(2)}) collective-permute-start(bf16[8,16,1,64]{3,2,1,0:T(2,128)(2,1)S(1)} %slice.734), channel_id=1, source_target_pairs={{0,8},{16,24},{1,9},{17,25},{2,10},{18,26},{3,11},{19,27},{4,12},{... | collective-permute-start | bytes 49160 | tf_op jit(solution)/shard_map/ppermute | solution.py:32
  8.2 4.5 %collective-permute-start.1 = (bf16[8,1,16,64]{3,2,1,0:T(8,128)(2,1)S(1)}, bf16[8,1,16,64]{3,2,1,0:T(8,128)(2,1)S(1)}, u32[]{:S(2)}, u32[]{:S(2)}) collective-permute-start(bf16[8,1,16,64]{3,2,1,0:T(8,128)(2,1)S(1)} %slice.735), channel_id=1, source_target_pairs={{0,16},{8,24},{1,17},{9,25},{2,18},{10,26},{3,19},{11,27},{4,20},{... | collective-permute-start | bytes 49160 | tf_op jit(solution)/shard_map/ppermute | solution.py:32
  12.7 1.3 %collective-permute-start.2 = (bf16[8,1,1,64]{3,2,1,0:T(2,128)(2,1)S(1)}, bf16[8,1,1,64]{3,2,1,0:T(2,128)(2,1)S(1)}, u32[]{:S(2)}, u32[]{:S(2)}) collective-permute-start(bf16[8,1,1,64]{3,2,1,0:T(2,128)(2,1)S(1)} %slice.736), channel_id=1, source_target_pairs={{0,24},{1,25},{2,26},{3,27},{4,28},{5,29},{6,30},{7,31}} | collective-permute-start | bytes 3080 | tf_op jit(solution)/shard_map/ppermute | solution.py:32
  14.0 0.0 copy-done.8
  14.1 0.1 convert_element_type.67
  14.2 0.0 copy-done.4
  14.2 0.7 bitcast_multiply_fusion
  15.0 0.3 pad.68
  15.2 0.1 convert_element_type.62
  15.3 0.3 mul.45
  15.7 0.3 mul.46
  16.0 0.0 collective-permute-done
  16.0 1.4 %scatter.46 = bf16[10,18,18,64]{3,2,1,0:T(8,128)(2,1)S(1)} dynamic-update-slice(bf16[10,18,18,64]{3,2,1,0:T(8,128)(2,1)S(1)} %pad.68, bf16[8,16,1,64]{3,2,1,0:T(2,128)(2,1)S(1)} %collective-permute-done, s32[]{:T(128)} %constant.472.clone.1, s32[]{:T(128)} %constant.472.clone.1, s32[]{:T(128)} %constant.473.clone.1, s32[]{:T(128)} %constant.473.clone.1) | dynamic-update-slice | bytes 32772 | tf_op jit(solution)/shard_map/scatter | solution.py:85
  17.4 0.0 collective-permute-done.1
  17.4 0.2 scatter.49
  17.7 0.0 collective-permute-done.2
  17.7 0.3 scatter.51
  18.0 0.1 scatter.54
  18.1 0.2 scatter.55
  18.4 0.4 reshape.617
  18.7 1.0 %fusion.19 = (bf16[4,1,8,1,8,1,64]{6,5,4,3,2,1,0:T(2,128)(2,1)S(1)}, bf16[4,1,8,1,8,1,64]{6,5,4,3,2,1,0:T(2,128)(2,1)S(1)}, bf16[4,1,8,1,8,1,64]{6,5,4,3,2,1,0:T...) fusion(bf16[5,2,9,2,9,2,64]{6,5,4,3,2,1,0:T(2,128)(2,1)S(1)} %r, ...), kind=kLoop, calls=%fused_computation.106 | loop fusion | bytes 524288 | tf_op jit(solution)/shard_map/slice | solution.py:95
  19.7 2.6 %fusion.18 = (bf16[4,1,8,1,8,1,64]{6,5,4,3,2,1,0:T(2,128)(2,1)S(1)}, bf16[4,1,8,1,8,1,64]{6,5,4,3,2,1,0:T(2,128)(2,1)S(1)}, bf16[4,1,8,1,8,1,64]{6,5,4,3,2,1,0:T...) fusion(bf16[5,2,9,2,9,2,64]{6,5,4,3,2,1,0:T(2,128)(2,1)S(1)} %r, ...), kind=kLoop, calls=%fused_computation.105 | loop fusion | bytes 1245184 | tf_op jit(solution)/shard_map/slice | solution.py:95
  22.6 0.0 copy-start.1
  23.0 0.4 copy-done.1
  23.4 1.6 %convolution_bitcast_fusion.1 = f32[27,64,128]{2,1,0:T(8,128)} fusion(bf16[27,4,8,8,64]{4,3,2,0,1:T(8,128)(2,1)S(1)} %constant_dynamic-update-slice_fusion, bf16[4,8,8,128]{3,2,1,0:T(8,128)(2,1)S(1)} %copy-done.1), kind=kOutput, calls=%fused_computation.3 | convolution fusion | flops 113246208 | bytes 1835008 | tf_op jit(solution)/shard_map/kabco,abci->koi/dot_general | solution.py:97
  25.0 0.0 copy-done.6
  25.1 0.1 pad_slice_fusion.1
  25.3 1.3 %collective-permute-start.3 = (bf16[4,8,1,128]{3,2,1,0:T(2,128)(2,1)S(1)}, bf16[4,8,1,128]{3,2,1,0:T(2,128)(2,1)}, u32[]{:S(2)}, u32[]{:S(2)}) collective-permute-start(bf16[4,8,1,128]{3,2,1,0:T(2,128)(2,1)S(1)} %slice.723), channel_id=1, source_target_pairs={{8,0},{24,16},{9,1},{25,17},{10,2},{26,18},{11,3},{27,19},{12,4},{... | collective-permute-start | bytes 24584 | tf_op jit(solution)/shard_map/ppermute | solution.py:32
  26.6 1.3 %collective-permute-start.4 = (bf16[4,1,8,128]{3,2,1,0:T(8,128)(2,1)S(1)}, bf16[4,1,8,128]{3,2,1,0:T(8,128)(2,1)}, u32[]{:S(2)}, u32[]{:S(2)}) collective-permute-start(bf16[4,1,8,128]{3,2,1,0:T(8,128)(2,1)S(1)} %slice.724), channel_id=1, source_target_pairs={{16,0},{24,8},{17,1},{25,9},{18,2},{26,10},{19,3},{27,11},{20,4},{... | collective-permute-start | bytes 24584 | tf_op jit(solution)/shard_map/ppermute | solution.py:32
  27.9 1.3 %collective-permute-start.5 = (bf16[4,1,1,128]{3,2,1,0:T(2,128)(2,1)S(1)}, bf16[4,1,1,128]{3,2,1,0:T(2,128)(2,1)S(1)}, u32[]{:S(2)}, u32[]{:S(2)}) collective-permute-start(bf16[4,1,1,128]{3,2,1,0:T(2,128)(2,1)S(1)} %slice.725), channel_id=1, source_target_pairs={{24,0},{25,1},{26,2},{27,3},{28,4},{29,5},{30,6},{31,7}} | collective-permute-start | bytes 3080 | tf_op jit(solution)/shard_map/ppermute | solution.py:32
  29.2 9.0 %all-to-all-start = ((f32[32,1,6912]{2,1,0:T(1,128)}), f32[32,1,6912]{2,1,0:T(1,128)S(1)}, u32[]{:S(2)}, u32[]{:S(2)}) async-start(f32[32,1,6912]{2,1,0:T(1,128)} %bitcast.191), calls=%async_computation | async-start | bytes 1769472 | tf_op jit(solution)/shard_map/all_to_all | solution.py:49
  38.2 0.1 fusion.14
  38.3 0.1 fusion.12
  38.4 0.1 slice.766
  38.4 1.3 %copy-done.7 = bf16[27,4,8,8,64]{4,3,2,0,1:T(8,128)(2,1)S(1)} copy-done((bf16[27,4,8,8,64]{4,3,2,0,1:T(8,128)(2,1)S(1)}, bf16[27,4,8,8,64]{4,3,2,0,1:T(8,128)(2,1)}, u32[]{:S(2)}) %copy-start.7) | copy-done | bytes 884760
  39.7 1.2 %fusion.8 = bf16[4,8,8,128]{3,2,0,1:T(8,128)(2,1)} fusion(bf16[27,4,8,8,64]{4,3,2,0,1:T(8,128)(2,1)S(1)} %copy-done.7, bf16[27,64,128]{2,1,0:T(8,128)(2,1)S(1)} %copy-done, f32[4,8,8]{2,0,1:T(4,128)S(1)} %copy.143), kind=kOutput, calls=%fused_computation.8 | convolution fusion | flops 113311744 | bytes 1393664 | tf_op jit(solution)/shard_map/kabco,koi->abci/dot_general | solution.py:103
  40.9 0.1 fusion.11
  41.0 0.8 copy-done.2
  41.8 0.9 reshape.623
  42.7 0.7 copy.145
  43.3 0.0 collective-permute-done.3
  43.3 0.7 constant_dynamic-update-slice_fusion.39
  44.1 0.0 collective-permute-done.4
  44.1 0.7 constant_dynamic-update-slice_fusion.38
  44.8 0.0 collective-permute-done.5
  44.9 16.0 %all-to-all-done = f32[32,1,6912]{2,1,0:T(1,128)S(1)} async-done(((f32[32,1,6912]{2,1,0:T(1,128)}), f32[32,1,6912]{2,1,0:T(1,128)S(1)}, u32[]{:S(2)}, u32[]{:S(2)}) %all-to-all-start) | async-done | bytes 884768 | tf_op jit(solution)/shard_map/all_to_all | solution.py:49
  60.9 0.5 reduce_sum.9
  61.4 1.4 %broadcast_in_dim.2 = f32[32,1,6912]{2,1,0:T(1,128)} broadcast(f32[6912]{0:T(1024)S(1)} %broadcast_multiply_fusion.1), dimensions={2} | broadcast | bytes 912384 | tf_op jit(solution)/shard_map/broadcast_in_dim | solution.py:55
  62.8 3.8 %all-to-all-start.1 = ((f32[32,1,6912]{2,1,0:T(1,128)}), f32[32,1,6912]{2,1,0:T(1,128)S(1)}, u32[]{:S(2)}, u32[]{:S(2)}) async-start(f32[32,1,6912]{2,1,0:T(1,128)} %broadcast_in_dim.2), calls=%async_computation.1 | async-start | bytes 1769472 | tf_op jit(solution)/shard_map/all_to_all | solution.py:56
  66.8 0.7 convolution_bitcast_fusion
  67.5 0.0 copy-start.3
  67.6 0.8 copy.141
  68.4 0.9 %reshape.622 = f32[1,1,8,16,1024]{4,3,2,1,0:T(8,128)S(1)} reshape(f32[4,2,8,2,8,2,64]{6,5,4,3,2,1,0:T(2,128)S(1)} %copy.141) | data formatting | bytes 1048576 | tf_op jit(solution)/shard_map/reshape | solution.py:132
  69.3 0.8 multiply_convert_fusion
  70.1 19.0 %all-to-all-done.1 = f32[32,1,6912]{2,1,0:T(1,128)S(1)} async-done(((f32[32,1,6912]{2,1,0:T(1,128)}), f32[32,1,6912]{2,1,0:T(1,128)S(1)}, u32[]{:S(2)}, u32[]{:S(2)}) %all-to-all-start.1) | async-done | bytes 884768 | tf_op jit(solution)/shard_map/all_to_all | solution.py:56
  89.2 0.9 %copy.327 = f32[27,64,128]{2,1,0:T(8,128)} copy(f32[27,64,128]{2,1,0:T(8,128)S(1)} %bitcast.187) | data formatting | bytes 1769472
  (64 shorter events, 1.1 us)
Async XLA Ops:
  0.6 14.3 %copy-start.5 = (s32[1,1,2048]{2,1,0:T(1,128)S(1)}, s32[1,1,2048]{2,1,0:T(1,128)}, u32[]{:S(2)}) copy-start(s32[1,1,2048]{2,1,0:T(1,128)} %param.37) | copy-start | bytes 24580
  0.6 13.4 %copy-start.8 = (s32[1,1,256]{2,1,0:T(1,128)S(1)}, s32[1,1,256]{2,1,0:T(1,128)}, u32[]{:S(2)}) copy-start(s32[1,1,256]{2,1,0:T(1,128)} %param.35) | copy-start | bytes 3076
  0.7 13.5 %copy-start.4 = (bf16[1,1,4,8,1024]{4,3,2,1,0:T(8,128)(2,1)S(1)}, bf16[1,1,4,8,1024]{4,3,2,1,0:T(8,128)(2,1)}, u32[]{:S(2)}) copy-start(bf16[1,1,4,8,1024]{4,3,2,1,0:T(8,128)(2,1)} %param.34) | copy-start | bytes 196612
  3.3 12.7 %collective-permute-start = (bf16[8,16,1,64]{3,2,1,0:T(2,128)(2,1)S(1)}, bf16[8,16,1,64]{3,2,1,0:T(2,128)(2,1)S(1)}, u32[]{:S(2)}, u32[]{:S(2)}) collective-permute-start(bf16[8,16,1,64]{3,2,1,0:T(2,128)(2,1)S(1)} %slice.734), channel_id=1, source_target_pairs={{0,8},{16,24},{1,9},{17,25},{2,10},{18,26},{3,11},{19,27},{4,12},{... | collective-permute-start | bytes 49160 | tf_op jit(solution)/shard_map/ppermute | solution.py:32
  8.2 9.2 %collective-permute-start.1 = (bf16[8,1,16,64]{3,2,1,0:T(8,128)(2,1)S(1)}, bf16[8,1,16,64]{3,2,1,0:T(8,128)(2,1)S(1)}, u32[]{:S(2)}, u32[]{:S(2)}) collective-permute-start(bf16[8,1,16,64]{3,2,1,0:T(8,128)(2,1)S(1)} %slice.735), channel_id=1, source_target_pairs={{0,16},{8,24},{1,17},{9,25},{2,18},{10,26},{3,19},{11,27},{4,20},{... | collective-permute-start | bytes 49160 | tf_op jit(solution)/shard_map/ppermute | solution.py:32
  12.7 4.9 %collective-permute-start.2 = (bf16[8,1,1,64]{3,2,1,0:T(2,128)(2,1)S(1)}, bf16[8,1,1,64]{3,2,1,0:T(2,128)(2,1)S(1)}, u32[]{:S(2)}, u32[]{:S(2)}) collective-permute-start(bf16[8,1,1,64]{3,2,1,0:T(2,128)(2,1)S(1)} %slice.736), channel_id=1, source_target_pairs={{0,24},{1,25},{2,26},{3,27},{4,28},{5,29},{6,30},{7,31}} | collective-permute-start | bytes 3080 | tf_op jit(solution)/shard_map/ppermute | solution.py:32
  22.6 0.8 copy-start.1
  23.4 1.6 %copy-start.6 = (bf16[27,4,8,8,64]{4,3,2,0,1:T(8,128)(2,1)}, bf16[27,4,8,8,64]{4,3,2,0,1:T(8,128)(2,1)S(1)}, u32[]{:S(2)}) copy-start(bf16[27,4,8,8,64]{4,3,2,0,1:T(8,128)(2,1)S(1)} %constant_dynamic-update-slice_fusion) | copy-start | bytes 2654212
  23.4 1.7 %copy-start = (bf16[27,64,128]{2,1,0:T(8,128)(2,1)S(1)}, bf16[27,64,128]{2,1,0:T(8,128)(2,1)}, u32[]{:S(2)}) copy-start(bf16[27,64,128]{2,1,0:T(8,128)(2,1)} %param.38) | copy-start | bytes 1327108
  25.3 18.1 %collective-permute-start.3 = (bf16[4,8,1,128]{3,2,1,0:T(2,128)(2,1)S(1)}, bf16[4,8,1,128]{3,2,1,0:T(2,128)(2,1)}, u32[]{:S(2)}, u32[]{:S(2)}) collective-permute-start(bf16[4,8,1,128]{3,2,1,0:T(2,128)(2,1)S(1)} %slice.723), channel_id=1, source_target_pairs={{8,0},{24,16},{9,1},{25,17},{10,2},{26,18},{11,3},{27,19},{12,4},{... | collective-permute-start | bytes 24584 | tf_op jit(solution)/shard_map/ppermute | solution.py:32
  26.6 17.5 %collective-permute-start.4 = (bf16[4,1,8,128]{3,2,1,0:T(8,128)(2,1)S(1)}, bf16[4,1,8,128]{3,2,1,0:T(8,128)(2,1)}, u32[]{:S(2)}, u32[]{:S(2)}) collective-permute-start(bf16[4,1,8,128]{3,2,1,0:T(8,128)(2,1)S(1)} %slice.724), channel_id=1, source_target_pairs={{16,0},{24,8},{17,1},{25,9},{18,2},{26,10},{19,3},{27,11},{20,4},{... | collective-permute-start | bytes 24584 | tf_op jit(solution)/shard_map/ppermute | solution.py:32
  27.9 16.9 %collective-permute-start.5 = (bf16[4,1,1,128]{3,2,1,0:T(2,128)(2,1)S(1)}, bf16[4,1,1,128]{3,2,1,0:T(2,128)(2,1)S(1)}, u32[]{:S(2)}, u32[]{:S(2)}) collective-permute-start(bf16[4,1,1,128]{3,2,1,0:T(2,128)(2,1)S(1)} %slice.725), channel_id=1, source_target_pairs={{24,0},{25,1},{26,2},{27,3},{28,4},{29,5},{30,6},{31,7}} | collective-permute-start | bytes 3080 | tf_op jit(solution)/shard_map/ppermute | solution.py:32
  29.2 31.8 %all-to-all-start = ((f32[32,1,6912]{2,1,0:T(1,128)}), f32[32,1,6912]{2,1,0:T(1,128)S(1)}, u32[]{:S(2)}, u32[]{:S(2)}) async-start(f32[32,1,6912]{2,1,0:T(1,128)} %bitcast.191), calls=%async_computation | async-start | bytes 1769472 | tf_op jit(solution)/shard_map/all_to_all | solution.py:49
  38.3 1.5 %copy-start.7 = (bf16[27,4,8,8,64]{4,3,2,0,1:T(8,128)(2,1)S(1)}, bf16[27,4,8,8,64]{4,3,2,0,1:T(8,128)(2,1)}, u32[]{:S(2)}) copy-start(bf16[27,4,8,8,64]{4,3,2,0,1:T(8,128)(2,1)} %copy-done.6) | copy-start | bytes 2654212
  40.9 0.8 copy-start.2
  62.8 26.4 %all-to-all-start.1 = ((f32[32,1,6912]{2,1,0:T(1,128)}), f32[32,1,6912]{2,1,0:T(1,128)S(1)}, u32[]{:S(2)}, u32[]{:S(2)}) async-start(f32[32,1,6912]{2,1,0:T(1,128)} %broadcast_in_dim.2), calls=%async_computation.1 | async-start | bytes 1769472 | tf_op jit(solution)/shard_map/all_to_all | solution.py:56
  67.5 1.8 %copy-start.3 = (bf16[1,1,8,16,1024]{4,3,2,1,0:T(8,128)(2,1)S(1)}, bf16[1,1,8,16,1024]{4,3,2,1,0:T(8,128)(2,1)}, u32[]{:S(2)}) copy-start(bf16[1,1,8,16,1024]{4,3,2,1,0:T(8,128)(2,1)} %param.36) | copy-start | bytes 786436

commit v4 on v3

--- a/solution.py
+++ b/solution.py
@@ -3,11 +3,12 @@
 import jax
 import jax.numpy as jnp
 from jax import lax
-from jax.sharding import PartitionSpec as P
+from jax.sharding import Mesh, PartitionSpec as P
 
 OFFSETS = tuple((dx, dy, dz) for dx in range(2) for dy in range(2) for dz in range(2))
 DIRECTIONS = OFFSETS[1:]
-AXES = ("brick", "batch")
+BATCH = ("chip", "core")
+OTHERS = ("brick", "chip")
 
 
 def region_of(rank):
@@ -41,20 +42,28 @@
 
 
 def all_reduce(grads):
-    devices = lax.axis_size("brick") * lax.axis_size("batch")
+    devices = lax.axis_size("brick") * lax.axis_size("chip")
     flat = grads.reshape(-1)
     size = flat.shape[0]
-    chunk = -(-size // devices)
-    flat = jnp.pad(flat, (0, chunk * devices - size))
-    parts = lax.all_to_all(flat.reshape(devices, chunk), AXES, 0, 0, tiled=True)
+    chunk = -(-size // (2 * devices))
+    flat = jnp.pad(flat, (0, 2 * chunk * devices - size)).reshape(2, devices * chunk)
+    core = lax.axis_index("core")
+    got = lax.ppermute(jnp.where(core == 0, flat[1], flat[0]), "core", [(0, 1), (1, 0)])
+    half = jnp.where(core == 0, flat[0], flat[1]) + got
+    parts = lax.all_to_all(half.reshape(devices, chunk), OTHERS, 0, 0, tiled=True)
     return parts.sum(axis=0), (devices, chunk, size)
 
 
 def all_spread(reduced, plan):
     devices, chunk, size = plan
     spread = jnp.broadcast_to(reduced[None], (devices, chunk))
-    whole = lax.all_to_all(spread, AXES, 0, 0, tiled=True)
-    return whole.reshape(-1)[:size]
+    half = lax.all_to_all(spread, OTHERS, 0, 0, tiled=True).reshape(-1)
+    other = lax.ppermute(half, "core", [(0, 1), (1, 0)])
+    core = lax.axis_index("core")
+    whole = jnp.where(
+        core == 0, jnp.concatenate([half, other]), jnp.concatenate([other, half])
+    )
+    return whole[:size]
 
 
 def body(coarse, coarse_mask, skip, fine_mask, up_weight, fine_grad):
@@ -135,19 +144,23 @@
     )
     fine_out = fine.astype(jnp.bfloat16).reshape(skip.shape)
 
-    scale = 1.0 / math.sqrt(regions * lax.axis_size("batch") * size_x * size_y * size_z)
+    scale = 1.0 / math.sqrt(regions * lax.axis_size("chip") * lax.axis_size("core") * size_x * size_y * size_z)
     weight_grad = all_spread(reduced * scale, plan).reshape(grads.shape)
     return (fine_out, coarse_grad, weight_grad)
 
 
 def solution(mesh):
+    brick, batch = mesh.shape["brick"], mesh.shape["batch"]
+    pairs = Mesh(
+        mesh.devices.reshape(brick, batch // 2, 2), ("brick", "chip", "core")
+    )
     in_specs = (
-        P("batch", "brick", None, None, None),
-        P("batch", "brick", None),
-        P("batch", "brick", None, None, None),
-        P("batch", "brick", None),
+        P(BATCH, "brick", None, None, None),
+        P(BATCH, "brick", None),
+        P(BATCH, "brick", None, None, None),
+        P(BATCH, "brick", None),
         P(),
-        P("batch", "brick", None, None, None),
+        P(BATCH, "brick", None, None, None),
     )
-    out_specs = (P("batch", "brick", None, None, None), P("batch", "brick", None, None, None), P())
-    return jax.shard_map(body, mesh=mesh, in_specs=in_specs, out_specs=out_specs, check_vma=False)
+    out_specs = (P(BATCH, "brick", None, None, None), P(BATCH, "brick", None, None, None), P())
+    return jax.shard_map(body, mesh=pairs, in_specs=in_specs, out_specs=out_specs, check_vma=False)

time: 90.8 us -> 83.7 us (0.922)
  waiting for transfers between devices: 35 us -> 24.6 us
  other arithmetic: 3.42 us -> 6.7 us
  starting transfers between devices: 27.4 us -> 24.2 us
  local copies, waits for them, and re-layouts: 19.5 us -> 22.3 us
    all_to_all x2, waiting for transfers between devices: 35 us -> 21.4 us  [the longest x1 11.1 us: all_reduce(): lax.all_to_all(half.reshape(devices, chunk), OTHERS, 0, 0, tiled=True)]
    all_to_all x2, starting transfers between devices: 12.8 us -> 9.61 us  [the longest x1 5.84 us: all_reduce(): lax.all_to_all(half.reshape(devices, chunk), OTHERS, 0, 0, tiled=True)]
    ppermute x6, waiting for transfers between devices: 0.02 us -> 3.2 us  [exchange(): return lax.ppermute(piece, 'brick', pairs)]
    select_n x0 -> x2, other arithmetic: none -> 2.35 us  [the longest x1 1.38 us: all_reduce(): jnp.where(core == 0, flat[1], flat[0])]
    unnamed x53 -> x54, local copies, waits for them, and re-layouts: 4.76 us -> 7.08 us
    reshape x0 -> x1, local copies, waits for them, and re-layouts: none -> 1.73 us  [all_reduce(): jnp.pad(flat, (0, 2 * chunk * devices - size)).reshape(2, devices * chunk)]
    scatter x7, local copies, waits for them, and re-layouts: 1.5 us -> 0.09 us  [body(): extended = extended.at[target].set(got)]
    dot_general x1, matrix products: 0.74 us -> 1.78 us  [body(): jnp.einsum('xyzabci,xpyqzroi->apbqcro', shifted, forward_weight(weight_la...]
  transfers between devices with their start and end apart: 8 -> 10, of which waited for: 2 -> 3; matrix products, arithmetic and copies ran while one was open for 13% -> 18% of each run, Pallas kernels for 0% -> 0%
where the time goes in v4:
time: 83.7 us; the launch traced here: 83 us
  waiting for transfers between devices  24.6 us (29%)
  starting transfers between devices  24.2 us (29%)
  local copies, waits for them, and re-layouts  22.3 us (27%)
  other arithmetic  6.7 us (8%)
  matrix products  3.95 us (5%)
  between operations  1.24 us (1%)
    ppermute x6, starting transfers between devices, exchange(): return lax.ppermute(piece, 'brick', pairs)  14.6 us
    all_to_all x1, waiting for transfers between devices, all_reduce(): lax.all_to_all(half.reshape(devices, chunk), OTHERS, 0, 0, tiled=True)  11.1 us
    all_to_all x1, waiting for transfers between devices, all_spread(): half = lax.all_to_all(spread, OTHERS, 0, 0, tiled=True).reshape(-1)  10.3 us
    unnamed x54, local copies, waits for them, and re-layouts  7.08 us
    all_to_all x1, starting transfers between devices, all_reduce(): lax.all_to_all(half.reshape(devices, chunk), OTHERS, 0, 0, tiled=True)  5.84 us
    slice x2, local copies, waits for them, and re-layouts, body(): windows.append(paired[tuple(index)])  3.81 us
    all_to_all x1, starting transfers between devices, all_spread(): half = lax.all_to_all(spread, OTHERS, 0, 0, tiled=True).reshape(-1)  3.78 us
    ppermute x6, waiting for transfers between devices, exchange(): return lax.ppermute(piece, 'brick', pairs)  3.2 us
  transfers between devices with their start and end apart: 10, of which 3 were waited for; matrix products, arithmetic and copies ran while one was open for 18% of the time, Pallas kernels for 0%

profile of v4, /device:TPU:0, one launch (start us, length us, event | category | flops | bytes accessed | tf_op | source)
XLA Modules:
  0.0 83.0 jit_solution(17895018787326937900)
XLA Ops:
  0.6 0.0 copy-start.6
  0.7 1.4 %reshape.631 = bf16[8,16,16,64]{3,2,1,0:T(8,128)(2,1)S(1)} reshape(bf16[1,1,8,16,1024]{4,3,2,1,0:T(8,128)(2,1)} %param.39) | data formatting | bytes 524288 | tf_op jit(solution)/shard_map/reshape | solution.py:82
  2.0 0.7 convert_reduce_fusion
  2.8 0.1 convert_element_type.65
  2.9 0.3 broadcast_multiply_fusion
  3.2 0.1 slice.744
  3.3 4.9 %collective-permute-start = (bf16[8,16,1,64]{3,2,1,0:T(2,128)(2,1)S(1)}, bf16[8,16,1,64]{3,2,1,0:T(2,128)(2,1)S(1)}, u32[]{:S(2)}, u32[]{:S(2)}) collective-permute-start(bf16[8,16,1,64]{3,2,1,0:T(2,128)(2,1)S(1)} %slice.744), channel_id=1, source_target_pairs={{0,8},{16,24},{1,9},{17,25},{2,10},{18,26},{3,11},{19,27},{4,12},{... | collective-permute-start | bytes 49160 | tf_op jit(solution)/shard_map/ppermute | solution.py:33
  8.2 4.5 %collective-permute-start.1 = (bf16[8,1,16,64]{3,2,1,0:T(8,128)(2,1)S(1)}, bf16[8,1,16,64]{3,2,1,0:T(8,128)(2,1)S(1)}, u32[]{:S(2)}, u32[]{:S(2)}) collective-permute-start(bf16[8,1,16,64]{3,2,1,0:T(8,128)(2,1)S(1)} %slice.745), channel_id=1, source_target_pairs={{0,16},{8,24},{1,17},{9,25},{2,18},{10,26},{3,19},{11,27},{4,20},{... | collective-permute-start | bytes 49160 | tf_op jit(solution)/shard_map/ppermute | solution.py:33
  12.7 1.3 %collective-permute-start.2 = (bf16[8,1,1,64]{3,2,1,0:T(2,128)(2,1)S(1)}, bf16[8,1,1,64]{3,2,1,0:T(2,128)(2,1)S(1)}, u32[]{:S(2)}, u32[]{:S(2)}) collective-permute-start(bf16[8,1,1,64]{3,2,1,0:T(2,128)(2,1)S(1)} %slice.746), channel_id=1, source_target_pairs={{0,24},{1,25},{2,26},{3,27},{4,28},{5,29},{6,30},{7,31}} | collective-permute-start | bytes 3080 | tf_op jit(solution)/shard_map/ppermute | solution.py:33
  14.1 0.1 convert_element_type.67
  14.2 0.1 bitcast_multiply_fusion
  14.3 0.0 copy-start.2
  14.4 0.3 pad.68
  14.6 0.1 convert_element_type.62
  14.7 0.3 mul.45
  15.1 0.3 mul.46
  15.4 1.4 %scatter.46 = bf16[10,18,18,64]{3,2,1,0:T(8,128)(2,1)S(1)} dynamic-update-slice(bf16[10,18,18,64]{3,2,1,0:T(8,128)(2,1)S(1)} %pad.68, bf16[8,16,1,64]{3,2,1,0:T(2,128)(2,1)S(1)} %collective-permute-done, s32[]{:T(128)} %constant.475.clone.1, s32[]{:T(128)} %constant.475.clone.1, s32[]{:T(128)} %constant.476.clone.1, s32[]{:T(128)} %constant.476.clone.1) | dynamic-update-slice | bytes 32772 | tf_op jit(solution)/shard_map/scatter | solution.py:94
  16.8 0.0 collective-permute-done.1
  16.8 0.2 scatter.49
  17.1 0.3 scatter.51
  17.4 0.1 scatter.54
  17.5 0.2 scatter.55
  17.8 0.4 reshape.632
  18.1 1.0 %fusion.19 = (bf16[4,1,8,1,8,1,64]{6,5,4,3,2,1,0:T(2,128)(2,1)S(1)}, bf16[4,1,8,1,8,1,64]{6,5,4,3,2,1,0:T(2,128)(2,1)S(1)}, bf16[4,1,8,1,8,1,64]{6,5,4,3,2,1,0:T...) fusion(bf16[5,2,9,2,9,2,64]{6,5,4,3,2,1,0:T(2,128)(2,1)S(1)} %r, ...), kind=kLoop, calls=%fused_computation.109 | loop fusion | bytes 524288 | tf_op jit(solution)/shard_map/slice | solution.py:104
  19.1 2.8 %fusion.18 = (bf16[4,1,8,1,8,1,64]{6,5,4,3,2,1,0:T(2,128)(2,1)S(1)}, bf16[4,1,8,1,8,1,64]{6,5,4,3,2,1,0:T(2,128)(2,1)S(1)}, bf16[4,1,8,1,8,1,64]{6,5,4,3,2,1,0:T...) fusion(bf16[5,2,9,2,9,2,64]{6,5,4,3,2,1,0:T(2,128)(2,1)S(1)} %r, ...), kind=kLoop, calls=%fused_computation.108 | loop fusion | bytes 1245184 | tf_op jit(solution)/shard_map/slice | solution.py:104
  22.7 0.0 copy-start
  22.7 1.6 %convolution_bitcast_fusion.1 = f32[27,64,128]{2,1,0:T(8,128)} fusion(bf16[27,4,8,8,64]{4,3,2,0,1:T(8,128)(2,1)S(1)} %constant_dynamic-update-slice_fusion, bf16[4,8,8,128]{3,2,1,0:T(8,128)(2,1)S(1)} %bitcast_multiply_fusion), kind=kOutput, calls=%fused_computation.3 | convolution fusion | flops 113246208 | bytes 1835008 | tf_op jit(solution)/shard_map/kabco,abci->koi/dot_general | solution.py:106
  24.3 0.6 slice.731
  24.9 0.1 pad_slice_fusion.1
  25.1 1.7 %reshape.639 = f32[2,110592]{1,0:T(2,128)S(1)} reshape(f32[27,64,128]{2,1,0:T(8,128)} %convolution_bitcast_fusion.1) | data formatting | bytes 1769472 | tf_op jit(solution)/shard_map/reshape | solution.py:49
  26.8 1.4 %broadcast_select_fusion = (f32[1,110592]{1,0:T(1,128)}, f32[1,110592]{1,0:T(1,128)S(1)}) fusion(pred[]{:T(512)S(6)} %eq.2, f32[2,110592]{1,0:T(2,128)S(1)} %reshape.639), kind=kLoop, calls=%fused_computation.18 | loop fusion | flops 221184 | bytes 1769473 | tf_op jit(solution)/shard_map/jit(_where)/select_n | solution.py:51
  28.2 1.3 %collective-permute-start.3 = (bf16[4,8,1,128]{3,2,1,0:T(2,128)(2,1)}, bf16[4,8,1,128]{3,2,1,0:T(2,128)(2,1)S(1)}, u32[]{:S(2)}, u32[]{:S(2)}) collective-permute-start(bf16[4,8,1,128]{3,2,1,0:T(2,128)(2,1)} %slice.731), channel_id=1, source_target_pairs={{8,0},{24,16},{9,1},{25,17},{10,2},{26,18},{11,3},{27,19},{12,4},{... | collective-permute-start | bytes 24584 | tf_op jit(solution)/shard_map/ppermute | solution.py:33
  29.5 1.3 %collective-permute-start.4 = (bf16[4,1,8,128]{3,2,1,0:T(8,128)(2,1)S(1)}, bf16[4,1,8,128]{3,2,1,0:T(8,128)(2,1)S(1)}, u32[]{:S(2)}, u32[]{:S(2)}) collective-permute-start(bf16[4,1,8,128]{3,2,1,0:T(8,128)(2,1)S(1)} %slice.732), channel_id=1, source_target_pairs={{16,0},{24,8},{17,1},{25,9},{18,2},{26,10},{19,3},{27,11},{20,4},{... | collective-permute-start | bytes 24584 | tf_op jit(solution)/shard_map/ppermute | solution.py:33
  30.8 1.3 %collective-permute-start.5 = (bf16[4,1,1,128]{3,2,1,0:T(2,128)(2,1)S(1)}, bf16[4,1,1,128]{3,2,1,0:T(2,128)(2,1)S(1)}, u32[]{:S(2)}, u32[]{:S(2)}) collective-permute-start(bf16[4,1,1,128]{3,2,1,0:T(2,128)(2,1)S(1)} %slice.733), channel_id=1, source_target_pairs={{24,0},{25,1},{26,2},{27,3},{28,4},{29,5},{30,6},{31,7}} | collective-permute-start | bytes 3080 | tf_op jit(solution)/shard_map/ppermute | solution.py:33
  32.1 0.1 fusion.14
  32.2 0.1 fusion.12
  32.3 0.1 slice.776
  32.4 1.3 %copy-done.8 = bf16[27,4,8,8,64]{4,3,2,0,1:T(8,128)(2,1)S(1)} copy-done((bf16[27,4,8,8,64]{4,3,2,0,1:T(8,128)(2,1)S(1)}, bf16[27,4,8,8,64]{4,3,2,0,1:T(8,128)(2,1)}, u32[]{:S(2)}) %copy-start.8) | copy-done | bytes 884760
  33.7 0.6 fusion.8
  34.2 0.0 copy-start.3
  34.2 1.1 %fusion.11 = bf16[4,4,4,64,128]{4,3,2,1,0:T(8,128)(2,1)} fusion(bf16[4,3,4,64,128]{4,3,2,1,0:T(8,128)(2,1)S(1)} %fusion.14, bf16[1,4,4,64,128]{4,3,2,1,0:T(8,128)(2,1)S(1)} %pad_slice_fusion, bf16[3,4,4,64,128]{4,3,2,1,0:T(8,128)(2,1)S(1)} %pad_slice_fusion.1, bf16[4,4,3,64,128]{4,3,2,1,0:T(8,128)(2,1)S(1)} %slice.776), kind=kLoop, calls=%fused_computation.10 | loop fusion | flops 1572864 | bytes 3670016 | tf_op jit(solution)/shard_map/jit(_roll_static)/concatenate | solution.py:40
  35.3 0.7 copy.177
  36.1 3.2 %collective-permute-done.5 = bf16[4,1,1,128]{3,2,1,0:T(2,128)(2,1)S(1)} collective-permute-done((bf16[4,1,1,128]{3,2,1,0:T(2,128)(2,1)S(1)}, bf16[4,1,1,128]{3,2,1,0:T(2,128)(2,1)S(1)}, u32[]{:S(2)}, u32[]{:S(2)}) %collective-permute-start.5) | collective-permute-done | bytes 1056 | tf_op jit(solution)/shard_map/ppermute | solution.py:33
  39.3 0.8 add.42
  40.1 5.8 %all-to-all-start = ((f32[16,1,6912]{2,1,0:T(1,128)}), f32[16,1,6912]{2,1,0:T(1,128)S(1)}, u32[]{:S(2)}, u32[]{:S(2)}) async-start(f32[16,1,6912]{2,1,0:T(1,128)} %bitcast.52), calls=%async_computation | async-start | bytes 884736 | tf_op jit(solution)/shard_map/all_to_all | solution.py:53
  46.0 0.6 constant_dynamic-update-slice_fusion.34
  46.6 0.7 constant_dynamic-update-slice_fusion.33
  47.3 0.6 constant_dynamic-update-slice_fusion.32
  47.9 0.7 constant_dynamic-update-slice_fusion.31
  48.6 11.1 %all-to-all-done = f32[16,1,6912]{2,1,0:T(1,128)S(1)} async-done(((f32[16,1,6912]{2,1,0:T(1,128)}), f32[16,1,6912]{2,1,0:T(1,128)S(1)}, u32[]{:S(2)}, u32[]{:S(2)}) %all-to-all-start) | async-done | bytes 442400 | tf_op jit(solution)/shard_map/all_to_all | solution.py:53
  59.6 0.3 reduce_sum.9
  59.9 1.0 %broadcast_in_dim.2 = f32[16,1,6912]{2,1,0:T(1,128)} broadcast(f32[6912]{0:T(1024)S(1)} %broadcast_multiply_fusion.1), dimensions={2} | broadcast | bytes 470016 | tf_op jit(solution)/shard_map/broadcast_in_dim | solution.py:59
  60.9 3.8 %all-to-all-start.1 = ((f32[16,1,6912]{2,1,0:T(1,128)}), f32[16,1,6912]{2,1,0:T(1,128)S(1)}, u32[]{:S(2)}, u32[]{:S(2)}) async-start(f32[16,1,6912]{2,1,0:T(1,128)} %broadcast_in_dim.2), calls=%async_computation.1 | async-start | bytes 884736 | tf_op jit(solution)/shard_map/all_to_all | solution.py:60
  64.7 0.6 constant_dynamic-update-slice_fusion.30
  65.4 0.7 constant_dynamic-update-slice_fusion.29
  66.0 0.6 constant_dynamic-update-slice_fusion.28
  66.7 0.7 constant_dynamic-update-slice_fusion.27
  67.3 10.3 %all-to-all-done.1 = f32[16,1,6912]{2,1,0:T(1,128)S(1)} async-done(((f32[16,1,6912]{2,1,0:T(1,128)}), f32[16,1,6912]{2,1,0:T(1,128)S(1)}, u32[]{:S(2)}, u32[]{:S(2)}) %all-to-all-start.1) | async-done | bytes 442400 | tf_op jit(solution)/shard_map/all_to_all | solution.py:60
  77.6 1.8 %convolution_bitcast_fusion = f32[4,2,8,2,8,2,64]{6,4,2,0,5,3,1:T(8,128)S(1)} fusion(bf16[2,2,2,2,2,2,64,128,1,1]{7,6,5,4,3,2,1,0,9,8:T(8,128)(2,1)S(1)} %bitcast.195, bf16[2,2,2,4,8,8,128,1,1,1]{6,5,4,3,2,1,0,9,8,7:T(8,128)(2,1)} %bitcast.43), kind=kOutput, calls=%fused_computation.2 | convolution fusion | flops 268435456 | bytes 2097152 | tf_op jit(solution)/shard_map/xyzabci,xpyqzroi->apbqcro/dot_general | solution.py:135
  79.4 0.0 copy-start.4
  79.4 0.8 copy.173
  80.2 0.9 %reshape.637 = f32[1,1,8,16,1024]{4,3,2,1,0:T(8,128)S(1)} reshape(f32[4,2,8,2,8,2,64]{6,5,4,3,2,1,0:T(2,128)S(1)} %copy.173) | data formatting | bytes 1048576 | tf_op jit(solution)/shard_map/reshape | solution.py:141
  81.2 0.8 multiply_convert_fusion
  82.0 1.0 %maximum_select_fusion = f32[221184]{0:T(1024)} fusion(f32[110592]{0:T(1024)S(1)} %collective-permute-done.7, f32[110592]{0:T(1024)S(1)} %bitcast.193, pred[]{:T(512)S(6)} %eq.2), kind=kLoop, calls=%fused_computation.17 | loop fusion | flops 663552 | bytes 1769473 | tf_op jit(solution)/shard_map/jit(_where)/select_n | solution.py:63
  (73 shorter events, 1.0 us)
Async XLA Ops:
  0.6 13.7 %copy-start.6 = (s32[1,1,2048]{2,1,0:T(1,128)S(1)}, s32[1,1,2048]{2,1,0:T(1,128)}, u32[]{:S(2)}) copy-start(s32[1,1,2048]{2,1,0:T(1,128)} %param.37) | copy-start | bytes 24580
  0.6 13.4 %copy-start.9 = (s32[1,1,256]{2,1,0:T(1,128)S(1)}, s32[1,1,256]{2,1,0:T(1,128)}, u32[]{:S(2)}) copy-start(s32[1,1,256]{2,1,0:T(1,128)} %param.35) | copy-start | bytes 3076
  0.7 13.5 %copy-start.5 = (bf16[1,1,4,8,1024]{4,3,2,1,0:T(8,128)(2,1)S(1)}, bf16[1,1,4,8,1024]{4,3,2,1,0:T(8,128)(2,1)}, u32[]{:S(2)}) copy-start(bf16[1,1,4,8,1024]{4,3,2,1,0:T(8,128)(2,1)} %param.34) | copy-start | bytes 196612
  3.3 12.1 %collective-permute-start = (bf16[8,16,1,64]{3,2,1,0:T(2,128)(2,1)S(1)}, bf16[8,16,1,64]{3,2,1,0:T(2,128)(2,1)S(1)}, u32[]{:S(2)}, u32[]{:S(2)}) collective-permute-start(bf16[8,16,1,64]{3,2,1,0:T(2,128)(2,1)S(1)} %slice.744), channel_id=1, source_target_pairs={{0,8},{16,24},{1,9},{17,25},{2,10},{18,26},{3,11},{19,27},{4,12},{... | collective-permute-start | bytes 49160 | tf_op jit(solution)/shard_map/ppermute | solution.py:33
  8.2 8.6 %collective-permute-start.1 = (bf16[8,1,16,64]{3,2,1,0:T(8,128)(2,1)S(1)}, bf16[8,1,16,64]{3,2,1,0:T(8,128)(2,1)S(1)}, u32[]{:S(2)}, u32[]{:S(2)}) collective-permute-start(bf16[8,1,16,64]{3,2,1,0:T(8,128)(2,1)S(1)} %slice.745), channel_id=1, source_target_pairs={{0,16},{8,24},{1,17},{9,25},{2,18},{10,26},{3,19},{11,27},{4,20},{... | collective-permute-start | bytes 49160 | tf_op jit(solution)/shard_map/ppermute | solution.py:33
  12.7 4.3 %collective-permute-start.2 = (bf16[8,1,1,64]{3,2,1,0:T(2,128)(2,1)S(1)}, bf16[8,1,1,64]{3,2,1,0:T(2,128)(2,1)S(1)}, u32[]{:S(2)}, u32[]{:S(2)}) collective-permute-start(bf16[8,1,1,64]{3,2,1,0:T(2,128)(2,1)S(1)} %slice.746), channel_id=1, source_target_pairs={{0,24},{1,25},{2,26},{3,27},{4,28},{5,29},{6,30},{7,31}} | collective-permute-start | bytes 3080 | tf_op jit(solution)/shard_map/ppermute | solution.py:33
  14.3 10.6 %copy-start.2 = (bf16[4,8,8,128]{3,2,1,0:T(8,128)(2,1)}, bf16[4,8,8,128]{3,2,1,0:T(8,128)(2,1)S(1)}, u32[]{:S(2)}) copy-start(bf16[4,8,8,128]{3,2,1,0:T(8,128)(2,1)S(1)} %bitcast_multiply_fusion) | copy-start | bytes 196612
  22.6 1.6 %copy-start.7 = (bf16[27,4,8,8,64]{4,3,2,0,1:T(8,128)(2,1)}, bf16[27,4,8,8,64]{4,3,2,0,1:T(8,128)(2,1)S(1)}, u32[]{:S(2)}) copy-start(bf16[27,4,8,8,64]{4,3,2,0,1:T(8,128)(2,1)S(1)} %constant_dynamic-update-slice_fusion) | copy-start | bytes 2654212
  22.7 2.3 %copy-start = (bf16[27,64,128]{2,1,0:T(8,128)(2,1)S(1)}, bf16[27,64,128]{2,1,0:T(8,128)(2,1)}, u32[]{:S(2)}) copy-start(bf16[27,64,128]{2,1,0:T(8,128)(2,1)} %param.38) | copy-start | bytes 1327108
  28.2 11.1 %collective-permute-start.6 = (f32[110592]{0:T(1024)}, f32[110592]{0:T(1024)S(1)}, u32[]{:S(2)}, u32[]{:S(2)}) collective-permute-start(f32[110592]{0:T(1024)} %bitcast.51), channel_id=1, source_target_pairs={{0,1},{1,0},{2,3},{3,2},{4,5},{5,4},{6,7},{7,6},{8,9},{9,8},{10,11... | collective-permute-start | bytes 1327112 | tf_op jit(solution)/shard_map/ppermute | solution.py:51
  28.2 7.8 %collective-permute-start.3 = (bf16[4,8,1,128]{3,2,1,0:T(2,128)(2,1)}, bf16[4,8,1,128]{3,2,1,0:T(2,128)(2,1)S(1)}, u32[]{:S(2)}, u32[]{:S(2)}) collective-permute-start(bf16[4,8,1,128]{3,2,1,0:T(2,128)(2,1)} %slice.731), channel_id=1, source_target_pairs={{8,0},{24,16},{9,1},{25,17},{10,2},{26,18},{11,3},{27,19},{12,4},{... | collective-permute-start | bytes 24584 | tf_op jit(solution)/shard_map/ppermute | solution.py:33
  29.5 6.5 %collective-permute-start.4 = (bf16[4,1,8,128]{3,2,1,0:T(8,128)(2,1)S(1)}, bf16[4,1,8,128]{3,2,1,0:T(8,128)(2,1)S(1)}, u32[]{:S(2)}, u32[]{:S(2)}) collective-permute-start(bf16[4,1,8,128]{3,2,1,0:T(8,128)(2,1)S(1)} %slice.732), channel_id=1, source_target_pairs={{16,0},{24,8},{17,1},{25,9},{18,2},{26,10},{19,3},{27,11},{20,4},{... | collective-permute-start | bytes 24584 | tf_op jit(solution)/shard_map/ppermute | solution.py:33
  30.8 8.4 %collective-permute-start.5 = (bf16[4,1,1,128]{3,2,1,0:T(2,128)(2,1)S(1)}, bf16[4,1,1,128]{3,2,1,0:T(2,128)(2,1)S(1)}, u32[]{:S(2)}, u32[]{:S(2)}) collective-permute-start(bf16[4,1,1,128]{3,2,1,0:T(2,128)(2,1)S(1)} %slice.733), channel_id=1, source_target_pairs={{24,0},{25,1},{26,2},{27,3},{28,4},{29,5},{30,6},{31,7}} | collective-permute-start | bytes 3080 | tf_op jit(solution)/shard_map/ppermute | solution.py:33
  32.2 1.5 %copy-start.8 = (bf16[27,4,8,8,64]{4,3,2,0,1:T(8,128)(2,1)S(1)}, bf16[27,4,8,8,64]{4,3,2,0,1:T(8,128)(2,1)}, u32[]{:S(2)}) copy-start(bf16[27,4,8,8,64]{4,3,2,0,1:T(8,128)(2,1)} %copy-done.7) | copy-start | bytes 2654212
  34.2 1.1 %copy-start.3 = (bf16[4,8,8,128]{3,2,1,0:T(8,128)(2,1)S(1)}, bf16[4,8,8,128]{3,2,1,0:T(8,128)(2,1)}, u32[]{:S(2)}) copy-start(bf16[4,8,8,128]{3,2,1,0:T(8,128)(2,1)} %copy-done.2) | copy-start | bytes 196612
  40.1 37.5 %copy-start.1 = (bf16[4,4,4,64,128]{4,3,2,1,0:T(8,128)(2,1)S(1)}, bf16[4,4,4,64,128]{4,3,2,1,0:T(8,128)(2,1)}, u32[]{:S(2)}) copy-start(bf16[4,4,4,64,128]{4,3,2,1,0:T(8,128)(2,1)} %fusion.11) | copy-start | bytes 3145732
  40.1 19.5 %all-to-all-start = ((f32[16,1,6912]{2,1,0:T(1,128)}), f32[16,1,6912]{2,1,0:T(1,128)S(1)}, u32[]{:S(2)}, u32[]{:S(2)}) async-start(f32[16,1,6912]{2,1,0:T(1,128)} %bitcast.52), calls=%async_computation | async-start | bytes 884736 | tf_op jit(solution)/shard_map/all_to_all | solution.py:53
  60.9 16.7 %all-to-all-start.1 = ((f32[16,1,6912]{2,1,0:T(1,128)}), f32[16,1,6912]{2,1,0:T(1,128)S(1)}, u32[]{:S(2)}, u32[]{:S(2)}) async-start(f32[16,1,6912]{2,1,0:T(1,128)} %broadcast_in_dim.2), calls=%async_computation.1 | async-start | bytes 884736 | tf_op jit(solution)/shard_map/all_to_all | solution.py:60
  77.6 4.4 %collective-permute-start.7 = (f32[110592]{0:T(1024)S(1)}, f32[110592]{0:T(1024)S(1)}, u32[]{:S(2)}, u32[]{:S(2)}) collective-permute-start(f32[110592]{0:T(1024)S(1)} %bitcast.192), channel_id=1, source_target_pairs={{0,1},{1,0},{2,3},{3,2},{4,5},{5,4},{6,7},{7,6},{8,9},{9,8},{10,11... | collective-permute-start | bytes 1327112 | tf_op jit(solution)/shard_map/ppermute | solution.py:61
  79.4 1.8 %copy-start.4 = (bf16[1,1,8,16,1024]{4,3,2,1,0:T(8,128)(2,1)S(1)}, bf16[1,1,8,16,1024]{4,3,2,1,0:T(8,128)(2,1)}, u32[]{:S(2)}) copy-start(bf16[1,1,8,16,1024]{4,3,2,1,0:T(8,128)(2,1)} %param.36) | copy-start | bytes 786436

commit v5 on v4

--- a/solution.py
+++ b/solution.py
@@ -33,6 +33,30 @@
     return lax.ppermute(piece, "brick", pairs)
 
 
+def halo_exchange(masked_piece, cot_piece, regions, direction):
+    down = neighbour_pairs(regions, direction, 1)
+    up = neighbour_pairs(regions, direction, -1)
+    both = down + up
+    sources = [a for a, _ in both]
+    targets = [b for _, b in both]
+    if not both or len(set(sources)) < len(both) or len(set(targets)) < len(both):
+        return (
+            exchange(masked_piece, regions, direction, 1),
+            exchange(cot_piece, regions, direction, -1),
+        )
+    rank = lax.axis_index("brick")
+    from_above = jnp.asarray([r in {b for _, b in down} for r in range(regions)])[rank]
+    from_below = jnp.asarray([r in {b for _, b in up} for r in range(regions)])[rank]
+    cut = masked_piece.size
+    packed = jnp.concatenate([masked_piece.reshape(-1), cot_piece.reshape(-1)])
+    got = lax.ppermute(packed, "brick", both)
+    zero = jnp.zeros((), got.dtype)
+    return (
+        jnp.where(from_above, got[:cut], zero).reshape(masked_piece.shape),
+        jnp.where(from_below, got[cut:], zero).reshape(cot_piece.shape),
+    )
+
+
 def forward_weight(up_weight):
     channels = up_weight.shape[1:]
     taps = jnp.pad(up_weight.reshape((3, 3, 3) + channels), ((0, 1), (0, 1), (0, 1), (0, 0), (0, 0)))
@@ -43,27 +67,32 @@
 
 def all_reduce(grads):
     devices = lax.axis_size("brick") * lax.axis_size("chip")
-    flat = grads.reshape(-1)
-    size = flat.shape[0]
-    chunk = -(-size // (2 * devices))
-    flat = jnp.pad(flat, (0, 2 * chunk * devices - size)).reshape(2, devices * chunk)
+    lanes = grads.shape[-1]
+    rows = grads.reshape(-1, lanes)
+    size = rows.shape[0]
+    chunk = -(-size // (2 * devices * 8)) * 8
+    rows = jnp.pad(rows, ((0, 2 * chunk * devices - size), (0, 0)))
+    rows = rows.reshape(2, devices, chunk, lanes)
     core = lax.axis_index("core")
-    got = lax.ppermute(jnp.where(core == 0, flat[1], flat[0]), "core", [(0, 1), (1, 0)])
-    half = jnp.where(core == 0, flat[0], flat[1]) + got
-    parts = lax.all_to_all(half.reshape(devices, chunk), OTHERS, 0, 0, tiled=True)
+    got = lax.ppermute(
+        lax.dynamic_index_in_dim(rows, 1 - core, keepdims=False), "core", [(0, 1), (1, 0)]
+    )
+    half = lax.dynamic_index_in_dim(rows, core, keepdims=False) + got
+    parts = lax.all_to_all(half, OTHERS, 0, 0, tiled=True)
     return parts.sum(axis=0), (devices, chunk, size)
 
 
-def all_spread(reduced, plan):
+def all_spread(reduced, plan, riders):
     devices, chunk, size = plan
-    spread = jnp.broadcast_to(reduced[None], (devices, chunk))
-    half = lax.all_to_all(spread, OTHERS, 0, 0, tiled=True).reshape(-1)
+    spread = jnp.broadcast_to(reduced[None], (devices,) + reduced.shape)
+    half = lax.all_to_all(spread, OTHERS, 0, 0, tiled=True)
+    half, riders = lax.optimization_barrier((half, riders))
     other = lax.ppermute(half, "core", [(0, 1), (1, 0)])
     core = lax.axis_index("core")
     whole = jnp.where(
         core == 0, jnp.concatenate([half, other]), jnp.concatenate([other, half])
     )
-    return whole[:size]
+    return whole.reshape(-1, reduced.shape[-1])[:size], riders
 
 
 def body(coarse, coarse_mask, skip, fine_mask, up_weight, fine_grad):
@@ -83,15 +112,18 @@
         jnp.bfloat16
     )
 
+    halos = {}
+    for direction in DIRECTIONS:
+        masked_piece = masked[tuple(slice(0, 1) if flag else slice(None) for flag in direction)]
+        cot_piece = cotangent[tuple(slice(-1, None) if flag else slice(None) for flag in direction)]
+        halos[direction] = halo_exchange(masked_piece, cot_piece, regions, direction)
     widened = jnp.pad(cotangent, ((1, 1), (1, 1), (1, 1), (0, 0)))
     for direction in DIRECTIONS:
-        source = tuple(slice(-1, None) if flag else slice(None) for flag in direction)
-        got = exchange(cotangent[source], regions, direction, -1)
         target = tuple(
             slice(0, 1) if flag else slice(1, 1 + cotangent.shape[a])
             for a, flag in enumerate(direction)
         )
-        widened = widened.at[target].set(got)
+        widened = widened.at[target].set(halos[direction][1])
     paired = widened.reshape(size_x + 1, 2, size_y + 1, 2, size_z + 1, 2, channels_out)
     windows = []
     for kx in range(3):
@@ -118,13 +150,11 @@
 
     extended = jnp.pad(masked_late, ((0, 1), (0, 1), (0, 1), (0, 0)))
     for direction in DIRECTIONS:
-        source = tuple(slice(0, 1) if flag else slice(None) for flag in direction)
-        got = exchange(masked_late[source], regions, direction, 1)
         target = tuple(
             slice(counts[a], counts[a] + 1) if flag else slice(0, counts[a])
             for a, flag in enumerate(direction)
         )
-        extended = extended.at[target].set(got)
+        extended = extended.at[target].set(halos[direction][0])
 
     shifted = jnp.stack(
         [
@@ -145,8 +175,10 @@
     fine_out = fine.astype(jnp.bfloat16).reshape(skip.shape)
 
     scale = 1.0 / math.sqrt(regions * lax.axis_size("chip") * lax.axis_size("core") * size_x * size_y * size_z)
-    weight_grad = all_spread(reduced * scale, plan).reshape(grads.shape)
-    return (fine_out, coarse_grad, weight_grad)
+    weight_grad, (fine_out, coarse_grad) = all_spread(
+        reduced * scale, plan, (fine_out, coarse_grad)
+    )
+    return (fine_out, coarse_grad, weight_grad.reshape(grads.shape))
 
 
 def solution(mesh):

time: 83.7 us -> 75.5 us (0.902)
  starting transfers between devices: 24.2 us -> 18.8 us
  waiting for transfers between devices: 24.6 us -> 19.7 us
  local copies, waits for them, and re-layouts: 22.3 us -> 24.6 us
    ppermute x7 -> x4, starting transfers between devices: 14.6 us -> 7.72 us  [the longest x3 7.65 us: halo_exchange(): got = lax.ppermute(packed, 'brick', both)]
    dynamic_slice x0 -> x6, local copies, waits for them, and re-layouts: none -> 3.65 us  [the longest x3 1.84 us: halo_exchange(): jnp.asarray([r in {b for _, b in up} for r in range(regions)])[rank]]
    ppermute x7 -> x4, waiting for transfers between devices: 3.21 us -> 0.04 us  [the longest x1 0.03 us: all_reduce(): lax.ppermute(lax.dynamic_index_in_dim(rows, 1 - core, keepdims=False), 'c...]
    all_to_all x2, waiting for transfers between devices: 21.4 us -> 18.5 us  [the longest x1 11.8 us: all_reduce(): parts = lax.all_to_all(half, OTHERS, 0, 0, tiled=True)]
    select_n x1 -> x4, other arithmetic: 1.38 us -> 3.17 us  [the longest x2 1.92 us: halo_exchange(): jnp.where(from_above, got[:cut], zero).reshape(masked_piece.shape)]
    dot_general x1, matrix products: 0.56 us -> 2.08 us  [body(): jnp.einsum('kabco,koi->abci', gathered, up_weight, preferred_element_type...]
    reshape x1 -> x4, local copies, waits for them, and re-layouts: 1.73 us -> 0.27 us  [halo_exchange(): packed = jnp.concatenate([masked_piece.reshape(-1), cot_piece.reshape(-1)])]
    all_to_all x2, starting transfers between devices: 9.61 us -> 11 us  [the longest x1 7.08 us: all_reduce(): parts = lax.all_to_all(half, OTHERS, 0, 0, tiled=True)]
  transfers between devices with their start and end apart: 10 -> 7, of which waited for: 3 -> 3; matrix products, arithmetic and copies ran while one was open for 18% -> 24% of each run, Pallas kernels for 0% -> 0%
where the time goes in v5:
time: 75.5 us; the launch traced here: 74.9 us
  local copies, waits for them, and re-layouts  24.6 us (33%)
  waiting for transfers between devices  19.7 us (26%)
  starting transfers between devices  18.8 us (25%)
  other arithmetic  7.04 us (9%)
  matrix products  3.5 us (5%)
  between operations  1.34 us (2%)
    all_to_all x1, waiting for transfers between devices, all_reduce(): parts = lax.all_to_all(half, OTHERS, 0, 0, tiled=True)  11.8 us
    ppermute x3, starting transfers between devices, halo_exchange(): got = lax.ppermute(packed, 'brick', both)  7.65 us
    all_to_all x1, starting transfers between devices, all_reduce(): parts = lax.all_to_all(half, OTHERS, 0, 0, tiled=True)  7.08 us
    all_to_all x1, waiting for transfers between devices, all_spread(): half = lax.all_to_all(spread, OTHERS, 0, 0, tiled=True)  6.75 us
    unnamed x68, local copies, waits for them, and re-layouts  5.7 us
    all_to_all x1, starting transfers between devices, all_spread(): half = lax.all_to_all(spread, OTHERS, 0, 0, tiled=True)  3.97 us
    slice x2, local copies, waits for them, and re-layouts, body(): windows.append(paired[tuple(index)])  3.81 us
    scatter x7, local copies, waits for them, and re-layouts, body(): widened = widened.at[target].set(halos[direction][1])  2.25 us
  transfers between devices with their start and end apart: 7, of which 3 were waited for; matrix products, arithmetic and copies ran while one was open for 24% of the time, Pallas kernels for 0%

profile of v5, /device:TPU:0, one launch (start us, length us, event | category | flops | bytes accessed | tf_op | source)
XLA Modules:
  0.0 74.9 jit_solution(17652977940391876281)
XLA Ops:
  0.7 1.4 %reshape.743 = bf16[8,16,16,64]{3,2,1,0:T(8,128)(2,1)S(1)} reshape(bf16[1,1,8,16,1024]{4,3,2,1,0:T(8,128)(2,1)} %param.45) | data formatting | bytes 524288 | tf_op jit(solution)/shard_map/reshape | solution.py:111
  2.1 0.7 convert_reduce_fusion.1
  2.8 0.1 convert_element_type.64
  2.9 0.3 broadcast_multiply_fusion
  3.3 0.2 slice_reduce_fusion
  3.5 0.1 reshape.746
  3.6 0.1 convert_element_type.66
  3.7 0.1 bitcast_multiply_fusion
  3.9 3.1 %collective-permute-start = (bf16[12288]{0:T(1024)(128)(2,1)S(1)}, bf16[12288]{0:T(1024)(128)(2,1)S(1)}, u32[]{:S(2)}, u32[]{:S(2)}) collective-permute-start(bf16[12288]{0:T(1024)(128)(2,1)S(1)} %pad_maximum_fusion.3), channel_id=1, source_target_pairs={{8,0},{24,16},{0,8},{16,24},{9,1},{25,17},{1,9},{17,25},{10,2},{26... | collective-permute-start | bytes 73736 | tf_op jit(solution)/shard_map/ppermute | solution.py:52
  7.0 0.1 reshape.748
  7.1 2.7 %collective-permute-start.1 = (bf16[12288]{0:T(1024)(128)(2,1)S(1)}, bf16[12288]{0:T(1024)(128)(2,1)S(1)}, u32[]{:S(2)}, u32[]{:S(2)}) collective-permute-start(bf16[12288]{0:T(1024)(128)(2,1)S(1)} %pad_maximum_fusion.4), channel_id=1, source_target_pairs={{16,0},{24,8},{0,16},{8,24},{17,1},{25,9},{1,17},{9,25},{18,2},{26... | collective-permute-start | bytes 73736 | tf_op jit(solution)/shard_map/ppermute | solution.py:52
  9.8 0.1 reshape.750
  9.9 1.9 %collective-permute-start.2 = (bf16[1024]{0:T(1024)(128)(2,1)S(1)}, bf16[1024]{0:T(1024)(128)(2,1)S(1)}, u32[]{:S(2)}, u32[]{:S(2)}) collective-permute-start(bf16[1024]{0:T(1024)(128)(2,1)S(1)} %pad_maximum_fusion.5), channel_id=1, source_target_pairs={{24,0},{0,24},{25,1},{1,25},{26,2},{2,26},{27,3},{3,27},{28,4},{4,... | collective-permute-start | bytes 6152 | tf_op jit(solution)/shard_map/ppermute | solution.py:52
  11.9 0.3 pad.72
  12.2 0.6 dynamic_slice.25
  12.8 0.7 dynamic_slice.26
  13.4 0.6 dynamic_slice.32
  14.1 0.6 dynamic_slice.27
  14.7 0.1 convert_element_type.68
  14.7 0.3 mul.51
  15.1 1.1 %mul.52 = f32[1,1,8,16,1024]{4,3,2,1,0:T(8,128)} reshape(f32[8,16,16,64]{3,2,1,0:T(8,128)S(1)} %mul.51) | data formatting | bytes 1048576 | tf_op jit(solution)/shard_map/mul | solution.py:172
  16.2 0.6 dynamic_slice.30
  16.8 0.6 dynamic_slice.31
  17.4 1.3 %select_bitcast_fusion = (bf16[4,1,1,128]{3,0,2,1:T(4,128)(2,1)S(1)}, bf16[512]{0:T(512)(128)(2,1)S(1)}) fusion(bf16[1024]{0:T(1024)(128)(2,1)S(1)} %collective-permute-done.2, pred[]{:T(512)} %bitcast.47, pred[]{:T(512)} %bitcast.3), kind=kLoop, calls=%fused_computation.121 | loop fusion | flops 1024 | bytes 4098 | tf_op jit(solution)/shard_map/jit(_where)/select_n | solution.py:55
  18.6 0.1 select_n.112
  18.7 0.6 slice_select_fusion.1
  19.3 0.1 select_n.111
  19.4 0.7 slice_select_fusion
  20.1 0.1 select_n.93
  20.2 1.4 %scatter.46 = bf16[10,18,18,64]{3,2,1,0:T(8,128)(2,1)S(1)} dynamic-update-slice(bf16[10,18,18,64]{3,2,1,0:T(8,128)(2,1)S(1)} %pad.72, bf16[8,16,1,64]{3,2,1,0:T(2,128)(2,1)S(1)} %select_n.111, s32[]{:T(128)} %constant.505.clone.1, s32[]{:T(128)} %constant.505.clone.1, s32[]{:T(128)} %constant.503.clone.1, s32[]{:T(128)} %constant.503.clone.1) | dynamic-update-slice | bytes 32772 | tf_op jit(solution)/shard_map/scatter | solution.py:126
  21.6 0.2 scatter.49
  21.9 0.3 scatter.51
  22.3 0.2 scatter.55
  22.5 0.4 reshape.751
  22.9 1.0 %fusion.22 = (bf16[4,1,8,1,8,1,64]{6,5,4,3,2,1,0:T(2,128)(2,1)S(1)}, bf16[4,1,8,1,8,1,64]{6,5,4,3,2,1,0:T(2,128)(2,1)S(1)}, bf16[4,1,8,1,8,1,64]{6,5,4,3,2,1,0:T...) fusion(bf16[5,2,9,2,9,2,64]{6,5,4,3,2,1,0:T(2,128)(2,1)S(1)} %r, ...), kind=kLoop, calls=%fused_computation.125 | loop fusion | bytes 524288 | tf_op jit(solution)/shard_map/slice | solution.py:136
  23.9 2.8 %fusion.21 = (bf16[4,1,8,1,8,1,64]{6,5,4,3,2,1,0:T(2,128)(2,1)S(1)}, bf16[4,1,8,1,8,1,64]{6,5,4,3,2,1,0:T(2,128)(2,1)S(1)}, bf16[4,1,8,1,8,1,64]{6,5,4,3,2,1,0:T...) fusion(bf16[5,2,9,2,9,2,64]{6,5,4,3,2,1,0:T(2,128)(2,1)S(1)} %r, ...), kind=kLoop, calls=%fused_computation.124 | loop fusion | bytes 1245184 | tf_op jit(solution)/shard_map/slice | solution.py:136
  27.4 0.7 convolution_bitcast_fusion.1
  28.1 0.5 copy-done.9
  28.6 0.1 copy-done.2
  28.7 0.1 pad_slice_fusion.1
  29.1 0.7 fusion.20
  29.8 0.7 fusion.19
  30.7 0.1 fusion.12
  30.9 0.8 %copy-done.7 = bf16[8,4,8,8,128]{4,3,2,1,0:T(8,128)(2,1)} copy-done((bf16[8,4,8,8,128]{4,3,2,1,0:T(8,128)(2,1)}, bf16[8,4,8,8,128]{4,3,2,1,0:T(8,128)(2,1)S(1)}, u32[]{:S(2)}) %copy-start.7) | copy-done | bytes 524312
  31.8 0.8 %bitcast_add_fusion = f32[16,56,128]{2,1,0:T(8,128)} fusion(f32[16,56,128]{2,1,0:T(8,128)S(1)} %collective-permute-done.3, f32[2,16,56,128]{3,2,1,0:T(8,128)S(1)} %bitcast.216, s32[]{:T(128)S(6)} %select_n.97), kind=kLoop, calls=%fused_computation.21 | loop fusion | flops 114688 | bytes 1376260 | tf_op jit(solution)/shard_map/add | solution.py:80
  32.6 7.1 %all-to-all-start = ((f32[16,56,128]{2,1,0:T(8,128)}), f32[16,56,128]{2,1,0:T(8,128)S(1)}, u32[]{:S(2)}, u32[]{:S(2)}) async-start(f32[16,56,128]{2,1,0:T(8,128)} %bitcast_add_fusion), calls=%async_computation | async-start | bytes 917504 | tf_op jit(solution)/shard_map/all_to_all | solution.py:81
  39.7 0.6 constant_dynamic-update-slice_fusion.30
  40.3 0.6 constant_dynamic-update-slice_fusion.29
  40.9 0.6 constant_dynamic-update-slice_fusion.28
  41.6 0.6 constant_dynamic-update-slice_fusion.27
  42.2 11.8 %all-to-all-done = f32[16,56,128]{2,1,0:T(8,128)S(1)} async-done(((f32[16,56,128]{2,1,0:T(8,128)}), f32[16,56,128]{2,1,0:T(8,128)S(1)}, u32[]{:S(2)}, u32[]{:S(2)}) %all-to-all-start) | async-done | bytes 458784 | tf_op jit(solution)/shard_map/all_to_all | solution.py:81
  54.0 0.8 %broadcast_in_dim.31 = f32[16,56,128]{2,1,0:T(8,128)} broadcast(f32[56,128]{1,0:T(8,128)S(1)} %broadcast_multiply_fusion.1), dimensions={1,2} | broadcast | bytes 487424 | tf_op jit(solution)/shard_map/broadcast_in_dim | solution.py:87
  54.8 4.0 %all-to-all-start.1 = ((f32[16,56,128]{2,1,0:T(8,128)}), f32[16,56,128]{2,1,0:T(8,128)S(1)}, u32[]{:S(2)}, u32[]{:S(2)}) async-start(f32[16,56,128]{2,1,0:T(8,128)} %broadcast_in_dim.31), calls=%async_computation.1 | async-start | bytes 917504 | tf_op jit(solution)/shard_map/all_to_all | solution.py:88
  58.8 0.1 fusion.11
  58.9 0.9 %copy-done.8 = bf16[8,4,8,8,128]{4,3,2,1,0:T(8,128)(2,1)S(1)} copy-done((bf16[8,4,8,8,128]{4,3,2,1,0:T(8,128)(2,1)S(1)}, bf16[8,4,8,8,128]{4,3,2,1,0:T(8,128)(2,1)}, u32[]{:S(2)}) %copy-start.8) | copy-done | bytes 524312
  59.9 0.7 convolution_bitcast_fusion
  60.6 0.8 %copy.163 = f32[4,2,8,2,8,2,64]{6,5,4,3,2,1,0:T(2,128)S(1)} copy(f32[4,2,8,2,8,2,64]{6,4,0,5,3,1,2:T(8,128)S(1)} %convolution_bitcast_fusion) | data formatting | bytes 1048576 | tf_op jit(solution)/shard_map/xyzabci,xpyqzroi->apbqcro/transpose | solution.py:165
  61.4 0.9 %reshape.757 = f32[1,1,8,16,1024]{4,3,2,1,0:T(8,128)S(1)} reshape(f32[4,2,8,2,8,2,64]{6,5,4,3,2,1,0:T(2,128)S(1)} %copy.163) | data formatting | bytes 1048576 | tf_op jit(solution)/shard_map/reshape | solution.py:171
  62.4 2.1 %fusion.8 = bf16[4,8,8,128]{3,2,0,1:T(8,128)(2,1)S(1)} fusion(bf16[27,4,8,8,64]{4,3,2,0,1:T(8,128)(2,1)} %copy-done.9, bf16[27,64,128]{2,1,0:T(8,128)(2,1)S(1)} %copy-done.3, f32[4,8,8]{2,0,1:T(4,128)S(1)} %copy.165), kind=kOutput, calls=%fused_computation.8 | convolution fusion | flops 113311744 | bytes 1393664 | tf_op jit(solution)/shard_map/kabco,koi->abci/dot_general | solution.py:144
  64.5 0.8 %multiply_convert_fusion = bf16[1,1,8,16,1024]{4,3,2,1,0:T(8,128)(2,1)} fusion(f32[1,1,8,16,1024]{4,3,2,1,0:T(8,128)S(1)} %copy-done.1, f32[1,1,8,16,1024]{4,3,2,1,0:T(8,128)S(1)} %reshape.757, bf16[1,1,8,16,1024]{4,3,2,1,0:T(8,128)(2,1)S(1)} %copy-done.4), kind=kLoop, calls=%fused_computation.20 | loop fusion | flops 524288 | bytes 1572864 | tf_op jit(solution)/shard_map/convert_element_type | solution.py:175
  65.3 6.8 %all-to-all-done.1 = f32[16,56,128]{2,1,0:T(8,128)S(1)} async-done(((f32[16,56,128]{2,1,0:T(8,128)}), f32[16,56,128]{2,1,0:T(8,128)S(1)}, u32[]{:S(2)}, u32[]{:S(2)}) %all-to-all-start.1) | async-done | bytes 458784 | tf_op jit(solution)/shard_map/all_to_all | solution.py:88
  72.1 0.7 copy.166
  72.7 1.2 %collective-permute-done.4 = f32[16,56,128]{2,1,0:T(8,128)S(1)} collective-permute-done((f32[16,56,128]{2,1,0:T(8,128)S(1)}, f32[16,56,128]{2,1,0:T(8,128)S(1)}, u32[]{:S(2)}, u32[]{:S(2)}) %collective-permute-start.4) | collective-permute-done | bytes 458784 | tf_op jit(solution)/shard_map/ppermute | solution.py:90
  74.0 1.0 %slice.858 = f32[1728,128]{1,0:T(8,128)} slice(f32[1792,128]{1,0:T(8,128)S(1)} %bitcast.217), slice={[0:1728], [0:128]} | slice | bytes 1769472 | tf_op jit(solution)/shard_map/slice | solution.py:95
  (102 shorter events, 1.7 us)
Async XLA Ops:
  0.6 11.2 %copy-start.6 = (s32[1,1,2048]{2,1,0:T(1,128)S(1)}, s32[1,1,2048]{2,1,0:T(1,128)}, u32[]{:S(2)}) copy-start(s32[1,1,2048]{2,1,0:T(1,128)} %param.43) | copy-start | bytes 24580
  0.6 2.9 %copy-start.10 = (s32[1,1,256]{2,1,0:T(1,128)S(1)}, s32[1,1,256]{2,1,0:T(1,128)}, u32[]{:S(2)}) copy-start(s32[1,1,256]{2,1,0:T(1,128)} %param.41) | copy-start | bytes 3076
  0.7 3.0 %copy-start.5 = (bf16[1,1,4,8,1024]{4,3,2,1,0:T(8,128)(2,1)S(1)}, bf16[1,1,4,8,1024]{4,3,2,1,0:T(8,128)(2,1)}, u32[]{:S(2)}) copy-start(bf16[1,1,4,8,1024]{4,3,2,1,0:T(8,128)(2,1)} %param.40) | copy-start | bytes 196612
  2.0 10.1 %copy-start.16 = (pred[4]{0:T(512)(128)(4,1)S(1)}, pred[4]{0:T(512)(128)(4,1)}, u32[]{:S(2)}) copy-start(pred[4]{0:T(512)(128)(4,1)} %constant.513.clone) | copy-start | bytes 16
  2.0 10.7 %copy-start.15 = (pred[4]{0:T(512)(128)(4,1)S(1)}, pred[4]{0:T(512)(128)(4,1)}, u32[]{:S(2)}) copy-start(pred[4]{0:T(512)(128)(4,1)} %constant.515.clone) | copy-start | bytes 16
  2.1 11.4 %copy-start.14 = (pred[4]{0:T(512)(128)(4,1)S(1)}, pred[4]{0:T(512)(128)(4,1)}, u32[]{:S(2)}) copy-start(pred[4]{0:T(512)(128)(4,1)} %constant.516.clone) | copy-start | bytes 16
  2.1 12.0 %copy-start.13 = (pred[4]{0:T(512)(128)(4,1)S(1)}, pred[4]{0:T(512)(128)(4,1)}, u32[]{:S(2)}) copy-start(pred[4]{0:T(512)(128)(4,1)} %constant.517.clone) | copy-start | bytes 16
  3.9 14.9 %collective-permute-start = (bf16[12288]{0:T(1024)(128)(2,1)S(1)}, bf16[12288]{0:T(1024)(128)(2,1)S(1)}, u32[]{:S(2)}, u32[]{:S(2)}) collective-permute-start(bf16[12288]{0:T(1024)(128)(2,1)S(1)} %pad_maximum_fusion.3), channel_id=1, source_target_pairs={{8,0},{24,16},{0,8},{16,24},{9,1},{25,17},{1,9},{17,25},{10,2},{26... | collective-permute-start | bytes 73736 | tf_op jit(solution)/shard_map/ppermute | solution.py:52
  7.1 12.3 %collective-permute-start.1 = (bf16[12288]{0:T(1024)(128)(2,1)S(1)}, bf16[12288]{0:T(1024)(128)(2,1)S(1)}, u32[]{:S(2)}, u32[]{:S(2)}) collective-permute-start(bf16[12288]{0:T(1024)(128)(2,1)S(1)} %pad_maximum_fusion.4), channel_id=1, source_target_pairs={{16,0},{24,8},{0,16},{8,24},{17,1},{25,9},{1,17},{9,25},{18,2},{26... | collective-permute-start | bytes 73736 | tf_op jit(solution)/shard_map/ppermute | solution.py:52
  9.9 7.5 %collective-permute-start.2 = (bf16[1024]{0:T(1024)(128)(2,1)S(1)}, bf16[1024]{0:T(1024)(128)(2,1)S(1)}, u32[]{:S(2)}, u32[]{:S(2)}) collective-permute-start(bf16[1024]{0:T(1024)(128)(2,1)S(1)} %pad_maximum_fusion.5), channel_id=1, source_target_pairs={{24,0},{0,24},{25,1},{1,25},{26,2},{2,26},{27,3},{3,27},{28,4},{4,... | collective-permute-start | bytes 6152 | tf_op jit(solution)/shard_map/ppermute | solution.py:52
  12.1 4.1 %copy-start.12 = (pred[4]{0:T(512)(128)(4,1)S(1)}, pred[4]{0:T(512)(128)(4,1)}, u32[]{:S(2)}) copy-start(pred[4]{0:T(512)(128)(4,1)} %constant.512.clone) | copy-start | bytes 16
  12.1 4.6 %copy-start.11 = (pred[4]{0:T(512)(128)(4,1)S(1)}, pred[4]{0:T(512)(128)(4,1)}, u32[]{:S(2)}) copy-start(pred[4]{0:T(512)(128)(4,1)} %constant.514.clone) | copy-start | bytes 16
  27.4 1.2 %copy-start.9 = (bf16[27,4,8,8,64]{4,3,2,0,1:T(8,128)(2,1)}, bf16[27,4,8,8,64]{4,3,2,0,1:T(8,128)(2,1)S(1)}, u32[]{:S(2)}) copy-start(bf16[27,4,8,8,64]{4,3,2,0,1:T(8,128)(2,1)S(1)} %constant_dynamic-update-slice_fusion) | copy-start | bytes 2654212
  27.4 1.3 %copy-start.2 = (bf16[27,64,128]{2,1,0:T(8,128)(2,1)S(1)}, bf16[27,64,128]{2,1,0:T(8,128)(2,1)}, u32[]{:S(2)}) copy-start(bf16[27,64,128]{2,1,0:T(8,128)(2,1)} %param.44) | copy-start | bytes 1327108
  29.0 1.9 %collective-permute-start.3 = (f32[16,56,128]{2,1,0:T(8,128)S(1)}, f32[16,56,128]{2,1,0:T(8,128)S(1)}, u32[]{:S(2)}, u32[]{:S(2)}) collective-permute-start(f32[16,56,128]{2,1,0:T(8,128)S(1)} %dynamic-slice_bitcast_fusion), channel_id=1, source_target_pairs={{0,1},{1,0},{2,3},{3,2},{4,5},{5,4},{6,7},{7,6},{8,9},{9,8},{10,11... | collective-permute-start | bytes 1376264 | tf_op jit(solution)/shard_map/ppermute | solution.py:77
  30.8 1.8 %copy-start = (bf16[4,4,4,64,128]{4,3,2,1,0:T(8,128)(2,1)}, bf16[4,4,4,64,128]{4,3,2,1,0:T(8,128)(2,1)S(1)}, u32[]{:S(2)}) copy-start(bf16[4,4,4,64,128]{4,3,2,1,0:T(8,128)(2,1)S(1)} %fusion.12) | copy-start | bytes 3145732
  30.9 0.9 %copy-start.7 = (bf16[8,4,8,8,128]{4,3,2,1,0:T(8,128)(2,1)}, bf16[8,4,8,8,128]{4,3,2,1,0:T(8,128)(2,1)S(1)}, u32[]{:S(2)}) copy-start(bf16[8,4,8,8,128]{4,3,2,1,0:T(8,128)(2,1)S(1)} %constant_dynamic-update-slice_fusion.31) | copy-start | bytes 1572868
  32.6 21.4 %all-to-all-start = ((f32[16,56,128]{2,1,0:T(8,128)}), f32[16,56,128]{2,1,0:T(8,128)S(1)}, u32[]{:S(2)}, u32[]{:S(2)}) async-start(f32[16,56,128]{2,1,0:T(8,128)} %bitcast_add_fusion), calls=%async_computation | async-start | bytes 917504 | tf_op jit(solution)/shard_map/all_to_all | solution.py:81
  39.7 19.2 %slice-start = ((bf16[4,4,4,64,128]{4,3,2,1,0:T(8,128)(2,1)}), bf16[4,4,3,64,128]{4,3,2,1,0:T(8,128)(2,1)S(1)}, s32[]{:S(2)}) async-start(bf16[4,4,4,64,128]{4,3,2,1,0:T(8,128)(2,1)} %copy-done), calls=%async_computation.2 | async-start | bytes 1572864 | tf_op jit(solution)/shard_map/jit(_roll_static)/slice | solution.py:64
  54.8 17.2 %all-to-all-start.1 = ((f32[16,56,128]{2,1,0:T(8,128)}), f32[16,56,128]{2,1,0:T(8,128)S(1)}, u32[]{:S(2)}, u32[]{:S(2)}) async-start(f32[16,56,128]{2,1,0:T(8,128)} %broadcast_in_dim.31), calls=%async_computation.1 | async-start | bytes 917504 | tf_op jit(solution)/shard_map/all_to_all | solution.py:88
  58.8 1.0 %copy-start.8 = (bf16[8,4,8,8,128]{4,3,2,1,0:T(8,128)(2,1)S(1)}, bf16[8,4,8,8,128]{4,3,2,1,0:T(8,128)(2,1)}, u32[]{:S(2)}) copy-start(bf16[8,4,8,8,128]{4,3,2,1,0:T(8,128)(2,1)} %constant_dynamic-update-slice_fusion.27) | copy-start | bytes 1572868
  60.6 1.8 %copy-start.3 = (bf16[27,64,128]{2,1,0:T(8,128)(2,1)S(1)}, bf16[27,64,128]{2,1,0:T(8,128)(2,1)}, u32[]{:S(2)}) copy-start(bf16[27,64,128]{2,1,0:T(8,128)(2,1)} %param.44) | copy-start | bytes 1327108
  62.4 2.1 %copy-start.1 = (f32[1,1,8,16,1024]{4,3,2,1,0:T(8,128)S(1)}, f32[1,1,8,16,1024]{4,3,2,1,0:T(8,128)}, u32[]{:S(2)}) copy-start(f32[1,1,8,16,1024]{4,3,2,1,0:T(8,128)} %mul.52) | copy-start | bytes 1572868
  62.4 2.1 %copy-start.4 = (bf16[1,1,8,16,1024]{4,3,2,1,0:T(8,128)(2,1)S(1)}, bf16[1,1,8,16,1024]{4,3,2,1,0:T(8,128)(2,1)}, u32[]{:S(2)}) copy-start(bf16[1,1,8,16,1024]{4,3,2,1,0:T(8,128)(2,1)} %param.42) | copy-start | bytes 786436
  72.1 1.8 %collective-permute-start.4 = (f32[16,56,128]{2,1,0:T(8,128)S(1)}, f32[16,56,128]{2,1,0:T(8,128)S(1)}, u32[]{:S(2)}, u32[]{:S(2)}) collective-permute-start(f32[16,56,128]{2,1,0:T(8,128)S(1)} %all-to-all-done.1), channel_id=1, source_target_pairs={{0,1},{1,0},{2,3},{3,2},{4,5},{5,4},{6,7},{7,6},{8,9},{9,8},{10,11... | collective-permute-start | bytes 1376264 | tf_op jit(solution)/shard_map/ppermute | solution.py:90

commit v6 on v5

--- a/solution.py
+++ b/solution.py
@@ -44,17 +44,24 @@
             exchange(masked_piece, regions, direction, 1),
             exchange(cot_piece, regions, direction, -1),
         )
-    rank = lax.axis_index("brick")
-    from_above = jnp.asarray([r in {b for _, b in down} for r in range(regions)])[rank]
-    from_below = jnp.asarray([r in {b for _, b in up} for r in range(regions)])[rank]
+    spot = region_of(lax.axis_index("brick"))
+    grid = (regions // 4, 2, 2)
+    sends_down = jnp.bool_(True)
+    sends_up = jnp.bool_(True)
+    for a in range(3):
+        if direction[a]:
+            sends_down = sends_down & (spot[a] >= 1)
+            sends_up = sends_up & (spot[a] + 1 < grid[a])
     cut = masked_piece.size
-    packed = jnp.concatenate([masked_piece.reshape(-1), cot_piece.reshape(-1)])
+    zero = jnp.zeros((), masked_piece.dtype)
+    packed = jnp.concatenate(
+        [
+            jnp.where(sends_down, masked_piece.reshape(-1), zero),
+            jnp.where(sends_up, cot_piece.reshape(-1), zero),
+        ]
+    )
     got = lax.ppermute(packed, "brick", both)
-    zero = jnp.zeros((), got.dtype)
-    return (
-        jnp.where(from_above, got[:cut], zero).reshape(masked_piece.shape),
-        jnp.where(from_below, got[cut:], zero).reshape(cot_piece.shape),
-    )
+    return (got[:cut].reshape(masked_piece.shape), got[cut:].reshape(cot_piece.shape))
 
 
 def forward_weight(up_weight):
@@ -88,11 +95,11 @@
     half = lax.all_to_all(spread, OTHERS, 0, 0, tiled=True)
     half, riders = lax.optimization_barrier((half, riders))
     other = lax.ppermute(half, "core", [(0, 1), (1, 0)])
-    core = lax.axis_index("core")
-    whole = jnp.where(
-        core == 0, jnp.concatenate([half, other]), jnp.concatenate([other, half])
-    )
-    return whole.reshape(-1, reduced.shape[-1])[:size], riders
+    lanes = reduced.shape[-1]
+    rows = half.size // lanes
+    three = jnp.concatenate([half, other, half]).reshape(-1, lanes)
+    whole = lax.dynamic_slice_in_dim(three, lax.axis_index("core") * rows, size)
+    return whole, riders
 
 
 def body(coarse, coarse_mask, skip, fine_mask, up_weight, fine_grad):
@@ -138,7 +145,9 @@
     grads = jnp.einsum(
         "kabco,abci->koi", gathered, masked, preferred_element_type=jnp.float32
     )
-    grads, masked_late, weight_late = lax.optimization_barrier((grads, masked, up_weight))
+    grads, masked_late, weight_late, skip, fine_keep = lax.optimization_barrier(
+        (grads, masked, up_weight, skip, fine_keep)
+    )
     reduced, plan = all_reduce(grads)
 
     back = jnp.einsum(

time: 75.5 us -> 73.3 us (0.971)
  local copies, waits for them, and re-layouts: 24.6 us -> 21.8 us
  waiting for transfers between devices: 19.7 us -> 22.5 us
  starting transfers between devices: 18.8 us -> 16.3 us
  matrix products: 3.5 us -> 4.55 us
    ppermute x3, waiting for transfers between devices: 0.01 us -> 2.95 us  [halo_exchange(): got = lax.ppermute(packed, 'brick', both)]
    select_n x5 -> x6, other arithmetic: 3.23 us -> 0.35 us  [the longest x3 0.27 us: halo_exchange(): jnp.where(sends_up, cot_piece.reshape(-1), zero)]
    dynamic_slice x6 -> x1, local copies, waits for them, and re-layouts: 3.65 us -> 0.98 us  [all_spread(): whole = lax.dynamic_slice_in_dim(three, lax.axis_index('core') * rows, size)]
    all_to_all x1, starting transfers between devices: 7.08 us -> 4.74 us  [all_reduce(): parts = lax.all_to_all(half, OTHERS, 0, 0, tiled=True)]
    slice x6 -> x4, local copies, waits for them, and re-layouts: 1.29 us -> 0.01 us  [the longest x2 0.01 us: halo_exchange(): got[:cut].reshape(masked_piece.shape)]
    unnamed x68 -> x55, local copies, waits for them, and re-layouts: 5.7 us -> 6.86 us
    dot_general x1, matrix products: 0.73 us -> 1.78 us  [body(): jnp.einsum('xyzabci,xpyqzroi->apbqcro', shifted, forward_weight(weight_la...]
    add x1, other arithmetic: 0.82 us -> 1.85 us  [all_reduce(): half = lax.dynamic_index_in_dim(rows, core, keepdims=False) + got]
  transfers between devices with their start and end apart: 7 -> 7, of which waited for: 3 -> 5; matrix products, arithmetic and copies ran while one was open for 24% -> 23% of each run, Pallas kernels for 0% -> 0%
where the time goes in v6:
time: 73.3 us; the launch traced here: 72.7 us
  waiting for transfers between devices  22.5 us (31%)
  local copies, waits for them, and re-layouts  21.8 us (30%)
  starting transfers between devices  16.3 us (22%)
  other arithmetic  6.3 us (9%)
  matrix products  4.55 us (6%)
  between operations  1.24 us (2%)
    all_to_all x1, waiting for transfers between devices, all_reduce(): parts = lax.all_to_all(half, OTHERS, 0, 0, tiled=True)  11.7 us
    ppermute x3, starting transfers between devices, halo_exchange(): got = lax.ppermute(packed, 'brick', both)  7.54 us
    unnamed x55, local copies, waits for them, and re-layouts  6.86 us
    all_to_all x1, waiting for transfers between devices, all_spread(): half = lax.all_to_all(spread, OTHERS, 0, 0, tiled=True)  6.65 us
    all_to_all x1, starting transfers between devices, all_reduce(): parts = lax.all_to_all(half, OTHERS, 0, 0, tiled=True)  4.74 us
    all_to_all x1, starting transfers between devices, all_spread(): half = lax.all_to_all(spread, OTHERS, 0, 0, tiled=True)  3.94 us
    slice x2, local copies, waits for them, and re-layouts, body(): windows.append(paired[tuple(index)])  3.81 us
    ppermute x3, waiting for transfers between devices, halo_exchange(): got = lax.ppermute(packed, 'brick', both)  2.95 us
  transfers between devices with their start and end apart: 7, of which 5 were waited for; matrix products, arithmetic and copies ran while one was open for 23% of the time, Pallas kernels for 0%

profile of v6, /device:TPU:0, one launch (start us, length us, event | category | flops | bytes accessed | tf_op | source)
XLA Modules:
  0.0 72.7 jit_solution(11172845541573316223)
XLA Ops:
  0.7 1.4 %reshape.693 = bf16[8,16,16,64]{3,2,1,0:T(8,128)(2,1)S(1)} reshape(bf16[1,1,8,16,1024]{4,3,2,1,0:T(8,128)(2,1)} %param.39) | data formatting | bytes 524288 | tf_op jit(solution)/shard_map/reshape | solution.py:118
  2.0 0.8 %convert_reduce_fusion = bf16[2048]{0:T(1024)(128)(2,1)S(1)} fusion(s32[1,1,2048]{2,1,0:T(1,128)} %param.37), kind=kLoop, calls=%fused_computation.113 | loop fusion | flops 2048 | bytes 12288 | tf_op jit(solution)/shard_map/convert_element_type | solution.py:118
  2.8 0.1 convert_element_type.56
  2.9 0.3 broadcast_multiply_fusion
  3.3 0.2 fusion.17
  3.5 0.1 select_n.96
  3.6 0.1 convert_element_type.58
  3.7 0.1 bitcast_multiply_fusion
  3.9 3.1 %collective-permute-start = (bf16[12288]{0:T(1024)(128)(2,1)S(1)}, bf16[12288]{0:T(1024)(128)(2,1)S(1)}, u32[]{:S(2)}, u32[]{:S(2)}) collective-permute-start(bf16[12288]{0:T(1024)(128)(2,1)S(1)} %pad_maximum_fusion.4), channel_id=1, source_target_pairs={{8,0},{24,16},{0,8},{16,24},{9,1},{25,17},{1,9},{17,25},{10,2},{26... | collective-permute-start | bytes 73736 | tf_op jit(solution)/shard_map/ppermute | solution.py:63
  7.0 0.1 select_n.110
  7.2 4.4 %collective-permute-start.2 = (bf16[1024]{0:T(1024)(128)(2,1)S(1)}, bf16[1024]{0:T(1024)(128)(2,1)S(1)}, u32[]{:S(2)}, u32[]{:S(2)}) collective-permute-start(bf16[1024]{0:T(1024)(128)(2,1)S(1)} %pad_maximum_fusion.6), channel_id=1, source_target_pairs={{24,0},{0,24},{25,1},{1,25},{26,2},{2,26},{27,3},{3,27},{28,4},{4,... | collective-permute-start | bytes 6152 | tf_op jit(solution)/shard_map/ppermute | solution.py:63
  11.6 0.1 select_n.104
  11.7 0.1 collective-permute-start.1
  11.8 0.3 pad.72
  12.1 0.5 broadcast.274
  12.6 0.7 reduce.43
  13.2 0.1 reshape.699
  13.3 1.1 %collective-permute-done.2 = bf16[1024]{0:T(1024)(128)(2,1)S(1)} collective-permute-done((bf16[1024]{0:T(1024)(128)(2,1)S(1)}, bf16[1024]{0:T(1024)(128)(2,1)S(1)}, u32[]{:S(2)}, u32[]{:S(2)}) %collective-permute-start.2) | collective-permute-done | bytes 2080 | tf_op jit(solution)/shard_map/ppermute | solution.py:63
  14.4 0.1 reshape.717
  14.5 0.1 reshape.716
  14.6 1.9 %collective-permute-done.1 = bf16[12288]{0:T(1024)(128)(2,1)S(1)} collective-permute-done((bf16[12288]{0:T(1024)(128)(2,1)S(1)}, bf16[12288]{0:T(1024)(128)(2,1)S(1)}, u32[]{:S(2)}, u32[]{:S(2)}) %collective-permute-start.1) | collective-permute-done | bytes 24608 | tf_op jit(solution)/shard_map/ppermute | solution.py:63
  16.5 0.1 reshape.696
  16.6 1.4 %scatter.46 = bf16[10,18,18,64]{3,2,1,0:T(8,128)(2,1)S(1)} dynamic-update-slice(bf16[10,18,18,64]{3,2,1,0:T(8,128)(2,1)S(1)} %pad.72, bf16[8,16,1,64]{3,2,1,0:T(2,128)(2,1)S(1)} %reshape.716, s32[]{:T(128)} %constant.523.clone.1, s32[]{:T(128)} %constant.523.clone.1, s32[]{:T(128)} %constant.522.clone.1, s32[]{:T(128)} %constant.522.clone.1) | dynamic-update-slice | bytes 32772 | tf_op jit(solution)/shard_map/scatter | solution.py:133
  18.0 0.2 scatter.49
  18.3 0.3 scatter.51
  18.6 0.1 scatter.54
  18.7 0.2 scatter.55
  18.9 0.4 reshape.698
  19.3 1.0 %fusion.25 = (bf16[4,1,8,1,8,1,64]{6,5,4,3,2,1,0:T(2,128)(2,1)S(1)}, bf16[4,1,8,1,8,1,64]{6,5,4,3,2,1,0:T(2,128)(2,1)S(1)}, bf16[4,1,8,1,8,1,64]{6,5,4,3,2,1,0:T...) fusion(bf16[5,2,9,2,9,2,64]{6,5,4,3,2,1,0:T(2,128)(2,1)S(1)} %r, ...), kind=kLoop, calls=%fused_computation.127 | loop fusion | bytes 524288 | tf_op jit(solution)/shard_map/slice | solution.py:143
  20.3 2.8 %fusion.24 = (bf16[4,1,8,1,8,1,64]{6,5,4,3,2,1,0:T(2,128)(2,1)S(1)}, bf16[4,1,8,1,8,1,64]{6,5,4,3,2,1,0:T(2,128)(2,1)S(1)}, bf16[4,1,8,1,8,1,64]{6,5,4,3,2,1,0:T...) fusion(bf16[5,2,9,2,9,2,64]{6,5,4,3,2,1,0:T(2,128)(2,1)S(1)} %r, ...), kind=kLoop, calls=%fused_computation.126 | loop fusion | bytes 1245184 | tf_op jit(solution)/shard_map/slice | solution.py:143
  23.8 0.7 convolution_bitcast_fusion.1
  24.5 0.5 copy-done.8
  25.0 0.1 copy-done.3
  25.1 0.1 pad_slice_fusion.1
  25.3 0.1 pad.73
  25.4 0.1 collective-permute-start.3
  25.7 0.6 constant_dynamic-update-slice_fusion.34
  26.3 0.6 constant_dynamic-update-slice_fusion.33
  27.0 0.1 fusion.14
  27.0 1.1 %fusion.12 = bf16[4,4,4,64,128]{4,3,2,1,0:T(8,128)(2,1)} fusion(bf16[1,4,4,64,128]{4,3,2,1,0:T(8,128)(2,1)S(1)} %pad_slice_fusion, bf16[3,4,4,64,128]{4,3,2,1,0:T(8,128)(2,1)S(1)} %pad_slice_fusion.1, bf16[4,3,4,64,128]{4,3,2,1,0:T(8,128)(2,1)S(1)} %fusion.14), kind=kLoop, calls=%fused_computation.14 | loop fusion | flops 1048576 | bytes 2883584 | tf_op jit(solution)/shard_map/jit(_roll_static)/concatenate | solution.py:71
  28.1 0.3 mul.57
  28.4 1.1 %mul.58 = f32[1,1,8,16,1024]{4,3,2,1,0:T(8,128)} reshape(f32[8,16,16,64]{3,2,1,0:T(8,128)S(1)} %mul.57) | data formatting | bytes 1048576 | tf_op jit(solution)/shard_map/mul | solution.py:181
  29.6 0.6 constant_dynamic-update-slice_fusion.32
  30.2 0.6 constant_dynamic-update-slice_fusion.31
  30.8 1.9 %bitcast_add_fusion = f32[16,56,128]{2,1,0:T(8,128)} fusion(f32[16,56,128]{2,1,0:T(8,128)} %collective-permute-done.3, f32[2,16,56,128]{3,2,1,0:T(8,128)S(1)} %bitcast.213, s32[]{:T(128)S(6)} %select_n.111), kind=kLoop, calls=%fused_computation.21 | loop fusion | flops 114688 | bytes 1376260 | tf_op jit(solution)/shard_map/add | solution.py:87
  32.7 4.7 %all-to-all-start = ((f32[16,56,128]{2,1,0:T(8,128)}), f32[16,56,128]{2,1,0:T(8,128)S(1)}, u32[]{:S(2)}, u32[]{:S(2)}) async-start(f32[16,56,128]{2,1,0:T(8,128)} %bitcast_add_fusion), calls=%async_computation | async-start | bytes 917504 | tf_op jit(solution)/shard_map/all_to_all | solution.py:88
  37.4 0.6 constant_dynamic-update-slice_fusion.30
  38.1 0.7 constant_dynamic-update-slice_fusion.29
  38.7 0.6 constant_dynamic-update-slice_fusion.28
  39.4 0.7 constant_dynamic-update-slice_fusion.27
  40.0 11.7 %all-to-all-done = f32[16,56,128]{2,1,0:T(8,128)S(1)} async-done(((f32[16,56,128]{2,1,0:T(8,128)}), f32[16,56,128]{2,1,0:T(8,128)S(1)}, u32[]{:S(2)}, u32[]{:S(2)}) %all-to-all-start) | async-done | bytes 458784 | tf_op jit(solution)/shard_map/all_to_all | solution.py:88
  51.8 0.8 %broadcast_in_dim.41 = f32[16,56,128]{2,1,0:T(8,128)} broadcast(f32[56,128]{1,0:T(8,128)S(1)} %broadcast_multiply_fusion.1), dimensions={1,2} | broadcast | bytes 487424 | tf_op jit(solution)/shard_map/broadcast_in_dim | solution.py:94
  52.6 3.9 %all-to-all-start.1 = ((f32[16,56,128]{2,1,0:T(8,128)}), f32[16,56,128]{2,1,0:T(8,128)S(1)}, u32[]{:S(2)}, u32[]{:S(2)}) async-start(f32[16,56,128]{2,1,0:T(8,128)} %broadcast_in_dim.41), calls=%async_computation.1 | async-start | bytes 917504 | tf_op jit(solution)/shard_map/all_to_all | solution.py:95
  56.6 0.1 fusion.11
  56.7 1.8 %convolution_bitcast_fusion = f32[4,2,8,2,8,2,64]{6,4,0,5,3,1,2:T(8,128)S(1)} fusion(bf16[2,2,2,2,2,2,64,128,1,1]{7,6,5,4,3,2,1,0,9,8:T(8,128)(2,1)S(1)} %bitcast.216, bf16[2,2,2,4,8,8,128,1,1,1]{6,5,4,3,2,1,0,9,8,7:T(8,128)(2,1)} %bitcast.53), kind=kOutput, calls=%fused_computation.3 | convolution fusion | flops 268435456 | bytes 2097152 | tf_op jit(solution)/shard_map/xyzabci,xpyqzroi->apbqcro/dot_general | solution.py:174
  58.5 0.8 %copy.157 = f32[4,2,8,2,8,2,64]{6,5,4,3,2,1,0:T(2,128)S(1)} copy(f32[4,2,8,2,8,2,64]{6,4,0,5,3,1,2:T(8,128)S(1)} %convolution_bitcast_fusion) | data formatting | bytes 1048576 | tf_op jit(solution)/shard_map/xyzabci,xpyqzroi->apbqcro/transpose | solution.py:174
  59.3 0.9 %reshape.705 = f32[1,1,8,16,1024]{4,3,2,1,0:T(8,128)S(1)} reshape(f32[4,2,8,2,8,2,64]{6,5,4,3,2,1,0:T(2,128)S(1)} %copy.157) | data formatting | bytes 1048576 | tf_op jit(solution)/shard_map/reshape | solution.py:180
  60.2 2.1 %fusion.8 = bf16[4,8,8,128]{3,2,0,1:T(8,128)(2,1)S(1)} fusion(bf16[27,4,8,8,64]{4,3,2,0,1:T(8,128)(2,1)} %copy-done.8, bf16[27,64,128]{2,1,0:T(8,128)(2,1)S(1)} %copy-done.4, f32[4,8,8]{2,0,1:T(4,128)S(1)} %copy.159), kind=kOutput, calls=%fused_computation.9 | convolution fusion | flops 113311744 | bytes 1393664 | tf_op jit(solution)/shard_map/kabco,koi->abci/dot_general | solution.py:153
  62.4 0.8 %multiply_convert_fusion = bf16[1,1,8,16,1024]{4,3,2,1,0:T(8,128)(2,1)} fusion(f32[1,1,8,16,1024]{4,3,2,1,0:T(8,128)S(1)} %copy-done.2, f32[1,1,8,16,1024]{4,3,2,1,0:T(8,128)S(1)} %reshape.705, bf16[1,1,8,16,1024]{4,3,2,1,0:T(8,128)(2,1)S(1)} %copy-done.5), kind=kLoop, calls=%fused_computation.20 | loop fusion | flops 524288 | bytes 1572864 | tf_op jit(solution)/shard_map/convert_element_type | solution.py:184
  63.2 6.7 %all-to-all-done.1 = f32[16,56,128]{2,1,0:T(8,128)S(1)} async-done(((f32[16,56,128]{2,1,0:T(8,128)}), f32[16,56,128]{2,1,0:T(8,128)S(1)}, u32[]{:S(2)}, u32[]{:S(2)}) %all-to-all-start.1) | async-done | bytes 458784 | tf_op jit(solution)/shard_map/all_to_all | solution.py:95
  69.8 0.7 copy.160
  70.5 1.2 %collective-permute-done.4 = f32[16,56,128]{2,1,0:T(8,128)S(1)} collective-permute-done((f32[16,56,128]{2,1,0:T(8,128)S(1)}, f32[16,56,128]{2,1,0:T(8,128)S(1)}, u32[]{:S(2)}, u32[]{:S(2)}) %collective-permute-start.4) | collective-permute-done | bytes 458784 | tf_op jit(solution)/shard_map/ppermute | solution.py:97
  71.6 0.1 pad_maximum_fusion
  71.7 1.0 %constant_dynamic-slice_fusion = f32[1728,128]{1,0:T(8,128)} fusion(f32[2688,128]{1,0:T(8,128)S(1)} %bitcast.211, s32[]{:T(128)S(6)} %select_n.113), kind=kLoop, calls=%fused_computation.117 | loop fusion | bytes 1769476 | tf_op jit(solution)/shard_map/dynamic_slice | solution.py:101
  (84 shorter events, 1.2 us)
Async XLA Ops:
  0.6 3.0 %copy-start.9 = (s32[1,1,256]{2,1,0:T(1,128)S(1)}, s32[1,1,256]{2,1,0:T(1,128)}, u32[]{:S(2)}) copy-start(s32[1,1,256]{2,1,0:T(1,128)} %param.35) | copy-start | bytes 3076
  0.6 3.1 %copy-start.6 = (bf16[1,1,4,8,1024]{4,3,2,1,0:T(8,128)(2,1)S(1)}, bf16[1,1,4,8,1024]{4,3,2,1,0:T(8,128)(2,1)}, u32[]{:S(2)}) copy-start(bf16[1,1,4,8,1024]{4,3,2,1,0:T(8,128)(2,1)} %param.34) | copy-start | bytes 196612
  2.0 10.5 %copy-start.7 = (s32[1,1,2048]{2,1,0:T(1,128)S(1)}, s32[1,1,2048]{2,1,0:T(1,128)}, u32[]{:S(2)}) copy-start(s32[1,1,2048]{2,1,0:T(1,128)} %param.37) | copy-start | bytes 24580
  3.9 10.6 %collective-permute-start = (bf16[12288]{0:T(1024)(128)(2,1)S(1)}, bf16[12288]{0:T(1024)(128)(2,1)S(1)}, u32[]{:S(2)}, u32[]{:S(2)}) collective-permute-start(bf16[12288]{0:T(1024)(128)(2,1)S(1)} %pad_maximum_fusion.4), channel_id=1, source_target_pairs={{8,0},{24,16},{0,8},{16,24},{9,1},{25,17},{1,9},{17,25},{10,2},{26... | collective-permute-start | bytes 73736 | tf_op jit(solution)/shard_map/ppermute | solution.py:63
  7.2 7.3 %collective-permute-start.2 = (bf16[1024]{0:T(1024)(128)(2,1)S(1)}, bf16[1024]{0:T(1024)(128)(2,1)S(1)}, u32[]{:S(2)}, u32[]{:S(2)}) collective-permute-start(bf16[1024]{0:T(1024)(128)(2,1)S(1)} %pad_maximum_fusion.6), channel_id=1, source_target_pairs={{24,0},{0,24},{25,1},{1,25},{26,2},{2,26},{27,3},{3,27},{28,4},{4,... | collective-permute-start | bytes 6152 | tf_op jit(solution)/shard_map/ppermute | solution.py:63
  11.7 4.8 %collective-permute-start.1 = (bf16[12288]{0:T(1024)(128)(2,1)S(1)}, bf16[12288]{0:T(1024)(128)(2,1)S(1)}, u32[]{:S(2)}, u32[]{:S(2)}) collective-permute-start(bf16[12288]{0:T(1024)(128)(2,1)S(1)} %pad_maximum_fusion.5), channel_id=1, source_target_pairs={{16,0},{24,8},{0,16},{8,24},{17,1},{25,9},{1,17},{9,25},{18,2},{26... | collective-permute-start | bytes 73736 | tf_op jit(solution)/shard_map/ppermute | solution.py:63
  23.8 1.2 %copy-start.8 = (bf16[27,4,8,8,64]{4,3,2,0,1:T(8,128)(2,1)}, bf16[27,4,8,8,64]{4,3,2,0,1:T(8,128)(2,1)S(1)}, u32[]{:S(2)}) copy-start(bf16[27,4,8,8,64]{4,3,2,0,1:T(8,128)(2,1)S(1)} %constant_dynamic-update-slice_fusion) | copy-start | bytes 2654212
  23.8 1.3 %copy-start.3 = (bf16[27,64,128]{2,1,0:T(8,128)(2,1)S(1)}, bf16[27,64,128]{2,1,0:T(8,128)(2,1)}, u32[]{:S(2)}) copy-start(bf16[27,64,128]{2,1,0:T(8,128)(2,1)} %param.38) | copy-start | bytes 1327108
  25.4 1.0 %copy-start = (f32[1792,128]{1,0:T(8,128)}, f32[1792,128]{1,0:T(8,128)S(1)}, u32[]{:S(2)}) copy-start(f32[1792,128]{1,0:T(8,128)S(1)} %pad.73) | copy-start | bytes 2752516
  25.4 5.4 %collective-permute-start.3 = (f32[16,56,128]{2,1,0:T(8,128)S(1)}, f32[16,56,128]{2,1,0:T(8,128)}, u32[]{:S(2)}, u32[]{:S(2)}) collective-permute-start(f32[16,56,128]{2,1,0:T(8,128)S(1)} %dynamic-slice_bitcast_fusion), channel_id=1, source_target_pairs={{0,1},{1,0},{2,3},{3,2},{4,5},{5,4},{6,7},{7,6},{8,9},{9,8},{10,11... | collective-permute-start | bytes 1376264 | tf_op jit(solution)/shard_map/ppermute | solution.py:84
  29.6 1.3 %copy-start.1 = (f32[1792,128]{1,0:T(8,128)S(1)}, f32[1792,128]{1,0:T(8,128)}, u32[]{:S(2)}) copy-start(f32[1792,128]{1,0:T(8,128)} %copy-done) | copy-start | bytes 2752516
  32.7 23.9 %slice-start = ((bf16[4,4,4,64,128]{4,3,2,1,0:T(8,128)(2,1)}), bf16[4,4,3,64,128]{4,3,2,1,0:T(8,128)(2,1)S(1)}, s32[]{:S(2)}) async-start(bf16[4,4,4,64,128]{4,3,2,1,0:T(8,128)(2,1)} %fusion.12), calls=%async_computation.2 | async-start | bytes 1572864 | tf_op jit(solution)/shard_map/jit(_roll_static)/slice | solution.py:71
  32.7 19.1 %all-to-all-start = ((f32[16,56,128]{2,1,0:T(8,128)}), f32[16,56,128]{2,1,0:T(8,128)S(1)}, u32[]{:S(2)}, u32[]{:S(2)}) async-start(f32[16,56,128]{2,1,0:T(8,128)} %bitcast_add_fusion), calls=%async_computation | async-start | bytes 917504 | tf_op jit(solution)/shard_map/all_to_all | solution.py:88
  52.6 17.2 %all-to-all-start.1 = ((f32[16,56,128]{2,1,0:T(8,128)}), f32[16,56,128]{2,1,0:T(8,128)S(1)}, u32[]{:S(2)}, u32[]{:S(2)}) async-start(f32[16,56,128]{2,1,0:T(8,128)} %broadcast_in_dim.41), calls=%async_computation.1 | async-start | bytes 917504 | tf_op jit(solution)/shard_map/all_to_all | solution.py:95
  58.5 1.8 %copy-start.4 = (bf16[27,64,128]{2,1,0:T(8,128)(2,1)S(1)}, bf16[27,64,128]{2,1,0:T(8,128)(2,1)}, u32[]{:S(2)}) copy-start(bf16[27,64,128]{2,1,0:T(8,128)(2,1)} %param.38) | copy-start | bytes 1327108
  60.2 2.1 %copy-start.2 = (f32[1,1,8,16,1024]{4,3,2,1,0:T(8,128)S(1)}, f32[1,1,8,16,1024]{4,3,2,1,0:T(8,128)}, u32[]{:S(2)}) copy-start(f32[1,1,8,16,1024]{4,3,2,1,0:T(8,128)} %mul.58) | copy-start | bytes 1572868
  60.2 2.1 %copy-start.5 = (bf16[1,1,8,16,1024]{4,3,2,1,0:T(8,128)(2,1)S(1)}, bf16[1,1,8,16,1024]{4,3,2,1,0:T(8,128)(2,1)}, u32[]{:S(2)}) copy-start(bf16[1,1,8,16,1024]{4,3,2,1,0:T(8,128)(2,1)} %param.36) | copy-start | bytes 786436
  69.8 1.8 %collective-permute-start.4 = (f32[16,56,128]{2,1,0:T(8,128)S(1)}, f32[16,56,128]{2,1,0:T(8,128)S(1)}, u32[]{:S(2)}, u32[]{:S(2)}) collective-permute-start(f32[16,56,128]{2,1,0:T(8,128)S(1)} %all-to-all-done.1), channel_id=1, source_target_pairs={{0,1},{1,0},{2,3},{3,2},{4,5},{5,4},{6,7},{7,6},{8,9},{9,8},{10,11... | collective-permute-start | bytes 1376264 | tf_op jit(solution)/shard_map/ppermute | solution.py:97

commit v7 on v6

--- a/solution.py
+++ b/solution.py
@@ -131,6 +131,19 @@
             for a, flag in enumerate(direction)
         )
         widened = widened.at[target].set(halos[direction][1])
+    window = tuple(2 * c + 1 for c in counts)
+    grads = lax.conv_general_dilated(
+        widened[: window[0], : window[1], : window[2]].transpose(3, 0, 1, 2)[:, None],
+        masked.transpose(3, 0, 1, 2)[:, None],
+        (1, 1, 1),
+        "VALID",
+        rhs_dilation=(2, 2, 2),
+        preferred_element_type=jnp.float32,
+    )
+    grads = grads.transpose(2, 3, 4, 0, 1).reshape(27, channels_out, channels_in)
+    grads, masked_late, weight_late, skip, fine_keep, widened = lax.optimization_barrier(
+        (grads, masked, up_weight, skip, fine_keep, widened)
+    )
     paired = widened.reshape(size_x + 1, 2, size_y + 1, 2, size_z + 1, 2, channels_out)
     windows = []
     for kx in range(3):
@@ -142,12 +155,6 @@
                     index += [slice(start, start + count), 0 if k != 1 else 1]
                 windows.append(paired[tuple(index)])
     gathered = jnp.stack(windows)
-    grads = jnp.einsum(
-        "kabco,abci->koi", gathered, masked, preferred_element_type=jnp.float32
-    )
-    grads, masked_late, weight_late, skip, fine_keep = lax.optimization_barrier(
-        (grads, masked, up_weight, skip, fine_keep)
-    )
     reduced, plan = all_reduce(grads)
 
     back = jnp.einsum(

time: 73.3 us -> 86.8 us (1.18)
  local copies, waits for them, and re-layouts: 21.8 us -> 36.9 us
  matrix products: 4.55 us -> 7.18 us
  waiting for transfers between devices: 22.5 us -> 19.9 us
  other arithmetic: 6.3 us -> 5.34 us
    unnamed x55 -> x56, local copies, waits for them, and re-layouts: 6.86 us -> 19 us
    transpose x0 -> x1, matrix products: none -> 3.47 us  [body(): grads.transpose(2, 3, 4, 0, 1).reshape(27, channels_out, channels_in)]
    all_to_all x1, waiting for transfers between devices: 6.65 us -> 4.91 us  [all_spread(): half = lax.all_to_all(spread, OTHERS, 0, 0, tiled=True)]
    all_to_all x1, waiting for transfers between devices: 11.7 us -> 10.1 us  [all_reduce(): parts = lax.all_to_all(half, OTHERS, 0, 0, tiled=True)]
    add x1, other arithmetic: 1.85 us -> 0.82 us  [all_reduce(): half = lax.dynamic_index_in_dim(rows, core, keepdims=False) + got]
    reduce_sum x1, other arithmetic: 0.03 us -> 1.05 us  [all_reduce(): return (parts.sum(axis=0), (devices, chunk, size))]
    transpose x1, local copies, waits for them, and re-layouts: 0.81 us -> 1.83 us  [body(): jnp.einsum('xyzabci,xpyqzroi->apbqcro', shifted, forward_weight(weight_la...]
    concatenate x3, other arithmetic: 1.22 us -> 0.24 us  [forward_weight(): taps = jnp.roll(taps, -1, axis=axis)]
  transfers between devices with their start and end apart: 7 -> 7, of which waited for: 5 -> 4; matrix products, arithmetic and copies ran while one was open for 23% -> 35% of each run, Pallas kernels for 0% -> 0%
where the time goes in v7:
time: 86.8 us; the launch traced here: 86.2 us
  local copies, waits for them, and re-layouts  36.9 us (43%)
  waiting for transfers between devices  19.9 us (23%)
  starting transfers between devices  15.7 us (18%)
  matrix products  7.18 us (8%)
  other arithmetic  5.34 us (6%)
  between operations  1.15 us (1%)
    unnamed x56, local copies, waits for them, and re-layouts  19 us
    all_to_all x1, waiting for transfers between devices, all_reduce(): parts = lax.all_to_all(half, OTHERS, 0, 0, tiled=True)  10.1 us
    ppermute x3, starting transfers between devices, halo_exchange(): got = lax.ppermute(packed, 'brick', both)  7.66 us
    all_to_all x1, waiting for transfers between devices, all_spread(): half = lax.all_to_all(spread, OTHERS, 0, 0, tiled=True)  4.91 us
    slice x2, local copies, waits for them, and re-layouts, body(): windows.append(paired[tuple(index)])  4.41 us
    all_to_all x1, starting transfers between devices, all_reduce(): parts = lax.all_to_all(half, OTHERS, 0, 0, tiled=True)  4.22 us
    all_to_all x1, starting transfers between devices, all_spread(): half = lax.all_to_all(spread, OTHERS, 0, 0, tiled=True)  3.78 us
    transpose x1, matrix products, body(): grads.transpose(2, 3, 4, 0, 1).reshape(27, channels_out, channels_in)  3.47 us
  transfers between devices with their start and end apart: 7, of which 4 were waited for; matrix products, arithmetic and copies ran while one was open for 35% of the time, Pallas kernels for 0%

profile of v7, /device:TPU:0, one launch (start us, length us, event | category | flops | bytes accessed | tf_op | source)
XLA Modules:
  0.0 86.2 jit_solution(13025276975990461617)
XLA Ops:
  0.7 1.4 %reshape.696 = bf16[8,16,16,64]{3,2,1,0:T(8,128)(2,1)S(1)} reshape(bf16[1,1,8,16,1024]{4,3,2,1,0:T(8,128)(2,1)} %param.39) | data formatting | bytes 524288 | tf_op jit(solution)/shard_map/reshape | solution.py:118
  2.0 0.7 convert_reduce_fusion
  2.9 0.3 broadcast_multiply_fusion
  3.8 3.1 %collective-permute-start = (bf16[12288]{0:T(1024)(128)(2,1)S(1)}, bf16[12288]{0:T(1024)(128)(2,1)S(1)}, u32[]{:S(2)}, u32[]{:S(2)}) collective-permute-start(bf16[12288]{0:T(1024)(128)(2,1)S(1)} %pad_maximum_fusion.4), channel_id=1, source_target_pairs={{8,0},{24,16},{0,8},{16,24},{9,1},{25,17},{1,9},{17,25},{10,2},{26... | collective-permute-start | bytes 73736 | tf_op jit(solution)/shard_map/ppermute | solution.py:63
  7.1 2.7 %collective-permute-start.1 = (bf16[12288]{0:T(1024)(128)(2,1)S(1)}, bf16[12288]{0:T(1024)(128)(2,1)S(1)}, u32[]{:S(2)}, u32[]{:S(2)}) collective-permute-start(bf16[12288]{0:T(1024)(128)(2,1)S(1)} %pad_maximum_fusion.5), channel_id=1, source_target_pairs={{16,0},{24,8},{0,16},{8,24},{17,1},{25,9},{1,17},{9,25},{18,2},{26... | collective-permute-start | bytes 73736 | tf_op jit(solution)/shard_map/ppermute | solution.py:63
  9.9 1.9 %collective-permute-start.2 = (bf16[1024]{0:T(1024)(128)(2,1)S(1)}, bf16[1024]{0:T(1024)(128)(2,1)S(1)}, u32[]{:S(2)}, u32[]{:S(2)}) collective-permute-start(bf16[1024]{0:T(1024)(128)(2,1)S(1)} %pad_maximum_fusion.6), channel_id=1, source_target_pairs={{24,0},{0,24},{25,1},{1,25},{26,2},{2,26},{27,3},{3,27},{28,4},{4,... | collective-permute-start | bytes 6152 | tf_op jit(solution)/shard_map/ppermute | solution.py:63
  11.9 0.3 pad.72
  12.2 0.5 broadcast.274
  12.7 0.7 reduce.43
  13.4 0.7 reshape.702
  14.1 3.0 %collective-permute-done.2 = bf16[1024]{0:T(1024)(128)(2,1)S(1)} collective-permute-done((bf16[1024]{0:T(1024)(128)(2,1)S(1)}, bf16[1024]{0:T(1024)(128)(2,1)S(1)}, u32[]{:S(2)}, u32[]{:S(2)}) %collective-permute-start.2) | collective-permute-done | bytes 2080 | tf_op jit(solution)/shard_map/ppermute | solution.py:63
  17.5 1.4 %scatter.46 = bf16[10,18,18,64]{3,2,1,0:T(8,128)(2,1)S(1)} dynamic-update-slice(bf16[10,18,18,64]{3,2,1,0:T(8,128)(2,1)S(1)} %pad.72, bf16[8,16,1,64]{3,2,1,0:T(2,128)(2,1)S(1)} %reshape.718, s32[]{:T(128)} %constant.523.clone.1, s32[]{:T(128)} %constant.523.clone.1, s32[]{:T(128)} %constant.522.clone.1, s32[]{:T(128)} %constant.522.clone.1) | dynamic-update-slice | bytes 32772 | tf_op jit(solution)/shard_map/scatter | solution.py:133
  19.2 0.3 scatter.51
  20.0 3.5 %fusion = f32[3,3,3,64,128]{4,3,2,1,0:T(8,128)} fusion(bf16[64,1,9,17,17]{0,4,3,2,1:T(8,128)(2,1)S(1)} %slice_bitcast_fusion, bf16[128,1,4,8,8]{0,4,3,2,1:T(8,128)(2,1)S(1)} %fusion.20), kind=kOutput, calls=%fused_computation.2 | convolution fusion | flops 113246208 | bytes 1283200 | tf_op jit(solution)/shard_map/transpose | solution.py:143
  23.6 0.4 reshape.709
  24.0 1.0 %fusion.18 = (bf16[4,1,8,1,8,1,64]{6,5,4,3,2,1,0:T(2,128)(2,1)S(1)}, bf16[4,1,8,1,8,1,64]{6,5,4,3,2,1,0:T(2,128)(2,1)S(1)}, bf16[4,1,8,1,8,1,64]{6,5,4,3,2,1,0:T...) fusion(bf16[5,2,9,2,9,2,64]{6,5,4,3,2,1,0:T(2,128)(2,1)S(1)} %r, ...), kind=kLoop, calls=%fused_computation.127 | loop fusion | bytes 524288 | tf_op jit(solution)/shard_map/slice | solution.py:156
  25.0 3.4 %fusion.17 = (bf16[4,1,8,1,8,1,64]{6,5,4,3,2,1,0:T(2,128)(2,1)}, bf16[4,1,8,1,8,1,64]{6,5,4,3,2,1,0:T(2,128)(2,1)S(1)}, bf16[4,1,8,1,8,1,64]{6,5,4,3,2,1,0:T(2,1...) fusion(bf16[5,2,9,2,9,2,64]{6,5,4,3,2,1,0:T(2,128)(2,1)S(1)} %r, ...), kind=kLoop, calls=%fused_computation.126 | loop fusion | bytes 1245184 | tf_op jit(solution)/shard_map/slice | solution.py:156
  28.6 0.6 copy-done.6
  29.4 0.7 fusion.13
  30.4 0.7 constant_dynamic-update-slice_fusion.34
  31.0 0.7 constant_dynamic-update-slice_fusion.33
  31.7 0.6 constant_dynamic-update-slice_fusion.32
  32.3 0.7 constant_dynamic-update-slice_fusion.31
  33.0 0.6 constant_dynamic-update-slice_fusion.30
  33.6 0.7 constant_dynamic-update-slice_fusion.29
  34.3 0.7 constant_dynamic-update-slice_fusion.28
  34.9 0.7 constant_dynamic-update-slice_fusion.27
  35.6 0.6 constant_dynamic-update-slice_fusion.26
  36.2 0.6 constant_dynamic-update-slice_fusion.25
  36.9 0.6 constant_dynamic-update-slice_fusion.24
  37.5 0.6 constant_dynamic-update-slice_fusion.23
  38.2 0.6 constant_dynamic-update-slice_fusion.22
  38.8 0.7 constant_dynamic-update-slice_fusion.21
  39.5 0.7 constant_dynamic-update-slice_fusion.20
  40.1 0.6 constant_dynamic-update-slice_fusion.19
  40.8 0.6 constant_dynamic-update-slice_fusion.18
  41.4 0.6 constant_dynamic-update-slice_fusion.17
  42.1 0.6 constant_dynamic-update-slice_fusion.16
  42.7 0.6 constant_dynamic-update-slice_fusion.15
  43.3 0.6 constant_dynamic-update-slice_fusion.14
  44.0 0.7 constant_dynamic-update-slice_fusion.13
  44.7 0.6 constant_dynamic-update-slice_fusion.12
  45.3 0.8 bitcast_add_fusion
  46.1 4.2 %all-to-all-start = ((f32[16,56,128]{2,1,0:T(8,128)}), f32[16,56,128]{2,1,0:T(8,128)}, u32[]{:S(2)}, u32[]{:S(2)}) async-start(f32[16,56,128]{2,1,0:T(8,128)} %bitcast_add_fusion), calls=%async_computation | async-start | bytes 917504 | tf_op jit(solution)/shard_map/all_to_all | solution.py:88
  50.6 0.8 copy-done.4
  51.4 0.6 constant_dynamic-update-slice_fusion.11
  52.1 0.6 constant_dynamic-update-slice_fusion.10
  52.7 1.7 %convolution_bitcast_fusion = f32[4,2,8,2,8,2,64]{6,4,5,3,1,2,0:T(8,128)} fusion(bf16[2,2,2,2,2,2,64,128,1,1]{7,6,5,4,3,2,1,0,9,8:T(8,128)(2,1)S(1)} %bitcast.218, bf16[2,2,2,4,8,8,128,1,1,1]{6,5,4,3,2,1,0,9,8,7:T(8,128)(2,1)S(1)} %bitcast.224), kind=kOutput, calls=%fused_computation.1 | convolution fusion | flops 268435456 | bytes 2097152 | tf_op jit(solution)/shard_map/xyzabci,xpyqzroi->apbqcro/dot_general | solution.py:181
  54.4 10.1 %all-to-all-done = f32[16,56,128]{2,1,0:T(8,128)} async-done(((f32[16,56,128]{2,1,0:T(8,128)}), f32[16,56,128]{2,1,0:T(8,128)}, u32[]{:S(2)}, u32[]{:S(2)}) %all-to-all-start) | async-done | bytes 458784 | tf_op jit(solution)/shard_map/all_to_all | solution.py:88
  64.5 1.1 %reduce_sum.9 = f32[56,128]{1,0:T(8,128)S(1)} reduce(f32[16,56,128]{2,1,0:T(8,128)} %all-to-all-done, f32[]{:T(128)} %constant.526.clone.1), dimensions={0}, to_apply=%region_0.1 | reduce | flops 107520 | bytes 487428 | tf_op jit(solution)/shard_map/reduce_sum | solution.py:89
  65.6 0.8 broadcast_in_dim.49
  66.4 3.8 %all-to-all-start.1 = ((f32[16,56,128]{2,1,0:T(8,128)}), f32[16,56,128]{2,1,0:T(8,128)S(1)}, u32[]{:S(2)}, u32[]{:S(2)}) async-start(f32[16,56,128]{2,1,0:T(8,128)} %broadcast_in_dim.49), calls=%async_computation.1 | async-start | bytes 917504 | tf_op jit(solution)/shard_map/all_to_all | solution.py:95
  70.2 0.6 constant_dynamic-update-slice_fusion.9
  70.8 0.3 mul.57
  71.1 0.3 mul.58
  71.5 1.8 %copy.119 = f32[4,2,8,2,8,2,64]{6,5,4,3,2,1,0:T(2,128)S(1)} copy(f32[4,2,8,2,8,2,64]{6,4,5,3,1,2,0:T(8,128)} %convolution_bitcast_fusion) | data formatting | bytes 1048576 | tf_op jit(solution)/shard_map/xyzabci,xpyqzroi->apbqcro/transpose | solution.py:181
  73.3 0.9 %reshape.708 = f32[1,1,8,16,1024]{4,3,2,1,0:T(8,128)S(1)} reshape(f32[4,2,8,2,8,2,64]{6,5,4,3,2,1,0:T(2,128)S(1)} %copy.119) | data formatting | bytes 1048576 | tf_op jit(solution)/shard_map/reshape | solution.py:187
  74.3 0.7 constant_dynamic-update-slice_fusion.8
  74.9 2.0 %fusion.3 = bf16[4,8,8,128]{3,2,1,0:T(8,128)(2,1)S(1)} fusion(bf16[27,4,8,8,64]{4,3,0,2,1:T(8,128)(2,1)} %constant_dynamic-update-slice_fusion.8, bf16[27,64,128]{2,1,0:T(8,128)(2,1)S(1)} %copy-done, f32[4,8,8]{2,1,0:T(8,128)S(1)} %convert_element_type.62), kind=kOutput, calls=%fused_computation.8 | convolution fusion | flops 113311744 | bytes 1393664 | tf_op jit(solution)/shard_map/kabco,koi->abci/dot_general | solution.py:160
  76.9 0.7 reshape.710
  77.6 0.8 multiply_convert_fusion
  78.4 4.9 %all-to-all-done.1 = f32[16,56,128]{2,1,0:T(8,128)S(1)} async-done(((f32[16,56,128]{2,1,0:T(8,128)}), f32[16,56,128]{2,1,0:T(8,128)S(1)}, u32[]{:S(2)}, u32[]{:S(2)}) %all-to-all-start.1) | async-done | bytes 458784 | tf_op jit(solution)/shard_map/all_to_all | solution.py:95
  83.3 1.8 %collective-permute-done.4 = f32[16,56,128]{2,1,0:T(8,128)S(1)} collective-permute-done((f32[16,56,128]{2,1,0:T(8,128)S(1)}, f32[16,56,128]{2,1,0:T(8,128)S(1)}, u32[]{:S(2)}, u32[]{:S(2)}) %collective-permute-start.4) | collective-permute-done | bytes 458784 | tf_op jit(solution)/shard_map/ppermute | solution.py:97
  85.2 1.0 %constant_dynamic-slice_fusion = f32[1728,128]{1,0:T(8,128)} fusion(f32[2688,128]{1,0:T(8,128)S(1)} %bitcast.215, s32[]{:T(128)S(6)} %select_n.113), kind=kLoop, calls=%fused_computation.117 | loop fusion | bytes 1769476 | tf_op jit(solution)/shard_map/dynamic_slice | solution.py:101
  (86 shorter events, 3.2 us)
Async XLA Ops:
  0.6 2.9 %copy-start.10 = (s32[1,1,256]{2,1,0:T(1,128)S(1)}, s32[1,1,256]{2,1,0:T(1,128)}, u32[]{:S(2)}) copy-start(s32[1,1,256]{2,1,0:T(1,128)} %param.35) | copy-start | bytes 3076
  0.6 3.0 %copy-start.5 = (bf16[1,1,4,8,1024]{4,3,2,1,0:T(8,128)(2,1)S(1)}, bf16[1,1,4,8,1024]{4,3,2,1,0:T(8,128)(2,1)}, u32[]{:S(2)}) copy-start(bf16[1,1,4,8,1024]{4,3,2,1,0:T(8,128)(2,1)} %param.34) | copy-start | bytes 196612
  2.8 10.0 %copy-start.8 = (s32[1,1,2048]{2,1,0:T(1,128)S(1)}, s32[1,1,2048]{2,1,0:T(1,128)}, u32[]{:S(2)}) copy-start(s32[1,1,2048]{2,1,0:T(1,128)} %param.37) | copy-start | bytes 24580
  3.8 13.4 %collective-permute-start = (bf16[12288]{0:T(1024)(128)(2,1)S(1)}, bf16[12288]{0:T(1024)(128)(2,1)S(1)}, u32[]{:S(2)}, u32[]{:S(2)}) collective-permute-start(bf16[12288]{0:T(1024)(128)(2,1)S(1)} %pad_maximum_fusion.4), channel_id=1, source_target_pairs={{8,0},{24,16},{0,8},{16,24},{9,1},{25,17},{1,9},{17,25},{10,2},{26... | collective-permute-start | bytes 73736 | tf_op jit(solution)/shard_map/ppermute | solution.py:63
  7.1 10.3 %collective-permute-start.1 = (bf16[12288]{0:T(1024)(128)(2,1)S(1)}, bf16[12288]{0:T(1024)(128)(2,1)S(1)}, u32[]{:S(2)}, u32[]{:S(2)}) collective-permute-start(bf16[12288]{0:T(1024)(128)(2,1)S(1)} %pad_maximum_fusion.5), channel_id=1, source_target_pairs={{16,0},{24,8},{0,16},{8,24},{17,1},{25,9},{1,17},{9,25},{18,2},{26... | collective-permute-start | bytes 73736 | tf_op jit(solution)/shard_map/ppermute | solution.py:63
  9.9 7.3 %collective-permute-start.2 = (bf16[1024]{0:T(1024)(128)(2,1)S(1)}, bf16[1024]{0:T(1024)(128)(2,1)S(1)}, u32[]{:S(2)}, u32[]{:S(2)}) collective-permute-start(bf16[1024]{0:T(1024)(128)(2,1)S(1)} %pad_maximum_fusion.6), channel_id=1, source_target_pairs={{24,0},{0,24},{25,1},{1,25},{26,2},{2,26},{27,3},{3,27},{28,4},{4,... | collective-permute-start | bytes 6152 | tf_op jit(solution)/shard_map/ppermute | solution.py:63
  17.3 2.4 %copy-start.9 = (bf16[12288]{0:T(1024)(128)(2,1)}, bf16[12288]{0:T(1024)(128)(2,1)S(1)}, u32[]{:S(2)}) copy-start(bf16[12288]{0:T(1024)(128)(2,1)S(1)} %collective-permute-done.1) | copy-start | bytes 73732
  20.0 3.5 %copy-start = (bf16[27,64,128]{2,1,0:T(8,128)(2,1)S(1)}, bf16[27,64,128]{2,1,0:T(8,128)(2,1)}, u32[]{:S(2)}) copy-start(bf16[27,64,128]{2,1,0:T(8,128)(2,1)} %param.38) | copy-start | bytes 1327108
  25.0 3.4 %copy-start.1 = (f32[3,3,3,64,128]{4,3,2,1,0:T(8,128)S(1)}, f32[3,3,3,64,128]{4,3,2,1,0:T(8,128)}, u32[]{:S(2)}) copy-start(f32[3,3,3,64,128]{4,3,2,1,0:T(8,128)} %fusion) | copy-start | bytes 2654212
  28.4 0.8 copy-start.6
  28.6 16.8 %collective-permute-start.3 = (f32[16,56,128]{2,1,0:T(8,128)S(1)}, f32[16,56,128]{2,1,0:T(8,128)S(1)}, u32[]{:S(2)}, u32[]{:S(2)}) collective-permute-start(f32[16,56,128]{2,1,0:T(8,128)S(1)} %dynamic-slice_bitcast_fusion), channel_id=1, source_target_pairs={{0,1},{1,0},{2,3},{3,2},{4,5},{5,4},{6,7},{7,6},{8,9},{9,8},{10,11... | collective-permute-start | bytes 1376264 | tf_op jit(solution)/shard_map/ppermute | solution.py:84
  46.1 18.4 %all-to-all-start = ((f32[16,56,128]{2,1,0:T(8,128)}), f32[16,56,128]{2,1,0:T(8,128)}, u32[]{:S(2)}, u32[]{:S(2)}) async-start(f32[16,56,128]{2,1,0:T(8,128)} %bitcast_add_fusion), calls=%async_computation | async-start | bytes 917504 | tf_op jit(solution)/shard_map/all_to_all | solution.py:88
  50.5 0.9 %copy-start.4 = (bf16[4,1,8,1,8,1,64]{6,5,4,3,2,1,0:T(2,128)(2,1)S(1)}, bf16[4,1,8,1,8,1,64]{6,5,4,3,2,1,0:T(2,128)(2,1)}, u32[]{:S(2)}) copy-start(bf16[4,1,8,1,8,1,64]{6,5,4,3,2,1,0:T(2,128)(2,1)} %get-tuple-element.192) | copy-start | bytes 98308
  50.5 1.5 %copy-start.3 = (bf16[4,1,8,1,8,1,64]{6,5,4,3,2,1,0:T(2,128)(2,1)S(1)}, bf16[4,1,8,1,8,1,64]{6,5,4,3,2,1,0:T(2,128)(2,1)}, u32[]{:S(2)}) copy-start(bf16[4,1,8,1,8,1,64]{6,5,4,3,2,1,0:T(2,128)(2,1)} %get-tuple-element.191) | copy-start | bytes 98308
  66.4 16.9 %all-to-all-start.1 = ((f32[16,56,128]{2,1,0:T(8,128)}), f32[16,56,128]{2,1,0:T(8,128)S(1)}, u32[]{:S(2)}, u32[]{:S(2)}) async-start(f32[16,56,128]{2,1,0:T(8,128)} %broadcast_in_dim.49), calls=%async_computation.1 | async-start | bytes 917504 | tf_op jit(solution)/shard_map/all_to_all | solution.py:95
  71.5 2.8 %copy-start.2 = (bf16[4,1,8,1,8,1,64]{6,5,4,3,2,1,0:T(2,128)(2,1)S(1)}, bf16[4,1,8,1,8,1,64]{6,5,4,3,2,1,0:T(2,128)(2,1)}, u32[]{:S(2)}) copy-start(bf16[4,1,8,1,8,1,64]{6,5,4,3,2,1,0:T(2,128)(2,1)} %get-tuple-element.189) | copy-start | bytes 98308
  73.3 4.3 %copy-start.7 = (bf16[1,1,8,16,1024]{4,3,2,1,0:T(8,128)(2,1)S(1)}, bf16[1,1,8,16,1024]{4,3,2,1,0:T(8,128)(2,1)}, u32[]{:S(2)}) copy-start(bf16[1,1,8,16,1024]{4,3,2,1,0:T(8,128)(2,1)} %param.36) | copy-start | bytes 786436
  83.3 1.8 %collective-permute-start.4 = (f32[16,56,128]{2,1,0:T(8,128)S(1)}, f32[16,56,128]{2,1,0:T(8,128)S(1)}, u32[]{:S(2)}, u32[]{:S(2)}) collective-permute-start(f32[16,56,128]{2,1,0:T(8,128)S(1)} %all-to-all-done.1), channel_id=1, source_target_pairs={{0,1},{1,0},{2,3},{3,2},{4,5},{5,4},{6,7},{7,6},{8,9},{9,8},{10,11... | collective-permute-start | bytes 1376264 | tf_op jit(solution)/shard_map/ppermute | solution.py:97

commit v8 on v7

--- a/solution.py
+++ b/solution.py
@@ -141,25 +141,19 @@
         preferred_element_type=jnp.float32,
     )
     grads = grads.transpose(2, 3, 4, 0, 1).reshape(27, channels_out, channels_in)
-    grads, masked_late, weight_late, skip, fine_keep, widened = lax.optimization_barrier(
-        (grads, masked, up_weight, skip, fine_keep, widened)
-    )
-    paired = widened.reshape(size_x + 1, 2, size_y + 1, 2, size_z + 1, 2, channels_out)
-    windows = []
-    for kx in range(3):
-        for ky in range(3):
-            for kz in range(3):
-                index = []
-                for k, count in zip((kx, ky, kz), counts):
-                    start = 1 if k == 2 else 0
-                    index += [slice(start, start + count), 0 if k != 1 else 1]
-                windows.append(paired[tuple(index)])
-    gathered = jnp.stack(windows)
+    grads, masked_late, weight_late, skip, fine_keep = lax.optimization_barrier(
+        (grads, masked, up_weight, skip, fine_keep)
+    )
     reduced, plan = all_reduce(grads)
 
-    back = jnp.einsum(
-        "kabco,koi->abci", gathered, up_weight, preferred_element_type=jnp.float32
-    )
+    back = lax.conv_general_dilated(
+        widened[None, : window[0], : window[1], : window[2]],
+        up_weight.reshape((3, 3, 3, channels_out, channels_in)),
+        (2, 2, 2),
+        "VALID",
+        dimension_numbers=("NXYZC", "XYZIO", "NXYZC"),
+        preferred_element_type=jnp.float32,
+    )[0]
     coarse_grad = (
         (back * coarse_keep.astype(jnp.float32)).astype(jnp.bfloat16).reshape(coarse.shape)
     )

time: 86.8 us -> 73 us (0.84)
  local copies, waits for them, and re-layouts: 36.9 us -> 18.3 us
  waiting for transfers between devices: 19.9 us -> 24.3 us
  matrix products: 7.18 us -> 4.18 us
  other arithmetic: 5.34 us -> 7.76 us
  starting transfers between devices: 15.7 us -> 16.7 us
    unnamed x56 -> x28, local copies, waits for them, and re-layouts: 19 us -> 6.15 us
    slice x2 -> x0, local copies, waits for them, and re-layouts: 4.41 us -> none  [body(): windows.append(paired[tuple(index)])]
    all_to_all x1, waiting for transfers between devices: 4.91 us -> 8.36 us  [all_spread(): half = lax.all_to_all(spread, OTHERS, 0, 0, tiled=True)]
    dot_general x1 -> x0, matrix products: 2 us -> none  [body(): jnp.einsum('kabco,koi->abci', gathered, up_weight, preferred_element_type...]
    all_to_all x1, waiting for transfers between devices: 10.1 us -> 11.8 us  [all_reduce(): parts = lax.all_to_all(half, OTHERS, 0, 0, tiled=True)]
    transpose x1, local copies, waits for them, and re-layouts: 1.83 us -> 0.57 us  [body(): jnp.einsum('xyzabci,xpyqzroi->apbqcro', shifted, forward_weight(weight_la...]
    conv_general_dilated x0 -> x3, local copies, waits for them, and re-layouts: none -> 1.16 us  [body(): lax.conv_general_dilated(widened[None, :window[0], :window[1], :window[2]...]
    reshape x2 -> x0, local copies, waits for them, and re-layouts: 1.04 us -> none  [the longest x1 0.66 us: body(): (back * coarse_keep.astype(jnp.float32)).astype(jnp.bfloat16)]
  transfers between devices with their start and end apart: 7 -> 7, of which waited for: 4 -> 4; matrix products, arithmetic and copies ran while one was open for 35% -> 22% of each run, Pallas kernels for 0% -> 0%
where the time goes in v8:
time: 73 us; the launch traced here: 72.5 us
  waiting for transfers between devices  24.3 us (33%)
  local copies, waits for them, and re-layouts  18.3 us (25%)
  starting transfers between devices  16.7 us (23%)
  other arithmetic  7.76 us (11%)
  matrix products  4.18 us (6%)
  between operations  1.21 us (2%)
    all_to_all x1, waiting for transfers between devices, all_reduce(): parts = lax.all_to_all(half, OTHERS, 0, 0, tiled=True)  11.8 us
    all_to_all x1, waiting for transfers between devices, all_spread(): half = lax.all_to_all(spread, OTHERS, 0, 0, tiled=True)  8.36 us
    ppermute x3, starting transfers between devices, halo_exchange(): got = lax.ppermute(packed, 'brick', both)  7.64 us
    unnamed x28, local copies, waits for them, and re-layouts  6.15 us
    all_to_all x1, starting transfers between devices, all_reduce(): parts = lax.all_to_all(half, OTHERS, 0, 0, tiled=True)  5.26 us
    all_to_all x1, starting transfers between devices, all_spread(): half = lax.all_to_all(spread, OTHERS, 0, 0, tiled=True)  3.76 us
    transpose x1, matrix products, body(): grads.transpose(2, 3, 4, 0, 1).reshape(27, channels_out, channels_in)  2.69 us
    ppermute x3, waiting for transfers between devices, halo_exchange(): got = lax.ppermute(packed, 'brick', both)  2.34 us
  transfers between devices with their start and end apart: 7, of which 4 were waited for; matrix products, arithmetic and copies ran while one was open for 22% of the time, Pallas kernels for 0%

profile of v8, /device:TPU:0, one launch (start us, length us, event | category | flops | bytes accessed | tf_op | source)
XLA Modules:
  0.0 72.5 jit_solution(11136305475048723234)
XLA Ops:
  0.7 0.7 convert_reduce_fusion.1
  1.4 0.7 %convert_reduce_fusion = bf16[2048]{0:T(1024)(128)(2,1)S(1)} fusion(s32[1,1,2048]{2,1,0:T(1,128)} %param.37), kind=kLoop, calls=%fused_computation.69 | loop fusion | flops 2048 | bytes 12288 | tf_op jit(solution)/shard_map/convert_element_type | solution.py:118
  2.1 0.1 convert_element_type.65
  2.2 0.1 convert_element_type.63
  2.3 1.3 %reshape.716 = bf16[8,16,16,64]{3,2,1,0:T(8,128)(2,1)S(1)} reshape(bf16[1,1,8,16,1024]{4,3,2,1,0:T(8,128)(2,1)} %param.39) | data formatting | bytes 524288 | tf_op jit(solution)/shard_map/reshape | solution.py:118
  3.7 0.3 broadcast_multiply_fusion
  4.0 0.1 select_n.110
  4.1 0.1 bitcast_multiply_fusion
  4.3 7.0 %collective-permute-start.2 = (bf16[1024]{0:T(1024)(128)(2,1)S(1)}, bf16[1024]{0:T(1024)(128)(2,1)S(1)}, u32[]{:S(2)}, u32[]{:S(2)}) collective-permute-start(bf16[1024]{0:T(1024)(128)(2,1)S(1)} %pad_maximum_fusion.6), channel_id=1, source_target_pairs={{24,0},{0,24},{25,1},{1,25},{26,2},{2,26},{27,3},{3,27},{28,4},{4,... | collective-permute-start | bytes 6152 | tf_op jit(solution)/shard_map/ppermute | solution.py:63
  11.3 0.2 fusion.22
  11.5 0.1 select_n.96
  11.6 0.1 collective-permute-start
  11.7 0.1 select_n.104
  11.8 0.6 collective-permute-start.1
  12.5 0.1 fusion.40
  12.6 0.1 copy.52
  12.6 0.5 broadcast.292
  13.2 0.7 reduce.43
  13.8 0.1 reshape.722
  13.9 0.3 pad.72
  14.2 0.1 reshape.750
  14.3 2.3 %collective-permute-done.1 = bf16[12288]{0:T(1024)(128)(2,1)S(1)} collective-permute-done((bf16[12288]{0:T(1024)(128)(2,1)S(1)}, bf16[12288]{0:T(1024)(128)(2,1)S(1)}, u32[]{:S(2)}, u32[]{:S(2)}) %collective-permute-start.1) | collective-permute-done | bytes 24608 | tf_op jit(solution)/shard_map/ppermute | solution.py:63
  16.6 0.1 reshape.719
  16.7 0.1 reshape.749
  16.8 1.4 %scatter.46 = bf16[10,18,18,64]{3,2,1,0:T(8,128)(2,1)S(1)} dynamic-update-slice(bf16[10,18,18,64]{3,2,1,0:T(8,128)(2,1)S(1)} %pad.72, bf16[8,16,1,64]{3,2,1,0:T(2,128)(2,1)S(1)} %reshape.749, s32[]{:T(128)} %constant.523.clone.1, s32[]{:T(128)} %constant.523.clone.1, s32[]{:T(128)} %constant.522.clone.1, s32[]{:T(128)} %constant.522.clone.1) | dynamic-update-slice | bytes 32772 | tf_op jit(solution)/shard_map/scatter | solution.py:133
  18.3 0.2 scatter.49
  18.6 0.3 scatter.51
  18.9 0.2 scatter.55
  19.2 0.2 slice_bitcast_fusion
  19.4 2.7 %fusion.8 = f32[3,3,3,64,128]{4,3,2,1,0:T(8,128)S(1)} fusion(bf16[64,1,9,17,17]{0,4,3,2,1:T(8,128)(2,1)S(1)} %get-tuple-element.188, bf16[128,1,4,8,8]{0,4,3,2,1:T(8,128)(2,1)S(1)} %fusion.40), kind=kOutput, calls=%fused_computation.10 | convolution fusion | flops 113246208 | bytes 1283200 | tf_op jit(solution)/shard_map/transpose | solution.py:143
  22.2 0.1 pad_slice_fusion.1
  22.3 0.2 pad.76
  22.6 0.2 copy.50
  22.8 0.2 slice.736
  23.3 0.1 collective-permute-start.3
  23.4 0.8 %fusion.30 = bf16[8,4,8,8,128]{4,3,2,1,0:T(8,128)(2,1)} fusion(bf16[5,9,9,128]{3,2,1,0:T(8,128)(2,1)S(1)} %constant_dynamic-update-slice_fusion), kind=kLoop, calls=%fused_computation.54 | loop fusion | bytes 131072
  24.2 0.6 fusion.29
  24.9 0.8 %fusion.10 = f32[4,8,8,2,128]{4,2,3,1,0:T(8,128)S(1)} fusion(bf16[3,3,3,64,128]{4,3,2,1,0:T(8,128)(2,1)S(1)} %bitcast.115, bf16[9,17,1,7,2,64]{5,3,4,1,0,2:T(8,128)(2,1)S(1)} %slice.736, bf16[9,17,1,8,4,64]{5,3,4,1,0,2:T(8,128)(2,1)S(1)} %copy.50, pred[8,2]{0,1:T(4,128)(4,1)S(1)} %copy-done.9), kind=kOutput, calls=%fused_computation.14 | convolution fusion | flops 229378048 | bytes 1605392 | tf_op jit(solution)/shard_map/conv_general_dilated | solution.py:149
  25.7 1.1 %fusion.14 = bf16[4,4,4,64,128]{4,3,2,1,0:T(8,128)(2,1)} fusion(bf16[1,4,4,64,128]{4,3,2,1,0:T(8,128)(2,1)S(1)} %pad_slice_fusion, bf16[3,4,4,64,128]{4,3,2,1,0:T(8,128)(2,1)S(1)} %pad_slice_fusion.1, bf16[4,3,4,64,128]{4,3,2,1,0:T(8,128)(2,1)S(1)} %fusion.17), kind=kLoop, calls=%fused_computation.19 | loop fusion | flops 1048576 | bytes 2883584 | tf_op jit(solution)/shard_map/jit(_roll_static)/concatenate | solution.py:71
  26.8 0.8 %copy.51 = f32[4,8,8,2,128]{4,1,3,2,0:T(8,128)} copy(f32[4,8,8,2,128]{4,2,3,1,0:T(8,128)S(1)} %fusion.10) | data formatting | bytes 524288 | tf_op jit(solution)/shard_map/conv_general_dilated | solution.py:149
  27.5 0.3 mul.66
  27.9 1.1 %mul.67 = f32[1,1,8,16,1024]{4,3,2,1,0:T(8,128)} reshape(f32[8,16,16,64]{3,2,1,0:T(8,128)S(1)} %mul.66) | data formatting | bytes 1048576 | tf_op jit(solution)/shard_map/mul | solution.py:182
  29.0 0.6 fusion.28
  29.6 0.6 fusion.27
  30.3 1.8 %bitcast_add_fusion = f32[16,56,128]{2,1,0:T(8,128)} fusion(f32[16,56,128]{2,1,0:T(8,128)} %collective-permute-done.3, f32[2,16,56,128]{3,2,1,0:T(8,128)S(1)} %bitcast.112, s32[]{:T(128)S(6)} %select_n.111), kind=kLoop, calls=%fused_computation.29 | loop fusion | flops 114688 | bytes 1376260 | tf_op jit(solution)/shard_map/add | solution.py:87
  32.1 5.3 %all-to-all-start = ((f32[16,56,128]{2,1,0:T(8,128)}), f32[16,56,128]{2,1,0:T(8,128)S(1)}, u32[]{:S(2)}, u32[]{:S(2)}) async-start(f32[16,56,128]{2,1,0:T(8,128)} %bitcast_add_fusion), calls=%async_computation | async-start | bytes 917504 | tf_op jit(solution)/shard_map/all_to_all | solution.py:88
  37.4 0.6 fusion.26
  38.0 0.6 fusion.25
  38.7 0.6 fusion.24
  39.3 0.6 fusion.23
  39.9 11.8 %all-to-all-done = f32[16,56,128]{2,1,0:T(8,128)S(1)} async-done(((f32[16,56,128]{2,1,0:T(8,128)}), f32[16,56,128]{2,1,0:T(8,128)S(1)}, u32[]{:S(2)}, u32[]{:S(2)}) %all-to-all-start) | async-done | bytes 458784 | tf_op jit(solution)/shard_map/all_to_all | solution.py:88
  51.8 0.8 %broadcast_in_dim.52 = f32[16,56,128]{2,1,0:T(8,128)} broadcast(f32[56,128]{1,0:T(8,128)S(1)} %broadcast_multiply_fusion.1), dimensions={1,2} | broadcast | bytes 487424 | tf_op jit(solution)/shard_map/broadcast_in_dim | solution.py:94
  52.6 3.8 %all-to-all-start.1 = ((f32[16,56,128]{2,1,0:T(8,128)}), f32[16,56,128]{2,1,0:T(8,128)S(1)}, u32[]{:S(2)}, u32[]{:S(2)}) async-start(f32[16,56,128]{2,1,0:T(8,128)} %broadcast_in_dim.52), calls=%async_computation.1 | async-start | bytes 917504 | tf_op jit(solution)/shard_map/all_to_all | solution.py:95
  56.4 0.1 fusion.13
  56.4 0.9 %copy-done.8 = bf16[8,4,8,8,128]{4,3,2,1,0:T(8,128)(2,1)S(1)} copy-done((bf16[8,4,8,8,128]{4,3,2,1,0:T(8,128)(2,1)S(1)}, bf16[8,4,8,8,128]{4,3,2,1,0:T(8,128)(2,1)}, u32[]{:S(2)}) %copy-start.8) | copy-done | bytes 524312
  57.4 0.7 %convolution_bitcast_fusion = f32[4,2,8,2,8,2,64]{6,4,5,3,1,2,0:T(8,128)S(1)} fusion(bf16[2,2,2,2,2,2,64,128,1,1]{7,6,5,4,3,2,1,0,9,8:T(8,128)(2,1)S(1)} %bitcast.116, bf16[2,2,2,4,8,8,128,1,1,1]{6,5,4,3,2,1,0,9,8,7:T(8,128)(2,1)S(1)} %bitcast.123), kind=kOutput, calls=%fused_computation.9 | convolution fusion | flops 268435456 | bytes 2097152 | tf_op jit(solution)/shard_map/xyzabci,xpyqzroi->apbqcro/dot_general | solution.py:175
  58.1 0.6 copy.48
  58.7 0.9 %reshape.728 = f32[1,1,8,16,1024]{4,3,2,1,0:T(8,128)S(1)} reshape(f32[4,2,8,2,8,2,64]{6,5,4,3,2,1,0:T(2,128)S(1)} %copy.48) | data formatting | bytes 1048576 | tf_op jit(solution)/shard_map/reshape | solution.py:181
  59.7 0.7 %fusion.20 = bf16[1,1,4,8,1024]{4,3,2,1,0:T(8,128)(2,1)} fusion(f32[4,8,1,16,128]{4,1,3,0,2:T(8,128)S(1)} %bitcast.119, f32[4,8,8]{1,2,0:T(8,128)S(1)} %copy.52), kind=kLoop, calls=%fused_computation.34 | loop fusion | flops 65536 | bytes 197632 | tf_op jit(solution)/shard_map/convert_element_type | solution.py:158
  60.4 0.8 %multiply_convert_fusion = bf16[1,1,8,16,1024]{4,3,2,1,0:T(8,128)(2,1)} fusion(f32[1,1,8,16,1024]{4,3,2,1,0:T(8,128)S(1)} %copy-done.2, f32[1,1,8,16,1024]{4,3,2,1,0:T(8,128)S(1)} %reshape.728, bf16[1,1,8,16,1024]{4,3,2,1,0:T(8,128)(2,1)S(1)} %copy-done.6), kind=kLoop, calls=%fused_computation.28 | loop fusion | flops 524288 | bytes 1572864 | tf_op jit(solution)/shard_map/convert_element_type | solution.py:185
  61.2 8.4 %all-to-all-done.1 = f32[16,56,128]{2,1,0:T(8,128)S(1)} async-done(((f32[16,56,128]{2,1,0:T(8,128)}), f32[16,56,128]{2,1,0:T(8,128)S(1)}, u32[]{:S(2)}, u32[]{:S(2)}) %all-to-all-start.1) | async-done | bytes 458784 | tf_op jit(solution)/shard_map/all_to_all | solution.py:95
  69.6 1.8 %collective-permute-done.4 = f32[16,56,128]{2,1,0:T(8,128)S(1)} collective-permute-done((f32[16,56,128]{2,1,0:T(8,128)S(1)}, f32[16,56,128]{2,1,0:T(8,128)S(1)}, u32[]{:S(2)}, u32[]{:S(2)}) %collective-permute-start.4) | collective-permute-done | bytes 458784 | tf_op jit(solution)/shard_map/ppermute | solution.py:97
  71.4 0.1 pad_maximum_fusion
  71.5 1.0 %constant_dynamic-slice_fusion = f32[1728,128]{1,0:T(8,128)} fusion(f32[2688,128]{1,0:T(8,128)S(1)} %bitcast.110, s32[]{:T(128)S(6)} %select_n.113), kind=kLoop, calls=%fused_computation.73 | loop fusion | bytes 1769476 | tf_op jit(solution)/shard_map/dynamic_slice | solution.py:101
  (59 shorter events, 0.8 us)
Async XLA Ops:
  0.6 3.5 %copy-start.5 = (bf16[1,1,4,8,1024]{4,3,2,1,0:T(8,128)(2,1)S(1)}, bf16[1,1,4,8,1024]{4,3,2,1,0:T(8,128)(2,1)}, u32[]{:S(2)}) copy-start(bf16[1,1,4,8,1024]{4,3,2,1,0:T(8,128)(2,1)} %param.34) | copy-start | bytes 196612
  0.6 12.5 %copy-start.7 = (s32[1,1,2048]{2,1,0:T(1,128)S(1)}, s32[1,1,2048]{2,1,0:T(1,128)}, u32[]{:S(2)}) copy-start(s32[1,1,2048]{2,1,0:T(1,128)} %param.37) | copy-start | bytes 24580
  4.3 9.9 %collective-permute-start.2 = (bf16[1024]{0:T(1024)(128)(2,1)S(1)}, bf16[1024]{0:T(1024)(128)(2,1)S(1)}, u32[]{:S(2)}, u32[]{:S(2)}) collective-permute-start(bf16[1024]{0:T(1024)(128)(2,1)S(1)} %pad_maximum_fusion.6), channel_id=1, source_target_pairs={{24,0},{0,24},{25,1},{1,25},{26,2},{2,26},{27,3},{3,27},{28,4},{4,... | collective-permute-start | bytes 6152 | tf_op jit(solution)/shard_map/ppermute | solution.py:63
  11.6 5.1 %collective-permute-start = (bf16[12288]{0:T(1024)(128)(2,1)S(1)}, bf16[12288]{0:T(1024)(128)(2,1)S(1)}, u32[]{:S(2)}, u32[]{:S(2)}) collective-permute-start(bf16[12288]{0:T(1024)(128)(2,1)S(1)} %pad_maximum_fusion.4), channel_id=1, source_target_pairs={{8,0},{24,16},{0,8},{16,24},{9,1},{25,17},{1,9},{17,25},{10,2},{26... | collective-permute-start | bytes 73736 | tf_op jit(solution)/shard_map/ppermute | solution.py:63
  11.8 4.8 %collective-permute-start.1 = (bf16[12288]{0:T(1024)(128)(2,1)S(1)}, bf16[12288]{0:T(1024)(128)(2,1)S(1)}, u32[]{:S(2)}, u32[]{:S(2)}) collective-permute-start(bf16[12288]{0:T(1024)(128)(2,1)S(1)} %pad_maximum_fusion.5), channel_id=1, source_target_pairs={{16,0},{24,8},{0,16},{8,24},{17,1},{25,9},{1,17},{9,25},{18,2},{26... | collective-permute-start | bytes 73736 | tf_op jit(solution)/shard_map/ppermute | solution.py:63
  19.4 2.7 %copy-start.3 = (bf16[27,64,128]{2,1,0:T(8,128)(2,1)S(1)}, bf16[27,64,128]{2,1,0:T(8,128)(2,1)}, u32[]{:S(2)}) copy-start(bf16[27,64,128]{2,1,0:T(8,128)(2,1)} %param.38) | copy-start | bytes 1327108
  23.2 1.7 %copy-start = (f32[1792,128]{1,0:T(8,128)}, f32[1792,128]{1,0:T(8,128)S(1)}, u32[]{:S(2)}) copy-start(f32[1792,128]{1,0:T(8,128)S(1)} %pad.73) | copy-start | bytes 2752516
  23.2 1.7 %copy-start.9 = (pred[8,2]{0,1:T(4,128)(4,1)S(1)}, pred[8,2]{0,1:T(4,128)(4,1)}, u32[]{:S(2)}) copy-start(pred[8,2]{0,1:T(4,128)(4,1)} %constant.551) | copy-start | bytes 52
  23.3 7.0 %collective-permute-start.3 = (f32[16,56,128]{2,1,0:T(8,128)S(1)}, f32[16,56,128]{2,1,0:T(8,128)}, u32[]{:S(2)}, u32[]{:S(2)}) collective-permute-start(f32[16,56,128]{2,1,0:T(8,128)S(1)} %dynamic-slice_bitcast_fusion), channel_id=1, source_target_pairs={{0,1},{1,0},{2,3},{3,2},{4,5},{5,4},{6,7},{7,6},{8,9},{9,8},{10,11... | collective-permute-start | bytes 1376264 | tf_op jit(solution)/shard_map/ppermute | solution.py:84
  29.0 1.3 %copy-start.1 = (f32[1792,128]{1,0:T(8,128)S(1)}, f32[1792,128]{1,0:T(8,128)}, u32[]{:S(2)}) copy-start(f32[1792,128]{1,0:T(8,128)} %copy-done) | copy-start | bytes 2752516
  32.1 19.6 %all-to-all-start = ((f32[16,56,128]{2,1,0:T(8,128)}), f32[16,56,128]{2,1,0:T(8,128)S(1)}, u32[]{:S(2)}, u32[]{:S(2)}) async-start(f32[16,56,128]{2,1,0:T(8,128)} %bitcast_add_fusion), calls=%async_computation | async-start | bytes 917504 | tf_op jit(solution)/shard_map/all_to_all | solution.py:88
  37.4 19.0 %slice-start = ((bf16[4,4,4,64,128]{4,3,2,1,0:T(8,128)(2,1)}), bf16[4,4,3,64,128]{4,3,2,1,0:T(8,128)(2,1)S(1)}, s32[]{:S(2)}) async-start(bf16[4,4,4,64,128]{4,3,2,1,0:T(8,128)(2,1)} %fusion.14), calls=%async_computation.2 | async-start | bytes 1572864 | tf_op jit(solution)/shard_map/jit(_roll_static)/slice | solution.py:71
  52.6 17.0 %all-to-all-start.1 = ((f32[16,56,128]{2,1,0:T(8,128)}), f32[16,56,128]{2,1,0:T(8,128)S(1)}, u32[]{:S(2)}, u32[]{:S(2)}) async-start(f32[16,56,128]{2,1,0:T(8,128)} %broadcast_in_dim.52), calls=%async_computation.1 | async-start | bytes 917504 | tf_op jit(solution)/shard_map/all_to_all | solution.py:95
  56.3 1.0 %copy-start.8 = (bf16[8,4,8,8,128]{4,3,2,1,0:T(8,128)(2,1)S(1)}, bf16[8,4,8,8,128]{4,3,2,1,0:T(8,128)(2,1)}, u32[]{:S(2)}) copy-start(bf16[8,4,8,8,128]{4,3,2,1,0:T(8,128)(2,1)} %fusion.23) | copy-start | bytes 1572868
  58.1 1.6 %copy-start.4 = (f32[4,8,8,2,128]{4,1,3,2,0:T(8,128)S(1)}, f32[4,8,8,2,128]{4,1,3,2,0:T(8,128)}, u32[]{:S(2)}) copy-start(f32[4,8,8,2,128]{4,1,3,2,0:T(8,128)} %copy.51) | copy-start | bytes 786436
  58.7 1.7 %copy-start.2 = (f32[1,1,8,16,1024]{4,3,2,1,0:T(8,128)S(1)}, f32[1,1,8,16,1024]{4,3,2,1,0:T(8,128)}, u32[]{:S(2)}) copy-start(f32[1,1,8,16,1024]{4,3,2,1,0:T(8,128)} %mul.67) | copy-start | bytes 1572868
  58.7 1.7 %copy-start.6 = (bf16[1,1,8,16,1024]{4,3,2,1,0:T(8,128)(2,1)S(1)}, bf16[1,1,8,16,1024]{4,3,2,1,0:T(8,128)(2,1)}, u32[]{:S(2)}) copy-start(bf16[1,1,8,16,1024]{4,3,2,1,0:T(8,128)(2,1)} %param.36) | copy-start | bytes 786436
  69.6 1.8 %collective-permute-start.4 = (f32[16,56,128]{2,1,0:T(8,128)S(1)}, f32[16,56,128]{2,1,0:T(8,128)S(1)}, u32[]{:S(2)}, u32[]{:S(2)}) collective-permute-start(f32[16,56,128]{2,1,0:T(8,128)S(1)} %all-to-all-done.1), channel_id=1, source_target_pairs={{0,1},{1,0},{2,3},{3,2},{4,5},{5,4},{6,7},{7,6},{8,9},{9,8},{10,11... | collective-permute-start | bytes 1376264 | tf_op jit(solution)/shard_map/ppermute | solution.py:97

commit v9 on v8

--- a/solution.py
+++ b/solution.py
@@ -72,34 +72,27 @@
     return taps.reshape((2, 2, 2, 2, 2, 2) + channels)
 
 
-def all_reduce(grads):
+def all_reduce(half):
     devices = lax.axis_size("brick") * lax.axis_size("chip")
-    lanes = grads.shape[-1]
-    rows = grads.reshape(-1, lanes)
+    lanes = half.shape[-1]
+    rows = half.reshape(-1, lanes)
     size = rows.shape[0]
-    chunk = -(-size // (2 * devices * 8)) * 8
-    rows = jnp.pad(rows, ((0, 2 * chunk * devices - size), (0, 0)))
-    rows = rows.reshape(2, devices, chunk, lanes)
-    core = lax.axis_index("core")
-    got = lax.ppermute(
-        lax.dynamic_index_in_dim(rows, 1 - core, keepdims=False), "core", [(0, 1), (1, 0)]
-    )
-    half = lax.dynamic_index_in_dim(rows, core, keepdims=False) + got
-    parts = lax.all_to_all(half, OTHERS, 0, 0, tiled=True)
-    return parts.sum(axis=0), (devices, chunk, size)
+    chunk = -(-size // (devices * 8)) * 8
+    rows = jnp.pad(rows, ((0, chunk * devices - size), (0, 0)))
+    parts = lax.all_to_all(rows.reshape(devices, chunk, lanes), OTHERS, 0, 0, tiled=True)
+    return parts.sum(axis=0), (devices, chunk, size, half.shape)
 
 
 def all_spread(reduced, plan, riders):
-    devices, chunk, size = plan
+    devices, chunk, size, shape = plan
     spread = jnp.broadcast_to(reduced[None], (devices,) + reduced.shape)
     half = lax.all_to_all(spread, OTHERS, 0, 0, tiled=True)
     half, riders = lax.optimization_barrier((half, riders))
+    half = half.reshape(-1, reduced.shape[-1])[:size].reshape(shape)
     other = lax.ppermute(half, "core", [(0, 1), (1, 0)])
-    lanes = reduced.shape[-1]
-    rows = half.size // lanes
-    three = jnp.concatenate([half, other, half]).reshape(-1, lanes)
-    whole = lax.dynamic_slice_in_dim(three, lax.axis_index("core") * rows, size)
-    return whole, riders
+    three = jnp.stack([half, other, half], axis=1)
+    whole = lax.dynamic_slice_in_dim(three, lax.axis_index("core"), 2, axis=1)
+    return whole.reshape(shape[0], 2 * shape[1], shape[2]), riders
 
 
 def body(coarse, coarse_mask, skip, fine_mask, up_weight, fine_grad):
@@ -132,15 +125,24 @@
         )
         widened = widened.at[target].set(halos[direction][1])
     window = tuple(2 * c + 1 for c in counts)
+    trimmed = widened[: window[0], : window[1], : window[2]]
+    core = lax.axis_index("core")
+    share = channels_out // 2
+    mine = lax.dynamic_slice_in_dim(trimmed, core * share, share, axis=3)
+    theirs = lax.dynamic_slice_in_dim(trimmed, (1 - core) * share, share, axis=3)
+    cut = theirs.size
+    got = lax.ppermute(
+        jnp.concatenate([theirs.reshape(-1), masked.reshape(-1)]), "core", [(0, 1), (1, 0)]
+    )
     grads = lax.conv_general_dilated(
-        widened[: window[0], : window[1], : window[2]].transpose(3, 0, 1, 2)[:, None],
-        masked.transpose(3, 0, 1, 2)[:, None],
+        jnp.stack([mine, got[:cut].reshape(theirs.shape)], axis=-1),
+        jnp.stack([masked, got[cut:].reshape(masked.shape)], axis=-1),
         (1, 1, 1),
         "VALID",
         rhs_dilation=(2, 2, 2),
+        dimension_numbers=("XYZNC", "XYZOI", "XYZNC"),
         preferred_element_type=jnp.float32,
-    )
-    grads = grads.transpose(2, 3, 4, 0, 1).reshape(27, channels_out, channels_in)
+    ).reshape(27, share, channels_in)
     grads, masked_late, weight_late, skip, fine_keep = lax.optimization_barrier(
         (grads, masked, up_weight, skip, fine_keep)
     )
@@ -188,7 +190,7 @@
     weight_grad, (fine_out, coarse_grad) = all_spread(
         reduced * scale, plan, (fine_out, coarse_grad)
     )
-    return (fine_out, coarse_grad, weight_grad.reshape(grads.shape))
+    return (fine_out, coarse_grad, weight_grad)
 
 
 def solution(mesh):

time: 73 us -> 78.9 us (1.081)
  matrix products: 4.18 us -> 10.4 us
  waiting for transfers between devices: 24.3 us -> 19.4 us
  local copies, waits for them, and re-layouts: 18.3 us -> 22.7 us
  starting transfers between devices: 16.7 us -> 17.6 us
    conv_general_dilated x0 -> x1, matrix products: none -> 6.73 us  [body(): lax.conv_general_dilated(jnp.stack([mine, got[:cut].reshape(theirs.shape)...]
    another operation x7 -> x11, local copies, waits for them, and re-layouts: 0.28 us -> 4.27 us  [the longest x3 3.89 us: body(): jnp.stack([mine, got[:cut].reshape(theirs.shape)], axis=-1)]
    all_to_all x1, waiting for transfers between devices: 11.8 us -> 8.02 us  [all_reduce(): lax.all_to_all(rows.reshape(devices, chunk, lanes), OTHERS, 0, 0, tiled=T...]
    transpose x1 -> x0, matrix products: 2.69 us -> none  [body(): grads.transpose(2, 3, 4, 0, 1).reshape(27, channels_out, channels_in)]
    add x1 -> x0, other arithmetic: 1.85 us -> none  [all_reduce(): half = lax.dynamic_index_in_dim(rows, core, keepdims=False) + got]
    unnamed x28 -> x23, local copies, waits for them, and re-layouts: 6.15 us -> 5.02 us
    another operation x0 -> x1, other arithmetic: none -> 1.12 us  [all_spread(): three = jnp.stack([half, other, half], axis=1)]
    conv_general_dilated x1, matrix products: 0.75 us -> 1.87 us  [body(): lax.conv_general_dilated(widened[None, :window[0], :window[1], :window[2]...]
  transfers between devices with their start and end apart: 7 -> 7, of which waited for: 4 -> 4; matrix products, arithmetic and copies ran while one was open for 22% -> 24% of each run, Pallas kernels for 0% -> 0%
where the time goes in v9:
time: 78.9 us; the launch traced here: 78.3 us
  local copies, waits for them, and re-layouts  22.7 us (29%)
  waiting for transfers between devices  19.4 us (25%)
  starting transfers between devices  17.6 us (22%)
  matrix products  10.4 us (13%)
  other arithmetic  6.99 us (9%)
  between operations  1.24 us (2%)
    all_to_all x1, waiting for transfers between devices, all_spread(): half = lax.all_to_all(spread, OTHERS, 0, 0, tiled=True)  8.41 us
    all_to_all x1, waiting for transfers between devices, all_reduce(): lax.all_to_all(rows.reshape(devices, chunk, lanes), OTHERS, 0, 0, tiled=T...  8.02 us
    ppermute x3, starting transfers between devices, halo_exchange(): got = lax.ppermute(packed, 'brick', both)  7.64 us
    conv_general_dilated x1, matrix products, body(): lax.conv_general_dilated(jnp.stack([mine, got[:cut].reshape(theirs.shape)...  6.73 us
    all_to_all x1, starting transfers between devices, all_reduce(): lax.all_to_all(rows.reshape(devices, chunk, lanes), OTHERS, 0, 0, tiled=T...  5.85 us
    unnamed x23, local copies, waits for them, and re-layouts  5.02 us
    all_to_all x1, starting transfers between devices, all_spread(): half = lax.all_to_all(spread, OTHERS, 0, 0, tiled=True)  3.95 us
    another operation x3, local copies, waits for them, and re-layouts, body(): jnp.stack([mine, got[:cut].reshape(theirs.shape)], axis=-1)  3.89 us
  transfers between devices with their start and end apart: 7, of which 4 were waited for; matrix products, arithmetic and copies ran while one was open for 24% of the time, Pallas kernels for 0%

profile of v9, /device:TPU:0, one launch (start us, length us, event | category | flops | bytes accessed | tf_op | source)
XLA Modules:
  0.0 78.3 jit_solution(3745385475257963421)
XLA Ops:
  0.7 0.7 convert_reduce_fusion.1
  1.4 0.7 convert_reduce_fusion
  2.1 0.1 convert_element_type.65
  2.2 0.1 convert_element_type.63
  2.3 1.3 %reshape.739 = bf16[8,16,16,64]{3,2,1,0:T(8,128)(2,1)S(1)} reshape(bf16[1,1,8,16,1024]{4,3,2,1,0:T(8,128)(2,1)} %param.39) | data formatting | bytes 524288 | tf_op jit(solution)/shard_map/reshape | solution.py:111
  3.7 0.3 broadcast_multiply_fusion
  4.0 0.1 select_n.109
  4.1 0.1 bitcast_multiply_fusion
  4.3 7.0 %collective-permute-start.2 = (bf16[1024]{0:T(1024)(128)(2,1)S(1)}, bf16[1024]{0:T(1024)(128)(2,1)S(1)}, u32[]{:S(2)}, u32[]{:S(2)}) collective-permute-start(bf16[1024]{0:T(1024)(128)(2,1)S(1)} %pad_maximum_fusion.10), channel_id=1, source_target_pairs={{24,0},{0,24},{25,1},{1,25},{26,2},{2,26},{27,3},{3,27},{28,4},{4,... | collective-permute-start | bytes 6152 | tf_op jit(solution)/shard_map/ppermute | solution.py:63
  11.3 0.2 fusion.23
  11.5 0.1 select_n.95
  11.7 0.1 select_n.103
  11.8 0.6 collective-permute-start.1
  12.5 1.0 %broadcast_multiply_fusion.1 = bf16[4,8,8,128,1]{3,4,2,1,0:T(2,128)(2,1)} fusion(bf16[4,8,8,128,1]{3,4,2,1,0:T(2,128)(2,1)S(1)} %reshape.778, bf16[4,8,8]{2,1,0:T(8,128)(2,1)S(1)} %convert_element_type.65), kind=kLoop, calls=%fused_computation.59 | loop fusion | flops 32768 | bytes 131584 | tf_op jit(solution)/shard_map/mul | solution.py:109
  13.6 0.5 broadcast.300
  14.1 0.7 reduce.43
  14.9 0.3 pad.72
  15.2 0.1 mul.80
  15.4 1.2 %collective-permute-done.1 = bf16[12288]{0:T(1024)(128)(2,1)S(1)} collective-permute-done((bf16[12288]{0:T(1024)(128)(2,1)S(1)}, bf16[12288]{0:T(1024)(128)(2,1)S(1)}, u32[]{:S(2)}, u32[]{:S(2)}) %collective-permute-start.1) | collective-permute-done | bytes 24608 | tf_op jit(solution)/shard_map/ppermute | solution.py:63
  16.6 0.1 reshape.742
  16.8 1.4 %scatter.46 = bf16[10,18,18,64]{3,2,1,0:T(8,128)(2,1)S(1)} dynamic-update-slice(bf16[10,18,18,64]{3,2,1,0:T(8,128)(2,1)S(1)} %pad.72, bf16[8,16,1,64]{3,2,1,0:T(2,128)(2,1)S(1)} %reshape.776, s32[]{:T(128)} %constant.517.clone.1, s32[]{:T(128)} %constant.517.clone.1, s32[]{:T(128)} %constant.516.clone.1, s32[]{:T(128)} %constant.516.clone.1) | dynamic-update-slice | bytes 32772 | tf_op jit(solution)/shard_map/scatter | solution.py:126
  18.3 0.2 scatter.49
  18.6 0.3 scatter.51
  18.9 0.2 scatter.55
  19.1 0.2 scatter.56
  19.4 0.2 slice_bitcast_fusion.12
  19.6 0.2 pad.76
  19.9 0.2 copy.61
  20.1 1.0 %slice.750 = bf16[9,17,1,7,2,64]{5,3,4,1,0,2:T(8,128)(2,1)} slice(bf16[9,17,1,8,4,64]{5,3,4,1,0,2:T(8,128)(2,1)S(1)} %copy.61), slice={[0:9], [0:17], [0:1], [1:8], [0:2], [0:64]} | slice | bytes 548352 | tf_op jit(solution)/shard_map/conv_general_dilated | solution.py:151
  21.1 0.6 dynamic-slice_bitcast_fusion
  21.7 0.5 reshape.744
  22.2 0.1 pad_maximum_fusion.5
  22.4 1.9 %fusion.9 = f32[4,8,8,2,128]{4,2,3,1,0:T(8,128)S(1)} fusion(bf16[3,3,3,64,128]{4,3,2,1,0:T(8,128)(2,1)} %bitcast.108, bf16[9,17,1,7,2,64]{5,3,4,1,0,2:T(8,128)(2,1)} %slice.750, bf16[9,17,1,8,4,64]{5,3,4,1,0,2:T(8,128)(2,1)S(1)} %copy.61, pred[8,2]{0,1:T(4,128)(4,1)S(1)} %copy-done.6), kind=kOutput, calls=%fused_computation.16 | convolution fusion | flops 229378048 | bytes 1605392 | tf_op jit(solution)/shard_map/conv_general_dilated | solution.py:151
  24.2 0.7 slice_bitcast_fusion.10
  25.0 1.3 %copy.50 = bf16[9,17,17,32,1]{3,4,2,1,0:T(2,128)(2,1)S(1)} copy(bf16[9,17,17,32,1]{3,2,1,0,4:T(8,128)(2,1)S(1)} %get-tuple-element.189) | data formatting | bytes 332928 | tf_op jit(solution)/shard_map/stack | solution.py:138
  26.3 0.7 fusion.21
  27.0 0.1 slice.736
  27.1 0.1 copy.53
  27.2 2.1 %stack_reshape.13 = bf16[9,17,17,32,1]{3,4,2,1,0:T(2,128)(2,1)S(1)} reshape(bf16[83232]{0:T(1024)(128)(2,1)S(1)} %slice.735) | data formatting | bytes 332928 | tf_op jit(solution)/shard_map/stack;reshape | solution.py:138
  29.3 6.7 %fusion.8 = f32[3,3,3,32,128]{4,3,2,1,0:T(8,128)S(1)} fusion(bf16[9,17,17,32,1]{3,4,2,1,0:T(2,128)(2,1)S(1)} %stack_reshape.13, bf16[9,17,17,32,1]{3,4,2,1,0:T(2,128)(2,1)S(1)} %copy.50, bf16[4,8,8,128,1]{3,4,2,1,0:T(2,128)(2,1)S(1)} %copy.53, bf16[4,8,8,128,1]{3,4,2,1,0:T(2,128)(2,1)} %broadcast_multiply_fusion.1), kind=kOutput, calls=%fused_computation.10 | convolution fusion | flops 114174208 | bytes 906368 | tf_op jit(solution)/shard_map/conv_general_dilated | solution.py:137
  36.1 0.1 pad_slice_fusion.1
  36.2 0.8 %pad.73 = f32[896,128]{1,0:T(8,128)} pad(f32[864,128]{1,0:T(8,128)S(1)} %bitcast.118, f32[]{:T(128)} %constant.523.clone.1), padding=0_32x0_0 | pad | bytes 901124 | tf_op jit(solution)/shard_map/jit(_pad)/pad | solution.py:81
  37.1 5.9 %all-to-all-start = ((f32[16,56,128]{2,1,0:T(8,128)}), f32[16,56,128]{2,1,0:T(8,128)S(1)}, u32[]{:S(2)}, u32[]{:S(2)}) async-start(f32[16,56,128]{2,1,0:T(8,128)} %bitcast.6), calls=%async_computation | async-start | bytes 917504 | tf_op jit(solution)/shard_map/all_to_all | solution.py:82
  43.1 0.6 fusion.31
  43.7 0.6 fusion.30
  44.3 0.6 fusion.29
  45.0 0.3 mul.91
  45.3 1.1 %mul.92 = f32[1,1,8,16,1024]{4,3,2,1,0:T(8,128)} reshape(f32[8,16,16,64]{3,2,1,0:T(8,128)S(1)} %mul.91) | data formatting | bytes 1048576 | tf_op jit(solution)/shard_map/mul | solution.py:184
  46.5 0.1 fusion.13
  46.6 0.6 fusion.28
  47.3 0.6 fusion.27
  47.9 0.7 fusion.26
  48.6 0.6 fusion.25
  49.2 8.0 %all-to-all-done = f32[16,56,128]{2,1,0:T(8,128)S(1)} async-done(((f32[16,56,128]{2,1,0:T(8,128)}), f32[16,56,128]{2,1,0:T(8,128)S(1)}, u32[]{:S(2)}, u32[]{:S(2)}) %all-to-all-start) | async-done | bytes 458784 | tf_op jit(solution)/shard_map/all_to_all | solution.py:82
  57.3 0.8 %broadcast_in_dim.44 = f32[16,56,128]{2,1,0:T(8,128)} broadcast(f32[56,128]{1,0:T(8,128)S(1)} %broadcast_multiply_fusion.2), dimensions={1,2} | broadcast | bytes 487424 | tf_op jit(solution)/shard_map/broadcast_in_dim | solution.py:88
  58.1 4.0 %all-to-all-start.1 = ((f32[16,56,128]{2,1,0:T(8,128)}), f32[16,56,128]{2,1,0:T(8,128)S(1)}, u32[]{:S(2)}, u32[]{:S(2)}) async-start(f32[16,56,128]{2,1,0:T(8,128)} %broadcast_in_dim.44), calls=%async_computation.1 | async-start | bytes 917504 | tf_op jit(solution)/shard_map/all_to_all | solution.py:89
  62.1 0.6 fusion.24
  62.8 1.8 %convolution_bitcast_fusion = f32[4,2,8,2,8,2,64]{6,4,5,3,1,2,0:T(8,128)S(1)} fusion(bf16[2,2,2,2,2,2,64,128,1,1]{7,6,5,4,3,2,1,0,9,8:T(8,128)(2,1)S(1)} %bitcast.113, bf16[2,2,2,4,8,8,128,1,1,1]{6,5,4,3,2,1,0,9,8,7:T(8,128)(2,1)} %bitcast.24), kind=kOutput, calls=%fused_computation.8 | convolution fusion | flops 268435456 | bytes 2097152 | tf_op jit(solution)/shard_map/xyzabci,xpyqzroi->apbqcro/dot_general | solution.py:177
  64.6 0.5 copy.59
  65.1 0.9 %reshape.754 = f32[1,1,8,16,1024]{4,3,2,1,0:T(8,128)S(1)} reshape(f32[4,2,8,2,8,2,64]{6,5,4,3,2,1,0:T(2,128)S(1)} %copy.59) | data formatting | bytes 1048576 | tf_op jit(solution)/shard_map/reshape | solution.py:183
  66.1 0.8 %multiply_convert_fusion = bf16[1,1,8,16,1024]{4,3,2,1,0:T(8,128)(2,1)} fusion(f32[1,1,8,16,1024]{4,3,2,1,0:T(8,128)S(1)} %copy-done, f32[1,1,8,16,1024]{4,3,2,1,0:T(8,128)S(1)} %reshape.754, bf16[1,1,8,16,1024]{4,3,2,1,0:T(8,128)(2,1)S(1)} %copy-done.3), kind=kLoop, calls=%fused_computation.31 | loop fusion | flops 524288 | bytes 1572864 | tf_op jit(solution)/shard_map/convert_element_type | solution.py:187
  66.9 8.4 %all-to-all-done.1 = f32[16,56,128]{2,1,0:T(8,128)S(1)} async-done(((f32[16,56,128]{2,1,0:T(8,128)}), f32[16,56,128]{2,1,0:T(8,128)S(1)}, u32[]{:S(2)}, u32[]{:S(2)}) %all-to-all-start.1) | async-done | bytes 458784 | tf_op jit(solution)/shard_map/all_to_all | solution.py:89
  75.4 1.8 %collective-permute-done.4 = f32[27,32,128]{2,1,0:T(8,128)S(1)} collective-permute-done((f32[27,32,128]{2,1,0:T(8,128)S(1)}, f32[27,32,128]{2,1,0:T(8,128)S(1)}, u32[]{:S(2)}, u32[]{:S(2)}) %collective-permute-start.4) | collective-permute-done | bytes 442400 | tf_op jit(solution)/shard_map/ppermute | solution.py:92
  77.2 1.1 %fusion.17 = f32[27,2,32,128]{3,2,1,0:T(8,128)} fusion(s32[]{:T(128)S(6)} %select_n.112, f32[27,1,32,128]{3,2,1,0:T(8,128)S(1)} %bitcast.112, f32[27,1,32,128]{3,2,1,0:T(8,128)S(1)} %bitcast.119), kind=kLoop, calls=%fused_computation.28 | loop fusion | flops 442368 | bytes 1769476 | tf_op jit(solution)/shard_map/stack | solution.py:93
  (62 shorter events, 1.5 us)
Async XLA Ops:
  0.6 3.5 %copy-start.2 = (bf16[1,1,4,8,1024]{4,3,2,1,0:T(8,128)(2,1)S(1)}, bf16[1,1,4,8,1024]{4,3,2,1,0:T(8,128)(2,1)}, u32[]{:S(2)}) copy-start(bf16[1,1,4,8,1024]{4,3,2,1,0:T(8,128)(2,1)} %param.34) | copy-start | bytes 196612
  2.3 11.8 %copy-start.4 = (s32[1,1,2048]{2,1,0:T(1,128)S(1)}, s32[1,1,2048]{2,1,0:T(1,128)}, u32[]{:S(2)}) copy-start(s32[1,1,2048]{2,1,0:T(1,128)} %param.37) | copy-start | bytes 24580
  4.3 11.0 %collective-permute-start.2 = (bf16[1024]{0:T(1024)(128)(2,1)S(1)}, bf16[1024]{0:T(1024)(128)(2,1)S(1)}, u32[]{:S(2)}, u32[]{:S(2)}) collective-permute-start(bf16[1024]{0:T(1024)(128)(2,1)S(1)} %pad_maximum_fusion.10), channel_id=1, source_target_pairs={{24,0},{0,24},{25,1},{1,25},{26,2},{2,26},{27,3},{3,27},{28,4},{4,... | collective-permute-start | bytes 6152 | tf_op jit(solution)/shard_map/ppermute | solution.py:63
  11.6 5.1 %collective-permute-start = (bf16[12288]{0:T(1024)(128)(2,1)S(1)}, bf16[12288]{0:T(1024)(128)(2,1)S(1)}, u32[]{:S(2)}, u32[]{:S(2)}) collective-permute-start(bf16[12288]{0:T(1024)(128)(2,1)S(1)} %pad_maximum_fusion.8), channel_id=1, source_target_pairs={{8,0},{24,16},{0,8},{16,24},{9,1},{25,17},{1,9},{17,25},{10,2},{26... | collective-permute-start | bytes 73736 | tf_op jit(solution)/shard_map/ppermute | solution.py:63
  11.8 4.8 %collective-permute-start.1 = (bf16[12288]{0:T(1024)(128)(2,1)S(1)}, bf16[12288]{0:T(1024)(128)(2,1)S(1)}, u32[]{:S(2)}, u32[]{:S(2)}) collective-permute-start(bf16[12288]{0:T(1024)(128)(2,1)S(1)} %pad_maximum_fusion.9), channel_id=1, source_target_pairs={{16,0},{24,8},{0,16},{8,24},{17,1},{25,9},{1,17},{9,25},{18,2},{26... | collective-permute-start | bytes 73736 | tf_op jit(solution)/shard_map/ppermute | solution.py:63
  16.7 2.9 %copy-start.5 = (bf16[12288]{0:T(1024)(128)(2,1)}, bf16[12288]{0:T(1024)(128)(2,1)S(1)}, u32[]{:S(2)}) copy-start(bf16[12288]{0:T(1024)(128)(2,1)S(1)} %collective-permute-done) | copy-start | bytes 73732
  21.7 0.7 copy-start.6
  22.3 4.8 %collective-permute-start.3 = (bf16[116000]{0:T(1024)(128)(2,1)S(1)}, bf16[116000]{0:T(1024)(128)(2,1)S(1)}, u32[]{:S(2)}, u32[]{:S(2)}) collective-permute-start(bf16[116000]{0:T(1024)(128)(2,1)S(1)} %pad_maximum_fusion.5), channel_id=1, source_target_pairs={{0,1},{1,0},{2,3},{3,2},{4,5},{5,4},{6,7},{7,6},{8,9},{9,8},{10,11... | collective-permute-start | bytes 696008 | tf_op jit(solution)/shard_map/ppermute | solution.py:134
  29.3 6.8 %copy-start.1 = (bf16[27,64,128]{2,1,0:T(8,128)(2,1)S(1)}, bf16[27,64,128]{2,1,0:T(8,128)(2,1)}, u32[]{:S(2)}) copy-start(bf16[27,64,128]{2,1,0:T(8,128)(2,1)} %param.38) | copy-start | bytes 1327108
  37.1 20.2 %all-to-all-start = ((f32[16,56,128]{2,1,0:T(8,128)}), f32[16,56,128]{2,1,0:T(8,128)S(1)}, u32[]{:S(2)}, u32[]{:S(2)}) async-start(f32[16,56,128]{2,1,0:T(8,128)} %bitcast.6), calls=%async_computation | async-start | bytes 917504 | tf_op jit(solution)/shard_map/all_to_all | solution.py:82
  58.1 17.2 %all-to-all-start.1 = ((f32[16,56,128]{2,1,0:T(8,128)}), f32[16,56,128]{2,1,0:T(8,128)S(1)}, u32[]{:S(2)}, u32[]{:S(2)}) async-start(f32[16,56,128]{2,1,0:T(8,128)} %broadcast_in_dim.44), calls=%async_computation.1 | async-start | bytes 917504 | tf_op jit(solution)/shard_map/all_to_all | solution.py:89
  64.5 1.5 %copy-start = (f32[1,1,8,16,1024]{4,3,2,1,0:T(8,128)S(1)}, f32[1,1,8,16,1024]{4,3,2,1,0:T(8,128)}, u32[]{:S(2)}) copy-start(f32[1,1,8,16,1024]{4,3,2,1,0:T(8,128)} %mul.92) | copy-start | bytes 1572868
  64.6 1.5 %copy-start.3 = (bf16[1,1,8,16,1024]{4,3,2,1,0:T(8,128)(2,1)S(1)}, bf16[1,1,8,16,1024]{4,3,2,1,0:T(8,128)(2,1)}, u32[]{:S(2)}) copy-start(bf16[1,1,8,16,1024]{4,3,2,1,0:T(8,128)(2,1)} %param.36) | copy-start | bytes 786436
  75.3 1.9 %collective-permute-start.4 = (f32[27,32,128]{2,1,0:T(8,128)S(1)}, f32[27,32,128]{2,1,0:T(8,128)S(1)}, u32[]{:S(2)}, u32[]{:S(2)}) collective-permute-start(f32[27,32,128]{2,1,0:T(8,128)S(1)} %bitcast.111), channel_id=1, source_target_pairs={{0,1},{1,0},{2,3},{3,2},{4,5},{5,4},{6,7},{7,6},{8,9},{9,8},{10,11... | collective-permute-start | bytes 1327112 | tf_op jit(solution)/shard_map/ppermute | solution.py:92

commit v10 on v9

--- a/solution.py
+++ b/solution.py
@@ -128,21 +128,21 @@
     trimmed = widened[: window[0], : window[1], : window[2]]
     core = lax.axis_index("core")
     share = channels_out // 2
-    mine = lax.dynamic_slice_in_dim(trimmed, core * share, share, axis=3)
-    theirs = lax.dynamic_slice_in_dim(trimmed, (1 - core) * share, share, axis=3)
-    cut = theirs.size
-    got = lax.ppermute(
-        jnp.concatenate([theirs.reshape(-1), masked.reshape(-1)]), "core", [(0, 1), (1, 0)]
-    )
-    grads = lax.conv_general_dilated(
-        jnp.stack([mine, got[:cut].reshape(theirs.shape)], axis=-1),
-        jnp.stack([masked, got[cut:].reshape(masked.shape)], axis=-1),
-        (1, 1, 1),
-        "VALID",
-        rhs_dilation=(2, 2, 2),
-        dimension_numbers=("XYZNC", "XYZOI", "XYZNC"),
-        preferred_element_type=jnp.float32,
-    ).reshape(27, share, channels_in)
+
+    def channel_grads(start):
+        part = lax.dynamic_slice_in_dim(trimmed, start, share, axis=3)
+        return lax.conv_general_dilated(
+            part[..., None],
+            masked[..., None],
+            (1, 1, 1),
+            "VALID",
+            rhs_dilation=(2, 2, 2),
+            dimension_numbers=("XYZNC", "XYZOI", "XYZNC"),
+            preferred_element_type=jnp.float32,
+        ).reshape(27, share, channels_in)
+
+    got = lax.ppermute(channel_grads((1 - core) * share), "core", [(0, 1), (1, 0)])
+    grads = channel_grads(core * share) + got
     grads, masked_late, weight_late, skip, fine_keep = lax.optimization_barrier(
         (grads, masked, up_weight, skip, fine_keep)
     )

time: 78.9 us -> 71.6 us (0.907)
  local copies, waits for them, and re-layouts: 22.7 us -> 17.8 us
  matrix products: 10.4 us -> 8.02 us
  waiting for transfers between devices: 19.4 us -> 21.3 us
  other arithmetic: 6.99 us -> 5.91 us
  starting transfers between devices: 17.6 us -> 16.8 us
    another operation x11 -> x7, local copies, waits for them, and re-layouts: 4.27 us -> 0.28 us  [the longest x3 3.89 us: body(): jnp.stack([mine, got[:cut].reshape(theirs.shape)], axis=-1)]
    conv_general_dilated x1 -> x2, matrix products: 6.73 us -> 5.5 us  [channel_grads(): lax.conv_general_dilated(part[..., None], masked[..., None], (1, 1, 1), '...]
    ppermute x3, waiting for transfers between devices: 1.24 us -> 2.44 us  [halo_exchange(): got = lax.ppermute(packed, 'brick', both)]
    conv_general_dilated x1, matrix products: 1.87 us -> 0.75 us  [body(): lax.conv_general_dilated(widened[None, :window[0], :window[1], :window[2]...]
    ppermute x1, waiting for transfers between devices: 0.01 us -> 1.04 us  [body(): lax.ppermute(channel_grads((1 - core) * share), 'core', [(0, 1), (1, 0)])]
    mul x3 -> x1, other arithmetic: 1.11 us -> 0.1 us  [body(): masked = coarse.reshape(size_x, size_y, size_z, channels_in) * coarse_keep]
    unnamed x23 -> x22, local copies, waits for them, and re-layouts: 5.02 us -> 6.01 us
    conv_general_dilated x3, local copies, waits for them, and re-layouts: 1.28 us -> 0.45 us  [body(): lax.conv_general_dilated(widened[None, :window[0], :window[1], :window[2]...]
  transfers between devices with their start and end apart: 7 -> 7, of which waited for: 4 -> 5; matrix products, arithmetic and copies ran while one was open for 24% -> 20% of each run, Pallas kernels for 0% -> 0%
where the time goes in v10:
time: 71.6 us; the launch traced here: 71.1 us
  waiting for transfers between devices  21.3 us (30%)
  local copies, waits for them, and re-layouts  17.8 us (25%)
  starting transfers between devices  16.8 us (23%)
  matrix products  8.02 us (11%)
  other arithmetic  5.91 us (8%)
  between operations  1.18 us (2%)
    all_to_all x1, waiting for transfers between devices, all_spread(): half = lax.all_to_all(spread, OTHERS, 0, 0, tiled=True)  8.21 us
    all_to_all x1, waiting for transfers between devices, all_reduce(): lax.all_to_all(rows.reshape(devices, chunk, lanes), OTHERS, 0, 0, tiled=T...  7.88 us
    ppermute x3, starting transfers between devices, halo_exchange(): got = lax.ppermute(packed, 'brick', both)  7.64 us
    unnamed x22, local copies, waits for them, and re-layouts  6.01 us
    conv_general_dilated x2, matrix products, channel_grads(): lax.conv_general_dilated(part[..., None], masked[..., None], (1, 1, 1), '...  5.5 us
    all_to_all x1, starting transfers between devices, all_reduce(): lax.all_to_all(rows.reshape(devices, chunk, lanes), OTHERS, 0, 0, tiled=T...  5.26 us
    all_to_all x1, starting transfers between devices, all_spread(): half = lax.all_to_all(spread, OTHERS, 0, 0, tiled=True)  3.79 us
    ppermute x3, waiting for transfers between devices, halo_exchange(): got = lax.ppermute(packed, 'brick', both)  2.44 us
  transfers between devices with their start and end apart: 7, of which 5 were waited for; matrix products, arithmetic and copies ran while one was open for 20% of the time, Pallas kernels for 0%

profile of v10, /device:TPU:0, one launch (start us, length us, event | category | flops | bytes accessed | tf_op | source)
XLA Modules:
  0.0 71.1 jit_solution(18244438943584157476)
XLA Ops:
  0.7 0.7 convert_reduce_fusion.1
  1.4 0.7 %convert_reduce_fusion = bf16[2048]{0:T(1024)(128)(2,1)S(1)} fusion(s32[1,1,2048]{2,1,0:T(1,128)} %param.37), kind=kLoop, calls=%fused_computation.74 | loop fusion | flops 2048 | bytes 12288 | tf_op jit(solution)/shard_map/convert_element_type | solution.py:111
  2.1 0.1 convert_element_type.65
  2.2 0.1 convert_element_type.63
  2.3 1.3 %reshape.734 = bf16[8,16,16,64]{3,2,1,0:T(8,128)(2,1)S(1)} reshape(bf16[1,1,8,16,1024]{4,3,2,1,0:T(8,128)(2,1)} %param.39) | data formatting | bytes 524288 | tf_op jit(solution)/shard_map/reshape | solution.py:111
  3.6 0.3 broadcast_multiply_fusion
  4.0 0.1 select_n.109
  4.1 0.1 bitcast_multiply_fusion
  4.3 7.0 %collective-permute-start.2 = (bf16[1024]{0:T(1024)(128)(2,1)S(1)}, bf16[1024]{0:T(1024)(128)(2,1)S(1)}, u32[]{:S(2)}, u32[]{:S(2)}) collective-permute-start(bf16[1024]{0:T(1024)(128)(2,1)S(1)} %pad_maximum_fusion.5), channel_id=1, source_target_pairs={{24,0},{0,24},{25,1},{1,25},{26,2},{2,26},{27,3},{3,27},{28,4},{4,... | collective-permute-start | bytes 6152 | tf_op jit(solution)/shard_map/ppermute | solution.py:63
  11.3 0.2 fusion.25
  11.5 0.1 select_n.95
  11.7 0.1 select_n.103
  11.8 0.6 collective-permute-start.1
  12.4 0.1 copy.61
  12.5 0.5 broadcast.299
  13.0 0.7 reduce.43
  13.7 0.1 reshape.742
  13.8 0.3 pad.72
  14.1 0.1 reshape.771
  14.2 2.4 %collective-permute-done.1 = bf16[12288]{0:T(1024)(128)(2,1)S(1)} collective-permute-done((bf16[12288]{0:T(1024)(128)(2,1)S(1)}, bf16[12288]{0:T(1024)(128)(2,1)S(1)}, u32[]{:S(2)}, u32[]{:S(2)}) %collective-permute-start.1) | collective-permute-done | bytes 24608 | tf_op jit(solution)/shard_map/ppermute | solution.py:63
  16.6 0.1 reshape.737
  16.7 0.1 reshape.770
  16.8 1.4 %scatter.46 = bf16[10,18,18,64]{3,2,1,0:T(8,128)(2,1)S(1)} dynamic-update-slice(bf16[10,18,18,64]{3,2,1,0:T(8,128)(2,1)S(1)} %pad.72, bf16[8,16,1,64]{3,2,1,0:T(2,128)(2,1)S(1)} %reshape.770, s32[]{:T(128)} %constant.517.clone.1, s32[]{:T(128)} %constant.517.clone.1, s32[]{:T(128)} %constant.516.clone.1, s32[]{:T(128)} %constant.516.clone.1) | dynamic-update-slice | bytes 32772 | tf_op jit(solution)/shard_map/scatter | solution.py:126
  18.3 0.2 scatter.49
  18.5 0.3 scatter.51
  18.9 0.2 scatter.55
  19.2 0.2 slice_bitcast_fusion.12
  19.4 0.2 pad.76
  19.7 0.2 copy.59
  19.9 0.2 slice.740
  20.1 0.8 %copy-done.2 = bf16[27,64,128]{2,1,0:T(8,128)(2,1)S(1)} copy-done((bf16[27,64,128]{2,1,0:T(8,128)(2,1)S(1)}, bf16[27,64,128]{2,1,0:T(8,128)(2,1)}, u32[]{:S(2)}) %copy-start.2) | copy-done | bytes 442392
  20.9 0.8 %fusion.12 = f32[4,8,8,2,128]{4,2,3,1,0:T(8,128)S(1)} fusion(bf16[3,3,3,64,128]{4,3,2,1,0:T(8,128)(2,1)S(1)} %bitcast.107, bf16[9,17,1,7,2,64]{5,3,4,1,0,2:T(8,128)(2,1)S(1)} %slice.740, bf16[9,17,1,8,4,64]{5,3,4,1,0,2:T(8,128)(2,1)S(1)} %copy.59, pred[8,2]{0,1:T(4,128)(4,1)S(1)} %copy-done.6), kind=kOutput, calls=%fused_computation.18 | convolution fusion | flops 229378048 | bytes 1605392 | tf_op jit(solution)/shard_map/conv_general_dilated | solution.py:151
  21.7 0.1 copy.60
  21.7 0.6 dynamic-slice_bitcast_fusion.1
  22.3 2.8 %fusion.10 = f32[3,3,3,32,128]{4,3,2,1,0:T(8,128)S(1)} fusion(bf16[9,17,17,32,1]{3,2,1,0,4:T(8,128)(2,1)S(1)} %get-tuple-element.189, bf16[4,8,8,128,1]{3,1,2,0,4:T(8,128)(2,1)S(1)} %bitcast.118, bf16[4,8,8]{2,1,0:T(8,128)(2,1)S(1)} %convert_element_type.65), kind=kOutput, calls=%fused_computation.11 | convolution fusion | flops 56754176 | bytes 674880 | tf_op jit(solution)/shard_map/conv_general_dilated | solution.py:134
  25.1 2.7 %fusion.8 = f32[3,3,3,32,128]{4,3,2,1,0:T(8,128)S(1)} fusion(bf16[9,17,17,32,1]{3,2,1,0,4:T(8,128)(2,1)S(1)} %get-tuple-element.190, bf16[4,8,8,128,1]{3,1,2,0,4:T(8,128)(2,1)S(1)} %bitcast.119, bf16[4,8,8]{2,1,0:T(8,128)(2,1)S(1)} %convert_element_type.65), kind=kOutput, calls=%fused_computation.9 | convolution fusion | flops 56754176 | bytes 674880 | tf_op jit(solution)/shard_map/conv_general_dilated | solution.py:134
  27.9 0.7 %fusion.24 = bf16[1,1,4,8,1024]{4,3,2,1,0:T(8,128)(2,1)} fusion(f32[4,8,1,16,128]{4,1,3,0,2:T(8,128)S(1)} %bitcast.115, f32[4,8,8]{1,2,0:T(8,128)S(1)} %copy.61), kind=kLoop, calls=%fused_computation.39 | loop fusion | flops 65536 | bytes 197632 | tf_op jit(solution)/shard_map/convert_element_type | solution.py:160
  28.7 1.0 %collective-permute-done.3 = f32[27,32,128]{2,1,0:T(8,128)S(1)} collective-permute-done((f32[27,32,128]{2,1,0:T(8,128)S(1)}, f32[27,32,128]{2,1,0:T(8,128)S(1)}, u32[]{:S(2)}, u32[]{:S(2)}) %collective-permute-start.3) | collective-permute-done | bytes 442400 | tf_op jit(solution)/shard_map/ppermute | solution.py:144
  29.8 0.1 pad_slice_fusion.1
  29.9 0.8 %pad.73 = f32[896,128]{1,0:T(8,128)} pad(f32[864,128]{1,0:T(8,128)S(1)} %bitcast.112, f32[]{:T(128)} %constant.523.clone.1), padding=0_32x0_0 | pad | bytes 901124 | tf_op jit(solution)/shard_map/jit(_pad)/pad | solution.py:81
  30.8 5.3 %all-to-all-start = ((f32[16,56,128]{2,1,0:T(8,128)}), f32[16,56,128]{2,1,0:T(8,128)S(1)}, u32[]{:S(2)}, u32[]{:S(2)}) async-start(f32[16,56,128]{2,1,0:T(8,128)} %bitcast.7), calls=%async_computation | async-start | bytes 917504 | tf_op jit(solution)/shard_map/all_to_all | solution.py:82
  36.2 0.6 fusion.33
  36.8 0.6 fusion.32
  37.5 0.6 fusion.31
  38.1 0.3 mul.84
  38.4 1.1 %mul.85 = f32[1,1,8,16,1024]{4,3,2,1,0:T(8,128)} reshape(f32[8,16,16,64]{3,2,1,0:T(8,128)S(1)} %mul.84) | data formatting | bytes 1048576 | tf_op jit(solution)/shard_map/mul | solution.py:184
  39.6 0.1 fusion.16
  39.7 0.7 fusion.30
  40.4 0.6 fusion.29
  41.0 0.6 fusion.28
  41.7 0.6 fusion.27
  42.3 7.9 %all-to-all-done = f32[16,56,128]{2,1,0:T(8,128)S(1)} async-done(((f32[16,56,128]{2,1,0:T(8,128)}), f32[16,56,128]{2,1,0:T(8,128)S(1)}, u32[]{:S(2)}, u32[]{:S(2)}) %all-to-all-start) | async-done | bytes 458784 | tf_op jit(solution)/shard_map/all_to_all | solution.py:82
  50.3 0.8 %broadcast_in_dim.54 = f32[16,56,128]{2,1,0:T(8,128)} broadcast(f32[56,128]{1,0:T(8,128)S(1)} %broadcast_multiply_fusion.1), dimensions={1,2} | broadcast | bytes 487424 | tf_op jit(solution)/shard_map/broadcast_in_dim | solution.py:88
  51.1 3.8 %all-to-all-start.1 = ((f32[16,56,128]{2,1,0:T(8,128)}), f32[16,56,128]{2,1,0:T(8,128)S(1)}, u32[]{:S(2)}, u32[]{:S(2)}) async-start(f32[16,56,128]{2,1,0:T(8,128)} %broadcast_in_dim.54), calls=%async_computation.1 | async-start | bytes 917504 | tf_op jit(solution)/shard_map/all_to_all | solution.py:89
  54.9 0.1 fusion.15
  55.0 0.6 fusion.26
  55.6 1.8 %convolution_bitcast_fusion = f32[4,2,8,2,8,2,64]{6,4,5,3,1,2,0:T(8,128)S(1)} fusion(bf16[2,2,2,2,2,2,64,128,1,1]{7,6,5,4,3,2,1,0,9,8:T(8,128)(2,1)S(1)} %bitcast.113, bf16[2,2,2,4,8,8,128,1,1,1]{6,5,4,3,2,1,0,9,8,7:T(8,128)(2,1)} %bitcast.25), kind=kOutput, calls=%fused_computation.8 | convolution fusion | flops 268435456 | bytes 2097152 | tf_op jit(solution)/shard_map/xyzabci,xpyqzroi->apbqcro/dot_general | solution.py:177
  57.4 0.6 copy.57
  58.0 0.9 %reshape.748 = f32[1,1,8,16,1024]{4,3,2,1,0:T(8,128)S(1)} reshape(f32[4,2,8,2,8,2,64]{6,5,4,3,2,1,0:T(2,128)S(1)} %copy.57) | data formatting | bytes 1048576 | tf_op jit(solution)/shard_map/reshape | solution.py:183
  58.9 0.1 copy-done.1
  59.1 0.8 %multiply_convert_fusion = bf16[1,1,8,16,1024]{4,3,2,1,0:T(8,128)(2,1)} fusion(f32[1,1,8,16,1024]{4,3,2,1,0:T(8,128)S(1)} %copy-done.1, f32[1,1,8,16,1024]{4,3,2,1,0:T(8,128)S(1)} %reshape.748, bf16[1,1,8,16,1024]{4,3,2,1,0:T(8,128)(2,1)S(1)} %copy-done.3), kind=kLoop, calls=%fused_computation.34 | loop fusion | flops 524288 | bytes 1572864 | tf_op jit(solution)/shard_map/convert_element_type | solution.py:187
  59.9 8.2 %all-to-all-done.1 = f32[16,56,128]{2,1,0:T(8,128)S(1)} async-done(((f32[16,56,128]{2,1,0:T(8,128)}), f32[16,56,128]{2,1,0:T(8,128)S(1)}, u32[]{:S(2)}, u32[]{:S(2)}) %all-to-all-start.1) | async-done | bytes 458784 | tf_op jit(solution)/shard_map/all_to_all | solution.py:89
  68.2 1.8 %collective-permute-done.4 = f32[27,32,128]{2,1,0:T(8,128)S(1)} collective-permute-done((f32[27,32,128]{2,1,0:T(8,128)S(1)}, f32[27,32,128]{2,1,0:T(8,128)S(1)}, u32[]{:S(2)}, u32[]{:S(2)}) %collective-permute-start.4) | collective-permute-done | bytes 442400 | tf_op jit(solution)/shard_map/ppermute | solution.py:92
  70.0 1.1 %fusion.20 = f32[27,2,32,128]{3,2,1,0:T(8,128)} fusion(s32[]{:T(128)S(6)} %select_n.112, f32[27,1,32,128]{3,2,1,0:T(8,128)S(1)} %bitcast.111, f32[27,1,32,128]{3,2,1,0:T(8,128)S(1)} %bitcast.116), kind=kLoop, calls=%fused_computation.31 | loop fusion | flops 442368 | bytes 1769476 | tf_op jit(solution)/shard_map/stack | solution.py:93
  (53 shorter events, 1.0 us)
Async XLA Ops:
  0.6 3.5 %copy-start.4 = (bf16[1,1,4,8,1024]{4,3,2,1,0:T(8,128)(2,1)S(1)}, bf16[1,1,4,8,1024]{4,3,2,1,0:T(8,128)(2,1)}, u32[]{:S(2)}) copy-start(bf16[1,1,4,8,1024]{4,3,2,1,0:T(8,128)(2,1)} %param.34) | copy-start | bytes 196612
  2.2 10.8 %copy-start.5 = (s32[1,1,2048]{2,1,0:T(1,128)S(1)}, s32[1,1,2048]{2,1,0:T(1,128)}, u32[]{:S(2)}) copy-start(s32[1,1,2048]{2,1,0:T(1,128)} %param.37) | copy-start | bytes 24580
  4.3 9.8 %collective-permute-start.2 = (bf16[1024]{0:T(1024)(128)(2,1)S(1)}, bf16[1024]{0:T(1024)(128)(2,1)S(1)}, u32[]{:S(2)}, u32[]{:S(2)}) collective-permute-start(bf16[1024]{0:T(1024)(128)(2,1)S(1)} %pad_maximum_fusion.5), channel_id=1, source_target_pairs={{24,0},{0,24},{25,1},{1,25},{26,2},{2,26},{27,3},{3,27},{28,4},{4,... | collective-permute-start | bytes 6152 | tf_op jit(solution)/shard_map/ppermute | solution.py:63
  11.6 5.1 %collective-permute-start = (bf16[12288]{0:T(1024)(128)(2,1)S(1)}, bf16[12288]{0:T(1024)(128)(2,1)S(1)}, u32[]{:S(2)}, u32[]{:S(2)}) collective-permute-start(bf16[12288]{0:T(1024)(128)(2,1)S(1)} %pad_maximum_fusion.3), channel_id=1, source_target_pairs={{8,0},{24,16},{0,8},{16,24},{9,1},{25,17},{1,9},{17,25},{10,2},{26... | collective-permute-start | bytes 73736 | tf_op jit(solution)/shard_map/ppermute | solution.py:63
  11.8 4.8 %collective-permute-start.1 = (bf16[12288]{0:T(1024)(128)(2,1)S(1)}, bf16[12288]{0:T(1024)(128)(2,1)S(1)}, u32[]{:S(2)}, u32[]{:S(2)}) collective-permute-start(bf16[12288]{0:T(1024)(128)(2,1)S(1)} %pad_maximum_fusion.4), channel_id=1, source_target_pairs={{16,0},{24,8},{0,16},{8,24},{17,1},{25,9},{1,17},{9,25},{18,2},{26... | collective-permute-start | bytes 73736 | tf_op jit(solution)/shard_map/ppermute | solution.py:63
  19.9 1.0 %copy-start.2 = (bf16[27,64,128]{2,1,0:T(8,128)(2,1)S(1)}, bf16[27,64,128]{2,1,0:T(8,128)(2,1)}, u32[]{:S(2)}) copy-start(bf16[27,64,128]{2,1,0:T(8,128)(2,1)} %param.38) | copy-start | bytes 1327108
  19.9 1.0 %copy-start.6 = (pred[8,2]{0,1:T(4,128)(4,1)S(1)}, pred[8,2]{0,1:T(4,128)(4,1)}, u32[]{:S(2)}) copy-start(pred[8,2]{0,1:T(4,128)(4,1)} %constant.545) | copy-start | bytes 52
  27.8 1.9 %collective-permute-start.3 = (f32[27,32,128]{2,1,0:T(8,128)S(1)}, f32[27,32,128]{2,1,0:T(8,128)S(1)}, u32[]{:S(2)}, u32[]{:S(2)}) collective-permute-start(f32[27,32,128]{2,1,0:T(8,128)S(1)} %bitcast.122), channel_id=1, source_target_pairs={{0,1},{1,0},{2,3},{3,2},{4,5},{5,4},{6,7},{7,6},{8,9},{9,8},{10,11... | collective-permute-start | bytes 1327112 | tf_op jit(solution)/shard_map/ppermute | solution.py:144
  30.8 19.4 %all-to-all-start = ((f32[16,56,128]{2,1,0:T(8,128)}), f32[16,56,128]{2,1,0:T(8,128)S(1)}, u32[]{:S(2)}, u32[]{:S(2)}) async-start(f32[16,56,128]{2,1,0:T(8,128)} %bitcast.7), calls=%async_computation | async-start | bytes 917504 | tf_op jit(solution)/shard_map/all_to_all | solution.py:82
  39.7 10.5 %copy-start = (bf16[4,4,4,64,128]{4,3,2,1,0:T(8,128)(2,1)}, bf16[4,4,4,64,128]{4,3,2,1,0:T(8,128)(2,1)S(1)}, u32[]{:S(2)}) copy-start(bf16[4,4,4,64,128]{4,3,2,1,0:T(8,128)(2,1)S(1)} %fusion.16) | copy-start | bytes 3145732
  50.2 4.6 %slice-start = ((bf16[4,4,4,64,128]{4,3,2,1,0:T(8,128)(2,1)}), bf16[4,4,3,64,128]{4,3,2,1,0:T(8,128)(2,1)S(1)}, s32[]{:S(2)}) async-start(bf16[4,4,4,64,128]{4,3,2,1,0:T(8,128)(2,1)} %copy-done), calls=%async_computation.2 | async-start | bytes 1572864 | tf_op jit(solution)/shard_map/jit(_roll_static)/slice | solution.py:71
  51.1 17.0 %all-to-all-start.1 = ((f32[16,56,128]{2,1,0:T(8,128)}), f32[16,56,128]{2,1,0:T(8,128)S(1)}, u32[]{:S(2)}, u32[]{:S(2)}) async-start(f32[16,56,128]{2,1,0:T(8,128)} %broadcast_in_dim.54), calls=%async_computation.1 | async-start | bytes 917504 | tf_op jit(solution)/shard_map/all_to_all | solution.py:89
  58.0 1.0 %copy-start.1 = (f32[1,1,8,16,1024]{4,3,2,1,0:T(8,128)S(1)}, f32[1,1,8,16,1024]{4,3,2,1,0:T(8,128)}, u32[]{:S(2)}) copy-start(f32[1,1,8,16,1024]{4,3,2,1,0:T(8,128)} %mul.85) | copy-start | bytes 1572868
  58.0 1.1 %copy-start.3 = (bf16[1,1,8,16,1024]{4,3,2,1,0:T(8,128)(2,1)S(1)}, bf16[1,1,8,16,1024]{4,3,2,1,0:T(8,128)(2,1)}, u32[]{:S(2)}) copy-start(bf16[1,1,8,16,1024]{4,3,2,1,0:T(8,128)(2,1)} %param.36) | copy-start | bytes 786436
  68.1 1.9 %collective-permute-start.4 = (f32[27,32,128]{2,1,0:T(8,128)S(1)}, f32[27,32,128]{2,1,0:T(8,128)S(1)}, u32[]{:S(2)}, u32[]{:S(2)}) collective-permute-start(f32[27,32,128]{2,1,0:T(8,128)S(1)} %bitcast.110), channel_id=1, source_target_pairs={{0,1},{1,0},{2,3},{3,2},{4,5},{5,4},{6,7},{7,6},{8,9},{9,8},{10,11... | collective-permute-start | bytes 1327112 | tf_op jit(solution)/shard_map/ppermute | solution.py:92

commit v11 on v9

--- a/solution.py
+++ b/solution.py
@@ -126,23 +126,20 @@
         widened = widened.at[target].set(halos[direction][1])
     window = tuple(2 * c + 1 for c in counts)
     trimmed = widened[: window[0], : window[1], : window[2]]
-    core = lax.axis_index("core")
-    share = channels_out // 2
-    mine = lax.dynamic_slice_in_dim(trimmed, core * share, share, axis=3)
-    theirs = lax.dynamic_slice_in_dim(trimmed, (1 - core) * share, share, axis=3)
-    cut = theirs.size
-    got = lax.ppermute(
-        jnp.concatenate([theirs.reshape(-1), masked.reshape(-1)]), "core", [(0, 1), (1, 0)]
-    )
-    grads = lax.conv_general_dilated(
-        jnp.stack([mine, got[:cut].reshape(theirs.shape)], axis=-1),
-        jnp.stack([masked, got[cut:].reshape(masked.shape)], axis=-1),
+    full = lax.conv_general_dilated(
+        trimmed[..., None],
+        masked[..., None],
         (1, 1, 1),
         "VALID",
         rhs_dilation=(2, 2, 2),
         dimension_numbers=("XYZNC", "XYZOI", "XYZNC"),
         preferred_element_type=jnp.float32,
-    ).reshape(27, share, channels_in)
+    ).reshape(27, channels_out, channels_in)
+    core = lax.axis_index("core")
+    share = channels_out // 2
+    theirs = lax.dynamic_slice_in_dim(full, (1 - core) * share, share, axis=1)
+    got = lax.ppermute(theirs, "core", [(0, 1), (1, 0)])
+    grads = lax.dynamic_slice_in_dim(full, core * share, share, axis=1) + got
     grads, masked_late, weight_late, skip, fine_keep = lax.optimization_barrier(
         (grads, masked, up_weight, skip, fine_keep)
     )

time: 78.9 us -> 71 us (0.90)
  local copies, waits for them, and re-layouts: 22.7 us -> 17.6 us
  matrix products: 10.4 us -> 5.37 us
  waiting for transfers between devices: 19.4 us -> 23.8 us
  other arithmetic: 6.99 us -> 5.24 us
    another operation x11 -> x7, local copies, waits for them, and re-layouts: 4.27 us -> 0.28 us  [the longest x3 3.89 us: body(): jnp.stack([mine, got[:cut].reshape(theirs.shape)], axis=-1)]
    conv_general_dilated x1, matrix products: 6.73 us -> 2.85 us  [body(): lax.conv_general_dilated(trimmed[..., None], masked[..., None], (1, 1, 1)...]
    all_to_all x1, waiting for transfers between devices: 8.02 us -> 11.6 us  [all_reduce(): lax.all_to_all(rows.reshape(devices, chunk, lanes), OTHERS, 0, 0, tiled=T...]
    unnamed x23 -> x24, local copies, waits for them, and re-layouts: 5.02 us -> 6.46 us
    conv_general_dilated x1, matrix products: 1.87 us -> 0.75 us  [body(): lax.conv_general_dilated(widened[None, :window[0], :window[1], :window[2]...]
    ppermute x1, waiting for transfers between devices: 0.01 us -> 1.04 us  [body(): got = lax.ppermute(theirs, 'core', [(0, 1), (1, 0)])]
    mul x3 -> x1, other arithmetic: 1.11 us -> 0.1 us  [body(): masked = coarse.reshape(size_x, size_y, size_z, channels_in) * coarse_keep]
    conv_general_dilated x3, local copies, waits for them, and re-layouts: 1.28 us -> 0.45 us  [body(): lax.conv_general_dilated(widened[None, :window[0], :window[1], :window[2]...]
  transfers between devices with their start and end apart: 7 -> 7, of which waited for: 4 -> 5; matrix products, arithmetic and copies ran while one was open for 24% -> 16% of each run, Pallas kernels for 0% -> 0%
where the time goes in v11:
time: 71 us; the launch traced here: 70.5 us
  waiting for transfers between devices  23.8 us (34%)
  local copies, waits for them, and re-layouts  17.6 us (25%)
  starting transfers between devices  17.3 us (24%)
  matrix products  5.37 us (8%)
  other arithmetic  5.24 us (7%)
  between operations  1.17 us (2%)
    all_to_all x1, waiting for transfers between devices, all_reduce(): lax.all_to_all(rows.reshape(devices, chunk, lanes), OTHERS, 0, 0, tiled=T...  11.6 us
    all_to_all x1, waiting for transfers between devices, all_spread(): half = lax.all_to_all(spread, OTHERS, 0, 0, tiled=True)  8.06 us
    ppermute x3, starting transfers between devices, halo_exchange(): got = lax.ppermute(packed, 'brick', both)  7.65 us
    unnamed x24, local copies, waits for them, and re-layouts  6.46 us
    all_to_all x1, starting transfers between devices, all_reduce(): lax.all_to_all(rows.reshape(devices, chunk, lanes), OTHERS, 0, 0, tiled=T...  5.75 us
    all_to_all x1, starting transfers between devices, all_spread(): half = lax.all_to_all(spread, OTHERS, 0, 0, tiled=True)  3.76 us
    conv_general_dilated x1, matrix products, body(): lax.conv_general_dilated(trimmed[..., None], masked[..., None], (1, 1, 1)...  2.85 us
    scatter x7, local copies, waits for them, and re-layouts, body(): widened = widened.at[target].set(halos[direction][1])  2.25 us
  transfers between devices with their start and end apart: 7, of which 5 were waited for; matrix products, arithmetic and copies ran while one was open for 16% of the time, Pallas kernels for 0%

profile of v11, /device:TPU:0, one launch (start us, length us, event | category | flops | bytes accessed | tf_op | source)
XLA Modules:
  0.0 70.5 jit_solution(11912828293079342636)
XLA Ops:
  0.7 1.3 %reshape.731 = bf16[8,16,16,64]{3,2,1,0:T(8,128)(2,1)S(1)} reshape(bf16[1,1,8,16,1024]{4,3,2,1,0:T(8,128)(2,1)} %param.39) | data formatting | bytes 524288 | tf_op jit(solution)/shard_map/reshape | solution.py:111
  2.0 0.7 %convert_reduce_fusion = bf16[2048]{0:T(1024)(128)(2,1)S(1)} fusion(s32[1,1,2048]{2,1,0:T(1,128)} %param.37), kind=kLoop, calls=%fused_computation.73 | loop fusion | flops 2048 | bytes 12288 | tf_op jit(solution)/shard_map/convert_element_type | solution.py:111
  2.8 0.1 convert_element_type.63
  2.9 0.3 broadcast_multiply_fusion
  3.2 0.1 select_n.109
  3.4 0.1 convert_element_type.65
  3.5 0.1 bitcast_multiply_fusion
  3.6 7.0 %collective-permute-start.2 = (bf16[1024]{0:T(1024)(128)(2,1)S(1)}, bf16[1024]{0:T(1024)(128)(2,1)S(1)}, u32[]{:S(2)}, u32[]{:S(2)}) collective-permute-start(bf16[1024]{0:T(1024)(128)(2,1)S(1)} %pad_maximum_fusion.5), channel_id=1, source_target_pairs={{24,0},{0,24},{25,1},{1,25},{26,2},{2,26},{27,3},{3,27},{28,4},{4,... | collective-permute-start | bytes 6152 | tf_op jit(solution)/shard_map/ppermute | solution.py:63
  10.6 0.1 select_n.103
  10.7 0.1 collective-permute-start.1
  10.8 0.2 fusion.23
  11.1 0.1 select_n.95
  11.2 0.6 collective-permute-start
  11.8 0.1 copy.58
  11.9 0.3 pad.72
  12.2 0.5 broadcast.299
  12.7 0.7 reduce.43
  13.4 0.7 %reshape.738 = s32[8,16,16,1]{2,1,0,3:T(8,128)} reshape(s32[2048]{0:T(1024)S(1)} %reduce.43) | data formatting | bytes 16384 | tf_op jit(solution)/shard_map/reshape | solution.py:110
  14.1 0.1 reshape.767
  14.2 1.3 %collective-permute-done.1 = bf16[12288]{0:T(1024)(128)(2,1)S(1)} collective-permute-done((bf16[12288]{0:T(1024)(128)(2,1)S(1)}, bf16[12288]{0:T(1024)(128)(2,1)S(1)}, u32[]{:S(2)}, u32[]{:S(2)}) %collective-permute-start.1) | collective-permute-done | bytes 24608 | tf_op jit(solution)/shard_map/ppermute | solution.py:63
  15.5 0.1 reshape.734
  15.6 0.1 reshape.766
  15.7 1.4 %scatter.46 = bf16[10,18,18,64]{3,2,1,0:T(8,128)(2,1)S(1)} dynamic-update-slice(bf16[10,18,18,64]{3,2,1,0:T(8,128)(2,1)S(1)} %pad.72, bf16[8,16,1,64]{3,2,1,0:T(2,128)(2,1)S(1)} %reshape.766, s32[]{:T(128)} %constant.517.clone.1, s32[]{:T(128)} %constant.517.clone.1, s32[]{:T(128)} %constant.516.clone.1, s32[]{:T(128)} %constant.516.clone.1) | dynamic-update-slice | bytes 32772 | tf_op jit(solution)/shard_map/scatter | solution.py:126
  17.1 0.2 scatter.49
  17.4 0.3 scatter.51
  17.8 0.2 scatter.55
  18.0 0.2 slice_bitcast_fusion
  18.3 0.2 pad.76
  18.5 0.2 copy.56
  18.8 0.2 slice.740
  18.9 0.8 %copy-done.1 = bf16[27,64,128]{2,1,0:T(8,128)(2,1)S(1)} copy-done((bf16[27,64,128]{2,1,0:T(8,128)(2,1)S(1)}, bf16[27,64,128]{2,1,0:T(8,128)(2,1)}, u32[]{:S(2)}) %copy-start.1) | copy-done | bytes 442392
  19.8 0.8 %fusion.10 = f32[4,8,8,2,128]{4,2,3,1,0:T(8,128)S(1)} fusion(bf16[3,3,3,64,128]{4,3,2,1,0:T(8,128)(2,1)S(1)} %bitcast.105, bf16[9,17,1,7,2,64]{5,3,4,1,0,2:T(8,128)(2,1)S(1)} %slice.740, bf16[9,17,1,8,4,64]{5,3,4,1,0,2:T(8,128)(2,1)S(1)} %copy.56, pred[8,2]{0,1:T(4,128)(4,1)S(1)} %copy-done.7), kind=kOutput, calls=%fused_computation.16 | convolution fusion | flops 229378048 | bytes 1605392 | tf_op jit(solution)/shard_map/conv_general_dilated | solution.py:148
  20.5 0.1 copy.57
  20.6 2.8 %fusion.8 = f32[3,3,3,64,128]{4,3,2,1,0:T(8,128)S(1)} fusion(bf16[9,17,17,64,1]{3,2,1,0,4:T(8,128)(2,1)S(1)} %get-tuple-element.188, bf16[4,8,8,128,1]{3,1,2,0,4:T(8,128)(2,1)S(1)} %bitcast.117, bf16[4,8,8]{2,1,0:T(8,128)(2,1)S(1)} %convert_element_type.65), kind=kOutput, calls=%fused_computation.9 | convolution fusion | flops 113377280 | bytes 1283712 | tf_op jit(solution)/shard_map/conv_general_dilated | solution.py:129
  23.6 0.7 %fusion.22 = bf16[1,1,4,8,1024]{4,3,2,1,0:T(8,128)(2,1)} fusion(f32[4,8,1,16,128]{4,1,3,0,2:T(8,128)S(1)} %bitcast.114, f32[4,8,8]{1,2,0:T(8,128)S(1)} %copy.58), kind=kLoop, calls=%fused_computation.37 | loop fusion | flops 65536 | bytes 197632 | tf_op jit(solution)/shard_map/convert_element_type | solution.py:157
  24.3 1.0 %collective-permute-done.3 = f32[27,32,128]{2,1,0:T(8,128)S(1)} collective-permute-done((f32[27,32,128]{2,1,0:T(8,128)S(1)}, f32[27,32,128]{2,1,0:T(8,128)S(1)}, u32[]{:S(2)}, u32[]{:S(2)}) %collective-permute-start.3) | collective-permute-done | bytes 442400 | tf_op jit(solution)/shard_map/ppermute | solution.py:141
  25.4 0.1 pad_slice_fusion.1
  25.8 0.6 fusion.31
  26.4 0.7 fusion.30
  27.1 0.6 fusion.29
  27.7 0.7 fusion.28
  28.4 0.1 fusion.14
  28.5 0.9 %pad.73 = f32[896,128]{1,0:T(8,128)} pad(f32[864,128]{1,0:T(8,128)S(1)} %bitcast.104, f32[]{:T(128)} %constant.523.clone.1), padding=0_32x0_0 | pad | bytes 901124 | tf_op jit(solution)/shard_map/jit(_pad)/pad | solution.py:81
  29.4 0.3 copy-done
  29.7 5.7 %all-to-all-start = ((f32[16,56,128]{2,1,0:T(8,128)}), f32[16,56,128]{2,1,0:T(8,128)S(1)}, u32[]{:S(2)}, u32[]{:S(2)}) async-start(f32[16,56,128]{2,1,0:T(8,128)} %bitcast.102), calls=%async_computation | async-start | bytes 917504 | tf_op jit(solution)/shard_map/all_to_all | solution.py:82
  35.4 0.6 fusion.27
  36.1 0.7 fusion.26
  36.7 0.6 fusion.25
  37.4 0.7 fusion.24
  38.0 11.6 %all-to-all-done = f32[16,56,128]{2,1,0:T(8,128)S(1)} async-done(((f32[16,56,128]{2,1,0:T(8,128)}), f32[16,56,128]{2,1,0:T(8,128)S(1)}, u32[]{:S(2)}, u32[]{:S(2)}) %all-to-all-start) | async-done | bytes 458784 | tf_op jit(solution)/shard_map/all_to_all | solution.py:82
  49.6 0.8 %broadcast_in_dim.49 = f32[16,56,128]{2,1,0:T(8,128)} broadcast(f32[56,128]{1,0:T(8,128)S(1)} %broadcast_multiply_fusion.1), dimensions={1,2} | broadcast | bytes 487424 | tf_op jit(solution)/shard_map/broadcast_in_dim | solution.py:88
  50.5 3.8 %all-to-all-start.1 = ((f32[16,56,128]{2,1,0:T(8,128)}), f32[16,56,128]{2,1,0:T(8,128)S(1)}, u32[]{:S(2)}, u32[]{:S(2)}) async-start(f32[16,56,128]{2,1,0:T(8,128)} %broadcast_in_dim.49), calls=%async_computation.1 | async-start | bytes 917504 | tf_op jit(solution)/shard_map/all_to_all | solution.py:89
  54.2 0.1 fusion.13
  54.3 1.8 %convolution_bitcast_fusion = f32[4,2,8,2,8,2,64]{6,4,5,3,1,2,0:T(8,128)S(1)} fusion(bf16[2,2,2,2,2,2,64,128,1,1]{7,6,5,4,3,2,1,0,9,8:T(8,128)(2,1)S(1)} %bitcast.110, bf16[2,2,2,4,8,8,128,1,1,1]{6,5,4,3,2,1,0,9,8,7:T(8,128)(2,1)} %bitcast.23), kind=kOutput, calls=%fused_computation.8 | convolution fusion | flops 268435456 | bytes 2097152 | tf_op jit(solution)/shard_map/xyzabci,xpyqzroi->apbqcro/dot_general | solution.py:174
  56.1 0.6 copy.54
  56.7 0.9 %reshape.744 = f32[1,1,8,16,1024]{4,3,2,1,0:T(8,128)S(1)} reshape(f32[4,2,8,2,8,2,64]{6,5,4,3,2,1,0:T(2,128)S(1)} %copy.54) | data formatting | bytes 1048576 | tf_op jit(solution)/shard_map/reshape | solution.py:180
  57.7 0.3 mul.84
  58.0 0.3 mul.85
  58.3 0.3 copy-done.3
  58.6 0.8 %multiply_convert_fusion = bf16[1,1,8,16,1024]{4,3,2,1,0:T(8,128)(2,1)} fusion(f32[1,1,8,16,1024]{4,3,2,1,0:T(8,128)S(1)} %mul.85, f32[1,1,8,16,1024]{4,3,2,1,0:T(8,128)S(1)} %reshape.744, bf16[1,1,8,16,1024]{4,3,2,1,0:T(8,128)(2,1)S(1)} %copy-done.3), kind=kLoop, calls=%fused_computation.32 | loop fusion | flops 524288 | bytes 1572864 | tf_op jit(solution)/shard_map/convert_element_type | solution.py:184
  59.4 8.1 %all-to-all-done.1 = f32[16,56,128]{2,1,0:T(8,128)S(1)} async-done(((f32[16,56,128]{2,1,0:T(8,128)}), f32[16,56,128]{2,1,0:T(8,128)S(1)}, u32[]{:S(2)}, u32[]{:S(2)}) %all-to-all-start.1) | async-done | bytes 458784 | tf_op jit(solution)/shard_map/all_to_all | solution.py:89
  67.5 0.1 collective-permute-start.4
  67.6 1.8 %collective-permute-done.4 = f32[27,32,128]{2,1,0:T(8,128)S(1)} collective-permute-done((f32[27,32,128]{2,1,0:T(8,128)S(1)}, f32[27,32,128]{2,1,0:T(8,128)S(1)}, u32[]{:S(2)}, u32[]{:S(2)}) %collective-permute-start.4) | collective-permute-done | bytes 442400 | tf_op jit(solution)/shard_map/ppermute | solution.py:92
  69.4 1.1 %fusion.18 = f32[27,2,32,128]{3,2,1,0:T(8,128)} fusion(s32[]{:T(128)S(6)} %select_n.112, f32[27,1,32,128]{3,2,1,0:T(8,128)S(1)} %bitcast.109, f32[27,1,32,128]{3,2,1,0:T(8,128)S(1)} %bitcast.115), kind=kLoop, calls=%fused_computation.27 | loop fusion | flops 442368 | bytes 1769476 | tf_op jit(solution)/shard_map/stack | solution.py:93
  (54 shorter events, 0.9 us)
Async XLA Ops:
  0.6 2.7 %copy-start.6 = (s32[1,1,256]{2,1,0:T(1,128)S(1)}, s32[1,1,256]{2,1,0:T(1,128)}, u32[]{:S(2)}) copy-start(s32[1,1,256]{2,1,0:T(1,128)} %param.35) | copy-start | bytes 3076
  0.6 2.8 %copy-start.4 = (bf16[1,1,4,8,1024]{4,3,2,1,0:T(8,128)(2,1)S(1)}, bf16[1,1,4,8,1024]{4,3,2,1,0:T(8,128)(2,1)}, u32[]{:S(2)}) copy-start(bf16[1,1,4,8,1024]{4,3,2,1,0:T(8,128)(2,1)} %param.34) | copy-start | bytes 196612
  3.2 9.5 %copy-start.5 = (s32[1,1,2048]{2,1,0:T(1,128)S(1)}, s32[1,1,2048]{2,1,0:T(1,128)}, u32[]{:S(2)}) copy-start(s32[1,1,2048]{2,1,0:T(1,128)} %param.37) | copy-start | bytes 24580
  3.6 10.5 %collective-permute-start.2 = (bf16[1024]{0:T(1024)(128)(2,1)S(1)}, bf16[1024]{0:T(1024)(128)(2,1)S(1)}, u32[]{:S(2)}, u32[]{:S(2)}) collective-permute-start(bf16[1024]{0:T(1024)(128)(2,1)S(1)} %pad_maximum_fusion.5), channel_id=1, source_target_pairs={{24,0},{0,24},{25,1},{1,25},{26,2},{2,26},{27,3},{3,27},{28,4},{4,... | collective-permute-start | bytes 6152 | tf_op jit(solution)/shard_map/ppermute | solution.py:63
  10.7 4.8 %collective-permute-start.1 = (bf16[12288]{0:T(1024)(128)(2,1)S(1)}, bf16[12288]{0:T(1024)(128)(2,1)S(1)}, u32[]{:S(2)}, u32[]{:S(2)}) collective-permute-start(bf16[12288]{0:T(1024)(128)(2,1)S(1)} %pad_maximum_fusion.4), channel_id=1, source_target_pairs={{16,0},{24,8},{0,16},{8,24},{17,1},{25,9},{1,17},{9,25},{18,2},{26... | collective-permute-start | bytes 73736 | tf_op jit(solution)/shard_map/ppermute | solution.py:63
  11.2 4.4 %collective-permute-start = (bf16[12288]{0:T(1024)(128)(2,1)S(1)}, bf16[12288]{0:T(1024)(128)(2,1)S(1)}, u32[]{:S(2)}, u32[]{:S(2)}) collective-permute-start(bf16[12288]{0:T(1024)(128)(2,1)S(1)} %pad_maximum_fusion.3), channel_id=1, source_target_pairs={{8,0},{24,16},{0,8},{16,24},{9,1},{25,17},{1,9},{17,25},{10,2},{26... | collective-permute-start | bytes 73736 | tf_op jit(solution)/shard_map/ppermute | solution.py:63
  18.8 1.0 %copy-start.1 = (bf16[27,64,128]{2,1,0:T(8,128)(2,1)S(1)}, bf16[27,64,128]{2,1,0:T(8,128)(2,1)}, u32[]{:S(2)}) copy-start(bf16[27,64,128]{2,1,0:T(8,128)(2,1)} %param.38) | copy-start | bytes 1327108
  18.8 1.0 %copy-start.7 = (pred[8,2]{0,1:T(4,128)(4,1)S(1)}, pred[8,2]{0,1:T(4,128)(4,1)}, u32[]{:S(2)}) copy-start(pred[8,2]{0,1:T(4,128)(4,1)} %constant.545) | copy-start | bytes 52
  23.5 1.9 %collective-permute-start.3 = (f32[27,32,128]{2,1,0:T(8,128)S(1)}, f32[27,32,128]{2,1,0:T(8,128)S(1)}, u32[]{:S(2)}, u32[]{:S(2)}) collective-permute-start(f32[27,32,128]{2,1,0:T(8,128)S(1)} %constant_dynamic-slice_fusion), channel_id=1, source_target_pairs={{0,1},{1,0},{2,3},{3,2},{4,5},{5,4},{6,7},{7,6},{8,9},{9,8},{10,11... | collective-permute-start | bytes 1327112 | tf_op jit(solution)/shard_map/ppermute | solution.py:141
  28.5 1.2 %copy-start = (bf16[4,4,4,64,128]{4,3,2,1,0:T(8,128)(2,1)}, bf16[4,4,4,64,128]{4,3,2,1,0:T(8,128)(2,1)S(1)}, u32[]{:S(2)}) copy-start(bf16[4,4,4,64,128]{4,3,2,1,0:T(8,128)(2,1)S(1)} %fusion.14) | copy-start | bytes 3145732
  29.7 19.9 %all-to-all-start = ((f32[16,56,128]{2,1,0:T(8,128)}), f32[16,56,128]{2,1,0:T(8,128)S(1)}, u32[]{:S(2)}, u32[]{:S(2)}) async-start(f32[16,56,128]{2,1,0:T(8,128)} %bitcast.102), calls=%async_computation | async-start | bytes 917504 | tf_op jit(solution)/shard_map/all_to_all | solution.py:82
  35.4 18.8 %slice-start = ((bf16[4,4,4,64,128]{4,3,2,1,0:T(8,128)(2,1)}), bf16[4,4,3,64,128]{4,3,2,1,0:T(8,128)(2,1)S(1)}, s32[]{:S(2)}) async-start(bf16[4,4,4,64,128]{4,3,2,1,0:T(8,128)(2,1)} %copy-done), calls=%async_computation.2 | async-start | bytes 1572864 | tf_op jit(solution)/shard_map/jit(_roll_static)/slice | solution.py:71
  50.5 17.0 %all-to-all-start.1 = ((f32[16,56,128]{2,1,0:T(8,128)}), f32[16,56,128]{2,1,0:T(8,128)S(1)}, u32[]{:S(2)}, u32[]{:S(2)}) async-start(f32[16,56,128]{2,1,0:T(8,128)} %broadcast_in_dim.49), calls=%async_computation.1 | async-start | bytes 917504 | tf_op jit(solution)/shard_map/all_to_all | solution.py:89
  56.7 1.0 %copy-start.2 = (s32[8,16,16,1]{2,1,0,3:T(8,128)S(1)}, s32[8,16,16,1]{2,1,0,3:T(8,128)}, u32[]{:S(2)}) copy-start(s32[8,16,16,1]{2,1,0,3:T(8,128)} %reshape.738) | copy-start | bytes 24580
  57.7 1.0 %copy-start.3 = (bf16[1,1,8,16,1024]{4,3,2,1,0:T(8,128)(2,1)S(1)}, bf16[1,1,8,16,1024]{4,3,2,1,0:T(8,128)(2,1)}, u32[]{:S(2)}) copy-start(bf16[1,1,8,16,1024]{4,3,2,1,0:T(8,128)(2,1)} %param.36) | copy-start | bytes 786436
  67.5 1.9 %collective-permute-start.4 = (f32[27,32,128]{2,1,0:T(8,128)S(1)}, f32[27,32,128]{2,1,0:T(8,128)S(1)}, u32[]{:S(2)}, u32[]{:S(2)}) collective-permute-start(f32[27,32,128]{2,1,0:T(8,128)S(1)} %bitcast.108), channel_id=1, source_target_pairs={{0,1},{1,0},{2,3},{3,2},{4,5},{5,4},{6,7},{7,6},{8,9},{9,8},{10,11... | collective-permute-start | bytes 1327112 | tf_op jit(solution)/shard_map/ppermute | solution.py:92

commit v12 on v11

--- a/solution.py
+++ b/solution.py
@@ -62,14 +62,6 @@
     )
     got = lax.ppermute(packed, "brick", both)
     return (got[:cut].reshape(masked_piece.shape), got[cut:].reshape(cot_piece.shape))
-
-
-def forward_weight(up_weight):
-    channels = up_weight.shape[1:]
-    taps = jnp.pad(up_weight.reshape((3, 3, 3) + channels), ((0, 1), (0, 1), (0, 1), (0, 0), (0, 0)))
-    for axis in range(3):
-        taps = jnp.roll(taps, -1, axis=axis)
-    return taps.reshape((2, 2, 2, 2, 2, 2) + channels)
 
 
 def all_reduce(half):
@@ -165,19 +157,16 @@
         )
         extended = extended.at[target].set(halos[direction][0])
 
-    shifted = jnp.stack(
-        [
-            extended[dx : dx + size_x, dy : dy + size_y, dz : dz + size_z]
-            for dx, dy, dz in OFFSETS
-        ]
-    ).reshape((2, 2, 2, size_x, size_y, size_z, channels_in))
-    parities = jnp.einsum(
-        "xyzabci,xpyqzroi->apbqcro",
-        shifted,
-        forward_weight(weight_late),
+    flipped = weight_late.reshape((3, 3, 3, channels_out, channels_in))[::-1, ::-1, ::-1]
+    up = lax.conv_general_dilated(
+        extended[None],
+        flipped,
+        (1, 1, 1),
+        ((1, 0), (1, 0), (1, 0)),
+        lhs_dilation=(2, 2, 2),
+        dimension_numbers=("NXYZC", "XYZOI", "NXYZC"),
         preferred_element_type=jnp.float32,
-    )
-    up = parities.reshape(fine_x, fine_y, fine_z, channels_out)
+    )[0]
     fine = fine_keep.astype(jnp.float32) * (
         skip.reshape(fine_x, fine_y, fine_z, channels_out).astype(jnp.float32) + up
     )

time: 71 us -> 66.4 us (0.935)
  local copies, waits for them, and re-layouts: 17.6 us -> 10.2 us
  matrix products: 5.37 us -> 9.83 us
  starting transfers between devices: 17.3 us -> 15.6 us
    conv_general_dilated x0 -> x1, matrix products: none -> 6.19 us  [body(): lax.conv_general_dilated(extended[None], flipped, (1, 1, 1), ((1, 0), (1,...]
    unnamed x24 -> x14, local copies, waits for them, and re-layouts: 6.46 us -> 1.69 us
    all_to_all x1, waiting for transfers between devices: 8.06 us -> 4.65 us  [all_spread(): half = lax.all_to_all(spread, OTHERS, 0, 0, tiled=True)]
    all_to_all x1, waiting for transfers between devices: 11.6 us -> 14.1 us  [all_reduce(): lax.all_to_all(rows.reshape(devices, chunk, lanes), OTHERS, 0, 0, tiled=T...]
    ppermute x3, waiting for transfers between devices: 1.34 us -> 3.71 us  [halo_exchange(): got = lax.ppermute(packed, 'brick', both)]
    all_to_all x1, starting transfers between devices: 5.75 us -> 3.83 us  [all_reduce(): lax.all_to_all(rows.reshape(devices, chunk, lanes), OTHERS, 0, 0, tiled=T...]
    dot_general x1 -> x0, matrix products: 1.77 us -> none  [body(): jnp.einsum('xyzabci,xpyqzroi->apbqcro', shifted, forward_weight(weight_la...]
    ppermute x1, waiting for transfers between devices: 1.04 us -> 0.01 us  [body(): got = lax.ppermute(theirs, 'core', [(0, 1), (1, 0)])]
  transfers between devices with their start and end apart: 7 -> 7, of which waited for: 5 -> 4; matrix products, arithmetic and copies ran while one was open for 16% -> 19% of each run, Pallas kernels for 0% -> 0%
where the time goes in v12:
time: 66.4 us; the launch traced here: 65.9 us
  waiting for transfers between devices  24.2 us (36%)
  starting transfers between devices  15.6 us (23%)
  local copies, waits for them, and re-layouts  10.2 us (15%)
  matrix products  9.83 us (15%)
  other arithmetic  4.98 us (8%)
  between operations  1.09 us (2%)
    all_to_all x1, waiting for transfers between devices, all_reduce(): lax.all_to_all(rows.reshape(devices, chunk, lanes), OTHERS, 0, 0, tiled=T...  14.1 us
    ppermute x3, starting transfers between devices, halo_exchange(): got = lax.ppermute(packed, 'brick', both)  7.66 us
    conv_general_dilated x1, matrix products, body(): lax.conv_general_dilated(extended[None], flipped, (1, 1, 1), ((1, 0), (1,...  6.19 us
    all_to_all x1, waiting for transfers between devices, all_spread(): half = lax.all_to_all(spread, OTHERS, 0, 0, tiled=True)  4.65 us
    all_to_all x1, starting transfers between devices, all_spread(): half = lax.all_to_all(spread, OTHERS, 0, 0, tiled=True)  3.97 us
    all_to_all x1, starting transfers between devices, all_reduce(): lax.all_to_all(rows.reshape(devices, chunk, lanes), OTHERS, 0, 0, tiled=T...  3.83 us
    ppermute x3, waiting for transfers between devices, halo_exchange(): got = lax.ppermute(packed, 'brick', both)  3.71 us
    conv_general_dilated x1, matrix products, body(): lax.conv_general_dilated(trimmed[..., None], masked[..., None], (1, 1, 1)...  2.88 us
  transfers between devices with their start and end apart: 7, of which 4 were waited for; matrix products, arithmetic and copies ran while one was open for 19% of the time, Pallas kernels for 0%

profile of v12, /device:TPU:0, one launch (start us, length us, event | category | flops | bytes accessed | tf_op | source)
XLA Modules:
  0.0 65.9 jit_solution(15852384974589024434)
XLA Ops:
  0.6 0.0 copy-start
  0.7 1.4 %reshape.739 = bf16[8,16,16,64]{3,2,1,0:T(8,128)(2,1)S(1)} reshape(bf16[1,1,8,16,1024]{4,3,2,1,0:T(8,128)(2,1)} %param.39) | data formatting | bytes 524288 | tf_op jit(solution)/shard_map/reshape | solution.py:103
  2.1 0.7 %convert_reduce_fusion = bf16[2048]{0:T(1024)(128)(2,1)S(1)} fusion(s32[1,1,2048]{2,1,0:T(1,128)} %param.37), kind=kLoop, calls=%fused_computation.47 | loop fusion | flops 2048 | bytes 12288 | tf_op jit(solution)/shard_map/convert_element_type | solution.py:103
  2.8 0.1 convert_element_type.61
  2.9 0.3 broadcast_multiply_fusion
  3.2 0.0 copy-start.3
  3.2 0.2 fusion.19
  3.5 0.1 select_n.95
  3.6 0.0 copy-done.4
  3.6 0.1 convert_element_type.63
  3.7 0.1 bitcast_multiply_fusion
  3.8 0.1 fusion.21
  3.9 3.1 %collective-permute-start = (bf16[12288]{0:T(1024)(128)(2,1)S(1)}, bf16[12288]{0:T(1024)(128)(2,1)S(1)}, u32[]{:S(2)}, u32[]{:S(2)}) collective-permute-start(bf16[12288]{0:T(1024)(128)(2,1)S(1)} %pad_maximum_fusion), channel_id=1, source_target_pairs={{8,0},{24,16},{0,8},{16,24},{9,1},{25,17},{1,9},{17,25},{10,2},{26... | collective-permute-start | bytes 73736 | tf_op jit(solution)/shard_map/ppermute | solution.py:63
  7.0 0.1 select_n.103
  7.1 2.7 %collective-permute-start.1 = (bf16[12288]{0:T(1024)(128)(2,1)S(1)}, bf16[12288]{0:T(1024)(128)(2,1)S(1)}, u32[]{:S(2)}, u32[]{:S(2)}) collective-permute-start(bf16[12288]{0:T(1024)(128)(2,1)S(1)} %pad_maximum_fusion.1), channel_id=1, source_target_pairs={{16,0},{24,8},{0,16},{8,24},{17,1},{25,9},{1,17},{9,25},{18,2},{26... | collective-permute-start | bytes 73736 | tf_op jit(solution)/shard_map/ppermute | solution.py:63
  9.8 0.1 select_n.109
  9.9 1.9 %collective-permute-start.2 = (bf16[1024]{0:T(1024)(128)(2,1)S(1)}, bf16[1024]{0:T(1024)(128)(2,1)S(1)}, u32[]{:S(2)}, u32[]{:S(2)}) collective-permute-start(bf16[1024]{0:T(1024)(128)(2,1)S(1)} %pad_maximum_fusion.2), channel_id=1, source_target_pairs={{24,0},{0,24},{25,1},{1,25},{26,2},{2,26},{27,3},{3,27},{28,4},{4,... | collective-permute-start | bytes 6152 | tf_op jit(solution)/shard_map/ppermute | solution.py:63
  11.8 0.1 copy.36
  11.9 0.3 pad.68
  12.2 0.5 broadcast.291
  12.7 0.0 copy-done.3
  12.7 0.7 %reduce.47 = s32[2048]{0:T(1024)S(1)} reduce(s32[1,1,2048]{2,1,0:T(1,128)S(1)} %copy-done.3, s32[]{:T(128)} %broadcast.291), dimensions={0,1}, to_apply=%param.37.reduce_sub_computation.3 | reduce | bytes 16388 | tf_op args[3]
  13.4 0.1 reshape.746
  13.5 3.7 %collective-permute-done.2 = bf16[1024]{0:T(1024)(128)(2,1)S(1)} collective-permute-done((bf16[1024]{0:T(1024)(128)(2,1)S(1)}, bf16[1024]{0:T(1024)(128)(2,1)S(1)}, u32[]{:S(2)}, u32[]{:S(2)}) %collective-permute-start.2) | collective-permute-done | bytes 2080 | tf_op jit(solution)/shard_map/ppermute | solution.py:63
  17.2 0.1 reshape.769
  17.3 0.0 collective-permute-done
  17.3 0.1 reshape.768
  17.4 0.0 collective-permute-done.1
  17.4 0.1 reshape.742
  17.5 1.4 %scatter.46 = bf16[10,18,18,64]{3,2,1,0:T(8,128)(2,1)S(1)} dynamic-update-slice(bf16[10,18,18,64]{3,2,1,0:T(8,128)(2,1)S(1)} %pad.68, bf16[8,16,1,64]{3,2,1,0:T(2,128)(2,1)S(1)} %reshape.768, s32[]{:T(128)} %constant.524.clone.1, s32[]{:T(128)} %constant.524.clone.1, s32[]{:T(128)} %constant.523.clone.1, s32[]{:T(128)} %constant.523.clone.1) | dynamic-update-slice | bytes 32772 | tf_op jit(solution)/shard_map/scatter | solution.py:118
  18.9 0.2 scatter.49
  19.2 0.3 scatter.51
  19.5 0.1 scatter.54
  19.6 0.2 scatter.55
  19.8 0.2 slice_bitcast_fusion
  20.1 2.9 %fusion.8 = f32[3,3,3,64,128]{4,3,2,1,0:T(8,128)S(1)} fusion(bf16[9,17,17,64,1]{3,2,1,0,4:T(8,128)(2,1)S(1)} %get-tuple-element.188, bf16[4,8,8,128,1]{3,1,2,0,4:T(8,128)(2,1)S(1)} %bitcast.73, bf16[4,8,8]{2,1,0:T(8,128)(2,1)S(1)} %convert_element_type.63), kind=kOutput, calls=%fused_computation.9 | convolution fusion | flops 113377280 | bytes 1283712 | tf_op jit(solution)/shard_map/conv_general_dilated | solution.py:121
  23.0 0.1 collective-permute-start.3
  23.1 0.2 pad.71
  23.3 0.2 copy.34
  23.5 0.0 copy-start.5
  23.6 0.2 slice.667
  23.7 0.5 copy-done.5
  24.2 0.8 %fusion.10 = f32[4,8,8,2,128]{4,2,3,1,0:T(8,128)S(1)} fusion(bf16[3,3,3,64,128]{4,3,2,1,0:T(8,128)(2,1)S(1)} %bitcast.61, bf16[9,17,1,7,2,64]{5,3,4,1,0,2:T(8,128)(2,1)S(1)} %slice.667, bf16[9,17,1,8,4,64]{5,3,4,1,0,2:T(8,128)(2,1)S(1)} %copy.34, pred[8,2]{0,1:T(4,128)(4,1)S(1)} %copy-done.5), kind=kOutput, calls=%fused_computation.14 | convolution fusion | flops 229378048 | bytes 1605392 | tf_op jit(solution)/shard_map/conv_general_dilated | solution.py:140
  25.0 0.1 copy.35
  25.1 0.7 %fusion.18 = bf16[1,1,4,8,1024]{4,3,2,1,0:T(8,128)(2,1)} fusion(f32[4,8,1,16,128]{4,1,3,0,2:T(8,128)S(1)} %bitcast.70, f32[4,8,8]{1,2,0:T(8,128)S(1)} %copy.36), kind=kLoop, calls=%fused_computation.27 | loop fusion | flops 65536 | bytes 197632 | tf_op jit(solution)/shard_map/convert_element_type | solution.py:149
  25.8 0.0 collective-permute-done.3
  25.8 0.1 dynamic-slice_add_fusion
  25.9 0.8 %pad.69 = f32[896,128]{1,0:T(8,128)} pad(f32[864,128]{1,0:T(8,128)S(1)} %bitcast.64, f32[]{:T(128)} %constant.530.clone.1), padding=0_32x0_0 | pad | bytes 901124 | tf_op jit(solution)/shard_map/jit(_pad)/pad | solution.py:73
  26.7 3.8 %all-to-all-start = ((f32[16,56,128]{2,1,0:T(8,128)}), f32[16,56,128]{2,1,0:T(8,128)S(1)}, u32[]{:S(2)}, u32[]{:S(2)}) async-start(f32[16,56,128]{2,1,0:T(8,128)} %bitcast.5), calls=%async_computation | async-start | bytes 917504 | tf_op jit(solution)/shard_map/all_to_all | solution.py:74
  30.5 0.1 copy.37
  30.8 14.1 %all-to-all-done = f32[16,56,128]{2,1,0:T(8,128)S(1)} async-done(((f32[16,56,128]{2,1,0:T(8,128)}), f32[16,56,128]{2,1,0:T(8,128)S(1)}, u32[]{:S(2)}, u32[]{:S(2)}) %all-to-all-start) | async-done | bytes 458784 | tf_op jit(solution)/shard_map/all_to_all | solution.py:74
  44.9 0.8 %broadcast_in_dim.60 = f32[16,56,128]{2,1,0:T(8,128)} broadcast(f32[56,128]{1,0:T(8,128)S(1)} %broadcast_multiply_fusion.1), dimensions={1,2} | broadcast | bytes 487424 | tf_op jit(solution)/shard_map/broadcast_in_dim | solution.py:80
  45.7 4.0 %all-to-all-start.1 = ((f32[16,56,128]{2,1,0:T(8,128)}), f32[16,56,128]{2,1,0:T(8,128)S(1)}, u32[]{:S(2)}, u32[]{:S(2)}) async-start(f32[16,56,128]{2,1,0:T(8,128)} %broadcast_in_dim.60), calls=%async_computation.1 | async-start | bytes 917504 | tf_op jit(solution)/shard_map/all_to_all | solution.py:81
  49.7 6.2 %convolution_reduce_fusion = f32[8,16,16,64]{3,2,1,0:T(8,128)S(1)} fusion(bf16[3,3,3,64,128]{4,3,2,1,0:T(8,128)(2,1)S(1)} %bitcast.60, bf16[1,5,9,9,128]{4,1,3,2,0:T(8,128)(2,1)S(1)} %constant_dynamic-update-slice_fusion), kind=kOutput, calls=%fused_computation.8 | convolution fusion | flops 113246208 | bytes 1070336 | tf_op jit(solution)/shard_map/conv_general_dilated | solution.py:161
  55.9 0.3 mul.84
  56.2 0.3 mul.85
  56.5 0.0 copy-start.1
  56.5 0.3 squeeze.6
  56.9 0.6 copy-done.1
  57.5 0.8 %multiply_convert_fusion = bf16[1,1,8,16,1024]{4,3,2,1,0:T(8,128)(2,1)} fusion(f32[1,1,8,16,1024]{4,3,2,1,0:T(8,128)S(1)} %mul.85, f32[1,1,8,16,1024]{4,3,2,1,0:T(8,128)S(1)} %squeeze.6, bf16[1,1,8,16,1024]{4,3,2,1,0:T(8,128)(2,1)S(1)} %copy-done.1), kind=kLoop, calls=%fused_computation.20 | loop fusion | flops 524288 | bytes 1572864 | tf_op jit(solution)/shard_map/convert_element_type | solution.py:173
  58.3 4.6 %all-to-all-done.1 = f32[16,56,128]{2,1,0:T(8,128)S(1)} async-done(((f32[16,56,128]{2,1,0:T(8,128)}), f32[16,56,128]{2,1,0:T(8,128)S(1)}, u32[]{:S(2)}, u32[]{:S(2)}) %all-to-all-start.1) | async-done | bytes 458784 | tf_op jit(solution)/shard_map/all_to_all | solution.py:81
  63.0 0.1 collective-permute-start.4
  63.0 1.8 %collective-permute-done.4 = f32[27,32,128]{2,1,0:T(8,128)S(1)} collective-permute-done((f32[27,32,128]{2,1,0:T(8,128)S(1)}, f32[27,32,128]{2,1,0:T(8,128)S(1)}, u32[]{:S(2)}, u32[]{:S(2)}) %collective-permute-start.4) | collective-permute-done | bytes 442400 | tf_op jit(solution)/shard_map/ppermute | solution.py:84
  64.8 1.1 %fusion.15 = f32[27,2,32,128]{3,2,1,0:T(8,128)} fusion(s32[]{:T(128)S(6)} %select_n.112, f32[27,1,32,128]{3,2,1,0:T(8,128)S(1)} %bitcast.66, f32[27,1,32,128]{3,2,1,0:T(8,128)S(1)} %bitcast.71), kind=kLoop, calls=%fused_computation.17 | loop fusion | flops 442368 | bytes 1769476 | tf_op jit(solution)/shard_map/stack | solution.py:85
  (36 shorter events, 0.5 us)
Async XLA Ops:
  0.6 23.1 %copy-start = (bf16[27,64,128]{2,1,0:T(8,128)(2,1)S(1)}, bf16[27,64,128]{2,1,0:T(8,128)(2,1)}, u32[]{:S(2)}) copy-start(bf16[27,64,128]{2,1,0:T(8,128)(2,1)} %param.38) | copy-start | bytes 1327108
  0.6 2.9 %copy-start.4 = (s32[1,1,256]{2,1,0:T(1,128)S(1)}, s32[1,1,256]{2,1,0:T(1,128)}, u32[]{:S(2)}) copy-start(s32[1,1,256]{2,1,0:T(1,128)} %param.35) | copy-start | bytes 3076
  0.7 3.0 %copy-start.2 = (bf16[1,1,4,8,1024]{4,3,2,1,0:T(8,128)(2,1)S(1)}, bf16[1,1,4,8,1024]{4,3,2,1,0:T(8,128)(2,1)}, u32[]{:S(2)}) copy-start(bf16[1,1,4,8,1024]{4,3,2,1,0:T(8,128)(2,1)} %param.34) | copy-start | bytes 196612
  3.2 9.5 %copy-start.3 = (s32[1,1,2048]{2,1,0:T(1,128)S(1)}, s32[1,1,2048]{2,1,0:T(1,128)}, u32[]{:S(2)}) copy-start(s32[1,1,2048]{2,1,0:T(1,128)} %param.37) | copy-start | bytes 24580
  3.9 13.4 %collective-permute-start = (bf16[12288]{0:T(1024)(128)(2,1)S(1)}, bf16[12288]{0:T(1024)(128)(2,1)S(1)}, u32[]{:S(2)}, u32[]{:S(2)}) collective-permute-start(bf16[12288]{0:T(1024)(128)(2,1)S(1)} %pad_maximum_fusion), channel_id=1, source_target_pairs={{8,0},{24,16},{0,8},{16,24},{9,1},{25,17},{1,9},{17,25},{10,2},{26... | collective-permute-start | bytes 73736 | tf_op jit(solution)/shard_map/ppermute | solution.py:63
  7.1 10.3 %collective-permute-start.1 = (bf16[12288]{0:T(1024)(128)(2,1)S(1)}, bf16[12288]{0:T(1024)(128)(2,1)S(1)}, u32[]{:S(2)}, u32[]{:S(2)}) collective-permute-start(bf16[12288]{0:T(1024)(128)(2,1)S(1)} %pad_maximum_fusion.1), channel_id=1, source_target_pairs={{16,0},{24,8},{0,16},{8,24},{17,1},{25,9},{1,17},{9,25},{18,2},{26... | collective-permute-start | bytes 73736 | tf_op jit(solution)/shard_map/ppermute | solution.py:63
  9.9 7.3 %collective-permute-start.2 = (bf16[1024]{0:T(1024)(128)(2,1)S(1)}, bf16[1024]{0:T(1024)(128)(2,1)S(1)}, u32[]{:S(2)}, u32[]{:S(2)}) collective-permute-start(bf16[1024]{0:T(1024)(128)(2,1)S(1)} %pad_maximum_fusion.2), channel_id=1, source_target_pairs={{24,0},{0,24},{25,1},{1,25},{26,2},{2,26},{27,3},{3,27},{28,4},{4,... | collective-permute-start | bytes 6152 | tf_op jit(solution)/shard_map/ppermute | solution.py:63
  23.0 2.8 %collective-permute-start.3 = (f32[27,32,128]{2,1,0:T(8,128)S(1)}, f32[27,32,128]{2,1,0:T(8,128)S(1)}, u32[]{:S(2)}, u32[]{:S(2)}) collective-permute-start(f32[27,32,128]{2,1,0:T(8,128)S(1)} %constant_dynamic-slice_fusion), channel_id=1, source_target_pairs={{0,1},{1,0},{2,3},{3,2},{4,5},{5,4},{6,7},{7,6},{8,9},{9,8},{10,11... | collective-permute-start | bytes 1327112 | tf_op jit(solution)/shard_map/ppermute | solution.py:133
  23.5 0.7 copy-start.5
  26.7 18.2 %all-to-all-start = ((f32[16,56,128]{2,1,0:T(8,128)}), f32[16,56,128]{2,1,0:T(8,128)S(1)}, u32[]{:S(2)}, u32[]{:S(2)}) async-start(f32[16,56,128]{2,1,0:T(8,128)} %bitcast.5), calls=%async_computation | async-start | bytes 917504 | tf_op jit(solution)/shard_map/all_to_all | solution.py:74
  45.7 17.2 %all-to-all-start.1 = ((f32[16,56,128]{2,1,0:T(8,128)}), f32[16,56,128]{2,1,0:T(8,128)S(1)}, u32[]{:S(2)}, u32[]{:S(2)}) async-start(f32[16,56,128]{2,1,0:T(8,128)} %broadcast_in_dim.60), calls=%async_computation.1 | async-start | bytes 917504 | tf_op jit(solution)/shard_map/all_to_all | solution.py:81
  56.5 1.0 %copy-start.1 = (bf16[1,1,8,16,1024]{4,3,2,1,0:T(8,128)(2,1)S(1)}, bf16[1,1,8,16,1024]{4,3,2,1,0:T(8,128)(2,1)}, u32[]{:S(2)}) copy-start(bf16[1,1,8,16,1024]{4,3,2,1,0:T(8,128)(2,1)} %param.36) | copy-start | bytes 786436
  63.0 1.9 %collective-permute-start.4 = (f32[27,32,128]{2,1,0:T(8,128)S(1)}, f32[27,32,128]{2,1,0:T(8,128)S(1)}, u32[]{:S(2)}, u32[]{:S(2)}) collective-permute-start(f32[27,32,128]{2,1,0:T(8,128)S(1)} %bitcast.65), channel_id=1, source_target_pairs={{0,1},{1,0},{2,3},{3,2},{4,5},{5,4},{6,7},{7,6},{8,9},{9,8},{10,11... | collective-permute-start | bytes 1327112 | tf_op jit(solution)/shard_map/ppermute | solution.py:84

commit v13 on v12

--- a/solution.py
+++ b/solution.py
@@ -82,8 +82,10 @@
     half, riders = lax.optimization_barrier((half, riders))
     half = half.reshape(-1, reduced.shape[-1])[:size].reshape(shape)
     other = lax.ppermute(half, "core", [(0, 1), (1, 0)])
-    three = jnp.stack([half, other, half], axis=1)
-    whole = lax.dynamic_slice_in_dim(three, lax.axis_index("core"), 2, axis=1)
+    core = lax.axis_index("core")
+    whole = jnp.zeros((shape[0], 2) + shape[1:], half.dtype)
+    whole = lax.dynamic_update_index_in_dim(whole, half, core, 1)
+    whole = lax.dynamic_update_index_in_dim(whole, other, 1 - core, 1)
     return whole.reshape(shape[0], 2 * shape[1], shape[2]), riders
 
 
@@ -109,17 +111,15 @@
         masked_piece = masked[tuple(slice(0, 1) if flag else slice(None) for flag in direction)]
         cot_piece = cotangent[tuple(slice(-1, None) if flag else slice(None) for flag in direction)]
         halos[direction] = halo_exchange(masked_piece, cot_piece, regions, direction)
-    widened = jnp.pad(cotangent, ((1, 1), (1, 1), (1, 1), (0, 0)))
+    widened = jnp.pad(cotangent, ((1, 0), (1, 0), (1, 0), (0, 0)))
     for direction in DIRECTIONS:
         target = tuple(
             slice(0, 1) if flag else slice(1, 1 + cotangent.shape[a])
             for a, flag in enumerate(direction)
         )
         widened = widened.at[target].set(halos[direction][1])
-    window = tuple(2 * c + 1 for c in counts)
-    trimmed = widened[: window[0], : window[1], : window[2]]
     full = lax.conv_general_dilated(
-        trimmed[..., None],
+        widened[..., None],
         masked[..., None],
         (1, 1, 1),
         "VALID",
@@ -138,7 +138,7 @@
     reduced, plan = all_reduce(grads)
 
     back = lax.conv_general_dilated(
-        widened[None, : window[0], : window[1], : window[2]],
+        widened[None],
         up_weight.reshape((3, 3, 3, channels_out, channels_in)),
         (2, 2, 2),
         "VALID",

time: 66.4 us -> 65.8 us (level)
  other arithmetic: 4.98 us -> 3.87 us
  local copies, waits for them, and re-layouts: 10.2 us -> 11 us
    another operation x1 -> x0, other arithmetic: 1.12 us -> none  [all_spread(): three = jnp.stack([half, other, half], axis=1)]
    unnamed x14 -> x16, local copies, waits for them, and re-layouts: 1.69 us -> 2.6 us
where the time goes in v13:
time: 65.8 us; the launch traced here: 65.4 us
  waiting for transfers between devices  24.1 us (37%)
  starting transfers between devices  15.6 us (24%)
  local copies, waits for them, and re-layouts  11 us (17%)
  matrix products  9.65 us (15%)
  other arithmetic  3.87 us (6%)
  between operations  1.12 us (2%)
    all_to_all x1, waiting for transfers between devices, all_reduce(): lax.all_to_all(rows.reshape(devices, chunk, lanes), OTHERS, 0, 0, tiled=T...  14.1 us
    ppermute x3, starting transfers between devices, halo_exchange(): got = lax.ppermute(packed, 'brick', both)  7.66 us
    conv_general_dilated x1, matrix products, body(): lax.conv_general_dilated(extended[None], flipped, (1, 1, 1), ((1, 0), (1,...  6.19 us
    all_to_all x1, waiting for transfers between devices, all_spread(): half = lax.all_to_all(spread, OTHERS, 0, 0, tiled=True)  4.65 us
    all_to_all x1, starting transfers between devices, all_spread(): half = lax.all_to_all(spread, OTHERS, 0, 0, tiled=True)  3.97 us
    all_to_all x1, starting transfers between devices, all_reduce(): lax.all_to_all(rows.reshape(devices, chunk, lanes), OTHERS, 0, 0, tiled=T...  3.83 us
    ppermute x3, waiting for transfers between devices, halo_exchange(): got = lax.ppermute(packed, 'brick', both)  3.74 us
    conv_general_dilated x1, matrix products, body(): lax.conv_general_dilated(widened[..., None], masked[..., None], (1, 1, 1)...  2.7 us
  transfers between devices with their start and end apart: 7, of which 4 were waited for; matrix products, arithmetic and copies ran while one was open for 19% of the time, Pallas kernels for 0%

profile of v13, /device:TPU:0, one launch (start us, length us, event | category | flops | bytes accessed | tf_op | source)
XLA Modules:
  0.0 65.4 jit_solution(7698761881832440110)
XLA Ops:
  0.6 0.0 copy-start
  0.7 1.4 %reshape.740 = bf16[8,16,16,64]{3,2,1,0:T(8,128)(2,1)S(1)} reshape(bf16[1,1,8,16,1024]{4,3,2,1,0:T(8,128)(2,1)} %param.39) | data formatting | bytes 524288 | tf_op jit(solution)/shard_map/reshape | solution.py:105
  2.1 0.7 %convert_reduce_fusion = bf16[2048]{0:T(1024)(128)(2,1)S(1)} fusion(s32[1,1,2048]{2,1,0:T(1,128)} %param.37), kind=kLoop, calls=%fused_computation.41 | loop fusion | flops 2048 | bytes 12288 | tf_op jit(solution)/shard_map/convert_element_type | solution.py:105
  2.8 0.1 convert_element_type.61
  2.9 0.3 broadcast_multiply_fusion
  3.2 0.0 copy-start.4
  3.2 0.2 fusion.17
  3.5 0.1 select_n.99
  3.6 0.0 copy-done.5
  3.6 0.1 convert_element_type.63
  3.7 0.1 bitcast_multiply_fusion
  3.8 0.1 fusion.19
  3.9 3.1 %collective-permute-start = (bf16[12288]{0:T(1024)(128)(2,1)S(1)}, bf16[12288]{0:T(1024)(128)(2,1)S(1)}, u32[]{:S(2)}, u32[]{:S(2)}) collective-permute-start(bf16[12288]{0:T(1024)(128)(2,1)S(1)} %pad_maximum_fusion), channel_id=1, source_target_pairs={{8,0},{24,16},{0,8},{16,24},{9,1},{25,17},{1,9},{17,25},{10,2},{26... | collective-permute-start | bytes 73736 | tf_op jit(solution)/shard_map/ppermute | solution.py:63
  7.0 0.1 select_n.107
  7.1 2.7 %collective-permute-start.1 = (bf16[12288]{0:T(1024)(128)(2,1)S(1)}, bf16[12288]{0:T(1024)(128)(2,1)S(1)}, u32[]{:S(2)}, u32[]{:S(2)}) collective-permute-start(bf16[12288]{0:T(1024)(128)(2,1)S(1)} %pad_maximum_fusion.1), channel_id=1, source_target_pairs={{16,0},{24,8},{0,16},{8,24},{17,1},{25,9},{1,17},{9,25},{18,2},{26... | collective-permute-start | bytes 73736 | tf_op jit(solution)/shard_map/ppermute | solution.py:63
  9.8 0.1 select_n.113
  9.9 1.9 %collective-permute-start.2 = (bf16[1024]{0:T(1024)(128)(2,1)S(1)}, bf16[1024]{0:T(1024)(128)(2,1)S(1)}, u32[]{:S(2)}, u32[]{:S(2)}) collective-permute-start(bf16[1024]{0:T(1024)(128)(2,1)S(1)} %pad_maximum_fusion.2), channel_id=1, source_target_pairs={{24,0},{0,24},{25,1},{1,25},{26,2},{2,26},{27,3},{3,27},{28,4},{4,... | collective-permute-start | bytes 6152 | tf_op jit(solution)/shard_map/ppermute | solution.py:63
  11.8 0.1 copy.36
  11.9 0.3 pad.68
  12.2 0.5 broadcast.291
  12.7 0.7 %reduce.47 = s32[2048]{0:T(1024)S(1)} reduce(s32[1,1,2048]{2,1,0:T(1,128)S(1)} %copy-done.4, s32[]{:T(128)} %broadcast.291), dimensions={0,1}, to_apply=%param.37.reduce_sub_computation.3 | reduce | bytes 16388 | tf_op args[3]
  13.4 0.1 reshape.747
  13.5 3.7 %collective-permute-done.2 = bf16[1024]{0:T(1024)(128)(2,1)S(1)} collective-permute-done((bf16[1024]{0:T(1024)(128)(2,1)S(1)}, bf16[1024]{0:T(1024)(128)(2,1)S(1)}, u32[]{:S(2)}, u32[]{:S(2)}) %collective-permute-start.2) | collective-permute-done | bytes 2080 | tf_op jit(solution)/shard_map/ppermute | solution.py:63
  17.2 0.1 reshape.770
  17.3 0.0 collective-permute-done
  17.3 0.1 reshape.769
  17.4 0.0 collective-permute-done.1
  17.4 0.1 reshape.743
  17.5 1.4 %scatter.46 = bf16[9,17,17,64]{3,2,1,0:T(8,128)(2,1)S(1)} dynamic-update-slice(bf16[9,17,17,64]{3,2,1,0:T(8,128)(2,1)S(1)} %pad.68, bf16[8,16,1,64]{3,2,1,0:T(2,128)(2,1)S(1)} %reshape.769, s32[]{:T(128)} %constant.531.clone.1, s32[]{:T(128)} %constant.531.clone.1, s32[]{:T(128)} %constant.530.clone.1, s32[]{:T(128)} %constant.530.clone.1) | dynamic-update-slice | bytes 32772 | tf_op jit(solution)/shard_map/scatter | solution.py:120
  18.9 0.2 scatter.49
  19.2 0.3 scatter.51
  19.5 0.1 scatter.54
  19.6 0.2 scatter.55
  19.8 2.7 %fusion.8 = f32[3,3,3,64,128]{4,3,2,1,0:T(8,128)S(1)} fusion(bf16[9,17,17,64,1]{3,2,1,0,4:T(8,128)(2,1)S(1)} %bitcast.62, bf16[4,8,8,128,1]{3,1,2,0,4:T(8,128)(2,1)S(1)} %bitcast.73, bf16[4,8,8]{2,1,0:T(8,128)(2,1)S(1)} %convert_element_type.63), kind=kOutput, calls=%fused_computation.9 | convolution fusion | flops 113377280 | bytes 1283712 | tf_op jit(solution)/shard_map/conv_general_dilated | solution.py:121
  22.6 0.1 collective-permute-start.3
  22.6 0.2 pad.71
  22.9 0.2 copy.34
  23.1 0.0 copy-start.6
  23.1 0.2 slice.661
  23.3 0.5 copy-done.6
  23.8 0.8 %fusion.10 = f32[4,8,8,2,128]{4,2,3,1,0:T(8,128)S(1)} fusion(bf16[3,3,3,64,128]{4,3,2,1,0:T(8,128)(2,1)S(1)} %bitcast.60, bf16[9,17,1,7,2,64]{5,3,4,1,0,2:T(8,128)(2,1)S(1)} %slice.661, bf16[9,17,1,8,4,64]{5,3,4,1,0,2:T(8,128)(2,1)S(1)} %copy.34, pred[8,2]{0,1:T(4,128)(4,1)S(1)} %copy-done.6), kind=kOutput, calls=%fused_computation.11 | convolution fusion | flops 229378048 | bytes 1605392 | tf_op jit(solution)/shard_map/conv_general_dilated | solution.py:140
  24.5 0.1 copy.35
  24.6 0.7 %fusion.16 = bf16[1,1,4,8,1024]{4,3,2,1,0:T(8,128)(2,1)} fusion(f32[4,8,1,16,128]{4,1,3,0,2:T(8,128)S(1)} %bitcast.71, f32[4,8,8]{1,2,0:T(8,128)S(1)} %copy.36), kind=kLoop, calls=%fused_computation.21 | loop fusion | flops 65536 | bytes 197632 | tf_op jit(solution)/shard_map/convert_element_type | solution.py:149
  25.4 0.0 collective-permute-done.3
  25.4 0.1 dynamic-slice_add_fusion
  25.5 0.8 %pad.69 = f32[896,128]{1,0:T(8,128)} pad(f32[864,128]{1,0:T(8,128)S(1)} %bitcast.67, f32[]{:T(128)} %constant.537.clone.1), padding=0_32x0_0 | pad | bytes 901124 | tf_op jit(solution)/shard_map/jit(_pad)/pad | solution.py:73
  26.3 3.8 %all-to-all-start = ((f32[16,56,128]{2,1,0:T(8,128)}), f32[16,56,128]{2,1,0:T(8,128)S(1)}, u32[]{:S(2)}, u32[]{:S(2)}) async-start(f32[16,56,128]{2,1,0:T(8,128)} %bitcast.5), calls=%async_computation | async-start | bytes 917504 | tf_op jit(solution)/shard_map/all_to_all | solution.py:74
  30.1 0.1 copy.37
  30.3 14.1 %all-to-all-done = f32[16,56,128]{2,1,0:T(8,128)S(1)} async-done(((f32[16,56,128]{2,1,0:T(8,128)}), f32[16,56,128]{2,1,0:T(8,128)S(1)}, u32[]{:S(2)}, u32[]{:S(2)}) %all-to-all-start) | async-done | bytes 458784 | tf_op jit(solution)/shard_map/all_to_all | solution.py:74
  44.5 0.8 %broadcast_in_dim.70 = f32[16,56,128]{2,1,0:T(8,128)} broadcast(f32[56,128]{1,0:T(8,128)S(1)} %broadcast_multiply_fusion.1), dimensions={1,2} | broadcast | bytes 487424 | tf_op jit(solution)/shard_map/broadcast_in_dim | solution.py:80
  45.3 4.0 %all-to-all-start.1 = ((f32[16,56,128]{2,1,0:T(8,128)}), f32[16,56,128]{2,1,0:T(8,128)S(1)}, u32[]{:S(2)}, u32[]{:S(2)}) async-start(f32[16,56,128]{2,1,0:T(8,128)} %broadcast_in_dim.70), calls=%async_computation.1 | async-start | bytes 917504 | tf_op jit(solution)/shard_map/all_to_all | solution.py:81
  49.2 6.2 %convolution_reduce_fusion = f32[8,16,16,64]{3,2,1,0:T(8,128)S(1)} fusion(bf16[3,3,3,64,128]{4,3,2,1,0:T(8,128)(2,1)S(1)} %bitcast.59, bf16[1,5,9,9,128]{4,1,3,2,0:T(8,128)(2,1)S(1)} %constant_dynamic-update-slice_fusion.1), kind=kOutput, calls=%fused_computation.8 | convolution fusion | flops 113246208 | bytes 1070336 | tf_op jit(solution)/shard_map/conv_general_dilated | solution.py:161
  55.5 0.3 mul.84
  55.8 0.3 mul.85
  56.1 0.0 copy-start.2
  56.1 0.3 squeeze.6
  56.4 0.6 copy-done.2
  57.1 0.8 %multiply_convert_fusion = bf16[1,1,8,16,1024]{4,3,2,1,0:T(8,128)(2,1)} fusion(f32[1,1,8,16,1024]{4,3,2,1,0:T(8,128)S(1)} %mul.85, f32[1,1,8,16,1024]{4,3,2,1,0:T(8,128)S(1)} %squeeze.6, bf16[1,1,8,16,1024]{4,3,2,1,0:T(8,128)(2,1)S(1)} %copy-done.2), kind=kLoop, calls=%fused_computation.13 | loop fusion | flops 524288 | bytes 1572864 | tf_op jit(solution)/shard_map/convert_element_type | solution.py:173
  57.9 4.6 %all-to-all-done.1 = f32[16,56,128]{2,1,0:T(8,128)S(1)} async-done(((f32[16,56,128]{2,1,0:T(8,128)}), f32[16,56,128]{2,1,0:T(8,128)S(1)}, u32[]{:S(2)}, u32[]{:S(2)}) %all-to-all-start.1) | async-done | bytes 458784 | tf_op jit(solution)/shard_map/all_to_all | solution.py:81
  62.5 0.1 collective-permute-start.4
  62.6 0.1 broadcast_in_dim.77
  62.8 1.6 %collective-permute-done.4 = f32[27,32,128]{2,1,0:T(8,128)S(1)} collective-permute-done((f32[27,32,128]{2,1,0:T(8,128)S(1)}, f32[27,32,128]{2,1,0:T(8,128)S(1)}, u32[]{:S(2)}, u32[]{:S(2)}) %collective-permute-start.4) | collective-permute-done | bytes 442400 | tf_op jit(solution)/shard_map/ppermute | solution.py:84
  64.4 0.0 copy-start.1
  64.5 0.9 %copy-done.1 = f32[27,2,32,128]{3,2,1,0:T(8,128)} copy-done((f32[27,2,32,128]{3,2,1,0:T(8,128)}, f32[27,2,32,128]{3,2,1,0:T(8,128)S(1)}, u32[]{:S(2)}) %copy-start.1) | copy-done | bytes 884760
  (39 shorter events, 0.6 us)
Async XLA Ops:
  0.6 22.7 %copy-start = (bf16[27,64,128]{2,1,0:T(8,128)(2,1)S(1)}, bf16[27,64,128]{2,1,0:T(8,128)(2,1)}, u32[]{:S(2)}) copy-start(bf16[27,64,128]{2,1,0:T(8,128)(2,1)} %param.38) | copy-start | bytes 1327108
  0.6 2.9 %copy-start.5 = (s32[1,1,256]{2,1,0:T(1,128)S(1)}, s32[1,1,256]{2,1,0:T(1,128)}, u32[]{:S(2)}) copy-start(s32[1,1,256]{2,1,0:T(1,128)} %param.35) | copy-start | bytes 3076
  0.7 3.0 %copy-start.3 = (bf16[1,1,4,8,1024]{4,3,2,1,0:T(8,128)(2,1)S(1)}, bf16[1,1,4,8,1024]{4,3,2,1,0:T(8,128)(2,1)}, u32[]{:S(2)}) copy-start(bf16[1,1,4,8,1024]{4,3,2,1,0:T(8,128)(2,1)} %param.34) | copy-start | bytes 196612
  3.2 9.5 %copy-start.4 = (s32[1,1,2048]{2,1,0:T(1,128)S(1)}, s32[1,1,2048]{2,1,0:T(1,128)}, u32[]{:S(2)}) copy-start(s32[1,1,2048]{2,1,0:T(1,128)} %param.37) | copy-start | bytes 24580
  3.9 13.4 %collective-permute-start = (bf16[12288]{0:T(1024)(128)(2,1)S(1)}, bf16[12288]{0:T(1024)(128)(2,1)S(1)}, u32[]{:S(2)}, u32[]{:S(2)}) collective-permute-start(bf16[12288]{0:T(1024)(128)(2,1)S(1)} %pad_maximum_fusion), channel_id=1, source_target_pairs={{8,0},{24,16},{0,8},{16,24},{9,1},{25,17},{1,9},{17,25},{10,2},{26... | collective-permute-start | bytes 73736 | tf_op jit(solution)/shard_map/ppermute | solution.py:63
  7.1 10.3 %collective-permute-start.1 = (bf16[12288]{0:T(1024)(128)(2,1)S(1)}, bf16[12288]{0:T(1024)(128)(2,1)S(1)}, u32[]{:S(2)}, u32[]{:S(2)}) collective-permute-start(bf16[12288]{0:T(1024)(128)(2,1)S(1)} %pad_maximum_fusion.1), channel_id=1, source_target_pairs={{16,0},{24,8},{0,16},{8,24},{17,1},{25,9},{1,17},{9,25},{18,2},{26... | collective-permute-start | bytes 73736 | tf_op jit(solution)/shard_map/ppermute | solution.py:63
  9.9 7.3 %collective-permute-start.2 = (bf16[1024]{0:T(1024)(128)(2,1)S(1)}, bf16[1024]{0:T(1024)(128)(2,1)S(1)}, u32[]{:S(2)}, u32[]{:S(2)}) collective-permute-start(bf16[1024]{0:T(1024)(128)(2,1)S(1)} %pad_maximum_fusion.2), channel_id=1, source_target_pairs={{24,0},{0,24},{25,1},{1,25},{26,2},{2,26},{27,3},{3,27},{28,4},{4,... | collective-permute-start | bytes 6152 | tf_op jit(solution)/shard_map/ppermute | solution.py:63
  22.6 2.8 %collective-permute-start.3 = (f32[27,32,128]{2,1,0:T(8,128)S(1)}, f32[27,32,128]{2,1,0:T(8,128)S(1)}, u32[]{:S(2)}, u32[]{:S(2)}) collective-permute-start(f32[27,32,128]{2,1,0:T(8,128)S(1)} %constant_dynamic-slice_fusion), channel_id=1, source_target_pairs={{0,1},{1,0},{2,3},{3,2},{4,5},{5,4},{6,7},{7,6},{8,9},{9,8},{10,11... | collective-permute-start | bytes 1327112 | tf_op jit(solution)/shard_map/ppermute | solution.py:133
  23.1 0.7 %copy-start.6 = (pred[8,2]{0,1:T(4,128)(4,1)S(1)}, pred[8,2]{0,1:T(4,128)(4,1)}, u32[]{:S(2)}) copy-start(pred[8,2]{0,1:T(4,128)(4,1)} %constant.557) | copy-start | bytes 52
  26.3 18.2 %all-to-all-start = ((f32[16,56,128]{2,1,0:T(8,128)}), f32[16,56,128]{2,1,0:T(8,128)S(1)}, u32[]{:S(2)}, u32[]{:S(2)}) async-start(f32[16,56,128]{2,1,0:T(8,128)} %bitcast.5), calls=%async_computation | async-start | bytes 917504 | tf_op jit(solution)/shard_map/all_to_all | solution.py:74
  45.3 17.2 %all-to-all-start.1 = ((f32[16,56,128]{2,1,0:T(8,128)}), f32[16,56,128]{2,1,0:T(8,128)S(1)}, u32[]{:S(2)}, u32[]{:S(2)}) async-start(f32[16,56,128]{2,1,0:T(8,128)} %broadcast_in_dim.70), calls=%async_computation.1 | async-start | bytes 917504 | tf_op jit(solution)/shard_map/all_to_all | solution.py:81
  56.1 1.0 %copy-start.2 = (bf16[1,1,8,16,1024]{4,3,2,1,0:T(8,128)(2,1)S(1)}, bf16[1,1,8,16,1024]{4,3,2,1,0:T(8,128)(2,1)}, u32[]{:S(2)}) copy-start(bf16[1,1,8,16,1024]{4,3,2,1,0:T(8,128)(2,1)} %param.36) | copy-start | bytes 786436
  62.5 1.9 %collective-permute-start.4 = (f32[27,32,128]{2,1,0:T(8,128)S(1)}, f32[27,32,128]{2,1,0:T(8,128)S(1)}, u32[]{:S(2)}, u32[]{:S(2)}) collective-permute-start(f32[27,32,128]{2,1,0:T(8,128)S(1)} %bitcast.65), channel_id=1, source_target_pairs={{0,1},{1,0},{2,3},{3,2},{4,5},{5,4},{6,7},{7,6},{8,9},{9,8},{10,11... | collective-permute-start | bytes 1327112 | tf_op jit(solution)/shard_map/ppermute | solution.py:84
  64.4 0.9 %copy-start.1 = (f32[27,2,32,128]{3,2,1,0:T(8,128)}, f32[27,2,32,128]{3,2,1,0:T(8,128)S(1)}, u32[]{:S(2)}) copy-start(f32[27,2,32,128]{3,2,1,0:T(8,128)S(1)} %bitcast_dynamic-update-slice_fusion) | copy-start | bytes 2654212

commit v14 on v13

--- a/solution.py
+++ b/solution.py
@@ -106,18 +106,19 @@
         jnp.bfloat16
     )
 
-    halos = {}
-    for direction in DIRECTIONS:
-        masked_piece = masked[tuple(slice(0, 1) if flag else slice(None) for flag in direction)]
-        cot_piece = cotangent[tuple(slice(-1, None) if flag else slice(None) for flag in direction)]
-        halos[direction] = halo_exchange(masked_piece, cot_piece, regions, direction)
-    widened = jnp.pad(cotangent, ((1, 0), (1, 0), (1, 0), (0, 0)))
-    for direction in DIRECTIONS:
-        target = tuple(
-            slice(0, 1) if flag else slice(1, 1 + cotangent.shape[a])
-            for a, flag in enumerate(direction)
+    extended = masked
+    widened = cotangent
+    for axis in (2, 1, 0):
+        direction = tuple(1 if other == axis else 0 for other in range(3))
+        last = widened.shape[axis]
+        got_masked, got_cot = halo_exchange(
+            lax.slice_in_dim(extended, 0, 1, axis=axis),
+            lax.slice_in_dim(widened, last - 1, last, axis=axis),
+            regions,
+            direction,
         )
-        widened = widened.at[target].set(halos[direction][1])
+        extended = jnp.concatenate([extended, got_masked], axis=axis)
+        widened = jnp.concatenate([got_cot, widened], axis=axis)
     full = lax.conv_general_dilated(
         widened[..., None],
         masked[..., None],
@@ -132,8 +133,8 @@
     theirs = lax.dynamic_slice_in_dim(full, (1 - core) * share, share, axis=1)
     got = lax.ppermute(theirs, "core", [(0, 1), (1, 0)])
     grads = lax.dynamic_slice_in_dim(full, core * share, share, axis=1) + got
-    grads, masked_late, weight_late, skip, fine_keep = lax.optimization_barrier(
-        (grads, masked, up_weight, skip, fine_keep)
+    grads, extended, weight_late, skip, fine_keep = lax.optimization_barrier(
+        (grads, extended, up_weight, skip, fine_keep)
     )
     reduced, plan = all_reduce(grads)
 
@@ -148,14 +149,6 @@
     coarse_grad = (
         (back * coarse_keep.astype(jnp.float32)).astype(jnp.bfloat16).reshape(coarse.shape)
     )
-
-    extended = jnp.pad(masked_late, ((0, 1), (0, 1), (0, 1), (0, 0)))
-    for direction in DIRECTIONS:
-        target = tuple(
-            slice(counts[a], counts[a] + 1) if flag else slice(0, counts[a])
-            for a, flag in enumerate(direction)
-        )
-        extended = extended.at[target].set(halos[direction][0])
 
     flipped = weight_late.reshape((3, 3, 3, channels_out, channels_in))[::-1, ::-1, ::-1]
     up = lax.conv_general_dilated(

time: 65.8 us -> 63.5 us (0.965)
  local copies, waits for them, and re-layouts: 11 us -> 8.19 us
  waiting for transfers between devices: 24.1 us -> 21.4 us
  starting transfers between devices: 15.6 us -> 17.7 us
  other arithmetic: 3.87 us -> 4.95 us
    all_to_all x1, starting transfers between devices: 3.83 us -> 7.37 us  [all_reduce(): lax.all_to_all(rows.reshape(devices, chunk, lanes), OTHERS, 0, 0, tiled=T...]
    all_to_all x1, waiting for transfers between devices: 14.1 us -> 11.5 us  [all_reduce(): lax.all_to_all(rows.reshape(devices, chunk, lanes), OTHERS, 0, 0, tiled=T...]
    scatter x14 -> x0, local copies, waits for them, and re-layouts: 2.36 us -> none  [the longest x7 2.25 us: body(): widened = widened.at[target].set(halos[direction][1])]
    ppermute x3 -> x2, starting transfers between devices: 7.66 us -> 6.19 us  [halo_exchange(): got = lax.ppermute(packed, 'brick', both)]
    concatenate x0 -> x1, other arithmetic: none -> 0.71 us  [body(): extended = jnp.concatenate([extended, got_masked], axis=axis)]
    ppermute x3 -> x2, waiting for transfers between devices: 3.74 us -> 3.63 us  [halo_exchange(): got = lax.ppermute(packed, 'brick', both)]
    unnamed x16 -> x17, local copies, waits for them, and re-layouts: 2.6 us -> 2.55 us
  transfers between devices with their start and end apart: 7 -> 6, of which waited for: 4 -> 5; matrix products, arithmetic and copies ran while one was open for 19% -> 20% of each run, Pallas kernels for 0% -> 0%
where the time goes in v14:
time: 63.5 us; the launch traced here: 63 us
  waiting for transfers between devices  21.4 us (34%)
  starting transfers between devices  17.7 us (28%)
  matrix products  9.78 us (15%)
  local copies, waits for them, and re-layouts  8.19 us (13%)
  other arithmetic  4.95 us (8%)
  between operations  1.02 us (2%)
    all_to_all x1, waiting for transfers between devices, all_reduce(): lax.all_to_all(rows.reshape(devices, chunk, lanes), OTHERS, 0, 0, tiled=T...  11.5 us
    all_to_all x1, starting transfers between devices, all_reduce(): lax.all_to_all(rows.reshape(devices, chunk, lanes), OTHERS, 0, 0, tiled=T...  7.37 us
    ppermute x2, starting transfers between devices, halo_exchange(): got = lax.ppermute(packed, 'brick', both)  6.19 us
    conv_general_dilated x1, matrix products, body(): lax.conv_general_dilated(extended[None], flipped, (1, 1, 1), ((1, 0), (1,...  6.18 us
    all_to_all x1, waiting for transfers between devices, all_spread(): half = lax.all_to_all(spread, OTHERS, 0, 0, tiled=True)  4.66 us
    all_to_all x1, starting transfers between devices, all_spread(): half = lax.all_to_all(spread, OTHERS, 0, 0, tiled=True)  3.97 us
    ppermute x2, waiting for transfers between devices, halo_exchange(): got = lax.ppermute(packed, 'brick', both)  3.63 us
    conv_general_dilated x1, matrix products, body(): lax.conv_general_dilated(widened[..., None], masked[..., None], (1, 1, 1)...  2.85 us
  transfers between devices with their start and end apart: 6, of which 5 were waited for; matrix products, arithmetic and copies ran while one was open for 20% of the time, Pallas kernels for 0%

profile of v14, /device:TPU:0, one launch (start us, length us, event | category | flops | bytes accessed | tf_op | source)
XLA Modules:
  0.0 63.0 jit_solution(4071481932355048519)
XLA Ops:
  0.6 0.0 copy-start
  0.6 0.0 copy-start.6
  0.7 0.0 copy-start.4
  0.7 1.4 %reshape.149 = bf16[8,16,16,64]{3,2,1,0:T(8,128)(2,1)S(1)} reshape(bf16[1,1,8,16,1024]{4,3,2,1,0:T(8,128)(2,1)} %param.11) | data formatting | bytes 524288 | tf_op jit(solution)/shard_map/reshape | solution.py:105
  2.1 0.7 %convert_reduce_fusion = bf16[2048]{0:T(1024)(128)(2,1)S(1)} fusion(s32[1,1,2048]{2,1,0:T(1,128)} %param.9), kind=kLoop, calls=%fused_computation.49 | loop fusion | flops 2048 | bytes 12288 | tf_op jit(solution)/shard_map/convert_element_type | solution.py:105
  2.8 0.1 convert_element_type.59
  2.9 0.3 broadcast_multiply_fusion
  3.2 0.2 fusion.27
  3.5 0.1 select_n.81
  3.6 0.0 copy-done.6
  3.6 0.1 convert_element_type.57
  3.7 0.0 copy-done.4
  3.7 0.1 bitcast_multiply_fusion
  3.8 0.1 fusion.30
  3.9 3.1 %collective-permute-start = (bf16[12288]{0:T(1024)(128)(2,1)S(1)}, bf16[12288]{0:T(1024)(128)(2,1)S(1)}, u32[]{:S(2)}, u32[]{:S(2)}) collective-permute-start(bf16[12288]{0:T(1024)(128)(2,1)S(1)} %pad_maximum_fusion.2), channel_id=1, source_target_pairs={{8,0},{24,16},{0,8},{16,24},{9,1},{25,17},{1,9},{17,25},{10,2},{26... | collective-permute-start | bytes 73736 | tf_op jit(solution)/shard_map/ppermute | solution.py:63
  7.0 1.8 %collective-permute-done = bf16[12288]{0:T(1024)(128)(2,1)S(1)} collective-permute-done((bf16[12288]{0:T(1024)(128)(2,1)S(1)}, bf16[12288]{0:T(1024)(128)(2,1)S(1)}, u32[]{:S(2)}, u32[]{:S(2)}) %collective-permute-start) | collective-permute-done | bytes 24608 | tf_op jit(solution)/shard_map/ppermute | solution.py:63
  8.8 0.1 reshape.177
  8.9 0.1 select_n.86
  9.1 3.1 %collective-permute-start.1 = (bf16[13312]{0:T(1024)(128)(2,1)S(1)}, bf16[13312]{0:T(1024)(128)(2,1)S(1)}, u32[]{:S(2)}, u32[]{:S(2)}) collective-permute-start(bf16[13312]{0:T(1024)(128)(2,1)S(1)} %pad_maximum_fusion.1), channel_id=1, source_target_pairs={{16,0},{24,8},{0,16},{8,24},{17,1},{25,9},{1,17},{9,25},{18,2},{26... | collective-permute-start | bytes 79880 | tf_op jit(solution)/shard_map/ppermute | solution.py:63
  12.2 1.8 %collective-permute-done.1 = bf16[13312]{0:T(1024)(128)(2,1)S(1)} collective-permute-done((bf16[13312]{0:T(1024)(128)(2,1)S(1)}, bf16[13312]{0:T(1024)(128)(2,1)S(1)}, u32[]{:S(2)}, u32[]{:S(2)}) %collective-permute-start.1) | collective-permute-done | bytes 26656 | tf_op jit(solution)/shard_map/ppermute | solution.py:63
  14.0 0.1 reshape.151
  14.1 0.4 fusion.36
  14.5 0.0 copy-start.5
  14.5 2.9 %fusion.11 = f32[3,3,3,64,128]{4,3,2,1,0:T(8,128)S(1)} fusion(bf16[9,17,17,64,1]{3,2,1,0,4:T(8,128)(2,1)S(1)} %get-tuple-element.20, bf16[4,8,8,128,1]{3,1,2,0,4:T(8,128)(2,1)S(1)} %bitcast.68, bf16[4,8,8]{2,1,0:T(8,128)(2,1)S(1)} %convert_element_type.57), kind=kOutput, calls=%fused_computation.13 | convolution fusion | flops 113377280 | bytes 1283712 | tf_op jit(solution)/shard_map/conv_general_dilated | solution.py:122
  17.4 0.1 collective-permute-start.2
  17.5 0.5 broadcast.90
  18.0 0.0 copy-done.5
  18.0 0.7 %reduce.15 = s32[2048]{0:T(1024)S(1)} reduce(s32[1,1,2048]{2,1,0:T(1,128)S(1)} %copy-done.5, s32[]{:T(128)} %broadcast.90), dimensions={0,1}, to_apply=%param.9.reduce_sub_computation.3 | reduce | bytes 16388 | tf_op args[3]
  18.7 0.1 reshape.155
  18.8 0.7 %fusion.24 = bf16[5,9,9,128]{3,2,1,0:T(8,128)(2,1)} fusion(bf16[4,1,9,128]{3,2,1,0:T(8,128)(2,1)S(1)} %bitcast.66, bf16[4,8,1,128]{3,2,1,0:T(2,128)(2,1)S(1)} %copy.25, bf16[4,8,8,128]{3,2,1,0:T(8,128)(2,1)S(1)} %bitcast_multiply_fusion), kind=kLoop, calls=%fused_computation.29 | loop fusion | flops 518400 | bytes 186624 | tf_op jit(solution)/shard_map/concatenate | solution.py:120
  19.5 0.0 collective-permute-done.2
  19.5 0.1 dynamic-slice_add_fusion
  19.6 0.8 %pad.6 = f32[896,128]{1,0:T(8,128)} pad(f32[864,128]{1,0:T(8,128)S(1)} %bitcast.59, f32[]{:T(128)} %constant.58.clone.1), padding=0_32x0_0 | pad | bytes 901124 | tf_op jit(solution)/shard_map/jit(_pad)/pad | solution.py:73
  20.4 7.4 %all-to-all-start = ((f32[16,56,128]{2,1,0:T(8,128)}), f32[16,56,128]{2,1,0:T(8,128)S(1)}, u32[]{:S(2)}, u32[]{:S(2)}) async-start(f32[16,56,128]{2,1,0:T(8,128)} %bitcast.7), calls=%async_computation | async-start | bytes 917504 | tf_op jit(solution)/shard_map/all_to_all | solution.py:74
  27.8 0.1 copy.36
  27.9 0.2 pad.7
  28.1 0.2 copy.34
  28.3 0.0 copy-start.7
  28.3 0.2 slice.63
  28.5 0.0 copy-done
  28.5 0.5 copy-done.7
  29.0 0.8 %fusion.13 = f32[4,8,8,2,128]{4,2,3,1,0:T(8,128)S(1)} fusion(bf16[3,3,3,64,128]{4,3,2,1,0:T(8,128)(2,1)S(1)} %bitcast.54, bf16[9,17,1,7,2,64]{5,3,4,1,0,2:T(8,128)(2,1)S(1)} %slice.63, bf16[9,17,1,8,4,64]{5,3,4,1,0,2:T(8,128)(2,1)S(1)} %copy.34, pred[8,2]{0,1:T(4,128)(4,1)S(1)} %copy-done.7), kind=kOutput, calls=%fused_computation.15 | convolution fusion | flops 229378048 | bytes 1605392 | tf_op jit(solution)/shard_map/conv_general_dilated | solution.py:141
  29.7 0.0 copy-start.3
  29.8 0.1 copy.35
  29.8 0.7 %fusion.26 = bf16[1,1,4,8,1024]{4,3,2,1,0:T(8,128)(2,1)} fusion(f32[4,8,1,16,128]{4,1,3,0,2:T(8,128)S(1)} %bitcast.63, f32[4,8,8]{1,2,0:T(8,128)S(1)} %copy.36), kind=kLoop, calls=%fused_computation.32 | loop fusion | flops 65536 | bytes 197632 | tf_op jit(solution)/shard_map/convert_element_type | solution.py:150
  30.6 11.5 %all-to-all-done = f32[16,56,128]{2,1,0:T(8,128)S(1)} async-done(((f32[16,56,128]{2,1,0:T(8,128)}), f32[16,56,128]{2,1,0:T(8,128)S(1)}, u32[]{:S(2)}, u32[]{:S(2)}) %all-to-all-start) | async-done | bytes 458784 | tf_op jit(solution)/shard_map/all_to_all | solution.py:74
  42.1 0.8 %broadcast_in_dim.49 = f32[16,56,128]{2,1,0:T(8,128)} broadcast(f32[56,128]{1,0:T(8,128)S(1)} %broadcast_multiply_fusion.1), dimensions={1,2} | broadcast | bytes 487424 | tf_op jit(solution)/shard_map/broadcast_in_dim | solution.py:80
  42.9 4.0 %all-to-all-start.1 = ((f32[16,56,128]{2,1,0:T(8,128)}), f32[16,56,128]{2,1,0:T(8,128)S(1)}, u32[]{:S(2)}, u32[]{:S(2)}) async-start(f32[16,56,128]{2,1,0:T(8,128)} %broadcast_in_dim.49), calls=%async_computation.1 | async-start | bytes 917504 | tf_op jit(solution)/shard_map/all_to_all | solution.py:81
  46.9 0.0 copy-done.3
  46.9 6.2 %convolution_reduce_fusion = f32[8,16,16,64]{3,2,1,0:T(8,128)S(1)} fusion(bf16[3,3,3,64,128]{4,3,2,1,0:T(8,128)(2,1)S(1)} %bitcast.53, bf16[1,5,9,9,128]{4,3,2,1,0:T(8,128)(2,1)S(1)} %bitcast.65), kind=kOutput, calls=%fused_computation.12 | convolution fusion | flops 113246208 | bytes 1070336 | tf_op jit(solution)/shard_map/conv_general_dilated | solution.py:154
  53.1 0.3 mul.84
  53.5 0.3 mul.85
  53.8 0.0 copy-start.2
  53.8 0.3 squeeze.6
  54.1 0.6 copy-done.2
  54.7 0.8 %multiply_convert_fusion = bf16[1,1,8,16,1024]{4,3,2,1,0:T(8,128)(2,1)} fusion(f32[1,1,8,16,1024]{4,3,2,1,0:T(8,128)S(1)} %mul.85, f32[1,1,8,16,1024]{4,3,2,1,0:T(8,128)S(1)} %squeeze.6, bf16[1,1,8,16,1024]{4,3,2,1,0:T(8,128)(2,1)S(1)} %copy-done.2), kind=kLoop, calls=%fused_computation.19 | loop fusion | flops 524288 | bytes 1572864 | tf_op jit(solution)/shard_map/convert_element_type | solution.py:166
  55.5 4.7 %all-to-all-done.1 = f32[16,56,128]{2,1,0:T(8,128)S(1)} async-done(((f32[16,56,128]{2,1,0:T(8,128)}), f32[16,56,128]{2,1,0:T(8,128)S(1)}, u32[]{:S(2)}, u32[]{:S(2)}) %all-to-all-start.1) | async-done | bytes 458784 | tf_op jit(solution)/shard_map/all_to_all | solution.py:81
  60.2 0.1 collective-permute-start.3
  60.3 0.1 broadcast_in_dim.52
  60.5 1.6 %collective-permute-done.3 = f32[27,32,128]{2,1,0:T(8,128)S(1)} collective-permute-done((f32[27,32,128]{2,1,0:T(8,128)S(1)}, f32[27,32,128]{2,1,0:T(8,128)S(1)}, u32[]{:S(2)}, u32[]{:S(2)}) %collective-permute-start.3) | collective-permute-done | bytes 442400 | tf_op jit(solution)/shard_map/ppermute | solution.py:84
  62.1 0.0 copy-start.1
  62.1 0.9 %copy-done.1 = f32[27,2,32,128]{3,2,1,0:T(8,128)} copy-done((f32[27,2,32,128]{3,2,1,0:T(8,128)}, f32[27,2,32,128]{3,2,1,0:T(8,128)S(1)}, u32[]{:S(2)}) %copy-start.1) | copy-done | bytes 884760
  (19 shorter events, 0.3 us)
Async XLA Ops:
  0.6 27.9 %copy-start = (bf16[27,64,128]{2,1,0:T(8,128)(2,1)S(1)}, bf16[27,64,128]{2,1,0:T(8,128)(2,1)}, u32[]{:S(2)}) copy-start(bf16[27,64,128]{2,1,0:T(8,128)(2,1)} %param.10) | copy-start | bytes 1327108
  0.6 2.9 %copy-start.6 = (s32[1,1,256]{2,1,0:T(1,128)S(1)}, s32[1,1,256]{2,1,0:T(1,128)}, u32[]{:S(2)}) copy-start(s32[1,1,256]{2,1,0:T(1,128)} %param.7) | copy-start | bytes 3076
  0.7 3.0 %copy-start.4 = (bf16[1,1,4,8,1024]{4,3,2,1,0:T(8,128)(2,1)S(1)}, bf16[1,1,4,8,1024]{4,3,2,1,0:T(8,128)(2,1)}, u32[]{:S(2)}) copy-start(bf16[1,1,4,8,1024]{4,3,2,1,0:T(8,128)(2,1)} %param.6) | copy-start | bytes 196612
  3.9 4.9 %collective-permute-start = (bf16[12288]{0:T(1024)(128)(2,1)S(1)}, bf16[12288]{0:T(1024)(128)(2,1)S(1)}, u32[]{:S(2)}, u32[]{:S(2)}) collective-permute-start(bf16[12288]{0:T(1024)(128)(2,1)S(1)} %pad_maximum_fusion.2), channel_id=1, source_target_pairs={{8,0},{24,16},{0,8},{16,24},{9,1},{25,17},{1,9},{17,25},{10,2},{26... | collective-permute-start | bytes 73736 | tf_op jit(solution)/shard_map/ppermute | solution.py:63
  9.1 4.9 %collective-permute-start.1 = (bf16[13312]{0:T(1024)(128)(2,1)S(1)}, bf16[13312]{0:T(1024)(128)(2,1)S(1)}, u32[]{:S(2)}, u32[]{:S(2)}) collective-permute-start(bf16[13312]{0:T(1024)(128)(2,1)S(1)} %pad_maximum_fusion.1), channel_id=1, source_target_pairs={{16,0},{24,8},{0,16},{8,24},{17,1},{25,9},{1,17},{9,25},{18,2},{26... | collective-permute-start | bytes 79880 | tf_op jit(solution)/shard_map/ppermute | solution.py:63
  14.5 3.5 %copy-start.5 = (s32[1,1,2048]{2,1,0:T(1,128)S(1)}, s32[1,1,2048]{2,1,0:T(1,128)}, u32[]{:S(2)}) copy-start(s32[1,1,2048]{2,1,0:T(1,128)} %param.9) | copy-start | bytes 24580
  17.4 2.1 %collective-permute-start.2 = (f32[27,32,128]{2,1,0:T(8,128)S(1)}, f32[27,32,128]{2,1,0:T(8,128)S(1)}, u32[]{:S(2)}, u32[]{:S(2)}) collective-permute-start(f32[27,32,128]{2,1,0:T(8,128)S(1)} %constant_dynamic-slice_fusion), channel_id=1, source_target_pairs={{0,1},{1,0},{2,3},{3,2},{4,5},{5,4},{6,7},{7,6},{8,9},{9,8},{10,11... | collective-permute-start | bytes 1327112 | tf_op jit(solution)/shard_map/ppermute | solution.py:134
  20.4 21.7 %all-to-all-start = ((f32[16,56,128]{2,1,0:T(8,128)}), f32[16,56,128]{2,1,0:T(8,128)S(1)}, u32[]{:S(2)}, u32[]{:S(2)}) async-start(f32[16,56,128]{2,1,0:T(8,128)} %bitcast.7), calls=%async_computation | async-start | bytes 917504 | tf_op jit(solution)/shard_map/all_to_all | solution.py:74
  28.3 0.7 %copy-start.7 = (pred[8,2]{0,1:T(4,128)(4,1)S(1)}, pred[8,2]{0,1:T(4,128)(4,1)}, u32[]{:S(2)}) copy-start(pred[8,2]{0,1:T(4,128)(4,1)} %constant.76) | copy-start | bytes 52
  29.7 17.2 %copy-start.3 = (bf16[5,9,9,128]{3,2,1,0:T(8,128)(2,1)S(1)}, bf16[5,9,9,128]{3,2,1,0:T(8,128)(2,1)}, u32[]{:S(2)}) copy-start(bf16[5,9,9,128]{3,2,1,0:T(8,128)(2,1)} %fusion.24) | copy-start | bytes 311044
  42.9 17.2 %all-to-all-start.1 = ((f32[16,56,128]{2,1,0:T(8,128)}), f32[16,56,128]{2,1,0:T(8,128)S(1)}, u32[]{:S(2)}, u32[]{:S(2)}) async-start(f32[16,56,128]{2,1,0:T(8,128)} %broadcast_in_dim.49), calls=%async_computation.1 | async-start | bytes 917504 | tf_op jit(solution)/shard_map/all_to_all | solution.py:81
  53.8 1.0 %copy-start.2 = (bf16[1,1,8,16,1024]{4,3,2,1,0:T(8,128)(2,1)S(1)}, bf16[1,1,8,16,1024]{4,3,2,1,0:T(8,128)(2,1)}, u32[]{:S(2)}) copy-start(bf16[1,1,8,16,1024]{4,3,2,1,0:T(8,128)(2,1)} %param.8) | copy-start | bytes 786436
  60.2 1.9 %collective-permute-start.3 = (f32[27,32,128]{2,1,0:T(8,128)S(1)}, f32[27,32,128]{2,1,0:T(8,128)S(1)}, u32[]{:S(2)}, u32[]{:S(2)}) collective-permute-start(f32[27,32,128]{2,1,0:T(8,128)S(1)} %bitcast.57), channel_id=1, source_target_pairs={{0,1},{1,0},{2,3},{3,2},{4,5},{5,4},{6,7},{7,6},{8,9},{9,8},{10,11... | collective-permute-start | bytes 1327112 | tf_op jit(solution)/shard_map/ppermute | solution.py:84
  62.1 0.9 %copy-start.1 = (f32[27,2,32,128]{3,2,1,0:T(8,128)}, f32[27,2,32,128]{3,2,1,0:T(8,128)S(1)}, u32[]{:S(2)}) copy-start(f32[27,2,32,128]{3,2,1,0:T(8,128)S(1)} %bitcast_dynamic-update-slice_fusion) | copy-start | bytes 2654212

commit v15 on v14

--- a/solution.py
+++ b/solution.py
@@ -64,29 +64,33 @@
     return (got[:cut].reshape(masked_piece.shape), got[cut:].reshape(cot_piece.shape))
 
 
-def all_reduce(half):
+def all_reduce(half, taps):
     devices = lax.axis_size("brick") * lax.axis_size("chip")
     lanes = half.shape[-1]
     rows = half.reshape(-1, lanes)
-    size = rows.shape[0]
-    chunk = -(-size // (devices * 8)) * 8
-    rows = jnp.pad(rows, ((0, chunk * devices - size), (0, 0)))
+    chunk = rows.shape[0] // devices
     parts = lax.all_to_all(rows.reshape(devices, chunk, lanes), OTHERS, 0, 0, tiled=True)
-    return parts.sum(axis=0), (devices, chunk, size, half.shape)
+    return parts.sum(axis=0), (half.shape, taps)
 
 
 def all_spread(reduced, plan, riders):
-    devices, chunk, size, shape = plan
+    shape, taps = plan
+    devices = lax.axis_size("brick") * lax.axis_size("chip")
     spread = jnp.broadcast_to(reduced[None], (devices,) + reduced.shape)
     half = lax.all_to_all(spread, OTHERS, 0, 0, tiled=True)
     half, riders = lax.optimization_barrier((half, riders))
-    half = half.reshape(-1, reduced.shape[-1])[:size].reshape(shape)
+    half = half.reshape(shape)[:taps]
     other = lax.ppermute(half, "core", [(0, 1), (1, 0)])
     core = lax.axis_index("core")
-    whole = jnp.zeros((shape[0], 2) + shape[1:], half.dtype)
+    whole = jnp.zeros((taps, 2) + shape[1:], half.dtype)
     whole = lax.dynamic_update_index_in_dim(whole, half, core, 1)
     whole = lax.dynamic_update_index_in_dim(whole, other, 1 - core, 1)
-    return whole.reshape(shape[0], 2 * shape[1], shape[2]), riders
+    return whole.reshape(taps, 2 * shape[1], shape[2]), riders
+
+
+def padded_taps(taps, share, devices):
+    step = devices * 8 // math.gcd(devices * 8, share)
+    return -(-taps // step) * step
 
 
 def body(coarse, coarse_mask, skip, fine_mask, up_weight, fine_grad):
@@ -130,13 +134,17 @@
     ).reshape(27, channels_out, channels_in)
     core = lax.axis_index("core")
     share = channels_out // 2
+    spare = padded_taps(full.shape[0], share, regions * lax.axis_size("chip")) - full.shape[0]
     theirs = lax.dynamic_slice_in_dim(full, (1 - core) * share, share, axis=1)
-    got = lax.ppermute(theirs, "core", [(0, 1), (1, 0)])
-    grads = lax.dynamic_slice_in_dim(full, core * share, share, axis=1) + got
+    got = lax.ppermute(
+        jnp.pad(theirs, ((0, spare), (0, 0), (0, 0))), "core", [(0, 1), (1, 0)]
+    )
+    mine = lax.dynamic_slice_in_dim(full, core * share, share, axis=1)
+    grads = jnp.pad(mine, ((0, spare), (0, 0), (0, 0))) + got
     grads, extended, weight_late, skip, fine_keep = lax.optimization_barrier(
         (grads, extended, up_weight, skip, fine_keep)
     )
-    reduced, plan = all_reduce(grads)
+    reduced, plan = all_reduce(grads, full.shape[0])
 
     back = lax.conv_general_dilated(
         widened[None],

time: 63.5 us -> 63.5 us (level)
  other arithmetic: 4.95 us -> 5.72 us
  local copies, waits for them, and re-layouts: 8.19 us -> 7.46 us
    add x1, other arithmetic: 0.07 us -> 0.84 us  [body(): grads = jnp.pad(mine, ((0, spare), (0, 0), (0, 0))) + got]
    pad x1, local copies, waits for them, and re-layouts: 0.8 us -> 0.03 us  [body(): jnp.pad(theirs, ((0, spare), (0, 0), (0, 0)))]
where the time goes in v15:
time: 63.5 us; the launch traced here: 63.1 us
  waiting for transfers between devices  21.4 us (34%)
  starting transfers between devices  17.7 us (28%)
  matrix products  9.78 us (15%)
  local copies, waits for them, and re-layouts  7.46 us (12%)
  other arithmetic  5.72 us (9%)
  between operations  1.02 us (2%)
    all_to_all x1, waiting for transfers between devices, all_reduce(): lax.all_to_all(rows.reshape(devices, chunk, lanes), OTHERS, 0, 0, tiled=T...  11.5 us
    all_to_all x1, starting transfers between devices, all_reduce(): lax.all_to_all(rows.reshape(devices, chunk, lanes), OTHERS, 0, 0, tiled=T...  7.37 us
    ppermute x2, starting transfers between devices, halo_exchange(): got = lax.ppermute(packed, 'brick', both)  6.19 us
    conv_general_dilated x1, matrix products, body(): lax.conv_general_dilated(extended[None], flipped, (1, 1, 1), ((1, 0), (1,...  6.18 us
    all_to_all x1, waiting for transfers between devices, all_spread(): half = lax.all_to_all(spread, OTHERS, 0, 0, tiled=True)  4.66 us
    all_to_all x1, starting transfers between devices, all_spread(): half = lax.all_to_all(spread, OTHERS, 0, 0, tiled=True)  3.97 us
    ppermute x2, waiting for transfers between devices, halo_exchange(): got = lax.ppermute(packed, 'brick', both)  3.63 us
    conv_general_dilated x1, matrix products, body(): lax.conv_general_dilated(widened[..., None], masked[..., None], (1, 1, 1)...  2.85 us
  transfers between devices with their start and end apart: 6, of which 5 were waited for; matrix products, arithmetic and copies ran while one was open for 20% of the time, Pallas kernels for 0%

profile of v15, /device:TPU:0, one launch (start us, length us, event | category | flops | bytes accessed | tf_op | source)
XLA Modules:
  0.0 63.1 jit_solution(1664621983481440053)
XLA Ops:
  0.6 0.0 copy-start
  0.6 0.0 copy-start.6
  0.7 0.0 copy-start.4
  0.7 1.4 %reshape.139 = bf16[8,16,16,64]{3,2,1,0:T(8,128)(2,1)S(1)} reshape(bf16[1,1,8,16,1024]{4,3,2,1,0:T(8,128)(2,1)} %param.11) | data formatting | bytes 524288 | tf_op jit(solution)/shard_map/reshape | solution.py:109
  2.1 0.7 %convert_reduce_fusion = bf16[2048]{0:T(1024)(128)(2,1)S(1)} fusion(s32[1,1,2048]{2,1,0:T(1,128)} %param.9), kind=kLoop, calls=%fused_computation.50 | loop fusion | flops 2048 | bytes 12288 | tf_op jit(solution)/shard_map/convert_element_type | solution.py:109
  2.8 0.1 convert_element_type.60
  2.9 0.3 broadcast_multiply_fusion
  3.2 0.2 fusion.27
  3.5 0.1 select_n.81
  3.6 0.0 copy-done.6
  3.6 0.1 convert_element_type.58
  3.7 0.0 copy-done.4
  3.7 0.1 bitcast_multiply_fusion
  3.8 0.1 fusion.30
  3.9 3.1 %collective-permute-start = (bf16[12288]{0:T(1024)(128)(2,1)S(1)}, bf16[12288]{0:T(1024)(128)(2,1)S(1)}, u32[]{:S(2)}, u32[]{:S(2)}) collective-permute-start(bf16[12288]{0:T(1024)(128)(2,1)S(1)} %pad_maximum_fusion.2), channel_id=1, source_target_pairs={{8,0},{24,16},{0,8},{16,24},{9,1},{25,17},{1,9},{17,25},{10,2},{26... | collective-permute-start | bytes 73736 | tf_op jit(solution)/shard_map/ppermute | solution.py:63
  7.0 1.8 %collective-permute-done = bf16[12288]{0:T(1024)(128)(2,1)S(1)} collective-permute-done((bf16[12288]{0:T(1024)(128)(2,1)S(1)}, bf16[12288]{0:T(1024)(128)(2,1)S(1)}, u32[]{:S(2)}, u32[]{:S(2)}) %collective-permute-start) | collective-permute-done | bytes 24608 | tf_op jit(solution)/shard_map/ppermute | solution.py:63
  8.8 0.1 reshape.164
  8.9 0.1 select_n.86
  9.1 3.1 %collective-permute-start.1 = (bf16[13312]{0:T(1024)(128)(2,1)S(1)}, bf16[13312]{0:T(1024)(128)(2,1)S(1)}, u32[]{:S(2)}, u32[]{:S(2)}) collective-permute-start(bf16[13312]{0:T(1024)(128)(2,1)S(1)} %pad_maximum_fusion.1), channel_id=1, source_target_pairs={{16,0},{24,8},{0,16},{8,24},{17,1},{25,9},{1,17},{9,25},{18,2},{26... | collective-permute-start | bytes 79880 | tf_op jit(solution)/shard_map/ppermute | solution.py:63
  12.2 1.8 %collective-permute-done.1 = bf16[13312]{0:T(1024)(128)(2,1)S(1)} collective-permute-done((bf16[13312]{0:T(1024)(128)(2,1)S(1)}, bf16[13312]{0:T(1024)(128)(2,1)S(1)}, u32[]{:S(2)}, u32[]{:S(2)}) %collective-permute-start.1) | collective-permute-done | bytes 26656 | tf_op jit(solution)/shard_map/ppermute | solution.py:63
  14.0 0.1 reshape.141
  14.1 0.4 fusion.36
  14.5 2.9 %fusion.11 = f32[3,3,3,64,128]{4,3,2,1,0:T(8,128)S(1)} fusion(bf16[9,17,17,64,1]{3,2,1,0,4:T(8,128)(2,1)S(1)} %get-tuple-element.22, bf16[4,8,8,128,1]{3,1,2,0,4:T(8,128)(2,1)S(1)} %bitcast.66, bf16[4,8,8]{2,1,0:T(8,128)(2,1)S(1)} %convert_element_type.58), kind=kOutput, calls=%fused_computation.13 | convolution fusion | flops 113377280 | bytes 1283712 | tf_op jit(solution)/shard_map/conv_general_dilated | solution.py:126
  17.4 0.0 copy-start.5
  17.4 0.1 constant_dynamic-slice_fusion.1
  17.5 0.1 collective-permute-start.2
  17.6 0.5 broadcast.92
  18.1 0.0 copy-done.5
  18.1 0.7 %reduce.15 = s32[2048]{0:T(1024)S(1)} reduce(s32[1,1,2048]{2,1,0:T(1,128)S(1)} %copy-done.5, s32[]{:T(128)} %broadcast.92), dimensions={0,1}, to_apply=%param.9.reduce_sub_computation.3 | reduce | bytes 16388 | tf_op args[3]
  18.8 0.1 reshape.145
  18.9 0.7 %fusion.24 = bf16[5,9,9,128]{3,2,1,0:T(8,128)(2,1)} fusion(bf16[4,1,9,128]{3,2,1,0:T(8,128)(2,1)S(1)} %bitcast.64, bf16[4,8,1,128]{3,2,1,0:T(2,128)(2,1)S(1)} %copy.27, bf16[4,8,8,128]{3,2,1,0:T(8,128)(2,1)S(1)} %bitcast_multiply_fusion), kind=kLoop, calls=%fused_computation.30 | loop fusion | flops 518400 | bytes 186624 | tf_op jit(solution)/shard_map/concatenate | solution.py:124
  19.6 0.0 collective-permute-done.2
  19.6 0.8 %pad_add_fusion = f32[28,32,128]{2,1,0:T(8,128)} fusion(f32[28,32,128]{2,1,0:T(8,128)S(1)} %collective-permute-done.2, f32[27,32,128]{2,1,0:T(8,128)S(1)} %get-tuple-element.19), kind=kLoop, calls=%fused_computation.20 | loop fusion | flops 114688 | bytes 1359872 | tf_op jit(solution)/shard_map/add | solution.py:143
  20.4 7.4 %all-to-all-start = ((f32[16,56,128]{2,1,0:T(8,128)}), f32[16,56,128]{2,1,0:T(8,128)S(1)}, u32[]{:S(2)}, u32[]{:S(2)}) async-start(f32[16,56,128]{2,1,0:T(8,128)} %bitcast.6), calls=%async_computation | async-start | bytes 917504 | tf_op jit(solution)/shard_map/all_to_all | solution.py:72
  27.8 0.1 copy.38
  27.9 0.2 pad.11
  28.1 0.2 copy.36
  28.4 0.0 copy-start.7
  28.4 0.2 slice.63
  28.5 0.0 copy-done
  28.6 0.5 copy-done.7
  29.0 0.8 %fusion.13 = f32[4,8,8,2,128]{4,2,3,1,0:T(8,128)S(1)} fusion(bf16[3,3,3,64,128]{4,3,2,1,0:T(8,128)(2,1)S(1)} %bitcast.55, bf16[9,17,1,7,2,64]{5,3,4,1,0,2:T(8,128)(2,1)S(1)} %slice.63, bf16[9,17,1,8,4,64]{5,3,4,1,0,2:T(8,128)(2,1)S(1)} %copy.36, pred[8,2]{0,1:T(4,128)(4,1)S(1)} %copy-done.7), kind=kOutput, calls=%fused_computation.15 | convolution fusion | flops 229378048 | bytes 1605392 | tf_op jit(solution)/shard_map/conv_general_dilated | solution.py:149
  29.8 0.0 copy-start.3
  29.8 0.1 copy.37
  29.9 0.7 %fusion.26 = bf16[1,1,4,8,1024]{4,3,2,1,0:T(8,128)(2,1)} fusion(f32[4,8,1,16,128]{4,1,3,0,2:T(8,128)S(1)} %bitcast.61, f32[4,8,8]{1,2,0:T(8,128)S(1)} %copy.38), kind=kLoop, calls=%fused_computation.33 | loop fusion | flops 65536 | bytes 197632 | tf_op jit(solution)/shard_map/convert_element_type | solution.py:158
  30.6 11.5 %all-to-all-done = f32[16,56,128]{2,1,0:T(8,128)S(1)} async-done(((f32[16,56,128]{2,1,0:T(8,128)}), f32[16,56,128]{2,1,0:T(8,128)S(1)}, u32[]{:S(2)}, u32[]{:S(2)}) %all-to-all-start) | async-done | bytes 458784 | tf_op jit(solution)/shard_map/all_to_all | solution.py:72
  42.2 0.8 %broadcast_in_dim.49 = f32[16,56,128]{2,1,0:T(8,128)} broadcast(f32[56,128]{1,0:T(8,128)S(1)} %broadcast_multiply_fusion.1), dimensions={1,2} | broadcast | bytes 487424 | tf_op jit(solution)/shard_map/broadcast_in_dim | solution.py:79
  43.0 4.0 %all-to-all-start.1 = ((f32[16,56,128]{2,1,0:T(8,128)}), f32[16,56,128]{2,1,0:T(8,128)S(1)}, u32[]{:S(2)}, u32[]{:S(2)}) async-start(f32[16,56,128]{2,1,0:T(8,128)} %broadcast_in_dim.49), calls=%async_computation.1 | async-start | bytes 917504 | tf_op jit(solution)/shard_map/all_to_all | solution.py:80
  47.0 0.0 copy-done.3
  47.0 6.2 %convolution_reduce_fusion = f32[8,16,16,64]{3,2,1,0:T(8,128)S(1)} fusion(bf16[3,3,3,64,128]{4,3,2,1,0:T(8,128)(2,1)S(1)} %bitcast.54, bf16[1,5,9,9,128]{4,3,2,1,0:T(8,128)(2,1)S(1)} %bitcast.63), kind=kOutput, calls=%fused_computation.12 | convolution fusion | flops 113246208 | bytes 1070336 | tf_op jit(solution)/shard_map/conv_general_dilated | solution.py:162
  53.2 0.3 mul.84
  53.5 0.3 mul.85
  53.8 0.0 copy-start.2
  53.8 0.3 squeeze.6
  54.1 0.6 copy-done.2
  54.8 0.8 %multiply_convert_fusion = bf16[1,1,8,16,1024]{4,3,2,1,0:T(8,128)(2,1)} fusion(f32[1,1,8,16,1024]{4,3,2,1,0:T(8,128)S(1)} %mul.85, f32[1,1,8,16,1024]{4,3,2,1,0:T(8,128)S(1)} %squeeze.6, bf16[1,1,8,16,1024]{4,3,2,1,0:T(8,128)(2,1)S(1)} %copy-done.2), kind=kLoop, calls=%fused_computation.19 | loop fusion | flops 524288 | bytes 1572864 | tf_op jit(solution)/shard_map/convert_element_type | solution.py:174
  55.6 4.7 %all-to-all-done.1 = f32[16,56,128]{2,1,0:T(8,128)S(1)} async-done(((f32[16,56,128]{2,1,0:T(8,128)}), f32[16,56,128]{2,1,0:T(8,128)S(1)}, u32[]{:S(2)}, u32[]{:S(2)}) %all-to-all-start.1) | async-done | bytes 458784 | tf_op jit(solution)/shard_map/all_to_all | solution.py:80
  60.3 0.1 collective-permute-start.3
  60.3 0.1 broadcast_in_dim.52
  60.5 1.6 %collective-permute-done.3 = f32[27,32,128]{2,1,0:T(8,128)S(1)} collective-permute-done((f32[27,32,128]{2,1,0:T(8,128)S(1)}, f32[27,32,128]{2,1,0:T(8,128)S(1)}, u32[]{:S(2)}, u32[]{:S(2)}) %collective-permute-start.3) | collective-permute-done | bytes 442400 | tf_op jit(solution)/shard_map/ppermute | solution.py:83
  62.2 0.0 copy-start.1
  62.2 0.9 %copy-done.1 = f32[27,2,32,128]{3,2,1,0:T(8,128)} copy-done((f32[27,2,32,128]{3,2,1,0:T(8,128)}, f32[27,2,32,128]{3,2,1,0:T(8,128)S(1)}, u32[]{:S(2)}) %copy-start.1) | copy-done | bytes 884760
  (19 shorter events, 0.3 us)
Async XLA Ops:
  0.6 27.9 %copy-start = (bf16[27,64,128]{2,1,0:T(8,128)(2,1)S(1)}, bf16[27,64,128]{2,1,0:T(8,128)(2,1)}, u32[]{:S(2)}) copy-start(bf16[27,64,128]{2,1,0:T(8,128)(2,1)} %param.10) | copy-start | bytes 1327108
  0.6 2.9 %copy-start.6 = (s32[1,1,256]{2,1,0:T(1,128)S(1)}, s32[1,1,256]{2,1,0:T(1,128)}, u32[]{:S(2)}) copy-start(s32[1,1,256]{2,1,0:T(1,128)} %param.7) | copy-start | bytes 3076
  0.7 3.0 %copy-start.4 = (bf16[1,1,4,8,1024]{4,3,2,1,0:T(8,128)(2,1)S(1)}, bf16[1,1,4,8,1024]{4,3,2,1,0:T(8,128)(2,1)}, u32[]{:S(2)}) copy-start(bf16[1,1,4,8,1024]{4,3,2,1,0:T(8,128)(2,1)} %param.6) | copy-start | bytes 196612
  3.9 4.9 %collective-permute-start = (bf16[12288]{0:T(1024)(128)(2,1)S(1)}, bf16[12288]{0:T(1024)(128)(2,1)S(1)}, u32[]{:S(2)}, u32[]{:S(2)}) collective-permute-start(bf16[12288]{0:T(1024)(128)(2,1)S(1)} %pad_maximum_fusion.2), channel_id=1, source_target_pairs={{8,0},{24,16},{0,8},{16,24},{9,1},{25,17},{1,9},{17,25},{10,2},{26... | collective-permute-start | bytes 73736 | tf_op jit(solution)/shard_map/ppermute | solution.py:63
  9.1 4.9 %collective-permute-start.1 = (bf16[13312]{0:T(1024)(128)(2,1)S(1)}, bf16[13312]{0:T(1024)(128)(2,1)S(1)}, u32[]{:S(2)}, u32[]{:S(2)}) collective-permute-start(bf16[13312]{0:T(1024)(128)(2,1)S(1)} %pad_maximum_fusion.1), channel_id=1, source_target_pairs={{16,0},{24,8},{0,16},{8,24},{17,1},{25,9},{1,17},{9,25},{18,2},{26... | collective-permute-start | bytes 79880 | tf_op jit(solution)/shard_map/ppermute | solution.py:63
  17.4 0.7 %copy-start.5 = (s32[1,1,2048]{2,1,0:T(1,128)S(1)}, s32[1,1,2048]{2,1,0:T(1,128)}, u32[]{:S(2)}) copy-start(s32[1,1,2048]{2,1,0:T(1,128)} %param.9) | copy-start | bytes 24580
  17.5 2.1 %collective-permute-start.2 = (f32[28,32,128]{2,1,0:T(8,128)S(1)}, f32[28,32,128]{2,1,0:T(8,128)S(1)}, u32[]{:S(2)}, u32[]{:S(2)}) collective-permute-start(f32[28,32,128]{2,1,0:T(8,128)S(1)} %pad.10), channel_id=1, source_target_pairs={{0,1},{1,0},{2,3},{3,2},{4,5},{5,4},{6,7},{7,6},{8,9},{9,8},{10,11... | collective-permute-start | bytes 1376264 | tf_op jit(solution)/shard_map/ppermute | solution.py:139
  20.4 21.7 %all-to-all-start = ((f32[16,56,128]{2,1,0:T(8,128)}), f32[16,56,128]{2,1,0:T(8,128)S(1)}, u32[]{:S(2)}, u32[]{:S(2)}) async-start(f32[16,56,128]{2,1,0:T(8,128)} %bitcast.6), calls=%async_computation | async-start | bytes 917504 | tf_op jit(solution)/shard_map/all_to_all | solution.py:72
  28.4 0.7 %copy-start.7 = (pred[8,2]{0,1:T(4,128)(4,1)S(1)}, pred[8,2]{0,1:T(4,128)(4,1)}, u32[]{:S(2)}) copy-start(pred[8,2]{0,1:T(4,128)(4,1)} %constant.78) | copy-start | bytes 52
  29.8 17.2 %copy-start.3 = (bf16[5,9,9,128]{3,2,1,0:T(8,128)(2,1)S(1)}, bf16[5,9,9,128]{3,2,1,0:T(8,128)(2,1)}, u32[]{:S(2)}) copy-start(bf16[5,9,9,128]{3,2,1,0:T(8,128)(2,1)} %fusion.24) | copy-start | bytes 311044
  43.0 17.2 %all-to-all-start.1 = ((f32[16,56,128]{2,1,0:T(8,128)}), f32[16,56,128]{2,1,0:T(8,128)S(1)}, u32[]{:S(2)}, u32[]{:S(2)}) async-start(f32[16,56,128]{2,1,0:T(8,128)} %broadcast_in_dim.49), calls=%async_computation.1 | async-start | bytes 917504 | tf_op jit(solution)/shard_map/all_to_all | solution.py:80
  53.8 1.0 %copy-start.2 = (bf16[1,1,8,16,1024]{4,3,2,1,0:T(8,128)(2,1)S(1)}, bf16[1,1,8,16,1024]{4,3,2,1,0:T(8,128)(2,1)}, u32[]{:S(2)}) copy-start(bf16[1,1,8,16,1024]{4,3,2,1,0:T(8,128)(2,1)} %param.8) | copy-start | bytes 786436
  60.3 1.9 %collective-permute-start.3 = (f32[27,32,128]{2,1,0:T(8,128)S(1)}, f32[27,32,128]{2,1,0:T(8,128)S(1)}, u32[]{:S(2)}, u32[]{:S(2)}) collective-permute-start(f32[27,32,128]{2,1,0:T(8,128)S(1)} %slice.65), channel_id=1, source_target_pairs={{0,1},{1,0},{2,3},{3,2},{4,5},{5,4},{6,7},{7,6},{8,9},{9,8},{10,11... | collective-permute-start | bytes 1327112 | tf_op jit(solution)/shard_map/ppermute | solution.py:83
  62.2 0.9 %copy-start.1 = (f32[27,2,32,128]{3,2,1,0:T(8,128)}, f32[27,2,32,128]{3,2,1,0:T(8,128)S(1)}, u32[]{:S(2)}) copy-start(f32[27,2,32,128]{3,2,1,0:T(8,128)S(1)} %bitcast_dynamic-update-slice_fusion.1) | copy-start | bytes 2654212

commit v16 on v14

--- a/solution.py
+++ b/solution.py
@@ -108,15 +108,24 @@
 
     extended = masked
     widened = cotangent
+    first_masked = (
+        coarse.reshape(size_x, size_y, merged)[:, :, :channels_in]
+        * coarse_keep[:, :, :1, 0]
+    ).reshape(size_x, size_y, 1, channels_in)
+    first_cot = (
+        fine_grad.reshape(fine_x, fine_y, fine_merged)[:, :, (fine_z - 1) * channels_out :]
+        * fine_keep[:, :, fine_z - 1 :, 0].astype(jnp.bfloat16)
+    ).reshape(fine_x, fine_y, 1, channels_out)
     for axis in (2, 1, 0):
         direction = tuple(1 if other == axis else 0 for other in range(3))
         last = widened.shape[axis]
-        got_masked, got_cot = halo_exchange(
+        faces = (
             lax.slice_in_dim(extended, 0, 1, axis=axis),
             lax.slice_in_dim(widened, last - 1, last, axis=axis),
-            regions,
-            direction,
         )
+        if axis == 2:
+            faces = (first_masked, first_cot)
+        got_masked, got_cot = halo_exchange(*faces, regions, direction)
         extended = jnp.concatenate([extended, got_masked], axis=axis)
         widened = jnp.concatenate([got_cot, widened], axis=axis)
     full = lax.conv_general_dilated(

time: 63.5 us -> 64.4 us (1.014)
  other arithmetic: 4.95 us -> 7.84 us
  starting transfers between devices: 17.7 us -> 15.9 us
    ppermute x2, waiting for transfers between devices: 3.63 us -> 2.16 us  [halo_exchange(): got = lax.ppermute(packed, 'brick', both)]
    ppermute x1, waiting for transfers between devices: 0.01 us -> 1.04 us  [body(): got = lax.ppermute(theirs, 'core', [(0, 1), (1, 0)])]
    all_to_all x1, starting transfers between devices: 7.37 us -> 6.35 us  [all_reduce(): lax.all_to_all(rows.reshape(devices, chunk, lanes), OTHERS, 0, 0, tiled=T...]
    select_n x2, other arithmetic: 0.07 us -> 0.79 us  [halo_exchange(): jnp.where(sends_down, masked_piece.reshape(-1), zero)]
    unnamed x1, other arithmetic: 0.67 us -> 1.36 us
    convert_element_type x1, other arithmetic: 0.02 us -> 0.7 us  [body(): coarse_mask.reshape(size_x, size_y, size_z, 1).astype(jnp.bfloat16)]
    unnamed x17 -> x18, local copies, waits for them, and re-layouts: 2.55 us -> 2.66 us
  transfers between devices with their start and end apart: 6 -> 6, of which waited for: 5 -> 5; matrix products, arithmetic and copies ran while one was open for 20% -> 22% of each run, Pallas kernels for 0% -> 0%
where the time goes in v16:
time: 64.4 us; the launch traced here: 63.8 us
  waiting for transfers between devices  20.8 us (32%)
  starting transfers between devices  15.9 us (25%)
  matrix products  9.78 us (15%)
  local copies, waits for them, and re-layouts  8.34 us (13%)
  other arithmetic  7.84 us (12%)
  between operations  1.07 us (2%)
    all_to_all x1, waiting for transfers between devices, all_reduce(): lax.all_to_all(rows.reshape(devices, chunk, lanes), OTHERS, 0, 0, tiled=T...  11.4 us
    all_to_all x1, starting transfers between devices, all_reduce(): lax.all_to_all(rows.reshape(devices, chunk, lanes), OTHERS, 0, 0, tiled=T...  6.35 us
    conv_general_dilated x1, matrix products, body(): lax.conv_general_dilated(extended[None], flipped, (1, 1, 1), ((1, 0), (1,...  6.18 us
    ppermute x2, starting transfers between devices, halo_exchange(): got = lax.ppermute(packed, 'brick', both)  5.68 us
    all_to_all x1, waiting for transfers between devices, all_spread(): half = lax.all_to_all(spread, OTHERS, 0, 0, tiled=True)  4.61 us
    all_to_all x1, starting transfers between devices, all_spread(): half = lax.all_to_all(spread, OTHERS, 0, 0, tiled=True)  3.76 us
    conv_general_dilated x1, matrix products, body(): lax.conv_general_dilated(widened[..., None], masked[..., None], (1, 1, 1)...  2.85 us
    unnamed x18, local copies, waits for them, and re-layouts  2.66 us
  transfers between devices with their start and end apart: 6, of which 5 were waited for; matrix products, arithmetic and copies ran while one was open for 22% of the time, Pallas kernels for 0%

profile of v16, /device:TPU:0, one launch (start us, length us, event | category | flops | bytes accessed | tf_op | source)
XLA Modules:
  0.0 63.8 jit_solution(7083152052703617500)
XLA Ops:
  0.6 0.0 copy-start
  0.6 0.0 copy-start.6
  0.7 0.5 broadcast.90
  1.2 1.4 %reduce.14 = s32[2048]{0:T(1024)S(1)} reduce(s32[1,1,2048]{2,1,0:T(1,128)} %param.9, s32[]{:T(128)} %broadcast.90), dimensions={0,1}, to_apply=%param.9.reduce_sub_computation.3 | reduce | bytes 16388 | tf_op args[3]
  2.6 0.1 reshape.171
  2.6 0.0 copy-start.2
  2.7 0.2 fusion.29
  2.8 0.9 %fusion.30 = bf16[8,16,64]{2,1,0:T(8,128)(2,1)S(1)} fusion(bf16[8,16,1024]{2,1,0:T(8,128)(2,1)} %bitcast.69, pred[]{:T(512)S(6)} %lt.31, bf16[8,16]{1,0:T(8,128)(2,1)S(1)} %fusion.29), kind=kLoop, calls=%fused_computation.42 | loop fusion | flops 16384 | bytes 33025 | tf_op jit(solution)/shard_map/jit(_where)/select_n | solution.py:60
  3.7 0.1 select_n.81
  3.8 0.7 %convert_reduce_fusion.1 = bf16[256]{0:T(256)(128)(2,1)S(1)} fusion(s32[1,1,256]{2,1,0:T(1,128)} %param.7), kind=kLoop, calls=%fused_computation.53 | loop fusion | flops 256 | bytes 1536 | tf_op jit(solution)/shard_map/convert_element_type | solution.py:102
  4.5 0.1 convert_element_type.74
  4.6 0.1 copy.43
  4.7 0.8 %fusion.33 = bf16[4096]{0:T(1024)(128)(2,1)S(1)} fusion(bf16[4,8,1024]{2,1,0:T(8,128)(2,1)} %bitcast.72, pred[]{:T(512)S(6)} %ge.7, bf16[4,8]{1,0:T(4,128)(2,1)S(1)} %bitcast.77), kind=kLoop, calls=%fused_computation.51 | loop fusion | flops 8192 | bytes 16449 | tf_op jit(solution)/shard_map/jit(_where)/select_n | solution.py:59
  5.5 3.0 %collective-permute-start = (bf16[12288]{0:T(1024)(128)(2,1)S(1)}, bf16[12288]{0:T(1024)(128)(2,1)S(1)}, u32[]{:S(2)}, u32[]{:S(2)}) collective-permute-start(bf16[12288]{0:T(1024)(128)(2,1)S(1)} %pad_maximum_fusion.2), channel_id=1, source_target_pairs={{8,0},{24,16},{0,8},{16,24},{9,1},{25,17},{1,9},{17,25},{10,2},{26... | collective-permute-start | bytes 73736 | tf_op jit(solution)/shard_map/ppermute | solution.py:63
  8.5 1.3 %reshape.173 = bf16[8,16,16,64]{3,2,1,0:T(8,128)(2,1)S(1)} reshape(bf16[1,1,8,16,1024]{4,3,2,1,0:T(8,128)(2,1)} %param.11) | data formatting | bytes 524288 | tf_op jit(solution)/shard_map/reshape | solution.py:105
  9.8 0.7 %convert_reduce_fusion = bf16[2048]{0:T(1024)(128)(2,1)S(1)} fusion(s32[1,1,2048]{2,1,0:T(1,128)} %param.9), kind=kLoop, calls=%fused_computation.52 | loop fusion | flops 2048 | bytes 12288 | tf_op jit(solution)/shard_map/convert_element_type | solution.py:105
  10.6 0.1 convert_element_type.73
  10.7 0.0 copy-done.2
  10.7 0.1 convert_element_type.77
  10.8 0.3 broadcast_multiply_fusion
  11.1 0.0 copy-done.6
  11.1 0.1 bitcast_multiply_fusion
  11.2 0.0 collective-permute-done
  11.3 0.1 reshape.199
  11.4 0.1 select_n.86
  11.6 2.7 %collective-permute-start.1 = (bf16[13312]{0:T(1024)(128)(2,1)S(1)}, bf16[13312]{0:T(1024)(128)(2,1)S(1)}, u32[]{:S(2)}, u32[]{:S(2)}) collective-permute-start(bf16[13312]{0:T(1024)(128)(2,1)S(1)} %pad_maximum_fusion.1), channel_id=1, source_target_pairs={{16,0},{24,8},{0,16},{8,24},{17,1},{25,9},{1,17},{9,25},{18,2},{26... | collective-permute-start | bytes 79880 | tf_op jit(solution)/shard_map/ppermute | solution.py:63
  14.2 2.2 %collective-permute-done.1 = bf16[13312]{0:T(1024)(128)(2,1)S(1)} collective-permute-done((bf16[13312]{0:T(1024)(128)(2,1)S(1)}, bf16[13312]{0:T(1024)(128)(2,1)S(1)}, u32[]{:S(2)}, u32[]{:S(2)}) %collective-permute-start.1) | collective-permute-done | bytes 26656 | tf_op jit(solution)/shard_map/ppermute | solution.py:63
  16.4 0.1 reshape.174
  16.5 0.4 fusion.38
  16.9 2.9 %fusion.11 = f32[3,3,3,64,128]{4,3,2,1,0:T(8,128)S(1)} fusion(bf16[9,17,17,64,1]{3,2,1,0,4:T(8,128)(2,1)S(1)} %get-tuple-element.20, bf16[4,8,8,128,1]{3,1,2,0,4:T(8,128)(2,1)S(1)} %bitcast.74, bf16[4,8,8]{2,1,0:T(8,128)(2,1)S(1)} %convert_element_type.73), kind=kOutput, calls=%fused_computation.13 | convolution fusion | flops 113377280 | bytes 1283712 | tf_op jit(solution)/shard_map/conv_general_dilated | solution.py:131
  19.8 0.1 collective-permute-start.2
  19.9 0.7 %fusion.24 = bf16[5,9,9,128]{3,2,1,0:T(8,128)(2,1)} fusion(bf16[4,1,9,128]{3,2,1,0:T(8,128)(2,1)S(1)} %bitcast.75, bf16[4,8,1,128]{3,2,1,0:T(2,128)(2,1)S(1)} %copy.29, bf16[4,8,8,128]{3,2,1,0:T(8,128)(2,1)S(1)} %bitcast_multiply_fusion), kind=kLoop, calls=%fused_computation.29 | loop fusion | flops 518400 | bytes 186624 | tf_op jit(solution)/shard_map/concatenate | solution.py:129
  20.6 1.0 %collective-permute-done.2 = f32[27,32,128]{2,1,0:T(8,128)S(1)} collective-permute-done((f32[27,32,128]{2,1,0:T(8,128)S(1)}, f32[27,32,128]{2,1,0:T(8,128)S(1)}, u32[]{:S(2)}, u32[]{:S(2)}) %collective-permute-start.2) | collective-permute-done | bytes 442400 | tf_op jit(solution)/shard_map/ppermute | solution.py:143
  21.7 0.1 dynamic-slice_add_fusion
  21.7 0.8 %pad.6 = f32[896,128]{1,0:T(8,128)} pad(f32[864,128]{1,0:T(8,128)S(1)} %bitcast.64, f32[]{:T(128)} %constant.58.clone.1), padding=0_32x0_0 | pad | bytes 901124 | tf_op jit(solution)/shard_map/jit(_pad)/pad | solution.py:73
  22.5 6.4 %all-to-all-start = ((f32[16,56,128]{2,1,0:T(8,128)}), f32[16,56,128]{2,1,0:T(8,128)S(1)}, u32[]{:S(2)}, u32[]{:S(2)}) async-start(f32[16,56,128]{2,1,0:T(8,128)} %bitcast.11), calls=%async_computation | async-start | bytes 917504 | tf_op jit(solution)/shard_map/all_to_all | solution.py:74
  28.9 0.1 copy.40
  29.0 0.2 pad.7
  29.2 0.2 copy.38
  29.4 0.0 copy-start.7
  29.4 0.2 slice.74
  29.6 0.0 copy-done
  29.6 0.5 copy-done.7
  30.1 0.8 %fusion.13 = f32[4,8,8,2,128]{4,2,3,1,0:T(8,128)S(1)} fusion(bf16[3,3,3,64,128]{4,3,2,1,0:T(8,128)(2,1)S(1)} %bitcast.59, bf16[9,17,1,7,2,64]{5,3,4,1,0,2:T(8,128)(2,1)S(1)} %slice.74, bf16[9,17,1,8,4,64]{5,3,4,1,0,2:T(8,128)(2,1)S(1)} %copy.38, pred[8,2]{0,1:T(4,128)(4,1)S(1)} %copy-done.7), kind=kOutput, calls=%fused_computation.15 | convolution fusion | flops 229378048 | bytes 1605392 | tf_op jit(solution)/shard_map/conv_general_dilated | solution.py:150
  30.9 0.0 copy-start.5
  30.9 0.1 copy.39
  31.0 0.7 %fusion.26 = bf16[1,1,4,8,1024]{4,3,2,1,0:T(8,128)(2,1)} fusion(f32[4,8,1,16,128]{4,1,3,0,2:T(8,128)S(1)} %bitcast.68, f32[4,8,8]{1,2,0:T(8,128)S(1)} %copy.40), kind=kLoop, calls=%fused_computation.32 | loop fusion | flops 65536 | bytes 197632 | tf_op jit(solution)/shard_map/convert_element_type | solution.py:159
  31.7 11.4 %all-to-all-done = f32[16,56,128]{2,1,0:T(8,128)S(1)} async-done(((f32[16,56,128]{2,1,0:T(8,128)}), f32[16,56,128]{2,1,0:T(8,128)S(1)}, u32[]{:S(2)}, u32[]{:S(2)}) %all-to-all-start) | async-done | bytes 458784 | tf_op jit(solution)/shard_map/all_to_all | solution.py:74
  43.1 0.8 %broadcast_in_dim.49 = f32[16,56,128]{2,1,0:T(8,128)} broadcast(f32[56,128]{1,0:T(8,128)S(1)} %broadcast_multiply_fusion.1), dimensions={1,2} | broadcast | bytes 487424 | tf_op jit(solution)/shard_map/broadcast_in_dim | solution.py:80
  43.9 3.8 %all-to-all-start.1 = ((f32[16,56,128]{2,1,0:T(8,128)}), f32[16,56,128]{2,1,0:T(8,128)S(1)}, u32[]{:S(2)}, u32[]{:S(2)}) async-start(f32[16,56,128]{2,1,0:T(8,128)} %broadcast_in_dim.49), calls=%async_computation.1 | async-start | bytes 917504 | tf_op jit(solution)/shard_map/all_to_all | solution.py:81
  47.7 0.0 copy-done.5
  47.7 6.2 %convolution_reduce_fusion = f32[8,16,16,64]{3,2,1,0:T(8,128)S(1)} fusion(bf16[3,3,3,64,128]{4,3,2,1,0:T(8,128)(2,1)S(1)} %bitcast.58, bf16[1,5,9,9,128]{4,3,2,1,0:T(8,128)(2,1)S(1)} %bitcast.71), kind=kOutput, calls=%fused_computation.12 | convolution fusion | flops 113246208 | bytes 1070336 | tf_op jit(solution)/shard_map/conv_general_dilated | solution.py:163
  53.9 0.3 mul.107
  54.2 0.3 mul.108
  54.6 0.0 copy-start.4
  54.6 0.3 squeeze.8
  54.9 0.6 copy-done.4
  55.5 0.8 %multiply_convert_fusion = bf16[1,1,8,16,1024]{4,3,2,1,0:T(8,128)(2,1)} fusion(f32[1,1,8,16,1024]{4,3,2,1,0:T(8,128)S(1)} %mul.108, f32[1,1,8,16,1024]{4,3,2,1,0:T(8,128)S(1)} %squeeze.8, bf16[1,1,8,16,1024]{4,3,2,1,0:T(8,128)(2,1)S(1)} %copy-done.4), kind=kLoop, calls=%fused_computation.19 | loop fusion | flops 524288 | bytes 1572864 | tf_op jit(solution)/shard_map/convert_element_type | solution.py:175
  56.3 4.6 %all-to-all-done.1 = f32[16,56,128]{2,1,0:T(8,128)S(1)} async-done(((f32[16,56,128]{2,1,0:T(8,128)}), f32[16,56,128]{2,1,0:T(8,128)S(1)}, u32[]{:S(2)}, u32[]{:S(2)}) %all-to-all-start.1) | async-done | bytes 458784 | tf_op jit(solution)/shard_map/all_to_all | solution.py:81
  60.9 0.1 collective-permute-start.3
  61.0 0.1 broadcast_in_dim.52
  61.2 1.6 %collective-permute-done.3 = f32[27,32,128]{2,1,0:T(8,128)S(1)} collective-permute-done((f32[27,32,128]{2,1,0:T(8,128)S(1)}, f32[27,32,128]{2,1,0:T(8,128)S(1)}, u32[]{:S(2)}, u32[]{:S(2)}) %collective-permute-start.3) | collective-permute-done | bytes 442400 | tf_op jit(solution)/shard_map/ppermute | solution.py:84
  62.9 0.0 copy-start.1
  62.9 0.9 %copy-done.1 = f32[27,2,32,128]{3,2,1,0:T(8,128)} copy-done((f32[27,2,32,128]{3,2,1,0:T(8,128)}, f32[27,2,32,128]{3,2,1,0:T(8,128)S(1)}, u32[]{:S(2)}) %copy-start.1) | copy-done | bytes 884760
  (20 shorter events, 0.3 us)
Async XLA Ops:
  0.6 29.0 %copy-start = (bf16[27,64,128]{2,1,0:T(8,128)(2,1)S(1)}, bf16[27,64,128]{2,1,0:T(8,128)(2,1)}, u32[]{:S(2)}) copy-start(bf16[27,64,128]{2,1,0:T(8,128)(2,1)} %param.10) | copy-start | bytes 1327108
  0.6 10.5 %copy-start.6 = (bf16[1,1,4,8,1024]{4,3,2,1,0:T(8,128)(2,1)S(1)}, bf16[1,1,4,8,1024]{4,3,2,1,0:T(8,128)(2,1)}, u32[]{:S(2)}) copy-start(bf16[1,1,4,8,1024]{4,3,2,1,0:T(8,128)(2,1)} %param.6) | copy-start | bytes 196612
  2.6 8.0 %copy-start.2 = (s32[8,16,16,1]{2,1,0,3:T(8,128)}, s32[8,16,16,1]{2,1,0,3:T(8,128)S(1)}, u32[]{:S(2)}) copy-start(s32[8,16,16,1]{2,1,0,3:T(8,128)S(1)} %reshape.171) | copy-start | bytes 24580
  5.5 5.8 %collective-permute-start = (bf16[12288]{0:T(1024)(128)(2,1)S(1)}, bf16[12288]{0:T(1024)(128)(2,1)S(1)}, u32[]{:S(2)}, u32[]{:S(2)}) collective-permute-start(bf16[12288]{0:T(1024)(128)(2,1)S(1)} %pad_maximum_fusion.2), channel_id=1, source_target_pairs={{8,0},{24,16},{0,8},{16,24},{9,1},{25,17},{1,9},{17,25},{10,2},{26... | collective-permute-start | bytes 73736 | tf_op jit(solution)/shard_map/ppermute | solution.py:63
  11.6 4.8 %collective-permute-start.1 = (bf16[13312]{0:T(1024)(128)(2,1)S(1)}, bf16[13312]{0:T(1024)(128)(2,1)S(1)}, u32[]{:S(2)}, u32[]{:S(2)}) collective-permute-start(bf16[13312]{0:T(1024)(128)(2,1)S(1)} %pad_maximum_fusion.1), channel_id=1, source_target_pairs={{16,0},{24,8},{0,16},{8,24},{17,1},{25,9},{1,17},{9,25},{18,2},{26... | collective-permute-start | bytes 79880 | tf_op jit(solution)/shard_map/ppermute | solution.py:63
  19.8 1.9 %collective-permute-start.2 = (f32[27,32,128]{2,1,0:T(8,128)S(1)}, f32[27,32,128]{2,1,0:T(8,128)S(1)}, u32[]{:S(2)}, u32[]{:S(2)}) collective-permute-start(f32[27,32,128]{2,1,0:T(8,128)S(1)} %constant_dynamic-slice_fusion), channel_id=1, source_target_pairs={{0,1},{1,0},{2,3},{3,2},{4,5},{5,4},{6,7},{7,6},{8,9},{9,8},{10,11... | collective-permute-start | bytes 1327112 | tf_op jit(solution)/shard_map/ppermute | solution.py:143
  22.5 20.5 %all-to-all-start = ((f32[16,56,128]{2,1,0:T(8,128)}), f32[16,56,128]{2,1,0:T(8,128)S(1)}, u32[]{:S(2)}, u32[]{:S(2)}) async-start(f32[16,56,128]{2,1,0:T(8,128)} %bitcast.11), calls=%async_computation | async-start | bytes 917504 | tf_op jit(solution)/shard_map/all_to_all | solution.py:74
  29.4 0.7 %copy-start.7 = (pred[8,2]{0,1:T(4,128)(4,1)S(1)}, pred[8,2]{0,1:T(4,128)(4,1)}, u32[]{:S(2)}) copy-start(pred[8,2]{0,1:T(4,128)(4,1)} %constant.76) | copy-start | bytes 52
  30.9 16.8 %copy-start.5 = (bf16[5,9,9,128]{3,2,1,0:T(8,128)(2,1)S(1)}, bf16[5,9,9,128]{3,2,1,0:T(8,128)(2,1)}, u32[]{:S(2)}) copy-start(bf16[5,9,9,128]{3,2,1,0:T(8,128)(2,1)} %fusion.24) | copy-start | bytes 311044
  43.9 17.0 %all-to-all-start.1 = ((f32[16,56,128]{2,1,0:T(8,128)}), f32[16,56,128]{2,1,0:T(8,128)S(1)}, u32[]{:S(2)}, u32[]{:S(2)}) async-start(f32[16,56,128]{2,1,0:T(8,128)} %broadcast_in_dim.49), calls=%async_computation.1 | async-start | bytes 917504 | tf_op jit(solution)/shard_map/all_to_all | solution.py:81
  47.7 6.2 %copy-start.3 = (s32[8,16,16,1]{2,1,0,3:T(8,128)S(1)}, s32[8,16,16,1]{2,1,0,3:T(8,128)}, u32[]{:S(2)}) copy-start(s32[8,16,16,1]{2,1,0,3:T(8,128)} %copy-done.2) | copy-start | bytes 24580
  54.6 1.0 %copy-start.4 = (bf16[1,1,8,16,1024]{4,3,2,1,0:T(8,128)(2,1)S(1)}, bf16[1,1,8,16,1024]{4,3,2,1,0:T(8,128)(2,1)}, u32[]{:S(2)}) copy-start(bf16[1,1,8,16,1024]{4,3,2,1,0:T(8,128)(2,1)} %param.8) | copy-start | bytes 786436
  60.9 1.9 %collective-permute-start.3 = (f32[27,32,128]{2,1,0:T(8,128)S(1)}, f32[27,32,128]{2,1,0:T(8,128)S(1)}, u32[]{:S(2)}, u32[]{:S(2)}) collective-permute-start(f32[27,32,128]{2,1,0:T(8,128)S(1)} %bitcast.62), channel_id=1, source_target_pairs={{0,1},{1,0},{2,3},{3,2},{4,5},{5,4},{6,7},{7,6},{8,9},{9,8},{10,11... | collective-permute-start | bytes 1327112 | tf_op jit(solution)/shard_map/ppermute | solution.py:84
  62.9 0.9 %copy-start.1 = (f32[27,2,32,128]{3,2,1,0:T(8,128)}, f32[27,2,32,128]{3,2,1,0:T(8,128)S(1)}, u32[]{:S(2)}) copy-start(f32[27,2,32,128]{3,2,1,0:T(8,128)S(1)} %bitcast_dynamic-update-slice_fusion) | copy-start | bytes 2654212

commit v17 on v14

--- a/solution.py
+++ b/solution.py
@@ -108,7 +108,7 @@
 
     extended = masked
     widened = cotangent
-    for axis in (2, 1, 0):
+    for axis in (1, 2, 0):
         direction = tuple(1 if other == axis else 0 for other in range(3))
         last = widened.shape[axis]
         got_masked, got_cot = halo_exchange(

time: 63.5 us -> 63.5 us (level)
  no operation moved by 1% of the time
where the time goes in v17:
time: 63.5 us; the launch traced here: 63 us
  waiting for transfers between devices  21.6 us (34%)
  starting transfers between devices  17.5 us (28%)
  matrix products  9.78 us (15%)
  local copies, waits for them, and re-layouts  8.17 us (13%)
  other arithmetic  4.98 us (8%)
  between operations  1.01 us (2%)
    all_to_all x1, waiting for transfers between devices, all_reduce(): lax.all_to_all(rows.reshape(devices, chunk, lanes), OTHERS, 0, 0, tiled=T...  11.5 us
    all_to_all x1, starting transfers between devices, all_reduce(): lax.all_to_all(rows.reshape(devices, chunk, lanes), OTHERS, 0, 0, tiled=T...  7.33 us
    conv_general_dilated x1, matrix products, body(): lax.conv_general_dilated(extended[None], flipped, (1, 1, 1), ((1, 0), (1,...  6.18 us
    ppermute x2, starting transfers between devices, halo_exchange(): got = lax.ppermute(packed, 'brick', both)  6.06 us
    all_to_all x1, waiting for transfers between devices, all_spread(): half = lax.all_to_all(spread, OTHERS, 0, 0, tiled=True)  4.66 us
    all_to_all x1, starting transfers between devices, all_spread(): half = lax.all_to_all(spread, OTHERS, 0, 0, tiled=True)  3.97 us
    ppermute x2, waiting for transfers between devices, halo_exchange(): got = lax.ppermute(packed, 'brick', both)  3.77 us
    conv_general_dilated x1, matrix products, body(): lax.conv_general_dilated(widened[..., None], masked[..., None], (1, 1, 1)...  2.85 us
  transfers between devices with their start and end apart: 6, of which 5 were waited for; matrix products, arithmetic and copies ran while one was open for 20% of the time, Pallas kernels for 0%

profile of v17, /device:TPU:0, one launch (start us, length us, event | category | flops | bytes accessed | tf_op | source)
XLA Modules:
  0.0 63.0 jit_solution(1112358461177870662)
XLA Ops:
  0.6 0.0 copy-start
  0.6 0.0 copy-start.6
  0.7 0.0 copy-start.4
  0.7 1.4 %reshape.149 = bf16[8,16,16,64]{3,2,1,0:T(8,128)(2,1)S(1)} reshape(bf16[1,1,8,16,1024]{4,3,2,1,0:T(8,128)(2,1)} %param.11) | data formatting | bytes 524288 | tf_op jit(solution)/shard_map/reshape | solution.py:105
  2.1 0.7 %convert_reduce_fusion = bf16[2048]{0:T(1024)(128)(2,1)S(1)} fusion(s32[1,1,2048]{2,1,0:T(1,128)} %param.9), kind=kLoop, calls=%fused_computation.50 | loop fusion | flops 2048 | bytes 12288 | tf_op jit(solution)/shard_map/convert_element_type | solution.py:105
  2.8 0.1 convert_element_type.59
  2.9 0.3 broadcast_multiply_fusion
  3.3 0.1 select_n.81
  3.4 0.0 copy-done.6
  3.4 0.1 convert_element_type.57
  3.5 0.0 copy-done.4
  3.5 0.1 bitcast_multiply_fusion
  3.6 4.1 %collective-permute-start = (bf16[12288]{0:T(1024)(128)(2,1)S(1)}, bf16[12288]{0:T(1024)(128)(2,1)S(1)}, u32[]{:S(2)}, u32[]{:S(2)}) collective-permute-start(bf16[12288]{0:T(1024)(128)(2,1)S(1)} %pad_maximum_fusion.2), channel_id=1, source_target_pairs={{16,0},{24,8},{0,16},{8,24},{17,1},{25,9},{1,17},{9,25},{18,2},{26... | collective-permute-start | bytes 73736 | tf_op jit(solution)/shard_map/ppermute | solution.py:63
  7.7 1.8 %collective-permute-done = bf16[12288]{0:T(1024)(128)(2,1)S(1)} collective-permute-done((bf16[12288]{0:T(1024)(128)(2,1)S(1)}, bf16[12288]{0:T(1024)(128)(2,1)S(1)}, u32[]{:S(2)}, u32[]{:S(2)}) %collective-permute-start) | collective-permute-done | bytes 24608 | tf_op jit(solution)/shard_map/ppermute | solution.py:63
  9.6 0.1 reshape.150
  9.6 0.3 fusion.27
  9.9 0.1 select_n.86
  10.0 0.1 fusion.29
  10.1 2.0 %collective-permute-start.1 = (bf16[13312]{0:T(1024)(128)(2,1)S(1)}, bf16[13312]{0:T(1024)(128)(2,1)S(1)}, u32[]{:S(2)}, u32[]{:S(2)}) collective-permute-start(bf16[13312]{0:T(1024)(128)(2,1)S(1)} %pad_maximum_fusion.1), channel_id=1, source_target_pairs={{8,0},{24,16},{0,8},{16,24},{9,1},{25,17},{1,9},{17,25},{10,2},{26... | collective-permute-start | bytes 79880 | tf_op jit(solution)/shard_map/ppermute | solution.py:63
  12.1 2.0 %collective-permute-done.1 = bf16[13312]{0:T(1024)(128)(2,1)S(1)} collective-permute-done((bf16[13312]{0:T(1024)(128)(2,1)S(1)}, bf16[13312]{0:T(1024)(128)(2,1)S(1)}, u32[]{:S(2)}, u32[]{:S(2)}) %collective-permute-start.1) | collective-permute-done | bytes 26656 | tf_op jit(solution)/shard_map/ppermute | solution.py:63
  14.0 0.1 reshape.177
  14.1 0.4 fusion.35
  14.5 0.0 copy-start.5
  14.6 2.9 %fusion.11 = f32[3,3,3,64,128]{4,3,2,1,0:T(8,128)S(1)} fusion(bf16[9,17,17,64,1]{3,2,1,0,4:T(8,128)(2,1)S(1)} %get-tuple-element.20, bf16[4,8,8,128,1]{3,1,2,0,4:T(8,128)(2,1)S(1)} %bitcast.69, bf16[4,8,8]{2,1,0:T(8,128)(2,1)S(1)} %convert_element_type.57), kind=kOutput, calls=%fused_computation.13 | convolution fusion | flops 113377280 | bytes 1283712 | tf_op jit(solution)/shard_map/conv_general_dilated | solution.py:122
  17.5 0.1 collective-permute-start.2
  17.5 0.5 broadcast.90
  18.0 0.0 copy-done.5
  18.0 0.7 %reduce.15 = s32[2048]{0:T(1024)S(1)} reduce(s32[1,1,2048]{2,1,0:T(1,128)S(1)} %copy-done.5, s32[]{:T(128)} %broadcast.90), dimensions={0,1}, to_apply=%param.9.reduce_sub_computation.3 | reduce | bytes 16388 | tf_op args[3]
  18.7 0.1 reshape.155
  18.8 0.7 %fusion.24 = bf16[5,9,9,128]{3,2,1,0:T(8,128)(2,1)} fusion(bf16[4,9,1,128]{3,2,1,0:T(2,128)(2,1)S(1)} %reshape.178, bf16[4,1,8,128]{3,2,1,0:T(8,128)(2,1)S(1)} %slice_bitcast_fusion.1, bf16[4,8,8,128]{3,2,1,0:T(8,128)(2,1)S(1)} %bitcast_multiply_fusion), kind=kLoop, calls=%fused_computation.29 | loop fusion | flops 518400 | bytes 186624 | tf_op jit(solution)/shard_map/concatenate | solution.py:120
  19.5 0.0 collective-permute-done.2
  19.5 0.1 dynamic-slice_add_fusion
  19.6 0.8 %pad.6 = f32[896,128]{1,0:T(8,128)} pad(f32[864,128]{1,0:T(8,128)S(1)} %bitcast.62, f32[]{:T(128)} %constant.58.clone.1), padding=0_32x0_0 | pad | bytes 901124 | tf_op jit(solution)/shard_map/jit(_pad)/pad | solution.py:73
  20.4 7.3 %all-to-all-start = ((f32[16,56,128]{2,1,0:T(8,128)}), f32[16,56,128]{2,1,0:T(8,128)S(1)}, u32[]{:S(2)}, u32[]{:S(2)}) async-start(f32[16,56,128]{2,1,0:T(8,128)} %bitcast.7), calls=%async_computation | async-start | bytes 917504 | tf_op jit(solution)/shard_map/all_to_all | solution.py:74
  27.8 0.1 copy.33
  27.8 0.2 pad.7
  28.1 0.2 copy.31
  28.3 0.0 copy-start.7
  28.3 0.2 slice.63
  28.5 0.0 copy-done
  28.5 0.5 copy-done.7
  29.0 0.8 %fusion.13 = f32[4,8,8,2,128]{4,2,3,1,0:T(8,128)S(1)} fusion(bf16[3,3,3,64,128]{4,3,2,1,0:T(8,128)(2,1)S(1)} %bitcast.57, bf16[9,17,1,7,2,64]{5,3,4,1,0,2:T(8,128)(2,1)S(1)} %slice.63, bf16[9,17,1,8,4,64]{5,3,4,1,0,2:T(8,128)(2,1)S(1)} %copy.31, pred[8,2]{0,1:T(4,128)(4,1)S(1)} %copy-done.7), kind=kOutput, calls=%fused_computation.15 | convolution fusion | flops 229378048 | bytes 1605392 | tf_op jit(solution)/shard_map/conv_general_dilated | solution.py:141
  29.7 0.0 copy-start.3
  29.7 0.1 copy.32
  29.8 0.7 %fusion.26 = bf16[1,1,4,8,1024]{4,3,2,1,0:T(8,128)(2,1)} fusion(f32[4,8,1,16,128]{4,1,3,0,2:T(8,128)S(1)} %bitcast.66, f32[4,8,8]{1,2,0:T(8,128)S(1)} %copy.33), kind=kLoop, calls=%fused_computation.33 | loop fusion | flops 65536 | bytes 197632 | tf_op jit(solution)/shard_map/convert_element_type | solution.py:150
  30.6 11.5 %all-to-all-done = f32[16,56,128]{2,1,0:T(8,128)S(1)} async-done(((f32[16,56,128]{2,1,0:T(8,128)}), f32[16,56,128]{2,1,0:T(8,128)S(1)}, u32[]{:S(2)}, u32[]{:S(2)}) %all-to-all-start) | async-done | bytes 458784 | tf_op jit(solution)/shard_map/all_to_all | solution.py:74
  42.1 0.8 %broadcast_in_dim.49 = f32[16,56,128]{2,1,0:T(8,128)} broadcast(f32[56,128]{1,0:T(8,128)S(1)} %broadcast_multiply_fusion.1), dimensions={1,2} | broadcast | bytes 487424 | tf_op jit(solution)/shard_map/broadcast_in_dim | solution.py:80
  42.9 4.0 %all-to-all-start.1 = ((f32[16,56,128]{2,1,0:T(8,128)}), f32[16,56,128]{2,1,0:T(8,128)S(1)}, u32[]{:S(2)}, u32[]{:S(2)}) async-start(f32[16,56,128]{2,1,0:T(8,128)} %broadcast_in_dim.49), calls=%async_computation.1 | async-start | bytes 917504 | tf_op jit(solution)/shard_map/all_to_all | solution.py:81
  46.9 0.0 copy-done.3
  46.9 6.2 %convolution_reduce_fusion = f32[8,16,16,64]{3,2,1,0:T(8,128)S(1)} fusion(bf16[3,3,3,64,128]{4,3,2,1,0:T(8,128)(2,1)S(1)} %bitcast.56, bf16[1,5,9,9,128]{4,3,2,1,0:T(8,128)(2,1)S(1)} %bitcast.67), kind=kOutput, calls=%fused_computation.12 | convolution fusion | flops 113246208 | bytes 1070336 | tf_op jit(solution)/shard_map/conv_general_dilated | solution.py:154
  53.1 0.3 mul.84
  53.4 0.3 mul.85
  53.8 0.0 copy-start.2
  53.8 0.3 squeeze.6
  54.1 0.6 copy-done.2
  54.7 0.8 %multiply_convert_fusion = bf16[1,1,8,16,1024]{4,3,2,1,0:T(8,128)(2,1)} fusion(f32[1,1,8,16,1024]{4,3,2,1,0:T(8,128)S(1)} %mul.85, f32[1,1,8,16,1024]{4,3,2,1,0:T(8,128)S(1)} %squeeze.6, bf16[1,1,8,16,1024]{4,3,2,1,0:T(8,128)(2,1)S(1)} %copy-done.2), kind=kLoop, calls=%fused_computation.19 | loop fusion | flops 524288 | bytes 1572864 | tf_op jit(solution)/shard_map/convert_element_type | solution.py:166
  55.5 4.7 %all-to-all-done.1 = f32[16,56,128]{2,1,0:T(8,128)S(1)} async-done(((f32[16,56,128]{2,1,0:T(8,128)}), f32[16,56,128]{2,1,0:T(8,128)S(1)}, u32[]{:S(2)}, u32[]{:S(2)}) %all-to-all-start.1) | async-done | bytes 458784 | tf_op jit(solution)/shard_map/all_to_all | solution.py:81
  60.2 0.1 collective-permute-start.3
  60.3 0.1 broadcast_in_dim.52
  60.4 1.6 %collective-permute-done.3 = f32[27,32,128]{2,1,0:T(8,128)S(1)} collective-permute-done((f32[27,32,128]{2,1,0:T(8,128)S(1)}, f32[27,32,128]{2,1,0:T(8,128)S(1)}, u32[]{:S(2)}, u32[]{:S(2)}) %collective-permute-start.3) | collective-permute-done | bytes 442400 | tf_op jit(solution)/shard_map/ppermute | solution.py:84
  62.1 0.0 copy-start.1
  62.1 0.9 %copy-done.1 = f32[27,2,32,128]{3,2,1,0:T(8,128)} copy-done((f32[27,2,32,128]{3,2,1,0:T(8,128)}, f32[27,2,32,128]{3,2,1,0:T(8,128)S(1)}, u32[]{:S(2)}) %copy-start.1) | copy-done | bytes 884760
  (18 shorter events, 0.3 us)
Async XLA Ops:
  0.6 27.9 %copy-start = (bf16[27,64,128]{2,1,0:T(8,128)(2,1)S(1)}, bf16[27,64,128]{2,1,0:T(8,128)(2,1)}, u32[]{:S(2)}) copy-start(bf16[27,64,128]{2,1,0:T(8,128)(2,1)} %param.10) | copy-start | bytes 1327108
  0.6 2.7 %copy-start.6 = (s32[1,1,256]{2,1,0:T(1,128)S(1)}, s32[1,1,256]{2,1,0:T(1,128)}, u32[]{:S(2)}) copy-start(s32[1,1,256]{2,1,0:T(1,128)} %param.7) | copy-start | bytes 3076
  0.7 2.8 %copy-start.4 = (bf16[1,1,4,8,1024]{4,3,2,1,0:T(8,128)(2,1)S(1)}, bf16[1,1,4,8,1024]{4,3,2,1,0:T(8,128)(2,1)}, u32[]{:S(2)}) copy-start(bf16[1,1,4,8,1024]{4,3,2,1,0:T(8,128)(2,1)} %param.6) | copy-start | bytes 196612
  3.6 5.9 %collective-permute-start = (bf16[12288]{0:T(1024)(128)(2,1)S(1)}, bf16[12288]{0:T(1024)(128)(2,1)S(1)}, u32[]{:S(2)}, u32[]{:S(2)}) collective-permute-start(bf16[12288]{0:T(1024)(128)(2,1)S(1)} %pad_maximum_fusion.2), channel_id=1, source_target_pairs={{16,0},{24,8},{0,16},{8,24},{17,1},{25,9},{1,17},{9,25},{18,2},{26... | collective-permute-start | bytes 73736 | tf_op jit(solution)/shard_map/ppermute | solution.py:63
  10.1 3.9 %collective-permute-start.1 = (bf16[13312]{0:T(1024)(128)(2,1)S(1)}, bf16[13312]{0:T(1024)(128)(2,1)S(1)}, u32[]{:S(2)}, u32[]{:S(2)}) collective-permute-start(bf16[13312]{0:T(1024)(128)(2,1)S(1)} %pad_maximum_fusion.1), channel_id=1, source_target_pairs={{8,0},{24,16},{0,8},{16,24},{9,1},{25,17},{1,9},{17,25},{10,2},{26... | collective-permute-start | bytes 79880 | tf_op jit(solution)/shard_map/ppermute | solution.py:63
  14.5 3.5 %copy-start.5 = (s32[1,1,2048]{2,1,0:T(1,128)S(1)}, s32[1,1,2048]{2,1,0:T(1,128)}, u32[]{:S(2)}) copy-start(s32[1,1,2048]{2,1,0:T(1,128)} %param.9) | copy-start | bytes 24580
  17.5 2.1 %collective-permute-start.2 = (f32[27,32,128]{2,1,0:T(8,128)S(1)}, f32[27,32,128]{2,1,0:T(8,128)S(1)}, u32[]{:S(2)}, u32[]{:S(2)}) collective-permute-start(f32[27,32,128]{2,1,0:T(8,128)S(1)} %constant_dynamic-slice_fusion), channel_id=1, source_target_pairs={{0,1},{1,0},{2,3},{3,2},{4,5},{5,4},{6,7},{7,6},{8,9},{9,8},{10,11... | collective-permute-start | bytes 1327112 | tf_op jit(solution)/shard_map/ppermute | solution.py:134
  20.4 21.7 %all-to-all-start = ((f32[16,56,128]{2,1,0:T(8,128)}), f32[16,56,128]{2,1,0:T(8,128)S(1)}, u32[]{:S(2)}, u32[]{:S(2)}) async-start(f32[16,56,128]{2,1,0:T(8,128)} %bitcast.7), calls=%async_computation | async-start | bytes 917504 | tf_op jit(solution)/shard_map/all_to_all | solution.py:74
  28.3 0.7 %copy-start.7 = (pred[8,2]{0,1:T(4,128)(4,1)S(1)}, pred[8,2]{0,1:T(4,128)(4,1)}, u32[]{:S(2)}) copy-start(pred[8,2]{0,1:T(4,128)(4,1)} %constant.76) | copy-start | bytes 52
  29.7 17.2 %copy-start.3 = (bf16[5,9,9,128]{3,2,1,0:T(8,128)(2,1)S(1)}, bf16[5,9,9,128]{3,2,1,0:T(8,128)(2,1)}, u32[]{:S(2)}) copy-start(bf16[5,9,9,128]{3,2,1,0:T(8,128)(2,1)} %fusion.24) | copy-start | bytes 311044
  42.9 17.2 %all-to-all-start.1 = ((f32[16,56,128]{2,1,0:T(8,128)}), f32[16,56,128]{2,1,0:T(8,128)S(1)}, u32[]{:S(2)}, u32[]{:S(2)}) async-start(f32[16,56,128]{2,1,0:T(8,128)} %broadcast_in_dim.49), calls=%async_computation.1 | async-start | bytes 917504 | tf_op jit(solution)/shard_map/all_to_all | solution.py:81
  53.8 1.0 %copy-start.2 = (bf16[1,1,8,16,1024]{4,3,2,1,0:T(8,128)(2,1)S(1)}, bf16[1,1,8,16,1024]{4,3,2,1,0:T(8,128)(2,1)}, u32[]{:S(2)}) copy-start(bf16[1,1,8,16,1024]{4,3,2,1,0:T(8,128)(2,1)} %param.8) | copy-start | bytes 786436
  60.2 1.9 %collective-permute-start.3 = (f32[27,32,128]{2,1,0:T(8,128)S(1)}, f32[27,32,128]{2,1,0:T(8,128)S(1)}, u32[]{:S(2)}, u32[]{:S(2)}) collective-permute-start(f32[27,32,128]{2,1,0:T(8,128)S(1)} %bitcast.60), channel_id=1, source_target_pairs={{0,1},{1,0},{2,3},{3,2},{4,5},{5,4},{6,7},{7,6},{8,9},{9,8},{10,11... | collective-permute-start | bytes 1327112 | tf_op jit(solution)/shard_map/ppermute | solution.py:84
  62.1 0.9 %copy-start.1 = (f32[27,2,32,128]{3,2,1,0:T(8,128)}, f32[27,2,32,128]{3,2,1,0:T(8,128)S(1)}, u32[]{:S(2)}) copy-start(f32[27,2,32,128]{3,2,1,0:T(8,128)S(1)} %bitcast_dynamic-update-slice_fusion) | copy-start | bytes 2654212

commit v18 on v14

--- a/solution.py
+++ b/solution.py
@@ -133,8 +133,8 @@
     theirs = lax.dynamic_slice_in_dim(full, (1 - core) * share, share, axis=1)
     got = lax.ppermute(theirs, "core", [(0, 1), (1, 0)])
     grads = lax.dynamic_slice_in_dim(full, core * share, share, axis=1) + got
-    grads, extended, weight_late, skip, fine_keep = lax.optimization_barrier(
-        (grads, extended, up_weight, skip, fine_keep)
+    grads, weight_late, skip, fine_keep = lax.optimization_barrier(
+        (grads, up_weight, skip, fine_keep)
     )
     reduced, plan = all_reduce(grads)
 

time: 63.5 us -> 63.4 us (level)
  other arithmetic: 4.95 us -> 4.28 us
  local copies, waits for them, and re-layouts: 8.19 us -> 8.83 us
    concatenate x1 -> x0, other arithmetic: 0.71 us -> none  [body(): extended = jnp.concatenate([extended, got_masked], axis=axis)]
    reshape x1, local copies, waits for them, and re-layouts: 0.08 us -> 0.71 us  [body(): fine_keep = fine_mask.reshape(fine_x, fine_y, fine_z, 1)]
where the time goes in v18:
time: 63.4 us; the launch traced here: 62.9 us
  waiting for transfers between devices  21.4 us (34%)
  starting transfers between devices  17.7 us (28%)
  matrix products  9.78 us (15%)
  local copies, waits for them, and re-layouts  8.83 us (14%)
  other arithmetic  4.28 us (7%)
  between operations  1.01 us (2%)
    all_to_all x1, waiting for transfers between devices, all_reduce(): lax.all_to_all(rows.reshape(devices, chunk, lanes), OTHERS, 0, 0, tiled=T...  11.5 us
    all_to_all x1, starting transfers between devices, all_reduce(): lax.all_to_all(rows.reshape(devices, chunk, lanes), OTHERS, 0, 0, tiled=T...  7.37 us
    ppermute x2, starting transfers between devices, halo_exchange(): got = lax.ppermute(packed, 'brick', both)  6.19 us
    conv_general_dilated x1, matrix products, body(): lax.conv_general_dilated(extended[None], flipped, (1, 1, 1), ((1, 0), (1,...  6.18 us
    all_to_all x1, waiting for transfers between devices, all_spread(): half = lax.all_to_all(spread, OTHERS, 0, 0, tiled=True)  4.65 us
    all_to_all x1, starting transfers between devices, all_spread(): half = lax.all_to_all(spread, OTHERS, 0, 0, tiled=True)  3.97 us
    ppermute x2, waiting for transfers between devices, halo_exchange(): got = lax.ppermute(packed, 'brick', both)  3.63 us
    conv_general_dilated x1, matrix products, body(): lax.conv_general_dilated(widened[..., None], masked[..., None], (1, 1, 1)...  2.85 us
  transfers between devices with their start and end apart: 6, of which 5 were waited for; matrix products, arithmetic and copies ran while one was open for 20% of the time, Pallas kernels for 0%

profile of v18, /device:TPU:0, one launch (start us, length us, event | category | flops | bytes accessed | tf_op | source)
XLA Modules:
  0.0 62.9 jit_solution(15262506927460749607)
XLA Ops:
  0.6 0.0 copy-start
  0.6 0.0 copy-start.6
  0.7 0.0 copy-start.4
  0.7 1.4 %reshape.149 = bf16[8,16,16,64]{3,2,1,0:T(8,128)(2,1)S(1)} reshape(bf16[1,1,8,16,1024]{4,3,2,1,0:T(8,128)(2,1)} %param.11) | data formatting | bytes 524288 | tf_op jit(solution)/shard_map/reshape | solution.py:105
  2.1 0.7 %convert_reduce_fusion = bf16[2048]{0:T(1024)(128)(2,1)S(1)} fusion(s32[1,1,2048]{2,1,0:T(1,128)} %param.9), kind=kLoop, calls=%fused_computation.50 | loop fusion | flops 2048 | bytes 12288 | tf_op jit(solution)/shard_map/convert_element_type | solution.py:105
  2.8 0.1 convert_element_type.59
  2.9 0.3 broadcast_multiply_fusion
  3.2 0.2 fusion.28
  3.5 0.1 select_n.81
  3.6 0.0 copy-done.6
  3.6 0.1 convert_element_type.57
  3.7 0.0 copy-done.4
  3.7 0.1 bitcast_multiply_fusion
  3.8 0.1 fusion.31
  3.9 3.1 %collective-permute-start = (bf16[12288]{0:T(1024)(128)(2,1)S(1)}, bf16[12288]{0:T(1024)(128)(2,1)S(1)}, u32[]{:S(2)}, u32[]{:S(2)}) collective-permute-start(bf16[12288]{0:T(1024)(128)(2,1)S(1)} %pad_maximum_fusion.2), channel_id=1, source_target_pairs={{8,0},{24,16},{0,8},{16,24},{9,1},{25,17},{1,9},{17,25},{10,2},{26... | collective-permute-start | bytes 73736 | tf_op jit(solution)/shard_map/ppermute | solution.py:63
  7.0 1.8 %collective-permute-done = bf16[12288]{0:T(1024)(128)(2,1)S(1)} collective-permute-done((bf16[12288]{0:T(1024)(128)(2,1)S(1)}, bf16[12288]{0:T(1024)(128)(2,1)S(1)}, u32[]{:S(2)}, u32[]{:S(2)}) %collective-permute-start) | collective-permute-done | bytes 24608 | tf_op jit(solution)/shard_map/ppermute | solution.py:63
  8.8 0.1 reshape.177
  8.9 0.1 select_n.86
  9.1 3.1 %collective-permute-start.1 = (bf16[13312]{0:T(1024)(128)(2,1)S(1)}, bf16[13312]{0:T(1024)(128)(2,1)S(1)}, u32[]{:S(2)}, u32[]{:S(2)}) collective-permute-start(bf16[13312]{0:T(1024)(128)(2,1)S(1)} %pad_maximum_fusion.1), channel_id=1, source_target_pairs={{16,0},{24,8},{0,16},{8,24},{17,1},{25,9},{1,17},{9,25},{18,2},{26... | collective-permute-start | bytes 79880 | tf_op jit(solution)/shard_map/ppermute | solution.py:63
  12.2 1.8 %collective-permute-done.1 = bf16[13312]{0:T(1024)(128)(2,1)S(1)} collective-permute-done((bf16[13312]{0:T(1024)(128)(2,1)S(1)}, bf16[13312]{0:T(1024)(128)(2,1)S(1)}, u32[]{:S(2)}, u32[]{:S(2)}) %collective-permute-start.1) | collective-permute-done | bytes 26656 | tf_op jit(solution)/shard_map/ppermute | solution.py:63
  14.0 0.1 reshape.151
  14.1 0.4 fusion.37
  14.5 0.0 copy-start.5
  14.5 2.9 %fusion.11 = f32[3,3,3,64,128]{4,3,2,1,0:T(8,128)S(1)} fusion(bf16[9,17,17,64,1]{3,2,1,0,4:T(8,128)(2,1)S(1)} %get-tuple-element.18, bf16[4,8,8,128,1]{3,1,2,0,4:T(8,128)(2,1)S(1)} %bitcast.68, bf16[4,8,8]{2,1,0:T(8,128)(2,1)S(1)} %convert_element_type.57), kind=kOutput, calls=%fused_computation.13 | convolution fusion | flops 113377280 | bytes 1283712 | tf_op jit(solution)/shard_map/conv_general_dilated | solution.py:122
  17.4 0.1 collective-permute-start.2
  17.5 0.5 broadcast.90
  18.0 0.0 copy-done.5
  18.0 0.7 %reduce.15 = s32[2048]{0:T(1024)S(1)} reduce(s32[1,1,2048]{2,1,0:T(1,128)S(1)} %copy-done.5, s32[]{:T(128)} %broadcast.90), dimensions={0,1}, to_apply=%param.9.reduce_sub_computation.3 | reduce | bytes 16388 | tf_op args[3]
  18.7 0.7 %reshape.154 = s32[8,16,16,1]{2,1,0,3:T(8,128)} reshape(s32[2048]{0:T(1024)S(1)} %reduce.15) | data formatting | bytes 16384 | tf_op jit(solution)/shard_map/reshape | solution.py:104
  19.4 0.0 collective-permute-done.2
  19.4 0.1 dynamic-slice_add_fusion
  19.5 0.8 %pad.6 = f32[896,128]{1,0:T(8,128)} pad(f32[864,128]{1,0:T(8,128)S(1)} %bitcast.60, f32[]{:T(128)} %constant.58.clone.1), padding=0_32x0_0 | pad | bytes 901124 | tf_op jit(solution)/shard_map/jit(_pad)/pad | solution.py:73
  20.3 7.4 %all-to-all-start = ((f32[16,56,128]{2,1,0:T(8,128)}), f32[16,56,128]{2,1,0:T(8,128)S(1)}, u32[]{:S(2)}, u32[]{:S(2)}) async-start(f32[16,56,128]{2,1,0:T(8,128)} %bitcast.6), calls=%async_computation | async-start | bytes 917504 | tf_op jit(solution)/shard_map/all_to_all | solution.py:74
  27.7 0.1 copy.35
  27.8 0.2 pad.7
  28.0 0.2 copy.33
  28.2 0.0 copy-start.7
  28.3 0.2 slice.63
  28.4 0.0 copy-done
  28.4 0.5 copy-done.7
  28.9 0.8 %fusion.13 = f32[4,8,8,2,128]{4,2,3,1,0:T(8,128)S(1)} fusion(bf16[3,3,3,64,128]{4,3,2,1,0:T(8,128)(2,1)S(1)} %bitcast.55, bf16[9,17,1,7,2,64]{5,3,4,1,0,2:T(8,128)(2,1)S(1)} %slice.63, bf16[9,17,1,8,4,64]{5,3,4,1,0,2:T(8,128)(2,1)S(1)} %copy.33, pred[8,2]{0,1:T(4,128)(4,1)S(1)} %copy-done.7), kind=kOutput, calls=%fused_computation.15 | convolution fusion | flops 229378048 | bytes 1605392 | tf_op jit(solution)/shard_map/conv_general_dilated | solution.py:141
  29.7 0.1 copy.34
  29.8 0.7 %fusion.27 = bf16[1,1,4,8,1024]{4,3,2,1,0:T(8,128)(2,1)} fusion(f32[4,8,1,16,128]{4,1,3,0,2:T(8,128)S(1)} %bitcast.64, f32[4,8,8]{1,2,0:T(8,128)S(1)} %copy.35), kind=kLoop, calls=%fused_computation.33 | loop fusion | flops 65536 | bytes 197632 | tf_op jit(solution)/shard_map/convert_element_type | solution.py:150
  30.5 11.5 %all-to-all-done = f32[16,56,128]{2,1,0:T(8,128)S(1)} async-done(((f32[16,56,128]{2,1,0:T(8,128)}), f32[16,56,128]{2,1,0:T(8,128)S(1)}, u32[]{:S(2)}, u32[]{:S(2)}) %all-to-all-start) | async-done | bytes 458784 | tf_op jit(solution)/shard_map/all_to_all | solution.py:74
  42.0 0.8 %broadcast_in_dim.49 = f32[16,56,128]{2,1,0:T(8,128)} broadcast(f32[56,128]{1,0:T(8,128)S(1)} %broadcast_multiply_fusion.1), dimensions={1,2} | broadcast | bytes 487424 | tf_op jit(solution)/shard_map/broadcast_in_dim | solution.py:80
  42.8 4.0 %all-to-all-start.1 = ((f32[16,56,128]{2,1,0:T(8,128)}), f32[16,56,128]{2,1,0:T(8,128)S(1)}, u32[]{:S(2)}, u32[]{:S(2)}) async-start(f32[16,56,128]{2,1,0:T(8,128)} %broadcast_in_dim.49), calls=%async_computation.1 | async-start | bytes 917504 | tf_op jit(solution)/shard_map/all_to_all | solution.py:81
  46.8 0.0 copy-start.2
  46.8 6.2 %convolution_reduce_fusion = f32[8,16,16,64]{3,2,1,0:T(8,128)S(1)} fusion(bf16[3,3,3,64,128]{4,3,2,1,0:T(8,128)(2,1)S(1)} %bitcast.54, bf16[1,5,9,9,128]{4,3,2,1,0:T(8,128)(2,1)S(1)} %fusion.25), kind=kOutput, calls=%fused_computation.12 | convolution fusion | flops 113246208 | bytes 1070336 | tf_op jit(solution)/shard_map/conv_general_dilated | solution.py:154
  53.0 0.0 copy-done.2
  53.0 0.3 mul.84
  53.4 0.3 mul.85
  53.7 0.0 copy-start.3
  53.7 0.3 squeeze.6
  54.0 0.6 copy-done.3
  54.6 0.8 %multiply_convert_fusion = bf16[1,1,8,16,1024]{4,3,2,1,0:T(8,128)(2,1)} fusion(f32[1,1,8,16,1024]{4,3,2,1,0:T(8,128)S(1)} %mul.85, f32[1,1,8,16,1024]{4,3,2,1,0:T(8,128)S(1)} %squeeze.6, bf16[1,1,8,16,1024]{4,3,2,1,0:T(8,128)(2,1)S(1)} %copy-done.3), kind=kLoop, calls=%fused_computation.19 | loop fusion | flops 524288 | bytes 1572864 | tf_op jit(solution)/shard_map/convert_element_type | solution.py:166
  55.4 4.6 %all-to-all-done.1 = f32[16,56,128]{2,1,0:T(8,128)S(1)} async-done(((f32[16,56,128]{2,1,0:T(8,128)}), f32[16,56,128]{2,1,0:T(8,128)S(1)}, u32[]{:S(2)}, u32[]{:S(2)}) %all-to-all-start.1) | async-done | bytes 458784 | tf_op jit(solution)/shard_map/all_to_all | solution.py:81
  60.1 0.1 collective-permute-start.3
  60.2 0.1 broadcast_in_dim.52
  60.3 1.6 %collective-permute-done.3 = f32[27,32,128]{2,1,0:T(8,128)S(1)} collective-permute-done((f32[27,32,128]{2,1,0:T(8,128)S(1)}, f32[27,32,128]{2,1,0:T(8,128)S(1)}, u32[]{:S(2)}, u32[]{:S(2)}) %collective-permute-start.3) | collective-permute-done | bytes 442400 | tf_op jit(solution)/shard_map/ppermute | solution.py:84
  62.0 0.0 copy-start.1
  62.0 0.9 %copy-done.1 = f32[27,2,32,128]{3,2,1,0:T(8,128)} copy-done((f32[27,2,32,128]{3,2,1,0:T(8,128)}, f32[27,2,32,128]{3,2,1,0:T(8,128)S(1)}, u32[]{:S(2)}) %copy-start.1) | copy-done | bytes 884760
  (20 shorter events, 0.4 us)
Async XLA Ops:
  0.6 27.8 %copy-start = (bf16[27,64,128]{2,1,0:T(8,128)(2,1)S(1)}, bf16[27,64,128]{2,1,0:T(8,128)(2,1)}, u32[]{:S(2)}) copy-start(bf16[27,64,128]{2,1,0:T(8,128)(2,1)} %param.10) | copy-start | bytes 1327108
  0.6 2.9 %copy-start.6 = (s32[1,1,256]{2,1,0:T(1,128)S(1)}, s32[1,1,256]{2,1,0:T(1,128)}, u32[]{:S(2)}) copy-start(s32[1,1,256]{2,1,0:T(1,128)} %param.7) | copy-start | bytes 3076
  0.7 3.0 %copy-start.4 = (bf16[1,1,4,8,1024]{4,3,2,1,0:T(8,128)(2,1)S(1)}, bf16[1,1,4,8,1024]{4,3,2,1,0:T(8,128)(2,1)}, u32[]{:S(2)}) copy-start(bf16[1,1,4,8,1024]{4,3,2,1,0:T(8,128)(2,1)} %param.6) | copy-start | bytes 196612
  3.9 4.9 %collective-permute-start = (bf16[12288]{0:T(1024)(128)(2,1)S(1)}, bf16[12288]{0:T(1024)(128)(2,1)S(1)}, u32[]{:S(2)}, u32[]{:S(2)}) collective-permute-start(bf16[12288]{0:T(1024)(128)(2,1)S(1)} %pad_maximum_fusion.2), channel_id=1, source_target_pairs={{8,0},{24,16},{0,8},{16,24},{9,1},{25,17},{1,9},{17,25},{10,2},{26... | collective-permute-start | bytes 73736 | tf_op jit(solution)/shard_map/ppermute | solution.py:63
  9.1 4.9 %collective-permute-start.1 = (bf16[13312]{0:T(1024)(128)(2,1)S(1)}, bf16[13312]{0:T(1024)(128)(2,1)S(1)}, u32[]{:S(2)}, u32[]{:S(2)}) collective-permute-start(bf16[13312]{0:T(1024)(128)(2,1)S(1)} %pad_maximum_fusion.1), channel_id=1, source_target_pairs={{16,0},{24,8},{0,16},{8,24},{17,1},{25,9},{1,17},{9,25},{18,2},{26... | collective-permute-start | bytes 79880 | tf_op jit(solution)/shard_map/ppermute | solution.py:63
  14.5 3.5 %copy-start.5 = (s32[1,1,2048]{2,1,0:T(1,128)S(1)}, s32[1,1,2048]{2,1,0:T(1,128)}, u32[]{:S(2)}) copy-start(s32[1,1,2048]{2,1,0:T(1,128)} %param.9) | copy-start | bytes 24580
  17.4 2.0 %collective-permute-start.2 = (f32[27,32,128]{2,1,0:T(8,128)S(1)}, f32[27,32,128]{2,1,0:T(8,128)S(1)}, u32[]{:S(2)}, u32[]{:S(2)}) collective-permute-start(f32[27,32,128]{2,1,0:T(8,128)S(1)} %constant_dynamic-slice_fusion), channel_id=1, source_target_pairs={{0,1},{1,0},{2,3},{3,2},{4,5},{5,4},{6,7},{7,6},{8,9},{9,8},{10,11... | collective-permute-start | bytes 1327112 | tf_op jit(solution)/shard_map/ppermute | solution.py:134
  20.3 21.7 %all-to-all-start = ((f32[16,56,128]{2,1,0:T(8,128)}), f32[16,56,128]{2,1,0:T(8,128)S(1)}, u32[]{:S(2)}, u32[]{:S(2)}) async-start(f32[16,56,128]{2,1,0:T(8,128)} %bitcast.6), calls=%async_computation | async-start | bytes 917504 | tf_op jit(solution)/shard_map/all_to_all | solution.py:74
  28.2 0.7 %copy-start.7 = (pred[8,2]{0,1:T(4,128)(4,1)S(1)}, pred[8,2]{0,1:T(4,128)(4,1)}, u32[]{:S(2)}) copy-start(pred[8,2]{0,1:T(4,128)(4,1)} %constant.76) | copy-start | bytes 52
  42.8 17.2 %all-to-all-start.1 = ((f32[16,56,128]{2,1,0:T(8,128)}), f32[16,56,128]{2,1,0:T(8,128)S(1)}, u32[]{:S(2)}, u32[]{:S(2)}) async-start(f32[16,56,128]{2,1,0:T(8,128)} %broadcast_in_dim.49), calls=%async_computation.1 | async-start | bytes 917504 | tf_op jit(solution)/shard_map/all_to_all | solution.py:81
  46.8 6.2 %copy-start.2 = (s32[8,16,16,1]{2,1,0,3:T(8,128)S(1)}, s32[8,16,16,1]{2,1,0,3:T(8,128)}, u32[]{:S(2)}) copy-start(s32[8,16,16,1]{2,1,0,3:T(8,128)} %reshape.154) | copy-start | bytes 24580
  53.7 1.0 %copy-start.3 = (bf16[1,1,8,16,1024]{4,3,2,1,0:T(8,128)(2,1)S(1)}, bf16[1,1,8,16,1024]{4,3,2,1,0:T(8,128)(2,1)}, u32[]{:S(2)}) copy-start(bf16[1,1,8,16,1024]{4,3,2,1,0:T(8,128)(2,1)} %param.8) | copy-start | bytes 786436
  60.1 1.9 %collective-permute-start.3 = (f32[27,32,128]{2,1,0:T(8,128)S(1)}, f32[27,32,128]{2,1,0:T(8,128)S(1)}, u32[]{:S(2)}, u32[]{:S(2)}) collective-permute-start(f32[27,32,128]{2,1,0:T(8,128)S(1)} %bitcast.58), channel_id=1, source_target_pairs={{0,1},{1,0},{2,3},{3,2},{4,5},{5,4},{6,7},{7,6},{8,9},{9,8},{10,11... | collective-permute-start | bytes 1327112 | tf_op jit(solution)/shard_map/ppermute | solution.py:84
  62.0 0.9 %copy-start.1 = (f32[27,2,32,128]{3,2,1,0:T(8,128)}, f32[27,2,32,128]{3,2,1,0:T(8,128)S(1)}, u32[]{:S(2)}) copy-start(f32[27,2,32,128]{3,2,1,0:T(8,128)S(1)} %bitcast_dynamic-update-slice_fusion) | copy-start | bytes 2654212
